TPU v7x, 32 devices: a whole 2x2x4 slice. The times are simulated.
32 devices in a mesh: segment: 4 (over z), ctx: 4 (over y, x), head: 2 (over core).
Axes of the slice: x: 2, y: 2, z: 4, core: 2. Of those that a mesh axis runs over, the one named last changes fastest.
Arguments:
- inputs: bfloat16 [4, 512, 5120], P('segment', 'ctx'), may hold values from -6 to 6
- query: bfloat16 [4, 512, 20, 128], P('segment', 'ctx', 'head'), may hold values from -32 to 32
- grad_out: bfloat16 [4, 512, 20, 128], P('segment', 'ctx', 'head'), may hold values from -6 to 6
- w_key: bfloat16 [4, 5120, 512], P('segment', None, 'head'), may hold values from -0.078125 to 0.078125
- w_value: bfloat16 [4, 5120, 512], P('segment', None, 'head'), may hold values from -0.078125 to 0.078125
- keep_mask: int32 [512], replicated, may hold values from 0 to 1
Outputs:
- grad_input: float32 [4, 512, 5120], P('segment', 'ctx', 'head')
All inputs are finite; a program needn't handle non-finite values.
Results may differ from a plain program's by a relative error of at most 0.022.
The roundings to bfloat16 on the way count: a program that leaves them out, or rounds other values in their place, can miss the bound.
Values may be sent and summed in bfloat16 or wider, within the bound.
No kernel may reach another device: no remote copies, remote signals or barrier semaphores. Data moves between devices by JAX's collectives and lax.ppermute only.
A program may use at most 192 MiB of HBM per device.

v0:
```python
import math

import jax
import jax.numpy as jnp
from jax import lax
from jax.sharding import PartitionSpec as P


def prefix(shard, axis, combine, identity):
    length, index = (lax.axis_size(axis), lax.axis_index(axis))
    everything = lax.all_gather(shard.astype(jnp.bfloat16), axis)
    start = jnp.broadcast_to(jnp.asarray(identity, shard.dtype), shard.shape)

    def hop(k, before):
        at = length - 1 - k
        reached = at > index
        new = combine(before, everything[at].astype(shard.dtype))
        return jnp.where(reached, new, before)

    return lax.fori_loop(0, length, hop, start)


def add_terms(earlier, later):
    return earlier + later


def per_device(inputs, query, grad_out, w_key, w_value, keep_mask):
    tok_rows = inputs.shape[1]
    local_heads = query.shape[2]
    head_dim = query.shape[3]
    kv_cols = w_key.shape[2]
    kv_local = kv_cols // head_dim
    group_size = local_heads // kv_local
    scaling = 1.0 / math.sqrt(head_dim)
    tokens = inputs[0]
    key_rows = jnp.dot(tokens, w_key[0], preferred_element_type=jnp.float32).astype(jnp.bfloat16)
    value_rows = jnp.dot(tokens, w_value[0], preferred_element_type=jnp.float32).astype(
        jnp.bfloat16
    )
    keys_all, values_all = (
        lax.all_gather(key_rows, "ctx", axis=0, tiled=True),
        lax.all_gather(value_rows, "ctx", axis=0, tiled=True),
    )
    seq_rows = keys_all.shape[0]
    key_heads = keys_all.reshape(seq_rows, kv_local, head_dim)
    value_heads = values_all.reshape(seq_rows, kv_local, head_dim)
    query_heads = query[0].reshape(tok_rows, kv_local, group_size, head_dim)
    grad_heads = grad_out[0].reshape(tok_rows, kv_local, group_size, head_dim)
    query_major = jnp.moveaxis(query_heads, 1, 0)
    grad_major = jnp.moveaxis(grad_heads, 1, 0)
    ctx_index = lax.axis_index("ctx")
    first_row = ctx_index * tok_rows
    row_pos = first_row + jnp.arange(tok_rows, dtype=jnp.int32)[:, None]
    col_pos = jnp.arange(seq_rows, dtype=jnp.int32)[None, :]
    allowed = (col_pos <= row_pos) & ((keep_mask[None, :] == 1) | (col_pos == row_pos))

    def one_group(packed):
        query_group, grad_group, key_group, value_group = packed
        scores = (
            jnp.einsum("tgd,sd->gts", query_group, key_group, preferred_element_type=jnp.float32)
            * scaling
        )
        masked = jnp.where(allowed, scores, -1e30)
        top_score = jnp.max(masked, axis=-1, keepdims=True)
        totals = jnp.sum(
            jnp.where(allowed, jnp.exp(masked - top_score), 0.0), axis=-1, keepdims=True
        )
        log_total = top_score + jnp.log(totals)
        prob_full = jnp.where(allowed, jnp.exp(masked - log_total), 0.0)
        prob_low = prob_full.astype(jnp.bfloat16)
        attended = jnp.einsum(
            "gts,sd->tgd", prob_low, value_group, preferred_element_type=jnp.float32
        )
        row_dots = jnp.sum(grad_group.astype(jnp.float32) * attended, axis=-1)
        dprob = jnp.einsum(
            "tgd,sd->gts", grad_group, value_group, preferred_element_type=jnp.float32
        )
        score_low = (prob_full * (dprob - jnp.transpose(row_dots, (1, 0))[..., None])).astype(
            jnp.bfloat16
        )
        return (prob_low, score_low)

    probs_b, dscore_b = lax.map(
        one_group,
        (query_major, grad_major, jnp.moveaxis(key_heads, 1, 0), jnp.moveaxis(value_heads, 1, 0)),
    )

    def per_group(packed):
        prob_group, score_group, query_group, grad_group = packed
        value_term = jnp.einsum(
            "gts,tgd->sd", prob_group, grad_group, preferred_element_type=jnp.float32
        )
        key_term = (
            jnp.einsum("gts,tgd->sd", score_group, query_group, preferred_element_type=jnp.float32)
            * scaling
        )
        return (key_term, value_term)

    key_term, value_term = lax.map(per_group, (probs_b, dscore_b, query_major, grad_major))
    key_flat = jnp.moveaxis(key_term, 0, 1).reshape(tok_rows * lax.axis_size("ctx"), kv_cols)
    value_flat = jnp.moveaxis(value_term, 0, 1).reshape(tok_rows * lax.axis_size("ctx"), kv_cols)
    key_grads = lax.psum_scatter(
        jnp.concatenate((key_flat, value_flat), axis=1).astype(jnp.bfloat16),
        "ctx",
        scatter_dimension=0,
        tiled=True,
    ).astype(jnp.float32)
    grad_key = key_grads[:, :kv_cols].astype(jnp.bfloat16)
    grad_value = key_grads[:, kv_cols:].astype(jnp.bfloat16)
    contract = (((1,), (1,)), ((), ()))
    partial_sum = lax.dot_general(grad_key, w_key[0], contract, preferred_element_type=jnp.float32)
    partial_sum = partial_sum + lax.dot_general(
        grad_value, w_value[0], contract, preferred_element_type=jnp.float32
    )
    reduced = lax.psum_scatter(
        partial_sum.astype(jnp.bfloat16), "head", scatter_dimension=1, tiled=True
    ).astype(jnp.float32)
    later = prefix(reduced, "segment", add_terms, jnp.zeros_like(reduced))
    result = reduced + later
    return result[None]


def solution(mesh):
    return jax.shard_map(
        per_device,
        mesh=mesh,
        in_specs=(
            P("segment", "ctx", None),
            P("segment", "ctx", "head", None),
            P("segment", "ctx", "head", None),
            P("segment", None, "head"),
            P("segment", None, "head"),
            P(),
        ),
        out_specs=P("segment", "ctx", "head"),
        check_vma=False,
    )
```

profile of v0, /device:TPU:0, one launch (start us, length us, event | category | flops | bytes accessed | tf_op | source)
XLA Modules:
  0.0 164.7 jit_solution(11332315639558818829)
XLA Ops:
  6.5 0.0 copy-start
  6.5 0.0 reduce-scatter.7.cloned.1.call-start
  6.6 0.0 copy-start.3
  6.6 2.8 %fusion.57 = bf16[128,256]{1,0:T(8,128)(2,1)S(1)} fusion(bf16[1,5120,256]{2,1,0:T(8,128)(2,1)} %param.16, bf16[1,128,5120]{2,1,0:T(8,128)(2,1)} %param.12), kind=kOutput, calls=%fused_computation.66 | convolution fusion | flops 335577088 | bytes 3997696 | tf_op jit(solution)/shard_map/dot_general | solution.py:37
  9.4 10.5 %all_gather.13 = bf16[512,256]{1,0:T(8,128)(2,1)S(1)} all-gather(bf16[128,256]{1,0:T(8,128)(2,1)S(1)} %fusion.57), channel_id=1, replica_groups=mesh['segment'=4,'ctx'=4,'head'=2] {'ctx'}, dimensions={0}, use_global_device_ids=true | all-gather | bytes 327680 | tf_op jit(solution)/shard_map/all_gather | solution.py:42
  19.8 0.7 bitcast_bitcast_fusion
  20.6 0.0 copy-done
  20.6 0.0 copy-done.3
  20.6 0.0 copy-start.7
  20.6 0.0 copy-start.2
  20.6 0.0 copy-start.4
  20.6 0.5 fusion.52
  21.1 9.0 %all_gather.12 = bf16[512,256]{1,0:T(8,128)(2,1)S(1)} all-gather(bf16[128,256]{1,0:T(8,128)(2,1)S(1)} %fusion.52), channel_id=1, replica_groups=mesh['segment'=4,'ctx'=4,'head'=2] {'ctx'}, dimensions={0}, use_global_device_ids=true | all-gather | bytes 327680 | tf_op jit(solution)/shard_map/all_gather | solution.py:41
  30.1 0.0 copy-done.7
  30.1 0.0 copy-done.2
  30.1 0.0 copy-done.4
  30.1 8.1 %while.42 = (s32[]{:T(128)}, bf16[2,5,128,512]{2,3,1,0:T(8,128)(2,1)}, bf16[2,5,128,512]{2,3,1,0:T(8,128)(2,1)}, bf16[2,512,128]{2,1,0:T(8,128)(2,1)S(1)}, bf16[...) while((s32[]{:T(128)}, ...), condition=%wide.region_4.5_spmd.clone, body=%wide.region_0.4_spmd.clone.sunk | while | flops 257735424 | bytes 10228865 | solution.py:83
  30.2 0.1 fusion.91
  30.3 0.0 copy-start.5
  30.3 0.4 fusion.92
  30.7 0.2 select_reduce_fusion.2
  30.9 0.3 copy-done.5
  31.3 0.6 fusion.93
  31.8 1.3 fusion.94
  33.1 1.1 bitcast_dynamic-update-slice_fusion.2
  34.2 0.1 fusion.91
  34.4 0.0 copy-start.5
  34.4 0.4 fusion.92
  34.7 0.2 select_reduce_fusion.2
  35.0 0.3 copy-done.5
  35.3 0.6 fusion.93
  35.9 1.3 fusion.94
  37.2 1.1 bitcast_dynamic-update-slice_fusion.2
  38.3 8.6 %while.41 = (s32[]{:T(128)}, bf16[2,512,128]{1,2,0:T(8,128)(2,1)}, bf16[2,512,128]{1,2,0:T(8,128)(2,1)}, bf16[2,5,128,512]{2,3,1,0:T(8,128)(2,1)}, bf16[2,128,5,...) while((s32[]{:T(128)}, bf16[2,512,128]{1,2,0:T(8,128)(2,1)}, ...), condition=%wide.region_6.7_spmd, body=%wide.region_5.6_spmd.sunk | while | flops 167903232 | bytes 2559061 | solution.py:99
  38.3 1.4 fusion.85
  39.7 0.1 copy.43
  39.8 0.7 constant_dynamic-update-slice_fusion.2
  40.5 2.1 %fusion.86 = bf16[2,512,128]{1,2,0:T(8,128)(2,1)} fusion(bf16[2,512,128]{1,2,0:T(8,128)(2,1)} %get-tuple-element.447, s32[]{:T(128)} %get-tuple-element.445, bf16[2,5,128,512]{2,3,1,0:T(8,128)(2,1)} %get-tuple-element.458, bf16[2,128,5,128]{3,1,2,0:T(8,128)(2,1)S(1)} %get-tuple-element.459), kind=kOutput, calls=%fused_computation.2.clone.1 | convolution fusion | flops 83886080 | bytes 1082880 | tf_op jit(solution)/shard_map/while/body/eval_jaxpr/gts,tgd->sd/dot_general | solution.py:90
  42.6 1.4 fusion.85
  44.0 0.1 copy.43
  44.1 0.7 constant_dynamic-update-slice_fusion.2
  44.8 2.1 %fusion.86 = bf16[2,512,128]{1,2,0:T(8,128)(2,1)} fusion(bf16[2,512,128]{1,2,0:T(8,128)(2,1)} %get-tuple-element.447, s32[]{:T(128)} %get-tuple-element.445, bf16[2,5,128,512]{2,3,1,0:T(8,128)(2,1)} %get-tuple-element.458, bf16[2,128,5,128]{3,1,2,0:T(8,128)(2,1)S(1)} %get-tuple-element.459), kind=kOutput, calls=%fused_computation.2.clone.1 | convolution fusion | flops 83886080 | bytes 1082880 | tf_op jit(solution)/shard_map/while/body/eval_jaxpr/gts,tgd->sd/dot_general | solution.py:90
  46.9 1.1 pad_maximum_fusion
  48.0 1.0 copy.30
  49.0 0.0 reduce-scatter.7.cloned.1.call-update
  49.0 0.0 reduce-scatter.5.cloned.1.call-start
  49.1 25.5 %reduce-scatter.7.cloned.1.call-done = bf16[128,512]{1,0:T(8,128)(2,1)} async-done(((bf16[512,512]{1,0:T(8,128)(2,1)}), bf16[128,512]{1,0:T(8,128)(2,1)}) %reduce-scatter.7.cloned.1.call-update) | async-done | bytes 131088
  74.5 0.0 copy-start.1
  74.5 0.0 copy-start.6
  74.5 2.0 %fusion.46 = f32[128,5120]{1,0:T(8,128)S(1)} fusion(bf16[1,5120,256]{2,1,0:T(8,128)(2,1)S(1)} %copy-done, bf16[128,512]{1,0:T(8,128)(2,1)} %reduce-scatter.7.cloned.1.call-done), kind=kOutput, calls=%fused_computation.58 | convolution fusion | flops 335544320 | bytes 5308416 | tf_op jit(solution)/shard_map/dot_general | solution.py:111
  76.5 0.0 copy-done.1
  76.5 0.0 copy-done.6
  76.5 2.1 %fusion.42 = bf16[128,5120]{1,0:T(8,128)(2,1)} fusion(f32[128,5120]{1,0:T(8,128)S(1)} %fusion.46, bf16[1,5120,256]{2,1,0:T(8,128)(2,1)S(1)} %copy-done.1, bf16[128,512]{1,0:T(8,128)(2,1)S(1)} %copy-done.6), kind=kOutput, calls=%fused_computation.54 | convolution fusion | flops 336855040 | bytes 6619136 | tf_op jit(solution)/shard_map/dot_general | solution.py:112
  78.6 0.0 reduce-scatter.5.cloned.1.call-update
  78.6 0.0 all-gather.3.cloned.1.call-start
  78.6 8.7 %reduce-scatter.5.cloned.1.call-done = bf16[128,2560]{1,0:T(8,128)(2,1)} async-done(((bf16[128,5120]{1,0:T(8,128)(2,1)}), bf16[128,2560]{1,0:T(8,128)(2,1)}) %reduce-scatter.5.cloned.1.call-update) | async-done | bytes 655376 | tf_op jit(solution)/shard_map/reduce_scatter | solution.py:115
  87.4 0.0 all-gather.3.cloned.1.call-update
  87.4 57.6 %all-gather.3.cloned.1.call-done = bf16[512,2560]{1,0:T(8,128)(2,1)} async-done(((bf16[128,2560]{1,0:T(8,128)(2,1)}), bf16[512,2560]{1,0:T(8,128)(2,1)}) %all-gather.3.cloned.1.call-update) | async-done | bytes 2621456 | tf_op jit(solution)/shard_map/all_gather | solution.py:11
  145.0 10.5 %while.43 = (s32[]{:T(128)}, f32[128,2560]{1,0:T(8,128)}, s32[]{:T(128)}, bf16[4,128,2560]{2,1,0:T(8,128)(2,1)}, s32[]{:T(128)}, /*index=5*/s32[]{:T(128)}, s32[]{:T(128)}, s32[]{:T(128)}) while((s32[]{:T(128)}, f32[128,2560]{1,0:T(8,128)}, s32[]{:T(128)}, bf16[4,128,2560]{2,1,0:T(8,128)(2,1)}, s32[]{:T(128)}, ...), condition=%wide.region_10.11_spmd.clone, body=%wide.region_9.10_spmd.clone.sunk | while | flops 1310728 | bytes 3276955 | solution.py:20
  145.0 2.3 %add_select_fusion.2 = f32[128,2560]{1,0:T(8,128)} fusion(f32[128,2560]{1,0:T(8,128)} %get-tuple-element.470, bf16[4,128,2560]{2,1,0:T(8,128)(2,1)} %get-tuple-element.480, s32[]{:T(128)S(6)} %select_n.73, pred[]{:T(512)S(6)} %compare.3, pred[]{:T(512)S(6)} %gt.12), kind=kLoop, calls=%fused_computation.52.clone.1 | loop fusion | flops 1310720 | bytes 3276806 | tf_op jit(solution)/shard_map/while/body/eval_jaxpr/jit(_where)/select_n | solution.py:18
  147.3 2.7 %add_select_fusion.2 = f32[128,2560]{1,0:T(8,128)} fusion(f32[128,2560]{1,0:T(8,128)} %get-tuple-element.470, bf16[4,128,2560]{2,1,0:T(8,128)(2,1)} %get-tuple-element.480, s32[]{:T(128)S(6)} %select_n.73, pred[]{:T(512)S(6)} %compare.3, pred[]{:T(512)S(6)} %gt.12), kind=kLoop, calls=%fused_computation.52.clone.1 | loop fusion | flops 1310720 | bytes 3276806 | tf_op jit(solution)/shard_map/while/body/eval_jaxpr/jit(_where)/select_n | solution.py:18
  150.0 2.7 %add_select_fusion.2 = f32[128,2560]{1,0:T(8,128)} fusion(f32[128,2560]{1,0:T(8,128)} %get-tuple-element.470, bf16[4,128,2560]{2,1,0:T(8,128)(2,1)} %get-tuple-element.480, s32[]{:T(128)S(6)} %select_n.73, pred[]{:T(512)S(6)} %compare.3, pred[]{:T(512)S(6)} %gt.12), kind=kLoop, calls=%fused_computation.52.clone.1 | loop fusion | flops 1310720 | bytes 3276806 | tf_op jit(solution)/shard_map/while/body/eval_jaxpr/jit(_where)/select_n | solution.py:18
  152.8 2.7 %add_select_fusion.2 = f32[128,2560]{1,0:T(8,128)} fusion(f32[128,2560]{1,0:T(8,128)} %get-tuple-element.470, bf16[4,128,2560]{2,1,0:T(8,128)(2,1)} %get-tuple-element.480, s32[]{:T(128)S(6)} %select_n.73, pred[]{:T(512)S(6)} %compare.3, pred[]{:T(512)S(6)} %gt.12), kind=kLoop, calls=%fused_computation.52.clone.1 | loop fusion | flops 1310720 | bytes 3276806 | tf_op jit(solution)/shard_map/while/body/eval_jaxpr/jit(_where)/select_n | solution.py:18
  155.5 2.7 %add_bitcast_fusion = f32[1,128,2560]{2,1,0:T(8,128)} fusion(f32[128,2560]{1,0:T(8,128)} %get-tuple-element.200, bf16[128,2560]{1,0:T(8,128)(2,1)} %reduce-scatter.5.cloned.1.call-done), kind=kLoop, calls=%fused_computation.64 | loop fusion | flops 655360 | bytes 3276800 | tf_op jit(solution)/shard_map/broadcast_in_dim | solution.py:120
  (10 shorter events, 0.0 us)
Async XLA Ops:
  6.5 14.0 %copy-start = (bf16[1,5120,256]{2,1,0:T(8,128)(2,1)S(1)}, bf16[1,5120,256]{2,1,0:T(8,128)(2,1)}, u32[]{:S(2)}) copy-start(bf16[1,5120,256]{2,1,0:T(8,128)(2,1)} %param.15) | copy-start | bytes 7864324
  6.5 68.0 %reduce-scatter.7.cloned.1.call-start = ((), (), s32[]{:S(2)}) async-start(), calls=%async_computation.4 | async-start | bytes 655360
  6.6 14.0 %copy-start.3 = (bf16[1,128,5120]{2,1,0:T(8,128)(2,1)S(1)}, bf16[1,128,5120]{2,1,0:T(8,128)(2,1)}, u32[]{:S(2)}) copy-start(bf16[1,128,5120]{2,1,0:T(8,128)(2,1)} %param.12) | copy-start | bytes 3932164
  20.6 9.5 %copy-start.7 = (s32[512]{0:T(512)S(1)}, s32[512]{0:T(512)}, u32[]{:S(2)}) copy-start(s32[512]{0:T(512)} %param.17) | copy-start | bytes 6148
  20.6 9.6 %copy-start.2 = (bf16[1,128,10,128]{3,1,2,0:T(8,128)(2,1)S(1)}, bf16[1,128,10,128]{3,1,2,0:T(8,128)(2,1)}, u32[]{:S(2)}) copy-start(bf16[1,128,10,128]{3,1,2,0:T(8,128)(2,1)} %param.13) | copy-start | bytes 983044
  20.6 9.6 %copy-start.4 = (bf16[1,128,10,128]{3,1,2,0:T(8,128)(2,1)S(1)}, bf16[1,128,10,128]{3,1,2,0:T(8,128)(2,1)}, u32[]{:S(2)}) copy-start(bf16[1,128,10,128]{3,1,2,0:T(8,128)(2,1)} %param.14) | copy-start | bytes 983044
  30.3 1.0 copy-start.5
  34.4 1.0 copy-start.5
  49.0 38.4 %reduce-scatter.5.cloned.1.call-start = ((), (), s32[]{:S(2)}) async-start(), calls=%async_computation.2 | async-start | bytes 1966080 | tf_op jit(solution)/shard_map/reduce_scatter | solution.py:115
  74.5 2.0 %copy-start.1 = (bf16[1,5120,256]{2,1,0:T(8,128)(2,1)S(1)}, bf16[1,5120,256]{2,1,0:T(8,128)(2,1)}, u32[]{:S(2)}) copy-start(bf16[1,5120,256]{2,1,0:T(8,128)(2,1)} %param.16) | copy-start | bytes 7864324
  74.5 2.0 %copy-start.6 = (bf16[128,512]{1,0:T(8,128)(2,1)S(1)}, bf16[128,512]{1,0:T(8,128)(2,1)}, u32[]{:S(2)}) copy-start(bf16[128,512]{1,0:T(8,128)(2,1)} %reduce-scatter.7.cloned.1.call-done) | copy-start | bytes 393220
  78.6 66.4 %all-gather.3.cloned.1.call-start = ((), (), s32[]{:S(2)}) async-start(), calls=%async_computation.3 | async-start | bytes 3276800 | tf_op jit(solution)/shard_map/all_gather | solution.py:11
Sparse Core Ops, SparseCore 0:
  49.1 25.3 reduce-scatter.6
  78.7 8.6 reduce-scatter.4
  88.9 56.0 all-gather.2
where the time goes:
time: 165 us
  waiting for transfers between devices  91.8 us (56%)
  blocking collectives  19.4 us (12%)
  matrix products  18.9 us (11%)
  other arithmetic  17.1 us (10%)
  between operations  13.2 us (8%)
  local copies, waits for them, and re-layouts  3.98 us (2%)
    all_gather x1, waiting for transfers between devices, prefix(): everything = lax.all_gather(shard.astype(jnp.bfloat16), axis)  57.6 us
    unnamed x4, waiting for transfers between devices  25.5 us
    all_gather x1, blocking collectives, per_device(): lax.all_gather(value_rows, 'ctx', axis=0, tiled=True)  10.5 us
    select_n x4, other arithmetic, hop(): return jnp.where(reached, new, before)  10.4 us
    all_gather x1, blocking collectives, per_device(): lax.all_gather(key_rows, 'ctx', axis=0, tiled=True)  8.97 us
    reduce_scatter x1, waiting for transfers between devices, per_device(): lax.psum_scatter(partial_sum.astype(jnp.bfloat16), 'head', scatter_dimens...  8.74 us
    dot_general x2, matrix products, per_group(): jnp.einsum('gts,tgd->sd', prob_group, grad_group, preferred_element_type=...  4.2 us
  transfers between devices with their start and end apart: 3, of which 3 were waited for; matrix products, arithmetic and copies ran while one was open for 0% of the time, Pallas kernels for 0%

commit v1 on v0

--- a/solution.py
+++ b/solution.py
@@ -6,22 +6,14 @@
 from jax.sharding import PartitionSpec as P
 
 
-def prefix(shard, axis, combine, identity):
+def suffix_chain(own, axis):
     length, index = (lax.axis_size(axis), lax.axis_index(axis))
-    everything = lax.all_gather(shard.astype(jnp.bfloat16), axis)
-    start = jnp.broadcast_to(jnp.asarray(identity, shard.dtype), shard.shape)
-
-    def hop(k, before):
-        at = length - 1 - k
-        reached = at > index
-        new = combine(before, everything[at].astype(shard.dtype))
-        return jnp.where(reached, new, before)
-
-    return lax.fori_loop(0, length, hop, start)
-
-
-def add_terms(earlier, later):
-    return earlier + later
+    total = own
+    for k in range(length - 1):
+        src_dev = length - 1 - k
+        got = lax.ppermute(total.astype(jnp.bfloat16), axis, [(src_dev, src_dev - 1)])
+        total = jnp.where(index == src_dev - 1, own + got.astype(jnp.float32), total)
+    return total
 
 
 def per_device(inputs, query, grad_out, w_key, w_value, keep_mask):
@@ -37,10 +29,8 @@
     value_rows = jnp.dot(tokens, w_value[0], preferred_element_type=jnp.float32).astype(
         jnp.bfloat16
     )
-    keys_all, values_all = (
-        lax.all_gather(key_rows, "ctx", axis=0, tiled=True),
-        lax.all_gather(value_rows, "ctx", axis=0, tiled=True),
-    )
+    kv_all = lax.all_gather(jnp.concatenate((key_rows, value_rows), axis=1), "ctx", axis=0, tiled=True)
+    keys_all, values_all = kv_all[:, : key_rows.shape[1]], kv_all[:, key_rows.shape[1] :]
     seq_rows = keys_all.shape[0]
     key_heads = keys_all.reshape(seq_rows, kv_local, head_dim)
     value_heads = values_all.reshape(seq_rows, kv_local, head_dim)
@@ -115,8 +105,7 @@
     reduced = lax.psum_scatter(
         partial_sum.astype(jnp.bfloat16), "head", scatter_dimension=1, tiled=True
     ).astype(jnp.float32)
-    later = prefix(reduced, "segment", add_terms, jnp.zeros_like(reduced))
-    result = reduced + later
+    result = suffix_chain(reduced, "segment")
     return result[None]
 
 

time: 165 us -> 151 us (0.915)
  waiting for transfers between devices: 91.8 us -> 83 us
  blocking collectives: 19.4 us -> 11.7 us
  other arithmetic: 17.1 us -> 11.1 us
  starting transfers between devices: 0.09 us -> 4.36 us
  local copies, waits for them, and re-layouts: 3.98 us -> 8.16 us
    all_gather x1 -> x0, waiting for transfers between devices: 57.6 us -> none  [prefix(): everything = lax.all_gather(shard.astype(jnp.bfloat16), axis)]
    ppermute x0 -> x3, waiting for transfers between devices: none -> 48.7 us  [suffix_chain(): lax.ppermute(total.astype(jnp.bfloat16), axis, [(src_dev, src_dev - 1)])]
    select_n x4 -> x0, other arithmetic: 10.4 us -> none  [hop(): return jnp.where(reached, new, before)]
    all_gather x2 -> x1, blocking collectives: 19.4 us -> 11.7 us  [per_device(): lax.all_gather(jnp.concatenate((key_rows, value_rows), axis=1), 'ctx', ax...]
    ppermute x0 -> x3, starting transfers between devices: none -> 4.32 us  [suffix_chain(): lax.ppermute(total.astype(jnp.bfloat16), axis, [(src_dev, src_dev - 1)])]
    convert_element_type x0 -> x2, other arithmetic: none -> 4.12 us  [suffix_chain(): total.astype(jnp.bfloat16)]
    unnamed x15 -> x18, local copies, waits for them, and re-layouts: 1.04 us -> 4.13 us
    dot_general x1, matrix products: 2.79 us -> 0.51 us  [per_device(): jnp.dot(tokens, w_value[0], preferred_element_type=jnp.float32)]
  transfers between devices with their start and end apart: 3 -> 5, of which waited for: 3 -> 3; matrix products, arithmetic and copies ran while one was open for 0% -> 0% of each run, Pallas kernels for 0% -> 0%
where the time goes in v1:
time: 151 us; the launch traced here: 150 us
  waiting for transfers between devices  83 us (55%)
  matrix products  18 us (12%)
  between operations  13.5 us (9%)
  blocking collectives  11.7 us (8%)
  other arithmetic  11.1 us (7%)
  local copies, waits for them, and re-layouts  8.16 us (5%)
  starting transfers between devices  4.36 us (3%)
    ppermute x3, waiting for transfers between devices, suffix_chain(): lax.ppermute(total.astype(jnp.bfloat16), axis, [(src_dev, src_dev - 1)])  48.7 us
    unnamed x3, waiting for transfers between devices  25.5 us
    all_gather x1, blocking collectives, per_device(): lax.all_gather(jnp.concatenate((key_rows, value_rows), axis=1), 'ctx', ax...  11.7 us
    reduce_scatter x1, waiting for transfers between devices, per_device(): lax.psum_scatter(partial_sum.astype(jnp.bfloat16), 'head', scatter_dimens...  8.79 us
    ppermute x3, starting transfers between devices, suffix_chain(): lax.ppermute(total.astype(jnp.bfloat16), axis, [(src_dev, src_dev - 1)])  4.32 us
    dot_general x2, matrix products, per_group(): jnp.einsum('gts,tgd->sd', prob_group, grad_group, preferred_element_type=...  4.2 us
    unnamed x18, local copies, waits for them, and re-layouts  4.13 us
    convert_element_type x2, other arithmetic, suffix_chain(): total.astype(jnp.bfloat16)  4.12 us
  transfers between devices with their start and end apart: 5, of which 3 were waited for; matrix products, arithmetic and copies ran while one was open for 0% of the time, Pallas kernels for 0%

profile of v1, /device:TPU:0, one launch (start us, length us, event | category | flops | bytes accessed | tf_op | source)
XLA Modules:
  0.0 149.9 jit_solution(10421825341742242223)
XLA Ops:
  6.5 0.0 copy-start
  6.5 0.0 reduce-scatter.7.cloned.1.call-start
  6.5 1.7 %copy-done = bf16[1,5120,256]{2,1,0:T(8,128)(2,1)S(1)} copy-done((bf16[1,5120,256]{2,1,0:T(8,128)(2,1)S(1)}, bf16[1,5120,256]{2,1,0:T(8,128)(2,1)}, u32[]{:S(2)}) %copy-start) | copy-done | bytes 2621464
  8.3 0.0 copy-start.1
  8.3 0.0 copy-start.4
  8.3 2.0 %fusion.56 = bf16[128,256]{1,0:T(8,128)(2,1)S(1)} fusion(bf16[1,5120,256]{2,1,0:T(8,128)(2,1)S(1)} %copy-done, bf16[1,128,5120]{2,1,0:T(8,128)(2,1)} %param.10), kind=kOutput, calls=%fused_computation.71 | convolution fusion | flops 335577088 | bytes 3997696 | tf_op jit(solution)/shard_map/dot_general | solution.py:28
  10.3 0.1 copy-done.1
  10.4 0.4 copy-done.4
  10.8 0.5 fusion.61
  11.3 0.0 copy-start.8
  11.3 0.0 copy-start.3
  11.3 0.0 copy-start.5
  11.3 11.7 %all_gather.3 = bf16[512,512]{1,0:T(8,128)(2,1)S(1)} all-gather(bf16[128,512]{1,0:T(8,128)(2,1)S(1)} %pad_maximum_fusion.1), channel_id=1, replica_groups=mesh['segment'=4,'ctx'=4,'head'=2] {'ctx'}, dimensions={0}, use_global_device_ids=true | all-gather | bytes 655360 | tf_op jit(solution)/shard_map/all_gather | solution.py:32
  23.0 0.8 slice_bitcast_fusion
  23.9 0.0 copy-done.8
  23.9 1.8 %bitcast_bitcast_fusion = (bf16[2,512,128]{2,1,0:T(8,128)(2,1)}, bf16[2,512,128]{2,1,0:T(8,128)(2,1)S(1)}) fusion(bf16[64,2,8,128]{3,2,1,0:T(8,128)(2,1)} %get-tuple-element.146, bf16[64,2,8,128]{3,2,1,0:T(8,128)(2,1)} %get-tuple-element.147), kind=kLoop, calls=%fused_computation.75 | loop fusion | bytes 1048576 | tf_op jit(solution)/shard_map/transpose | solution.py:75
  25.7 0.0 copy-done.3
  25.7 0.0 copy-done.5
  25.7 8.1 %while.26 = (s32[]{:T(128)}, bf16[2,5,128,512]{2,3,1,0:T(8,128)(2,1)}, bf16[2,5,128,512]{2,3,1,0:T(8,128)(2,1)}, bf16[2,512,128]{2,1,0:T(8,128)(2,1)S(1)}, bf16[...) while((s32[]{:T(128)}, ...), condition=%wide.region_4.5_spmd.clone, body=%wide.region_0.4_spmd.clone.sunk | while | flops 257735424 | bytes 10228865 | solution.py:73
  25.7 0.1 fusion.94
  25.8 0.0 copy-start.6
  25.9 0.4 fusion.95
  26.2 0.2 select_reduce_fusion.2
  26.5 0.3 copy-done.6
  26.8 0.6 fusion.96
  27.4 1.3 fusion.97
  28.7 1.1 bitcast_dynamic-update-slice_fusion.2
  29.8 0.1 fusion.94
  29.9 0.0 copy-start.6
  29.9 0.4 fusion.95
  30.3 0.2 select_reduce_fusion.2
  30.5 0.3 copy-done.6
  30.8 0.6 fusion.96
  31.4 1.3 fusion.97
  32.7 1.1 bitcast_dynamic-update-slice_fusion.2
  33.8 8.7 %while.25 = (s32[]{:T(128)}, bf16[2,512,128]{1,2,0:T(8,128)(2,1)}, bf16[2,512,128]{1,2,0:T(8,128)(2,1)}, bf16[2,5,128,512]{2,3,1,0:T(8,128)(2,1)}, bf16[2,128,5,...) while((s32[]{:T(128)}, bf16[2,512,128]{1,2,0:T(8,128)(2,1)}, ...), condition=%wide.region_6.7_spmd, body=%wide.region_5.6_spmd.sunk | while | flops 167903232 | bytes 2559061 | solution.py:89
  33.8 1.4 fusion.88
  35.2 0.1 copy.43
  35.4 0.7 constant_dynamic-update-slice_fusion.2
  36.0 2.1 %fusion.89 = bf16[2,512,128]{1,2,0:T(8,128)(2,1)} fusion(bf16[2,512,128]{1,2,0:T(8,128)(2,1)} %get-tuple-element.292, s32[]{:T(128)} %get-tuple-element.290, bf16[2,5,128,512]{2,3,1,0:T(8,128)(2,1)} %get-tuple-element.303, bf16[2,128,5,128]{3,1,2,0:T(8,128)(2,1)S(1)} %get-tuple-element.304), kind=kOutput, calls=%fused_computation.2.clone.1 | convolution fusion | flops 83886080 | bytes 1082880 | tf_op jit(solution)/shard_map/while/body/eval_jaxpr/gts,tgd->sd/dot_general | solution.py:80
  38.1 1.4 fusion.88
  39.6 0.1 copy.43
  39.7 0.7 constant_dynamic-update-slice_fusion.2
  40.4 2.1 %fusion.89 = bf16[2,512,128]{1,2,0:T(8,128)(2,1)} fusion(bf16[2,512,128]{1,2,0:T(8,128)(2,1)} %get-tuple-element.292, s32[]{:T(128)} %get-tuple-element.290, bf16[2,5,128,512]{2,3,1,0:T(8,128)(2,1)} %get-tuple-element.303, bf16[2,128,5,128]{3,1,2,0:T(8,128)(2,1)S(1)} %get-tuple-element.304), kind=kOutput, calls=%fused_computation.2.clone.1 | convolution fusion | flops 83886080 | bytes 1082880 | tf_op jit(solution)/shard_map/while/body/eval_jaxpr/gts,tgd->sd/dot_general | solution.py:80
  42.5 1.1 pad_maximum_fusion
  43.5 1.0 copy.30
  44.5 0.0 reduce-scatter.7.cloned.1.call-update
  44.6 0.0 reduce-scatter.5.cloned.1.call-start
  44.6 25.5 %reduce-scatter.7.cloned.1.call-done = bf16[128,512]{1,0:T(8,128)(2,1)} async-done(((bf16[512,512]{1,0:T(8,128)(2,1)}), bf16[128,512]{1,0:T(8,128)(2,1)}) %reduce-scatter.7.cloned.1.call-update) | async-done | bytes 131088
  70.1 2.0 %fusion.46 = f32[128,5120]{1,0:T(8,128)S(1)} fusion(bf16[1,5120,256]{2,1,0:T(8,128)(2,1)S(1)} %copy-done, bf16[128,512]{1,0:T(8,128)(2,1)} %reduce-scatter.7.cloned.1.call-done), kind=kOutput, calls=%fused_computation.57 | convolution fusion | flops 335544320 | bytes 5308416 | tf_op jit(solution)/shard_map/dot_general | solution.py:101
  72.1 0.0 copy-done.2
  72.1 0.0 copy-done.7
  72.1 2.1 %fusion.42 = bf16[128,5120]{1,0:T(8,128)(2,1)} fusion(f32[128,5120]{1,0:T(8,128)S(1)} %fusion.46, bf16[1,5120,256]{2,1,0:T(8,128)(2,1)S(1)} %copy-done.2, bf16[128,512]{1,0:T(8,128)(2,1)S(1)} %copy-done.7), kind=kOutput, calls=%fused_computation.53 | convolution fusion | flops 336855040 | bytes 6619136 | tf_op jit(solution)/shard_map/dot_general | solution.py:102
  74.1 0.0 reduce-scatter.5.cloned.1.call-update
  74.2 8.8 %reduce-scatter.5.cloned.1.call-done = bf16[128,2560]{1,0:T(8,128)(2,1)} async-done(((bf16[128,5120]{1,0:T(8,128)(2,1)}), bf16[128,2560]{1,0:T(8,128)(2,1)}) %reduce-scatter.5.cloned.1.call-update) | async-done | bytes 655376 | tf_op jit(solution)/shard_map/reduce_scatter | solution.py:105
  83.0 1.5 %collective-permute-start = (bf16[128,2560]{1,0:T(8,128)(2,1)}, bf16[128,2560]{1,0:T(8,128)(2,1)}, u32[]{:S(2)}, u32[]{:S(2)}) collective-permute-start(bf16[128,2560]{1,0:T(8,128)(2,1)} %reduce-scatter.5.cloned.1.call-done), channel_id=1, source_target_pairs={{24,16},{25,17},{26,18},{27,19},{28,20},{29,21},{30,22},{31,23}} | collective-permute-start | bytes 1966088 | tf_op jit(solution)/shard_map/ppermute | solution.py:14
  84.5 0.0 collective-permute-done
  84.5 1.5 fusion.55
  85.9 1.5 %collective-permute-start.1 = (bf16[128,2560]{1,0:T(8,128)(2,1)S(1)}, bf16[128,2560]{1,0:T(8,128)(2,1)}, u32[]{:S(2)}, u32[]{:S(2)}) collective-permute-start(bf16[128,2560]{1,0:T(8,128)(2,1)S(1)} %fusion.55), channel_id=1, source_target_pairs={{16,8},{17,9},{18,10},{19,11},{20,12},{21,13},{22,14},{23,15}} | collective-permute-start | bytes 1966088 | tf_op jit(solution)/shard_map/ppermute | solution.py:14
  87.5 0.0 collective-permute-done.1
  87.5 2.6 %fusion.66 = bf16[128,2560]{1,0:T(8,128)(2,1)} fusion(bf16[128,2560]{1,0:T(8,128)(2,1)} %collective-permute-done, bf16[128,2560]{1,0:T(8,128)(2,1)} %collective-permute-done.1, bf16[128,2560]{1,0:T(8,128)(2,1)} %reduce-scatter.5.cloned.1.call-done, pred[]{:T(512)S(6)} %eq.30, pred[]{:T(512)S(6)} %eq.29), kind=kLoop, calls=%fused_computation.73 | loop fusion | flops 2621440 | bytes 2621442 | tf_op jit(solution)/shard_map/convert_element_type | solution.py:14
  90.1 1.3 collective-permute-start.2
  91.4 48.7 %collective-permute-done.2 = bf16[128,2560]{1,0:T(8,128)(2,1)S(1)} collective-permute-done((bf16[128,2560]{1,0:T(8,128)(2,1)}, bf16[128,2560]{1,0:T(8,128)(2,1)S(1)}, u32[]{:S(2)}, u32[]{:S(2)}) %collective-permute-start.2) | collective-permute-done | bytes 655392 | tf_op jit(solution)/shard_map/ppermute | solution.py:14
  140.1 3.0 %fusion.52 = f32[1,128,2560]{2,1,0:T(8,128)} fusion(bf16[128,2560]{1,0:T(8,128)(2,1)} %reduce-scatter.5.cloned.1.call-done, bf16[128,2560]{1,0:T(8,128)(2,1)S(1)} %collective-permute-done.2, bf16[128,2560]{1,0:T(8,128)(2,1)} %collective-permute-done, bf16[128,2560]{1,0:T(8,128)(2,1)} %collective-permute-done.1, pred[]{:T(512)S(6)} %eq.30, pred[]{:T(512)S(6)} %eq.29, ...), kind=kLoop, calls=%fused_computation.67 | loop fusion | flops 3276800 | bytes 3932163 | tf_op jit(solution)/shard_map/broadcast_in_dim | solution.py:109
  (11 shorter events, 0.0 us)
Async XLA Ops:
  6.5 1.7 %copy-start = (bf16[1,5120,256]{2,1,0:T(8,128)(2,1)S(1)}, bf16[1,5120,256]{2,1,0:T(8,128)(2,1)}, u32[]{:S(2)}) copy-start(bf16[1,5120,256]{2,1,0:T(8,128)(2,1)} %param.13) | copy-start | bytes 7864324
  6.5 63.5 %reduce-scatter.7.cloned.1.call-start = ((), (), s32[]{:S(2)}) async-start(), calls=%async_computation.3 | async-start | bytes 655360
  8.3 2.1 %copy-start.1 = (bf16[1,5120,256]{2,1,0:T(8,128)(2,1)S(1)}, bf16[1,5120,256]{2,1,0:T(8,128)(2,1)}, u32[]{:S(2)}) copy-start(bf16[1,5120,256]{2,1,0:T(8,128)(2,1)} %param.14) | copy-start | bytes 7864324
  8.3 2.5 %copy-start.4 = (bf16[1,128,5120]{2,1,0:T(8,128)(2,1)S(1)}, bf16[1,128,5120]{2,1,0:T(8,128)(2,1)}, u32[]{:S(2)}) copy-start(bf16[1,128,5120]{2,1,0:T(8,128)(2,1)} %param.10) | copy-start | bytes 3932164
  11.3 12.6 %copy-start.8 = (s32[512]{0:T(512)S(1)}, s32[512]{0:T(512)}, u32[]{:S(2)}) copy-start(s32[512]{0:T(512)} %param.15) | copy-start | bytes 6148
  11.3 14.4 %copy-start.3 = (bf16[1,128,10,128]{3,1,2,0:T(8,128)(2,1)S(1)}, bf16[1,128,10,128]{3,1,2,0:T(8,128)(2,1)}, u32[]{:S(2)}) copy-start(bf16[1,128,10,128]{3,1,2,0:T(8,128)(2,1)} %param.11) | copy-start | bytes 983044
  11.3 14.4 %copy-start.5 = (bf16[1,128,10,128]{3,1,2,0:T(8,128)(2,1)S(1)}, bf16[1,128,10,128]{3,1,2,0:T(8,128)(2,1)}, u32[]{:S(2)}) copy-start(bf16[1,128,10,128]{3,1,2,0:T(8,128)(2,1)} %param.12) | copy-start | bytes 983044
  25.8 1.0 copy-start.6
  29.9 1.0 copy-start.6
  44.6 38.4 %reduce-scatter.5.cloned.1.call-start = ((), (), s32[]{:S(2)}) async-start(), calls=%async_computation.2 | async-start | bytes 1966080 | tf_op jit(solution)/shard_map/reduce_scatter | solution.py:105
  70.1 2.0 %copy-start.2 = (bf16[1,5120,256]{2,1,0:T(8,128)(2,1)S(1)}, bf16[1,5120,256]{2,1,0:T(8,128)(2,1)}, u32[]{:S(2)}) copy-start(bf16[1,5120,256]{2,1,0:T(8,128)(2,1)} %param.14) | copy-start | bytes 7864324
  70.1 2.0 %copy-start.7 = (bf16[128,512]{1,0:T(8,128)(2,1)S(1)}, bf16[128,512]{1,0:T(8,128)(2,1)}, u32[]{:S(2)}) copy-start(bf16[128,512]{1,0:T(8,128)(2,1)} %reduce-scatter.7.cloned.1.call-done) | copy-start | bytes 393220
  83.0 1.5 %collective-permute-start = (bf16[128,2560]{1,0:T(8,128)(2,1)}, bf16[128,2560]{1,0:T(8,128)(2,1)}, u32[]{:S(2)}, u32[]{:S(2)}) collective-permute-start(bf16[128,2560]{1,0:T(8,128)(2,1)} %reduce-scatter.5.cloned.1.call-done), channel_id=1, source_target_pairs={{24,16},{25,17},{26,18},{27,19},{28,20},{29,21},{30,22},{31,23}} | collective-permute-start | bytes 1966088 | tf_op jit(solution)/shard_map/ppermute | solution.py:14
  85.9 1.5 %collective-permute-start.1 = (bf16[128,2560]{1,0:T(8,128)(2,1)S(1)}, bf16[128,2560]{1,0:T(8,128)(2,1)}, u32[]{:S(2)}, u32[]{:S(2)}) collective-permute-start(bf16[128,2560]{1,0:T(8,128)(2,1)S(1)} %fusion.55), channel_id=1, source_target_pairs={{16,8},{17,9},{18,10},{19,11},{20,12},{21,13},{22,14},{23,15}} | collective-permute-start | bytes 1966088 | tf_op jit(solution)/shard_map/ppermute | solution.py:14
  90.1 50.0 %collective-permute-start.2 = (bf16[128,2560]{1,0:T(8,128)(2,1)}, bf16[128,2560]{1,0:T(8,128)(2,1)S(1)}, u32[]{:S(2)}, u32[]{:S(2)}) collective-permute-start(bf16[128,2560]{1,0:T(8,128)(2,1)} %fusion.66), channel_id=1, source_target_pairs={{8,0},{9,1},{10,2},{11,3},{12,4},{13,5},{14,6},{15,7}} | collective-permute-start | bytes 1966088 | tf_op jit(solution)/shard_map/ppermute | solution.py:14
Sparse Core Ops, SparseCore 0:
  44.7 25.3 reduce-scatter.6
  74.3 8.6 reduce-scatter.4

commit v2 on v1

--- a/solution.py
+++ b/solution.py
@@ -6,14 +6,36 @@
 from jax.sharding import PartitionSpec as P
 
 
-def suffix_chain(own, axis):
+CHAIN_CHUNKS = 4
+
+
+def shifted(x, axis, d, length, up):
+    if up:
+        perm = [(c, c + d) for c in range(length - d)]
+    else:
+        perm = [(c, c - d) for c in range(d, length)]
+    return lax.ppermute(x, axis, perm)
+
+
+def suffix_pipeline(own, axis, n_chunks):
     length, index = (lax.axis_size(axis), lax.axis_index(axis))
-    total = own
-    for k in range(length - 1):
-        src_dev = length - 1 - k
-        got = lax.ppermute(total.astype(jnp.bfloat16), axis, [(src_dev, src_dev - 1)])
-        total = jnp.where(index == src_dev - 1, own + got.astype(jnp.float32), total)
-    return total
+    rows, cols = own.shape
+    width = cols // n_chunks
+    out = jnp.zeros_like(own)
+    recv = jnp.zeros((rows, width), jnp.bfloat16)
+    perm = [(i, i - 1) for i in range(1, length)]
+    steps = n_chunks + length - 1
+    for tau in range(steps):
+        k = tau - (length - 1 - index)
+        valid = (k >= 0) & (k < n_chunks)
+        start = jnp.clip(k, 0, n_chunks - 1) * width
+        mine = lax.dynamic_slice_in_dim(own, start, width, axis=1)
+        acc = mine + recv.astype(jnp.float32)
+        cur = lax.dynamic_slice_in_dim(out, start, width, axis=1)
+        out = lax.dynamic_update_slice_in_dim(out, jnp.where(valid, acc, cur), start, axis=1)
+        if tau < steps - 1:
+            recv = lax.ppermute(acc.astype(jnp.bfloat16), axis, perm)
+    return out
 
 
 def per_device(inputs, query, grad_out, w_key, w_value, keep_mask):
@@ -24,25 +46,32 @@
     kv_local = kv_cols // head_dim
     group_size = local_heads // kv_local
     scaling = 1.0 / math.sqrt(head_dim)
+    ctx_len = lax.axis_size("ctx")
+    ctx_index = lax.axis_index("ctx")
     tokens = inputs[0]
     key_rows = jnp.dot(tokens, w_key[0], preferred_element_type=jnp.float32).astype(jnp.bfloat16)
     value_rows = jnp.dot(tokens, w_value[0], preferred_element_type=jnp.float32).astype(
         jnp.bfloat16
     )
-    kv_all = lax.all_gather(jnp.concatenate((key_rows, value_rows), axis=1), "ctx", axis=0, tiled=True)
-    keys_all, values_all = kv_all[:, : key_rows.shape[1]], kv_all[:, key_rows.shape[1] :]
-    seq_rows = keys_all.shape[0]
-    key_heads = keys_all.reshape(seq_rows, kv_local, head_dim)
-    value_heads = values_all.reshape(seq_rows, kv_local, head_dim)
+    kv_own = jnp.concatenate((key_rows, value_rows), axis=1)
+    blocks = [kv_own] + [shifted(kv_own, "ctx", d, ctx_len, True) for d in range(1, ctx_len)]
+    kv_all = jnp.concatenate(blocks, axis=0)
+    seq_rows = kv_all.shape[0]
+    key_heads = kv_all[:, :kv_cols].reshape(seq_rows, kv_local, head_dim)
+    value_heads = kv_all[:, kv_cols:].reshape(seq_rows, kv_local, head_dim)
     query_heads = query[0].reshape(tok_rows, kv_local, group_size, head_dim)
     grad_heads = grad_out[0].reshape(tok_rows, kv_local, group_size, head_dim)
     query_major = jnp.moveaxis(query_heads, 1, 0)
     grad_major = jnp.moveaxis(grad_heads, 1, 0)
-    ctx_index = lax.axis_index("ctx")
     first_row = ctx_index * tok_rows
     row_pos = first_row + jnp.arange(tok_rows, dtype=jnp.int32)[:, None]
-    col_pos = jnp.arange(seq_rows, dtype=jnp.int32)[None, :]
-    allowed = (col_pos <= row_pos) & ((keep_mask[None, :] == 1) | (col_pos == row_pos))
+    blk = jnp.arange(ctx_len, dtype=jnp.int32)
+    col_pos = (
+        (ctx_index - blk)[:, None] * tok_rows + jnp.arange(tok_rows, dtype=jnp.int32)[None, :]
+    ).reshape(1, seq_rows)
+    present = col_pos >= 0
+    kept = jnp.take(keep_mask, jnp.clip(col_pos, 0, keep_mask.shape[0] - 1))
+    allowed = present & (col_pos <= row_pos) & ((kept == 1) | (col_pos == row_pos))
 
     def one_group(packed):
         query_group, grad_group, key_group, value_group = packed
@@ -87,25 +116,38 @@
         return (key_term, value_term)
 
     key_term, value_term = lax.map(per_group, (probs_b, dscore_b, query_major, grad_major))
-    key_flat = jnp.moveaxis(key_term, 0, 1).reshape(tok_rows * lax.axis_size("ctx"), kv_cols)
-    value_flat = jnp.moveaxis(value_term, 0, 1).reshape(tok_rows * lax.axis_size("ctx"), kv_cols)
-    key_grads = lax.psum_scatter(
-        jnp.concatenate((key_flat, value_flat), axis=1).astype(jnp.bfloat16),
-        "ctx",
-        scatter_dimension=0,
-        tiled=True,
-    ).astype(jnp.float32)
-    grad_key = key_grads[:, :kv_cols].astype(jnp.bfloat16)
-    grad_value = key_grads[:, kv_cols:].astype(jnp.bfloat16)
+    key_flat = jnp.moveaxis(key_term, 0, 1).reshape(seq_rows, kv_cols)
+    value_flat = jnp.moveaxis(value_term, 0, 1).reshape(seq_rows, kv_cols)
+    terms = jnp.concatenate((key_flat, value_flat), axis=1)
+    terms_low = terms.astype(jnp.bfloat16)
+    kv_grad = terms[:tok_rows]
+    for d in range(1, ctx_len):
+        part = terms_low[d * tok_rows : (d + 1) * tok_rows]
+        kv_grad = kv_grad + shifted(part, "ctx", d, ctx_len, False).astype(jnp.float32)
+    grad_key = kv_grad[:, :kv_cols].astype(jnp.bfloat16)
+    grad_value = kv_grad[:, kv_cols:].astype(jnp.bfloat16)
     contract = (((1,), (1,)), ((), ()))
-    partial_sum = lax.dot_general(grad_key, w_key[0], contract, preferred_element_type=jnp.float32)
-    partial_sum = partial_sum + lax.dot_general(
-        grad_value, w_value[0], contract, preferred_element_type=jnp.float32
-    )
-    reduced = lax.psum_scatter(
-        partial_sum.astype(jnp.bfloat16), "head", scatter_dimension=1, tiled=True
-    ).astype(jnp.float32)
-    result = suffix_chain(reduced, "segment")
+    head_len = lax.axis_size("head")
+    head_index = lax.axis_index("head")
+    out_cols = w_key.shape[1] // head_len
+
+    def partial_for(b):
+        start = b * out_cols
+        wk = lax.dynamic_slice_in_dim(w_key[0], start, out_cols, axis=0)
+        wv = lax.dynamic_slice_in_dim(w_value[0], start, out_cols, axis=0)
+        part = lax.dot_general(grad_key, wk, contract, preferred_element_type=jnp.float32)
+        return part + lax.dot_general(grad_value, wv, contract, preferred_element_type=jnp.float32)
+
+    received = []
+    for d in range(1, head_len):
+        target = lax.rem(head_index + d, head_len)
+        send = partial_for(target).astype(jnp.bfloat16)
+        perm = [(h, (h + d) % head_len) for h in range(head_len)]
+        received.append(lax.ppermute(send, "head", perm))
+    reduced = partial_for(head_index)
+    for got in received:
+        reduced = reduced + got.astype(jnp.float32)
+    result = suffix_pipeline(reduced, "segment", CHAIN_CHUNKS)
     return result[None]
 
 

time: 151 us -> 118 us (0.78)
  waiting for transfers between devices: 83 us -> 41 us
  starting transfers between devices: 4.36 us -> 21.2 us
  between operations: 13.5 us -> 0.36 us
  blocking collectives: 11.7 us -> 0 us
  other arithmetic: 11.1 us -> 17.7 us
  local copies, waits for them, and re-layouts: 8.16 us -> 13.9 us
  matrix products: 18 us -> 22.9 us
    unnamed x3 -> x0, waiting for transfers between devices: 25.5 us -> none
    ppermute x3 -> x13, starting transfers between devices: 4.32 us -> 21.2 us  [the longest x6 13.5 us: shifted(): return lax.ppermute(x, axis, perm)]
    all_gather x1 -> x0, blocking collectives: 11.7 us -> none  [per_device(): lax.all_gather(jnp.concatenate((key_rows, value_rows), axis=1), 'ctx', ax...]
    reduce_scatter x1 -> x0, waiting for transfers between devices: 8.79 us -> none  [per_device(): lax.psum_scatter(partial_sum.astype(jnp.bfloat16), 'head', scatter_dimens...]
    ppermute x3 -> x13, waiting for transfers between devices: 48.7 us -> 41 us  [the longest x6 31.3 us: suffix_pipeline(): recv = lax.ppermute(acc.astype(jnp.bfloat16), axis, perm)]
    convert_element_type x2 -> x6, other arithmetic: 4.12 us -> 10.6 us  [the longest x5 9.27 us: suffix_pipeline(): recv = lax.ppermute(acc.astype(jnp.bfloat16), axis, perm)]
    gather x0 -> x1, local copies, waits for them, and re-layouts: none -> 3.49 us  [per_device(): kept = jnp.take(keep_mask, jnp.clip(col_pos, 0, keep_mask.shape[0] - 1))]
    broadcast_in_dim x1 -> x0, other arithmetic: 2.96 us -> none  [per_device(): return result[None]]
  transfers between devices with their start and end apart: 5 -> 13, of which waited for: 3 -> 10; matrix products, arithmetic and copies ran while one was open for 0% -> 7% of each run, Pallas kernels for 0% -> 0%
where the time goes in v2:
time: 118 us; the launch traced here: 117 us
  waiting for transfers between devices  41 us (35%)
  matrix products  22.9 us (19%)
  starting transfers between devices  21.2 us (18%)
  other arithmetic  17.7 us (15%)
  local copies, waits for them, and re-layouts  13.9 us (12%)
    ppermute x6, waiting for transfers between devices, suffix_pipeline(): recv = lax.ppermute(acc.astype(jnp.bfloat16), axis, perm)  31.3 us
    ppermute x6, starting transfers between devices, shifted(): return lax.ppermute(x, axis, perm)  13.5 us
    convert_element_type x5, other arithmetic, suffix_pipeline(): recv = lax.ppermute(acc.astype(jnp.bfloat16), axis, perm)  9.27 us
    ppermute x6, waiting for transfers between devices, shifted(): return lax.ppermute(x, axis, perm)  7.75 us
    ppermute x6, starting transfers between devices, suffix_pipeline(): recv = lax.ppermute(acc.astype(jnp.bfloat16), axis, perm)  7.69 us
    unnamed x20, local copies, waits for them, and re-layouts  6.65 us
    dot_general x2, matrix products, one_group(): jnp.einsum('tgd,sd->gts', grad_group, value_group, preferred_element_type...  4.5 us
    dot_general x2, matrix products, per_group(): jnp.einsum('gts,tgd->sd', prob_group, grad_group, preferred_element_type=...  4.34 us
  transfers between devices with their start and end apart: 13, of which 10 were waited for; matrix products, arithmetic and copies ran while one was open for 7% of the time, Pallas kernels for 0%

profile of v2, /device:TPU:0, one launch (start us, length us, event | category | flops | bytes accessed | tf_op | source)
XLA Modules:
  0.0 117.1 jit_solution(756999798284582731)
XLA Ops:
  0.0 2.8 %fusion.58 = bf16[128,256]{1,0:T(8,128)(2,1)S(1)} fusion(bf16[1,5120,256]{2,1,0:T(8,128)(2,1)} %param.13, bf16[1,128,5120]{2,1,0:T(8,128)(2,1)} %param.10), kind=kOutput, calls=%fused_computation.73 | convolution fusion | flops 335577088 | bytes 3997696 | tf_op jit(solution)/shard_map/dot_general | solution.py:52
  2.9 0.4 copy-done.7
  3.3 0.5 fusion.63
  3.8 4.9 %collective-permute-start = (bf16[128,512]{1,0:T(8,128)(2,1)S(1)}, bf16[128,512]{1,0:T(8,128)(2,1)S(1)}, u32[]{:S(2)}, u32[]{:S(2)}) collective-permute-start(bf16[128,512]{1,0:T(8,128)(2,1)S(1)} %pad_maximum_fusion.2), channel_id=1, source_target_pairs={{0,2},{2,4},{4,6},{1,3},{3,5},{5,7},{8,10},{10,12},{12,14},{9,11},... | collective-permute-start | bytes 393224 | tf_op jit(solution)/shard_map/ppermute | solution.py:17
  8.7 3.4 %collective-permute-start.1 = (bf16[128,512]{1,0:T(8,128)(2,1)S(1)}, bf16[128,512]{1,0:T(8,128)(2,1)S(1)}, u32[]{:S(2)}, u32[]{:S(2)}) collective-permute-start(bf16[128,512]{1,0:T(8,128)(2,1)S(1)} %pad_maximum_fusion.2), channel_id=1, source_target_pairs={{0,4},{2,6},{1,5},{3,7},{8,12},{10,14},{9,13},{11,15},{16,20},{18,... | collective-permute-start | bytes 393224 | tf_op jit(solution)/shard_map/ppermute | solution.py:17
  12.1 1.3 %collective-permute-start.2 = (bf16[128,512]{1,0:T(8,128)(2,1)S(1)}, bf16[128,512]{1,0:T(8,128)(2,1)S(1)}, u32[]{:S(2)}, u32[]{:S(2)}) collective-permute-start(bf16[128,512]{1,0:T(8,128)(2,1)S(1)} %pad_maximum_fusion.2), channel_id=1, source_target_pairs={{0,6},{1,7},{8,14},{9,15},{16,22},{17,23},{24,30},{25,31}} | collective-permute-start | bytes 393224 | tf_op jit(solution)/shard_map/ppermute | solution.py:17
  13.6 3.5 %gather_fusion = s32[512]{0:T(512)S(1)} fusion(s32[512]{0:T(512)S(1)} %copy-done.1, s32[1024]{0:T(1024)S(1)} %pad_clamp_fusion), kind=kCustom, calls=%fused_computation | custom fusion | bytes 6144 | tf_op jit(solution)/shard_map/jit(_take)/gather | solution.py:73
  17.4 0.8 copy-done.6
  18.2 11.4 %while.26 = (s32[]{:T(128)}, bf16[2,5,128,512]{2,3,1,0:T(8,128)(2,1)}, bf16[2,5,128,512]{2,3,1,0:T(8,128)(2,1)}, bf16[2,512,128]{2,1,0:T(8,128)(2,1)S(1)}, bf16[...) while((s32[]{:T(128)}, ...), condition=%wide.region_4.5_spmd.clone, body=%wide.region_0.4_spmd.clone.sunk | while | flops 257800960 | bytes 9182837 | solution.py:102
  18.2 0.3 or_and_fusion.2
  18.5 0.4 fusion.115
  19.1 1.5 %fusion.116 = f32[128,5]{0,1:T(8,128)S(1)} fusion(bf16[2,128,5,128]{3,1,2,0:T(8,128)(2,1)} %get-tuple-element.321, s32[]{:T(128)} %get-tuple-element.303, bf16[2,512,128]{2,1,0:T(8,128)(2,1)S(1)} %get-tuple-element.320, f32[5,128,512]{1,2,0:T(8,128)S(1)} %get-tuple-element.289, f32[5,128]{1,0:T(8,128)S(1)} %log_add_fusion.2, ...), kind=kOutput, calls=%fused_computation.31.clone.1 | convolution fusion | flops 85114240 | bytes 1678848 | tf_op jit(solution)/shard_map/while/body/eval_jaxpr/gts,sd->tgd/dot_general | solution.py:90
  20.6 2.2 %fusion.117 = bf16[2,5,128,512]{2,3,1,0:T(8,128)(2,1)} fusion(bf16[2,5,128,512]{2,3,1,0:T(8,128)(2,1)} %get-tuple-element.305, s32[]{:T(128)} %get-tuple-element.303, f32[5,128,512]{1,2,0:T(8,128)S(1)} %get-tuple-element.289, f32[5,128]{1,0:T(8,128)S(1)} %bitcast.188, f32[5,128]{1,0:T(8,128)S(1)} %log_add_fusion.2, ...), kind=kOutput, calls=%fused_computation.28.clone.1 | convolution fusion | flops 85524480 | bytes 2336256 | tf_op jit(solution)/shard_map/while/body/eval_jaxpr/tgd,sd->gts/dot_general | solution.py:94
  22.9 1.1 bitcast_dynamic-update-slice_fusion.3
  23.9 0.3 or_and_fusion.2
  24.2 0.4 fusion.115
  24.8 1.5 %fusion.116 = f32[128,5]{0,1:T(8,128)S(1)} fusion(bf16[2,128,5,128]{3,1,2,0:T(8,128)(2,1)} %get-tuple-element.321, s32[]{:T(128)} %get-tuple-element.303, bf16[2,512,128]{2,1,0:T(8,128)(2,1)S(1)} %get-tuple-element.320, f32[5,128,512]{1,2,0:T(8,128)S(1)} %get-tuple-element.289, f32[5,128]{1,0:T(8,128)S(1)} %log_add_fusion.2, ...), kind=kOutput, calls=%fused_computation.31.clone.1 | convolution fusion | flops 85114240 | bytes 1678848 | tf_op jit(solution)/shard_map/while/body/eval_jaxpr/gts,sd->tgd/dot_general | solution.py:90
  26.3 2.3 %fusion.117 = bf16[2,5,128,512]{2,3,1,0:T(8,128)(2,1)} fusion(bf16[2,5,128,512]{2,3,1,0:T(8,128)(2,1)} %get-tuple-element.305, s32[]{:T(128)} %get-tuple-element.303, f32[5,128,512]{1,2,0:T(8,128)S(1)} %get-tuple-element.289, f32[5,128]{1,0:T(8,128)S(1)} %bitcast.188, f32[5,128]{1,0:T(8,128)S(1)} %log_add_fusion.2, ...), kind=kOutput, calls=%fused_computation.28.clone.1 | convolution fusion | flops 85524480 | bytes 2336256 | tf_op jit(solution)/shard_map/while/body/eval_jaxpr/tgd,sd->gts/dot_general | solution.py:94
  28.6 1.1 bitcast_dynamic-update-slice_fusion.3
  29.7 9.0 %while.25 = (s32[]{:T(128)}, f32[2,512,128]{1,2,0:T(8,128)}, f32[2,512,128]{1,2,0:T(8,128)}, bf16[2,5,128,512]{2,3,1,0:T(8,128)(2,1)}, bf16[2,128,5,128]{3,1,2,0...) while((s32[]{:T(128)}, f32[2,512,128]{1,2,0:T(8,128)}, ...), condition=%wide.region_6.7_spmd, body=%wide.region_5.6_spmd.sunk | while | flops 167837696 | bytes 3214421 | solution.py:118
  29.7 1.4 %fusion.109 = f32[1,512,128]{2,1,0:T(8,128)S(1)} fusion(bf16[2,5,128,512]{2,3,1,0:T(8,128)(2,1)} %get-tuple-element.346, s32[]{:T(128)} %get-tuple-element.335, bf16[2,128,5,128]{3,1,2,0:T(8,128)(2,1)S(1)} %get-tuple-element.347), kind=kOutput, calls=%fused_computation.6.clone.1 | convolution fusion | flops 83951616 | bytes 1082368 | tf_op jit(solution)/shard_map/while/body/eval_jaxpr/gts,tgd->sd/dot_general | solution.py:113
  31.2 0.7 constant_dynamic-update-slice_fusion.2
  32.0 2.2 %fusion.110 = f32[2,512,128]{1,2,0:T(8,128)} fusion(f32[2,512,128]{1,2,0:T(8,128)} %get-tuple-element.337, s32[]{:T(128)} %get-tuple-element.335, bf16[2,5,128,512]{2,3,1,0:T(8,128)(2,1)} %get-tuple-element.348, bf16[2,128,5,128]{3,1,2,0:T(8,128)(2,1)} %get-tuple-element.349), kind=kOutput, calls=%fused_computation.3.clone.1 | convolution fusion | flops 83886080 | bytes 1082880 | tf_op jit(solution)/shard_map/while/body/eval_jaxpr/gts,tgd->sd/dot_general | solution.py:109
  34.1 1.4 %fusion.109 = f32[1,512,128]{2,1,0:T(8,128)S(1)} fusion(bf16[2,5,128,512]{2,3,1,0:T(8,128)(2,1)} %get-tuple-element.346, s32[]{:T(128)} %get-tuple-element.335, bf16[2,128,5,128]{3,1,2,0:T(8,128)(2,1)S(1)} %get-tuple-element.347), kind=kOutput, calls=%fused_computation.6.clone.1 | convolution fusion | flops 83951616 | bytes 1082368 | tf_op jit(solution)/shard_map/while/body/eval_jaxpr/gts,tgd->sd/dot_general | solution.py:113
  35.7 0.7 constant_dynamic-update-slice_fusion.2
  36.4 2.2 %fusion.110 = f32[2,512,128]{1,2,0:T(8,128)} fusion(f32[2,512,128]{1,2,0:T(8,128)} %get-tuple-element.337, s32[]{:T(128)} %get-tuple-element.335, bf16[2,5,128,512]{2,3,1,0:T(8,128)(2,1)} %get-tuple-element.348, bf16[2,128,5,128]{3,1,2,0:T(8,128)(2,1)} %get-tuple-element.349), kind=kOutput, calls=%fused_computation.3.clone.1 | convolution fusion | flops 83886080 | bytes 1082880 | tf_op jit(solution)/shard_map/while/body/eval_jaxpr/gts,tgd->sd/dot_general | solution.py:109
  38.6 1.3 %fusion.68 = bf16[512,512]{0,1:T(8,128)(2,1)S(1)} fusion(f32[512,256]{0,1:T(8,128)} %bitcast.183, f32[512,256]{0,1:T(8,128)} %bitcast.181), kind=kLoop, calls=%fused_computation.75 | loop fusion | flops 1048576 | bytes 1572864 | tf_op jit(solution)/shard_map/convert_element_type | solution.py:122
  39.9 0.8 fusion.91
  40.7 1.3 %collective-permute-start.3 = (bf16[128,512]{0,1:T(8,128)(2,1)}, bf16[128,512]{0,1:T(8,128)(2,1)S(1)}, u32[]{:S(2)}, u32[]{:S(2)}) collective-permute-start(bf16[128,512]{0,1:T(8,128)(2,1)} %get-tuple-element.166), channel_id=1, source_target_pairs={{2,0},{4,2},{6,4},{3,1},{5,3},{7,5},{10,8},{12,10},{14,12},{11,9},... | collective-permute-start | bytes 393224 | tf_op jit(solution)/shard_map/ppermute | solution.py:17
  42.0 1.3 %collective-permute-start.4 = (bf16[128,512]{0,1:T(8,128)(2,1)}, bf16[128,512]{0,1:T(8,128)(2,1)S(1)}, u32[]{:S(2)}, u32[]{:S(2)}) collective-permute-start(bf16[128,512]{0,1:T(8,128)(2,1)} %get-tuple-element.168), channel_id=1, source_target_pairs={{4,0},{6,2},{5,1},{7,3},{12,8},{14,10},{13,9},{15,11},{20,16},{22,... | collective-permute-start | bytes 393224 | tf_op jit(solution)/shard_map/ppermute | solution.py:17
  43.3 1.3 %collective-permute-start.5 = (bf16[128,512]{0,1:T(8,128)(2,1)S(1)}, bf16[128,512]{0,1:T(8,128)(2,1)}, u32[]{:S(2)}, u32[]{:S(2)}) collective-permute-start(bf16[128,512]{0,1:T(8,128)(2,1)S(1)} %get-tuple-element.167), channel_id=1, source_target_pairs={{6,0},{7,1},{14,8},{15,9},{22,16},{23,17},{30,24},{31,25}} | collective-permute-start | bytes 393224 | tf_op jit(solution)/shard_map/ppermute | solution.py:17
  44.6 3.2 %collective-permute-done.3 = bf16[128,512]{0,1:T(8,128)(2,1)S(1)} collective-permute-done((bf16[128,512]{0,1:T(8,128)(2,1)}, bf16[128,512]{0,1:T(8,128)(2,1)S(1)}, u32[]{:S(2)}, u32[]{:S(2)}) %collective-permute-start.3) | collective-permute-done | bytes 131104 | tf_op jit(solution)/shard_map/ppermute | solution.py:17
  47.8 2.7 %collective-permute-done.4 = bf16[128,512]{0,1:T(8,128)(2,1)S(1)} collective-permute-done((bf16[128,512]{0,1:T(8,128)(2,1)}, bf16[128,512]{0,1:T(8,128)(2,1)S(1)}, u32[]{:S(2)}, u32[]{:S(2)}) %collective-permute-start.4) | collective-permute-done | bytes 131104 | tf_op jit(solution)/shard_map/ppermute | solution.py:17
  50.5 1.9 %collective-permute-done.5 = bf16[128,512]{0,1:T(8,128)(2,1)} collective-permute-done((bf16[128,512]{0,1:T(8,128)(2,1)S(1)}, bf16[128,512]{0,1:T(8,128)(2,1)}, u32[]{:S(2)}, u32[]{:S(2)}) %collective-permute-start.5) | collective-permute-done | bytes 131104 | tf_op jit(solution)/shard_map/ppermute | solution.py:17
  52.3 1.0 fusion.73
  53.4 0.6 fusion.46
  54.0 1.2 copy-done.4
  55.1 1.4 %fusion.41 = bf16[128,2560]{1,0:T(8,128)(2,1)} fusion(f32[128,2560]{1,0:T(8,128)S(1)} %fusion.46, bf16[1,5120,256]{2,1,0:T(8,128)(2,1)S(1)} %copy-done.4, s32[]{:T(128)S(6)} %select_n.137, bf16[128,512]{0,1:T(8,128)(2,1)S(1)} %fusion.73), kind=kOutput, calls=%fused_computation.53 | convolution fusion | flops 168427520 | bytes 3342340 | tf_op jit(solution)/shard_map/dot_general | solution.py:138
  56.5 0.6 fusion.49
  57.1 1.9 %collective-permute-done.6 = bf16[128,2560]{1,0:T(8,128)(2,1)} collective-permute-done((bf16[128,2560]{1,0:T(8,128)(2,1)}, bf16[128,2560]{1,0:T(8,128)(2,1)}, u32[]{:S(2)}, u32[]{:S(2)}) %collective-permute-start.6) | collective-permute-done | bytes 655392 | tf_op jit(solution)/shard_map/ppermute | solution.py:146
  59.0 1.7 %fusion.40 = f32[128,2560]{1,0:T(8,128)S(1)} fusion(f32[128,2560]{1,0:T(8,128)S(1)} %fusion.49, bf16[128,2560]{1,0:T(8,128)(2,1)} %collective-permute-done.6, bf16[1,5120,256]{2,1,0:T(8,128)(2,1)S(1)} %copy-done.5, s32[]{:T(128)S(6)} %select_n.136, bf16[128,512]{0,1:T(8,128)(2,1)S(1)} %fusion.73), kind=kOutput, calls=%fused_computation.52 | convolution fusion | flops 168755200 | bytes 4653060 | tf_op jit(solution)/shard_map/dot_general | solution.py:138
  60.7 1.1 copy-done.2
  61.8 1.3 %collective-permute-start.7 = (bf16[128,640]{1,0:T(8,128)(2,1)S(1)}, bf16[128,640]{1,0:T(8,128)(2,1)S(1)}, u32[]{:S(2)}, u32[]{:S(2)}) collective-permute-start(bf16[128,640]{1,0:T(8,128)(2,1)S(1)} %dynamic-slice_convert_fusion), channel_id=1, source_target_pairs={{8,0},{16,8},{24,16},{9,1},{17,9},{25,17},{10,2},{18,10},{26,18},{... | collective-permute-start | bytes 491528 | tf_op jit(solution)/shard_map/ppermute | solution.py:37
  63.1 1.2 %broadcast_in_dim.51 = f32[128,2560]{1,0:T(8,128)} broadcast(f32[]{:T(128)} %constant.58.clone.1), dimensions={} | broadcast | bytes 1310724 | tf_op jit(solution)/shard_map/broadcast_in_dim | solution.py:24
  64.3 0.6 copy-done.3
  64.9 0.8 select_dynamic-update-slice_fusion.5
  65.7 4.2 %collective-permute-done.7 = bf16[128,640]{1,0:T(8,128)(2,1)S(1)} collective-permute-done((bf16[128,640]{1,0:T(8,128)(2,1)S(1)}, bf16[128,640]{1,0:T(8,128)(2,1)S(1)}, u32[]{:S(2)}, u32[]{:S(2)}) %collective-permute-start.7) | collective-permute-done | bytes 163872 | tf_op jit(solution)/shard_map/ppermute | solution.py:37
  69.9 1.8 %fusion.74 = (bf16[128,640]{1,0:T(8,128)(2,1)S(1)}, f32[128,2560]{1,0:T(8,128)}) fusion(bf16[128,640]{1,0:T(8,128)(2,1)S(1)} %collective-permute-done.7, f32[128,2560]{1,0:T(8,128)S(1)} %copy-done.3, s32[]{:T(128)S(6)} %select_n.141, f32[128,2560]{1,0:T(8,128)} %select_dynamic-update-slice_fusion.5, pred[]{:T(512)S(6)} %and.52), kind=kLoop, calls=%fused_computation.99 | loop fusion | flops 327680 | bytes 1310725 | tf_op jit(solution)/shard_map/convert_element_type | solution.py:37
  71.7 1.3 %collective-permute-start.8 = (bf16[128,640]{1,0:T(8,128)(2,1)S(1)}, bf16[128,640]{1,0:T(8,128)(2,1)S(1)}, u32[]{:S(2)}, u32[]{:S(2)}) collective-permute-start(bf16[128,640]{1,0:T(8,128)(2,1)S(1)} %get-tuple-element.164), channel_id=1, source_target_pairs={{8,0},{16,8},{24,16},{9,1},{17,9},{25,17},{10,2},{18,10},{26,18},{... | collective-permute-start | bytes 491528 | tf_op jit(solution)/shard_map/ppermute | solution.py:37
  73.0 6.0 %collective-permute-done.8 = bf16[128,640]{1,0:T(8,128)(2,1)S(1)} collective-permute-done((bf16[128,640]{1,0:T(8,128)(2,1)S(1)}, bf16[128,640]{1,0:T(8,128)(2,1)S(1)}, u32[]{:S(2)}, u32[]{:S(2)}) %collective-permute-start.8) | collective-permute-done | bytes 163872 | tf_op jit(solution)/shard_map/ppermute | solution.py:37
  78.9 1.9 %fusion.75 = (bf16[128,640]{1,0:T(8,128)(2,1)S(1)}, f32[128,2560]{1,0:T(8,128)}) fusion(bf16[128,640]{1,0:T(8,128)(2,1)S(1)} %collective-permute-done.8, f32[128,2560]{1,0:T(8,128)} %copy-done.2, s32[]{:T(128)S(6)} %select_n.144, f32[128,2560]{1,0:T(8,128)} %get-tuple-element.165, pred[]{:T(512)S(6)} %and.53), kind=kLoop, calls=%fused_computation.100 | loop fusion | flops 327680 | bytes 1310725 | tf_op jit(solution)/shard_map/convert_element_type | solution.py:37
  80.8 1.3 %collective-permute-start.9 = (bf16[128,640]{1,0:T(8,128)(2,1)S(1)}, bf16[128,640]{1,0:T(8,128)(2,1)S(1)}, u32[]{:S(2)}, u32[]{:S(2)}) collective-permute-start(bf16[128,640]{1,0:T(8,128)(2,1)S(1)} %get-tuple-element.162), channel_id=1, source_target_pairs={{8,0},{16,8},{24,16},{9,1},{17,9},{25,17},{10,2},{18,10},{26,18},{... | collective-permute-start | bytes 491528 | tf_op jit(solution)/shard_map/ppermute | solution.py:37
  82.1 5.9 %collective-permute-done.9 = bf16[128,640]{1,0:T(8,128)(2,1)S(1)} collective-permute-done((bf16[128,640]{1,0:T(8,128)(2,1)S(1)}, bf16[128,640]{1,0:T(8,128)(2,1)S(1)}, u32[]{:S(2)}, u32[]{:S(2)}) %collective-permute-start.9) | collective-permute-done | bytes 163872 | tf_op jit(solution)/shard_map/ppermute | solution.py:37
  88.0 1.9 %fusion.76 = (bf16[128,640]{1,0:T(8,128)(2,1)S(1)}, f32[128,2560]{1,0:T(8,128)}) fusion(bf16[128,640]{1,0:T(8,128)(2,1)S(1)} %collective-permute-done.9, f32[128,2560]{1,0:T(8,128)} %copy-done.2, s32[]{:T(128)S(6)} %select_n.147, f32[128,2560]{1,0:T(8,128)} %get-tuple-element.163, pred[]{:T(512)S(6)} %and.54), kind=kLoop, calls=%fused_computation.101 | loop fusion | flops 327680 | bytes 1310725 | tf_op jit(solution)/shard_map/convert_element_type | solution.py:37
  89.9 1.3 %collective-permute-start.10 = (bf16[128,640]{1,0:T(8,128)(2,1)S(1)}, bf16[128,640]{1,0:T(8,128)(2,1)S(1)}, u32[]{:S(2)}, u32[]{:S(2)}) collective-permute-start(bf16[128,640]{1,0:T(8,128)(2,1)S(1)} %get-tuple-element.160), channel_id=1, source_target_pairs={{8,0},{16,8},{24,16},{9,1},{17,9},{25,17},{10,2},{18,10},{26,18},{... | collective-permute-start | bytes 491528 | tf_op jit(solution)/shard_map/ppermute | solution.py:37
  91.2 5.9 %collective-permute-done.10 = bf16[128,640]{1,0:T(8,128)(2,1)S(1)} collective-permute-done((bf16[128,640]{1,0:T(8,128)(2,1)S(1)}, bf16[128,640]{1,0:T(8,128)(2,1)S(1)}, u32[]{:S(2)}, u32[]{:S(2)}) %collective-permute-start.10) | collective-permute-done | bytes 163872 | tf_op jit(solution)/shard_map/ppermute | solution.py:37
  97.1 1.9 %fusion.77 = (bf16[128,640]{1,0:T(8,128)(2,1)S(1)}, f32[128,2560]{1,0:T(8,128)}) fusion(bf16[128,640]{1,0:T(8,128)(2,1)S(1)} %collective-permute-done.10, f32[128,2560]{1,0:T(8,128)} %copy-done.2, s32[]{:T(128)S(6)} %select_n.150, f32[128,2560]{1,0:T(8,128)} %get-tuple-element.161, pred[]{:T(512)S(6)} %and.55), kind=kLoop, calls=%fused_computation.102 | loop fusion | flops 327680 | bytes 1310725 | tf_op jit(solution)/shard_map/convert_element_type | solution.py:37
  99.0 1.3 %collective-permute-start.11 = (bf16[128,640]{1,0:T(8,128)(2,1)S(1)}, bf16[128,640]{1,0:T(8,128)(2,1)S(1)}, u32[]{:S(2)}, u32[]{:S(2)}) collective-permute-start(bf16[128,640]{1,0:T(8,128)(2,1)S(1)} %get-tuple-element.158), channel_id=1, source_target_pairs={{8,0},{16,8},{24,16},{9,1},{17,9},{25,17},{10,2},{18,10},{26,18},{... | collective-permute-start | bytes 491528 | tf_op jit(solution)/shard_map/ppermute | solution.py:37
  100.3 5.9 %collective-permute-done.11 = bf16[128,640]{1,0:T(8,128)(2,1)S(1)} collective-permute-done((bf16[128,640]{1,0:T(8,128)(2,1)S(1)}, bf16[128,640]{1,0:T(8,128)(2,1)S(1)}, u32[]{:S(2)}, u32[]{:S(2)}) %collective-permute-start.11) | collective-permute-done | bytes 163872 | tf_op jit(solution)/shard_map/ppermute | solution.py:37
  106.2 1.8 %fusion.78 = (bf16[128,640]{1,0:T(8,128)(2,1)S(1)}, f32[128,2560]{1,0:T(8,128)}) fusion(bf16[128,640]{1,0:T(8,128)(2,1)S(1)} %collective-permute-done.11, f32[128,2560]{1,0:T(8,128)} %copy-done.2, s32[]{:T(128)S(6)} %select_n.153, f32[128,2560]{1,0:T(8,128)} %get-tuple-element.159, pred[]{:T(512)S(6)} %and.56), kind=kLoop, calls=%fused_computation.103 | loop fusion | flops 327680 | bytes 1310725 | tf_op jit(solution)/shard_map/convert_element_type | solution.py:37
  108.0 1.3 %collective-permute-start.12 = (bf16[128,640]{1,0:T(8,128)(2,1)S(1)}, bf16[128,640]{1,0:T(8,128)(2,1)S(1)}, u32[]{:S(2)}, u32[]{:S(2)}) collective-permute-start(bf16[128,640]{1,0:T(8,128)(2,1)S(1)} %get-tuple-element.156), channel_id=1, source_target_pairs={{8,0},{16,8},{24,16},{9,1},{17,9},{25,17},{10,2},{18,10},{26,18},{... | collective-permute-start | bytes 491528 | tf_op jit(solution)/shard_map/ppermute | solution.py:37
  109.3 2.5 %copy.61 = f32[1,128,2560]{2,1,0:T(8,128)} copy(f32[1,128,2560]{2,1,0:T(8,128)} %bitcast.28) | data formatting | bytes 2621440
  111.8 3.4 %collective-permute-done.12 = bf16[128,640]{1,0:T(8,128)(2,1)S(1)} collective-permute-done((bf16[128,640]{1,0:T(8,128)(2,1)S(1)}, bf16[128,640]{1,0:T(8,128)(2,1)S(1)}, u32[]{:S(2)}, u32[]{:S(2)}) %collective-permute-start.12) | collective-permute-done | bytes 163872 | tf_op jit(solution)/shard_map/ppermute | solution.py:37
  115.2 1.8 %bitcast_dynamic-update-slice_fusion.1 = f32[1,128,2560]{2,1,0:T(8,128)} fusion(f32[1,128,2560]{2,1,0:T(8,128)} %copy.61, s32[]{:T(128)S(6)} %select_n.156, f32[128,2560]{1,0:T(8,128)} %get-tuple-element.157, bf16[128,640]{1,0:T(8,128)(2,1)S(1)} %collective-permute-done.12, f32[128,2560]{1,0:T(8,128)} %copy-done.2, pred[]{:T(512)S(6)} %and.57), kind=kLoop, calls=%fused_computation.77 | loop fusion | flops 245760 | bytes 1146885 | tf_op jit(solution)/shard_map/dynamic_update_slice | solution.py:35
  (38 shorter events, 1.3 us)
Async XLA Ops:
  0.0 2.9 %copy-start = (bf16[1,5120,256]{2,1,0:T(8,128)(2,1)S(1)}, bf16[1,5120,256]{2,1,0:T(8,128)(2,1)}, u32[]{:S(2)}) copy-start(bf16[1,5120,256]{2,1,0:T(8,128)(2,1)} %param.14) | copy-start | bytes 7864324
  0.0 3.3 %copy-start.7 = (bf16[1,128,5120]{2,1,0:T(8,128)(2,1)S(1)}, bf16[1,128,5120]{2,1,0:T(8,128)(2,1)}, u32[]{:S(2)}) copy-start(bf16[1,128,5120]{2,1,0:T(8,128)(2,1)} %param.10) | copy-start | bytes 3932164
  3.3 10.3 %copy-start.1 = (s32[512]{0:T(512)S(1)}, s32[512]{0:T(512)}, u32[]{:S(2)}) copy-start(s32[512]{0:T(512)} %param.15) | copy-start | bytes 6148
  3.8 13.4 %collective-permute-start = (bf16[128,512]{1,0:T(8,128)(2,1)S(1)}, bf16[128,512]{1,0:T(8,128)(2,1)S(1)}, u32[]{:S(2)}, u32[]{:S(2)}) collective-permute-start(bf16[128,512]{1,0:T(8,128)(2,1)S(1)} %pad_maximum_fusion.2), channel_id=1, source_target_pairs={{0,2},{2,4},{4,6},{1,3},{3,5},{5,7},{8,10},{10,12},{12,14},{9,11},... | collective-permute-start | bytes 393224 | tf_op jit(solution)/shard_map/ppermute | solution.py:17
  8.7 8.5 %collective-permute-start.1 = (bf16[128,512]{1,0:T(8,128)(2,1)S(1)}, bf16[128,512]{1,0:T(8,128)(2,1)S(1)}, u32[]{:S(2)}, u32[]{:S(2)}) collective-permute-start(bf16[128,512]{1,0:T(8,128)(2,1)S(1)} %pad_maximum_fusion.2), channel_id=1, source_target_pairs={{0,4},{2,6},{1,5},{3,7},{8,12},{10,14},{9,13},{11,15},{16,20},{18,... | collective-permute-start | bytes 393224 | tf_op jit(solution)/shard_map/ppermute | solution.py:17
  12.1 5.1 %collective-permute-start.2 = (bf16[128,512]{1,0:T(8,128)(2,1)S(1)}, bf16[128,512]{1,0:T(8,128)(2,1)S(1)}, u32[]{:S(2)}, u32[]{:S(2)}) collective-permute-start(bf16[128,512]{1,0:T(8,128)(2,1)S(1)} %pad_maximum_fusion.2), channel_id=1, source_target_pairs={{0,6},{1,7},{8,14},{9,15},{16,22},{17,23},{24,30},{25,31}} | collective-permute-start | bytes 393224 | tf_op jit(solution)/shard_map/ppermute | solution.py:17
  17.3 1.0 copy-start.6
  38.6 13.7 %copy-start.8 = (f32[2,512,128]{1,2,0:T(8,128)S(1)}, f32[2,512,128]{1,2,0:T(8,128)}, u32[]{:S(2)}) copy-start(f32[2,512,128]{1,2,0:T(8,128)} %get-tuple-element.88) | copy-start | bytes 1572868
  40.7 7.1 %collective-permute-start.3 = (bf16[128,512]{0,1:T(8,128)(2,1)}, bf16[128,512]{0,1:T(8,128)(2,1)S(1)}, u32[]{:S(2)}, u32[]{:S(2)}) collective-permute-start(bf16[128,512]{0,1:T(8,128)(2,1)} %get-tuple-element.166), channel_id=1, source_target_pairs={{2,0},{4,2},{6,4},{3,1},{5,3},{7,5},{10,8},{12,10},{14,12},{11,9},... | collective-permute-start | bytes 393224 | tf_op jit(solution)/shard_map/ppermute | solution.py:17
  42.0 8.5 %collective-permute-start.4 = (bf16[128,512]{0,1:T(8,128)(2,1)}, bf16[128,512]{0,1:T(8,128)(2,1)S(1)}, u32[]{:S(2)}, u32[]{:S(2)}) collective-permute-start(bf16[128,512]{0,1:T(8,128)(2,1)} %get-tuple-element.168), channel_id=1, source_target_pairs={{4,0},{6,2},{5,1},{7,3},{12,8},{14,10},{13,9},{15,11},{20,16},{22,... | collective-permute-start | bytes 393224 | tf_op jit(solution)/shard_map/ppermute | solution.py:17
  43.3 9.1 %collective-permute-start.5 = (bf16[128,512]{0,1:T(8,128)(2,1)S(1)}, bf16[128,512]{0,1:T(8,128)(2,1)}, u32[]{:S(2)}, u32[]{:S(2)}) collective-permute-start(bf16[128,512]{0,1:T(8,128)(2,1)S(1)} %get-tuple-element.167), channel_id=1, source_target_pairs={{6,0},{7,1},{14,8},{15,9},{22,16},{23,17},{30,24},{31,25}} | collective-permute-start | bytes 393224 | tf_op jit(solution)/shard_map/ppermute | solution.py:17
  53.4 1.7 %copy-start.4 = (bf16[1,5120,256]{2,1,0:T(8,128)(2,1)S(1)}, bf16[1,5120,256]{2,1,0:T(8,128)(2,1)}, u32[]{:S(2)}) copy-start(bf16[1,5120,256]{2,1,0:T(8,128)(2,1)} %param.13) | copy-start | bytes 7864324
  56.5 2.4 %collective-permute-start.6 = (bf16[128,2560]{1,0:T(8,128)(2,1)}, bf16[128,2560]{1,0:T(8,128)(2,1)}, u32[]{:S(2)}, u32[]{:S(2)}) collective-permute-start(bf16[128,2560]{1,0:T(8,128)(2,1)} %fusion.41), channel_id=1, source_target_pairs={{0,1},{1,0},{2,3},{3,2},{4,5},{5,4},{6,7},{7,6},{8,9},{9,8},{10,11... | collective-permute-start | bytes 1966088 | tf_op jit(solution)/shard_map/ppermute | solution.py:146
  56.5 2.4 %copy-start.5 = (bf16[1,5120,256]{2,1,0:T(8,128)(2,1)S(1)}, bf16[1,5120,256]{2,1,0:T(8,128)(2,1)}, u32[]{:S(2)}) copy-start(bf16[1,5120,256]{2,1,0:T(8,128)(2,1)} %param.13) | copy-start | bytes 7864324
  60.7 1.1 copy-start.2
  61.8 8.1 %collective-permute-start.7 = (bf16[128,640]{1,0:T(8,128)(2,1)S(1)}, bf16[128,640]{1,0:T(8,128)(2,1)S(1)}, u32[]{:S(2)}, u32[]{:S(2)}) collective-permute-start(bf16[128,640]{1,0:T(8,128)(2,1)S(1)} %dynamic-slice_convert_fusion), channel_id=1, source_target_pairs={{8,0},{16,8},{24,16},{9,1},{17,9},{25,17},{10,2},{18,10},{26,18},{... | collective-permute-start | bytes 491528 | tf_op jit(solution)/shard_map/ppermute | solution.py:37
  63.1 1.8 %copy-start.3 = (f32[128,2560]{1,0:T(8,128)S(1)}, f32[128,2560]{1,0:T(8,128)}, u32[]{:S(2)}) copy-start(f32[128,2560]{1,0:T(8,128)} %copy-done.2) | copy-start | bytes 3932164
  71.7 7.3 %collective-permute-start.8 = (bf16[128,640]{1,0:T(8,128)(2,1)S(1)}, bf16[128,640]{1,0:T(8,128)(2,1)S(1)}, u32[]{:S(2)}, u32[]{:S(2)}) collective-permute-start(bf16[128,640]{1,0:T(8,128)(2,1)S(1)} %get-tuple-element.164), channel_id=1, source_target_pairs={{8,0},{16,8},{24,16},{9,1},{17,9},{25,17},{10,2},{18,10},{26,18},{... | collective-permute-start | bytes 491528 | tf_op jit(solution)/shard_map/ppermute | solution.py:37
  80.8 7.2 %collective-permute-start.9 = (bf16[128,640]{1,0:T(8,128)(2,1)S(1)}, bf16[128,640]{1,0:T(8,128)(2,1)S(1)}, u32[]{:S(2)}, u32[]{:S(2)}) collective-permute-start(bf16[128,640]{1,0:T(8,128)(2,1)S(1)} %get-tuple-element.162), channel_id=1, source_target_pairs={{8,0},{16,8},{24,16},{9,1},{17,9},{25,17},{10,2},{18,10},{26,18},{... | collective-permute-start | bytes 491528 | tf_op jit(solution)/shard_map/ppermute | solution.py:37
  89.9 7.2 %collective-permute-start.10 = (bf16[128,640]{1,0:T(8,128)(2,1)S(1)}, bf16[128,640]{1,0:T(8,128)(2,1)S(1)}, u32[]{:S(2)}, u32[]{:S(2)}) collective-permute-start(bf16[128,640]{1,0:T(8,128)(2,1)S(1)} %get-tuple-element.160), channel_id=1, source_target_pairs={{8,0},{16,8},{24,16},{9,1},{17,9},{25,17},{10,2},{18,10},{26,18},{... | collective-permute-start | bytes 491528 | tf_op jit(solution)/shard_map/ppermute | solution.py:37
  99.0 7.2 %collective-permute-start.11 = (bf16[128,640]{1,0:T(8,128)(2,1)S(1)}, bf16[128,640]{1,0:T(8,128)(2,1)S(1)}, u32[]{:S(2)}, u32[]{:S(2)}) collective-permute-start(bf16[128,640]{1,0:T(8,128)(2,1)S(1)} %get-tuple-element.158), channel_id=1, source_target_pairs={{8,0},{16,8},{24,16},{9,1},{17,9},{25,17},{10,2},{18,10},{26,18},{... | collective-permute-start | bytes 491528 | tf_op jit(solution)/shard_map/ppermute | solution.py:37
  108.0 7.2 %collective-permute-start.12 = (bf16[128,640]{1,0:T(8,128)(2,1)S(1)}, bf16[128,640]{1,0:T(8,128)(2,1)S(1)}, u32[]{:S(2)}, u32[]{:S(2)}) collective-permute-start(bf16[128,640]{1,0:T(8,128)(2,1)S(1)} %get-tuple-element.156), channel_id=1, source_target_pairs={{8,0},{16,8},{24,16},{9,1},{17,9},{25,17},{10,2},{18,10},{26,18},{... | collective-permute-start | bytes 491528 | tf_op jit(solution)/shard_map/ppermute | solution.py:37

commit v3 on v2

--- a/solution.py
+++ b/solution.py
@@ -20,22 +20,23 @@
 def suffix_pipeline(own, axis, n_chunks):
     length, index = (lax.axis_size(axis), lax.axis_index(axis))
     rows, cols = own.shape
-    width = cols // n_chunks
-    out = jnp.zeros_like(own)
-    recv = jnp.zeros((rows, width), jnp.bfloat16)
+    height = rows // n_chunks
+    chunks = own.reshape(n_chunks, height, cols)
+    pad = jnp.zeros((length - 1, height, cols), own.dtype)
+    padded = jnp.concatenate((pad, chunks, pad), axis=0)
+    steps = n_chunks + length - 1
+    ordered = lax.dynamic_slice_in_dim(padded, index, steps, axis=0)
     perm = [(i, i - 1) for i in range(1, length)]
-    steps = n_chunks + length - 1
+    recv = jnp.zeros((height, cols), jnp.bfloat16)
+    done = []
     for tau in range(steps):
-        k = tau - (length - 1 - index)
-        valid = (k >= 0) & (k < n_chunks)
-        start = jnp.clip(k, 0, n_chunks - 1) * width
-        mine = lax.dynamic_slice_in_dim(own, start, width, axis=1)
-        acc = mine + recv.astype(jnp.float32)
-        cur = lax.dynamic_slice_in_dim(out, start, width, axis=1)
-        out = lax.dynamic_update_slice_in_dim(out, jnp.where(valid, acc, cur), start, axis=1)
+        acc = ordered[tau] + recv.astype(jnp.float32)
+        done.append(acc)
         if tau < steps - 1:
             recv = lax.ppermute(acc.astype(jnp.bfloat16), axis, perm)
-    return out
+    stacked = jnp.stack(done, axis=0)
+    mine = lax.dynamic_slice_in_dim(stacked, length - 1 - index, n_chunks, axis=0)
+    return mine.reshape(rows, cols)
 
 
 def per_device(inputs, query, grad_out, w_key, w_value, keep_mask):
@@ -70,8 +71,16 @@
         (ctx_index - blk)[:, None] * tok_rows + jnp.arange(tok_rows, dtype=jnp.int32)[None, :]
     ).reshape(1, seq_rows)
     present = col_pos >= 0
-    kept = jnp.take(keep_mask, jnp.clip(col_pos, 0, keep_mask.shape[0] - 1))
+    keep_blocks = keep_mask.reshape(ctx_len, tok_rows)
+    kept = jnp.concatenate(
+        [
+            lax.dynamic_index_in_dim(keep_blocks, jnp.maximum(ctx_index - p, 0), 0, keepdims=True)
+            for p in range(ctx_len)
+        ],
+        axis=1,
+    )
     allowed = present & (col_pos <= row_pos) & ((kept == 1) | (col_pos == row_pos))
+    allowed = lax.optimization_barrier(allowed)
 
     def one_group(packed):
         query_group, grad_group, key_group, value_group = packed

time: 118 us -> 104 us (0.88)
  other arithmetic: 17.7 us -> 6.55 us
  waiting for transfers between devices: 41 us -> 47.8 us
  local copies, waits for them, and re-layouts: 13.9 us -> 7.72 us
  matrix products: 22.9 us -> 19.2 us
    convert_element_type x5, other arithmetic: 9.27 us -> 0.19 us  [suffix_pipeline(): recv = lax.ppermute(acc.astype(jnp.bfloat16), axis, perm)]
    ppermute x6, waiting for transfers between devices: 31.3 us -> 36.7 us  [suffix_pipeline(): recv = lax.ppermute(acc.astype(jnp.bfloat16), axis, perm)]
    gather x1 -> x0, local copies, waits for them, and re-layouts: 3.49 us -> none  [per_device(): kept = jnp.take(keep_mask, jnp.clip(col_pos, 0, keep_mask.shape[0] - 1))]
    unnamed x20 -> x18, local copies, waits for them, and re-layouts: 6.65 us -> 3.2 us
    dynamic_update_slice x2 -> x0, other arithmetic: 2.62 us -> none  [suffix_pipeline(): lax.dynamic_update_slice_in_dim(out, jnp.where(valid, acc, cur), start, a...]
    dot_general x2, matrix products: 4.5 us -> 2.65 us  [one_group(): jnp.einsum('tgd,sd->gts', grad_group, value_group, preferred_element_type...]
    dot_general x2, matrix products: 2.97 us -> 1.12 us  [one_group(): jnp.einsum('gts,sd->tgd', prob_low, value_group, preferred_element_type=j...]
    ppermute x6, waiting for transfers between devices: 7.75 us -> 9.26 us  [shifted(): return lax.ppermute(x, axis, perm)]
  transfers between devices with their start and end apart: 13 -> 13, of which waited for: 10 -> 12; matrix products, arithmetic and copies ran while one was open for 7% -> 1% of each run, Pallas kernels for 0% -> 0%
where the time goes in v3:
time: 104 us; the launch traced here: 103 us
  waiting for transfers between devices  47.8 us (46%)
  starting transfers between devices  21.2 us (20%)
  matrix products  19.2 us (18%)
  local copies, waits for them, and re-layouts  7.72 us (7%)
  other arithmetic  6.55 us (6%)
    ppermute x6, waiting for transfers between devices, suffix_pipeline(): recv = lax.ppermute(acc.astype(jnp.bfloat16), axis, perm)  36.7 us
    ppermute x6, starting transfers between devices, shifted(): return lax.ppermute(x, axis, perm)  13.5 us
    ppermute x6, waiting for transfers between devices, shifted(): return lax.ppermute(x, axis, perm)  9.26 us
    ppermute x6, starting transfers between devices, suffix_pipeline(): recv = lax.ppermute(acc.astype(jnp.bfloat16), axis, perm)  7.75 us
    dot_general x2, matrix products, per_group(): jnp.einsum('gts,tgd->sd', prob_group, grad_group, preferred_element_type=...  4.35 us
    unnamed x18, local copies, waits for them, and re-layouts  3.2 us
    dot_general x2, matrix products, partial_for(): lax.dot_general(grad_key, wk, contract, preferred_element_type=jnp.float32)  3.08 us
    dot_general x2, matrix products, per_group(): jnp.einsum('gts,tgd->sd', score_group, query_group, preferred_element_typ...  2.84 us
  transfers between devices with their start and end apart: 13, of which 12 were waited for; matrix products, arithmetic and copies ran while one was open for 1% of the time, Pallas kernels for 0%

profile of v3, /device:TPU:0, one launch (start us, length us, event | category | flops | bytes accessed | tf_op | source)
XLA Modules:
  0.0 102.9 jit_solution(2307239320225762958)
XLA Ops:
  0.0 2.8 %fusion.58 = bf16[128,256]{1,0:T(8,128)(2,1)S(1)} fusion(bf16[1,5120,256]{2,1,0:T(8,128)(2,1)} %param.13, bf16[1,128,5120]{2,1,0:T(8,128)(2,1)} %param.10), kind=kOutput, calls=%fused_computation.75 | convolution fusion | flops 335577088 | bytes 3997696 | tf_op jit(solution)/shard_map/dot_general | solution.py:53
  2.8 0.1 copy-done
  2.9 0.4 copy-done.4
  3.3 0.5 fusion.63
  3.8 4.9 %collective-permute-start = (bf16[128,512]{1,0:T(8,128)(2,1)S(1)}, bf16[128,512]{1,0:T(8,128)(2,1)S(1)}, u32[]{:S(2)}, u32[]{:S(2)}) collective-permute-start(bf16[128,512]{1,0:T(8,128)(2,1)S(1)} %pad_maximum_fusion.2), channel_id=1, source_target_pairs={{0,2},{2,4},{4,6},{1,3},{3,5},{5,7},{8,10},{10,12},{12,14},{9,11},... | collective-permute-start | bytes 393224 | tf_op jit(solution)/shard_map/ppermute | solution.py:17
  8.7 3.4 %collective-permute-start.1 = (bf16[128,512]{1,0:T(8,128)(2,1)S(1)}, bf16[128,512]{1,0:T(8,128)(2,1)S(1)}, u32[]{:S(2)}, u32[]{:S(2)}) collective-permute-start(bf16[128,512]{1,0:T(8,128)(2,1)S(1)} %pad_maximum_fusion.2), channel_id=1, source_target_pairs={{0,4},{2,6},{1,5},{3,7},{8,12},{10,14},{9,13},{11,15},{16,20},{18,... | collective-permute-start | bytes 393224 | tf_op jit(solution)/shard_map/ppermute | solution.py:17
  12.1 1.3 %collective-permute-start.2 = (bf16[128,512]{1,0:T(8,128)(2,1)S(1)}, bf16[128,512]{1,0:T(8,128)(2,1)S(1)}, u32[]{:S(2)}, u32[]{:S(2)}) collective-permute-start(bf16[128,512]{1,0:T(8,128)(2,1)S(1)} %pad_maximum_fusion.2), channel_id=1, source_target_pairs={{0,6},{1,7},{8,14},{9,15},{16,22},{17,23},{24,30},{25,31}} | collective-permute-start | bytes 393224 | tf_op jit(solution)/shard_map/ppermute | solution.py:17
  13.7 0.3 or_and_fusion
  14.0 1.2 %collective-permute-done.1 = bf16[128,512]{1,0:T(8,128)(2,1)S(1)} collective-permute-done((bf16[128,512]{1,0:T(8,128)(2,1)S(1)}, bf16[128,512]{1,0:T(8,128)(2,1)S(1)}, u32[]{:S(2)}, u32[]{:S(2)}) %collective-permute-start.1) | collective-permute-done | bytes 131104 | tf_op jit(solution)/shard_map/ppermute | solution.py:17
  15.2 0.8 collective-permute-done.2
  16.0 0.1 bitcast_bitcast_fusion
  16.1 0.8 copy-done.3
  17.0 7.9 %while.24 = (s32[]{:T(128)}, bf16[2,5,128,512]{2,3,1,0:T(8,128)(2,1)}, bf16[2,5,128,512]{2,3,1,0:T(8,128)(2,1)}, pred[128,512]{0,1:T(8,128)(4,1)S(1)}, bf16[2,51...) while((s32[]{:T(128)}, ...), condition=%wide.region_4.5_spmd, body=%wide.region_0.4_spmd.sunk | while | flops 257473280 | bytes 10424441 | solution.py:111
  17.0 0.3 fusion.119
  17.3 0.2 select_reduce_fusion.2
  17.6 0.4 copy-done.6
  17.9 0.6 fusion.120
  18.5 1.3 %fusion.121 = bf16[2,5,128,512]{2,3,1,0:T(8,128)(2,1)} fusion(bf16[2,5,128,512]{2,3,1,0:T(8,128)(2,1)} %get-tuple-element.242, s32[]{:T(128)} %get-tuple-element.240, f32[5,128,512]{1,2,0:T(8,128)S(1)} %get-tuple-element.222, f32[5,128]{1,0:T(8,128)S(1)} %bitcast.256, f32[5,128]{1,0:T(8,128)S(1)} %log_add_fusion.2, ...), kind=kOutput, calls=%fused_computation.10.clone.1 | convolution fusion | flops 85524480 | bytes 2336256 | tf_op jit(solution)/shard_map/while/body/eval_jaxpr/tgd,sd->gts/dot_general | solution.py:103
  19.8 1.1 %bitcast_dynamic-update-slice_fusion.7 = bf16[2,5,128,512]{2,3,1,0:T(8,128)(2,1)} fusion(bf16[2,5,128,512]{2,3,1,0:T(8,128)(2,1)} %get-tuple-element.241, s32[]{:T(128)} %get-tuple-element.240, f32[5,128,512]{1,2,0:T(8,128)S(1)} %get-tuple-element.222, f32[5,128]{1,0:T(8,128)S(1)} %log_add_fusion.2, pred[128,512]{0,1:T(8,128)(4,1)S(1)} %get-tuple-element.252), kind=kLoop, calls=%fused_computation.15.clone.1 | loop fusion | flops 983040 | bytes 2034688 | tf_op jit(solution)/shard_map/while/body/jit(dynamic_update_index_in_dim)/dynamic_update_slice | solution.py:111
  20.9 0.3 fusion.119
  21.2 0.2 select_reduce_fusion.2
  21.5 0.4 copy-done.6
  21.9 0.6 fusion.120
  22.4 1.3 %fusion.121 = bf16[2,5,128,512]{2,3,1,0:T(8,128)(2,1)} fusion(bf16[2,5,128,512]{2,3,1,0:T(8,128)(2,1)} %get-tuple-element.242, s32[]{:T(128)} %get-tuple-element.240, f32[5,128,512]{1,2,0:T(8,128)S(1)} %get-tuple-element.222, f32[5,128]{1,0:T(8,128)S(1)} %bitcast.256, f32[5,128]{1,0:T(8,128)S(1)} %log_add_fusion.2, ...), kind=kOutput, calls=%fused_computation.10.clone.1 | convolution fusion | flops 85524480 | bytes 2336256 | tf_op jit(solution)/shard_map/while/body/eval_jaxpr/tgd,sd->gts/dot_general | solution.py:103
  23.7 1.1 %bitcast_dynamic-update-slice_fusion.7 = bf16[2,5,128,512]{2,3,1,0:T(8,128)(2,1)} fusion(bf16[2,5,128,512]{2,3,1,0:T(8,128)(2,1)} %get-tuple-element.241, s32[]{:T(128)} %get-tuple-element.240, f32[5,128,512]{1,2,0:T(8,128)S(1)} %get-tuple-element.222, f32[5,128]{1,0:T(8,128)S(1)} %log_add_fusion.2, pred[128,512]{0,1:T(8,128)(4,1)S(1)} %get-tuple-element.252), kind=kLoop, calls=%fused_computation.15.clone.1 | loop fusion | flops 983040 | bytes 2034688 | tf_op jit(solution)/shard_map/while/body/jit(dynamic_update_index_in_dim)/dynamic_update_slice | solution.py:111
  24.8 8.9 %while.25 = (s32[]{:T(128)}, f32[2,512,128]{1,2,0:T(8,128)}, f32[2,512,128]{1,2,0:T(8,128)}, bf16[2,5,128,512]{2,3,1,0:T(8,128)(2,1)}, bf16[2,128,5,128]{3,1,2,0...) while((s32[]{:T(128)}, f32[2,512,128]{1,2,0:T(8,128)}, ...), condition=%wide.region_6.7_spmd, body=%wide.region_5.6_spmd.sunk | while | flops 167837696 | bytes 3214421 | solution.py:127
  24.8 1.4 %fusion.126 = f32[1,512,128]{2,1,0:T(8,128)S(1)} fusion(bf16[2,5,128,512]{2,3,1,0:T(8,128)(2,1)} %get-tuple-element.277, s32[]{:T(128)} %get-tuple-element.266, bf16[2,128,5,128]{3,1,2,0:T(8,128)(2,1)S(1)} %get-tuple-element.278), kind=kOutput, calls=%fused_computation.35.clone.1 | convolution fusion | flops 83951616 | bytes 1082368 | tf_op jit(solution)/shard_map/while/body/eval_jaxpr/gts,tgd->sd/dot_general | solution.py:122
  26.2 0.1 copy.32
  26.4 0.7 constant_dynamic-update-slice_fusion.2
  27.1 2.2 %fusion.127 = f32[2,512,128]{1,2,0:T(8,128)} fusion(f32[2,512,128]{1,2,0:T(8,128)} %get-tuple-element.268, s32[]{:T(128)} %get-tuple-element.266, bf16[2,5,128,512]{2,3,1,0:T(8,128)(2,1)} %get-tuple-element.279, bf16[2,128,5,128]{3,1,2,0:T(8,128)(2,1)} %get-tuple-element.280), kind=kOutput, calls=%fused_computation.32.clone.1 | convolution fusion | flops 83886080 | bytes 1082880 | tf_op jit(solution)/shard_map/while/body/eval_jaxpr/gts,tgd->sd/dot_general | solution.py:118
  29.3 1.4 %fusion.126 = f32[1,512,128]{2,1,0:T(8,128)S(1)} fusion(bf16[2,5,128,512]{2,3,1,0:T(8,128)(2,1)} %get-tuple-element.277, s32[]{:T(128)} %get-tuple-element.266, bf16[2,128,5,128]{3,1,2,0:T(8,128)(2,1)S(1)} %get-tuple-element.278), kind=kOutput, calls=%fused_computation.35.clone.1 | convolution fusion | flops 83951616 | bytes 1082368 | tf_op jit(solution)/shard_map/while/body/eval_jaxpr/gts,tgd->sd/dot_general | solution.py:122
  30.7 0.1 copy.32
  30.8 0.7 constant_dynamic-update-slice_fusion.2
  31.6 2.2 %fusion.127 = f32[2,512,128]{1,2,0:T(8,128)} fusion(f32[2,512,128]{1,2,0:T(8,128)} %get-tuple-element.268, s32[]{:T(128)} %get-tuple-element.266, bf16[2,5,128,512]{2,3,1,0:T(8,128)(2,1)} %get-tuple-element.279, bf16[2,128,5,128]{3,1,2,0:T(8,128)(2,1)} %get-tuple-element.280), kind=kOutput, calls=%fused_computation.32.clone.1 | convolution fusion | flops 83886080 | bytes 1082880 | tf_op jit(solution)/shard_map/while/body/eval_jaxpr/gts,tgd->sd/dot_general | solution.py:118
  33.7 1.3 %fusion.68 = bf16[512,512]{0,1:T(8,128)(2,1)S(1)} fusion(f32[512,256]{0,1:T(8,128)} %bitcast.252, f32[512,256]{0,1:T(8,128)} %bitcast.250), kind=kLoop, calls=%fused_computation.77 | loop fusion | flops 1048576 | bytes 1572864 | tf_op jit(solution)/shard_map/convert_element_type | solution.py:131
  35.1 0.8 fusion.101
  35.8 1.3 %collective-permute-start.3 = (bf16[128,512]{0,1:T(8,128)(2,1)}, bf16[128,512]{0,1:T(8,128)(2,1)S(1)}, u32[]{:S(2)}, u32[]{:S(2)}) collective-permute-start(bf16[128,512]{0,1:T(8,128)(2,1)} %get-tuple-element.122), channel_id=1, source_target_pairs={{2,0},{4,2},{6,4},{3,1},{5,3},{7,5},{10,8},{12,10},{14,12},{11,9},... | collective-permute-start | bytes 393224 | tf_op jit(solution)/shard_map/ppermute | solution.py:17
  37.1 1.3 %collective-permute-start.4 = (bf16[128,512]{0,1:T(8,128)(2,1)}, bf16[128,512]{0,1:T(8,128)(2,1)S(1)}, u32[]{:S(2)}, u32[]{:S(2)}) collective-permute-start(bf16[128,512]{0,1:T(8,128)(2,1)} %get-tuple-element.124), channel_id=1, source_target_pairs={{4,0},{6,2},{5,1},{7,3},{12,8},{14,10},{13,9},{15,11},{20,16},{22,... | collective-permute-start | bytes 393224 | tf_op jit(solution)/shard_map/ppermute | solution.py:17
  38.4 1.3 %collective-permute-start.5 = (bf16[128,512]{0,1:T(8,128)(2,1)}, bf16[128,512]{0,1:T(8,128)(2,1)}, u32[]{:S(2)}, u32[]{:S(2)}) collective-permute-start(bf16[128,512]{0,1:T(8,128)(2,1)} %get-tuple-element.123), channel_id=1, source_target_pairs={{6,0},{7,1},{14,8},{15,9},{22,16},{23,17},{30,24},{31,25}} | collective-permute-start | bytes 393224 | tf_op jit(solution)/shard_map/ppermute | solution.py:17
  39.7 3.2 %collective-permute-done.3 = bf16[128,512]{0,1:T(8,128)(2,1)S(1)} collective-permute-done((bf16[128,512]{0,1:T(8,128)(2,1)}, bf16[128,512]{0,1:T(8,128)(2,1)S(1)}, u32[]{:S(2)}, u32[]{:S(2)}) %collective-permute-start.3) | collective-permute-done | bytes 131104 | tf_op jit(solution)/shard_map/ppermute | solution.py:17
  42.9 2.7 %collective-permute-done.4 = bf16[128,512]{0,1:T(8,128)(2,1)S(1)} collective-permute-done((bf16[128,512]{0,1:T(8,128)(2,1)}, bf16[128,512]{0,1:T(8,128)(2,1)S(1)}, u32[]{:S(2)}, u32[]{:S(2)}) %collective-permute-start.4) | collective-permute-done | bytes 131104 | tf_op jit(solution)/shard_map/ppermute | solution.py:17
  45.6 0.7 copy-done.7
  46.2 1.4 %collective-permute-done.5 = bf16[128,512]{0,1:T(8,128)(2,1)} collective-permute-done((bf16[128,512]{0,1:T(8,128)(2,1)}, bf16[128,512]{0,1:T(8,128)(2,1)}, u32[]{:S(2)}, u32[]{:S(2)}) %collective-permute-start.5) | collective-permute-done | bytes 131104 | tf_op jit(solution)/shard_map/ppermute | solution.py:17
  47.7 1.1 %fusion.81 = bf16[128,512]{0,1:T(8,128)(2,1)S(1)} fusion(f32[512,256]{0,1:T(8,128)S(1)} %bitcast.251, f32[512,256]{0,1:T(8,128)} %bitcast.253, bf16[128,512]{0,1:T(8,128)(2,1)} %collective-permute-done.5, bf16[128,512]{0,1:T(8,128)(2,1)} %copy-done.7, bf16[128,512]{0,1:T(8,128)(2,1)S(1)} %collective-permute-done.3), kind=kLoop, calls=%fused_computation.104 | loop fusion | flops 524288 | bytes 1572864 | tf_op jit(solution)/shard_map/convert.1
  48.8 0.6 fusion.46
  49.4 1.2 %copy-done.1 = bf16[1,5120,256]{2,1,0:T(8,128)(2,1)S(1)} copy-done((bf16[1,5120,256]{2,1,0:T(8,128)(2,1)S(1)}, bf16[1,5120,256]{2,1,0:T(8,128)(2,1)}, u32[]{:S(2)}) %copy-start.1) | copy-done | bytes 2621464
  50.5 1.4 %fusion.39 = bf16[128,2560]{1,0:T(8,128)(2,1)} fusion(f32[128,2560]{1,0:T(8,128)S(1)} %fusion.46, bf16[1,5120,256]{2,1,0:T(8,128)(2,1)S(1)} %copy-done.1, s32[]{:T(128)S(6)} %select_n.30, bf16[128,512]{0,1:T(8,128)(2,1)S(1)} %fusion.81), kind=kOutput, calls=%fused_computation.50 | convolution fusion | flops 168427520 | bytes 3342340 | tf_op jit(solution)/shard_map/dot_general | solution.py:147
  51.9 0.6 fusion.49
  52.5 1.9 %collective-permute-done.6 = bf16[128,2560]{1,0:T(8,128)(2,1)} collective-permute-done((bf16[128,2560]{1,0:T(8,128)(2,1)}, bf16[128,2560]{1,0:T(8,128)(2,1)}, u32[]{:S(2)}, u32[]{:S(2)}) %collective-permute-start.6) | collective-permute-done | bytes 655392 | tf_op jit(solution)/shard_map/ppermute | solution.py:155
  54.4 1.7 %fusion.38 = f32[128,2560]{1,0:T(8,128)S(1)} fusion(f32[128,2560]{1,0:T(8,128)S(1)} %fusion.49, bf16[128,2560]{1,0:T(8,128)(2,1)} %collective-permute-done.6, bf16[1,5120,256]{2,1,0:T(8,128)(2,1)S(1)} %copy-done.2, s32[]{:T(128)S(6)} %select_n.29, bf16[128,512]{0,1:T(8,128)(2,1)S(1)} %fusion.81), kind=kOutput, calls=%fused_computation.49 | convolution fusion | flops 168755200 | bytes 4653060 | tf_op jit(solution)/shard_map/dot_general | solution.py:147
  56.1 0.6 fusion.45
  56.8 1.3 %collective-permute-start.7 = (bf16[32,2560]{1,0:T(8,128)(2,1)S(1)}, bf16[32,2560]{1,0:T(8,128)(2,1)S(1)}, u32[]{:S(2)}, u32[]{:S(2)}) collective-permute-start(bf16[32,2560]{1,0:T(8,128)(2,1)S(1)} %fusion.87), channel_id=1, source_target_pairs={{8,0},{16,8},{24,16},{9,1},{17,9},{25,17},{10,2},{18,10},{26,18},{... | collective-permute-start | bytes 491528 | tf_op jit(solution)/shard_map/ppermute | solution.py:36
  58.1 6.8 %collective-permute-done.7 = bf16[32,2560]{1,0:T(8,128)(2,1)S(1)} collective-permute-done((bf16[32,2560]{1,0:T(8,128)(2,1)S(1)}, bf16[32,2560]{1,0:T(8,128)(2,1)S(1)}, u32[]{:S(2)}, u32[]{:S(2)}) %collective-permute-start.7) | collective-permute-done | bytes 163872 | tf_op jit(solution)/shard_map/ppermute | solution.py:36
  64.9 1.3 %collective-permute-start.8 = (bf16[32,2560]{1,0:T(8,128)(2,1)S(1)}, bf16[32,2560]{1,0:T(8,128)(2,1)S(1)}, u32[]{:S(2)}, u32[]{:S(2)}) collective-permute-start(bf16[32,2560]{1,0:T(8,128)(2,1)S(1)} %fusion.82), channel_id=1, source_target_pairs={{8,0},{16,8},{24,16},{9,1},{17,9},{25,17},{10,2},{18,10},{26,18},{... | collective-permute-start | bytes 491528 | tf_op jit(solution)/shard_map/ppermute | solution.py:36
  66.3 5.9 %collective-permute-done.8 = bf16[32,2560]{1,0:T(8,128)(2,1)S(1)} collective-permute-done((bf16[32,2560]{1,0:T(8,128)(2,1)S(1)}, bf16[32,2560]{1,0:T(8,128)(2,1)S(1)}, u32[]{:S(2)}, u32[]{:S(2)}) %collective-permute-start.8) | collective-permute-done | bytes 163872 | tf_op jit(solution)/shard_map/ppermute | solution.py:36
  72.2 1.3 %collective-permute-start.9 = (bf16[32,2560]{1,0:T(8,128)(2,1)S(1)}, bf16[32,2560]{1,0:T(8,128)(2,1)S(1)}, u32[]{:S(2)}, u32[]{:S(2)}) collective-permute-start(bf16[32,2560]{1,0:T(8,128)(2,1)S(1)} %fusion.83), channel_id=1, source_target_pairs={{8,0},{16,8},{24,16},{9,1},{17,9},{25,17},{10,2},{18,10},{26,18},{... | collective-permute-start | bytes 491528 | tf_op jit(solution)/shard_map/ppermute | solution.py:36
  73.6 5.9 %collective-permute-done.9 = bf16[32,2560]{1,0:T(8,128)(2,1)S(1)} collective-permute-done((bf16[32,2560]{1,0:T(8,128)(2,1)S(1)}, bf16[32,2560]{1,0:T(8,128)(2,1)S(1)}, u32[]{:S(2)}, u32[]{:S(2)}) %collective-permute-start.9) | collective-permute-done | bytes 163872 | tf_op jit(solution)/shard_map/ppermute | solution.py:36
  79.5 1.3 %collective-permute-start.10 = (bf16[32,2560]{1,0:T(8,128)(2,1)S(1)}, bf16[32,2560]{1,0:T(8,128)(2,1)S(1)}, u32[]{:S(2)}, u32[]{:S(2)}) collective-permute-start(bf16[32,2560]{1,0:T(8,128)(2,1)S(1)} %fusion.84), channel_id=1, source_target_pairs={{8,0},{16,8},{24,16},{9,1},{17,9},{25,17},{10,2},{18,10},{26,18},{... | collective-permute-start | bytes 491528 | tf_op jit(solution)/shard_map/ppermute | solution.py:36
  80.8 5.9 %collective-permute-done.10 = bf16[32,2560]{1,0:T(8,128)(2,1)S(1)} collective-permute-done((bf16[32,2560]{1,0:T(8,128)(2,1)S(1)}, bf16[32,2560]{1,0:T(8,128)(2,1)S(1)}, u32[]{:S(2)}, u32[]{:S(2)}) %collective-permute-start.10) | collective-permute-done | bytes 163872 | tf_op jit(solution)/shard_map/ppermute | solution.py:36
  86.8 1.3 %collective-permute-start.11 = (bf16[32,2560]{1,0:T(8,128)(2,1)S(1)}, bf16[32,2560]{1,0:T(8,128)(2,1)S(1)}, u32[]{:S(2)}, u32[]{:S(2)}) collective-permute-start(bf16[32,2560]{1,0:T(8,128)(2,1)S(1)} %fusion.85), channel_id=1, source_target_pairs={{8,0},{16,8},{24,16},{9,1},{17,9},{25,17},{10,2},{18,10},{26,18},{... | collective-permute-start | bytes 491528 | tf_op jit(solution)/shard_map/ppermute | solution.py:36
  88.1 6.4 %collective-permute-done.11 = bf16[32,2560]{1,0:T(8,128)(2,1)S(1)} collective-permute-done((bf16[32,2560]{1,0:T(8,128)(2,1)S(1)}, bf16[32,2560]{1,0:T(8,128)(2,1)S(1)}, u32[]{:S(2)}, u32[]{:S(2)}) %collective-permute-start.11) | collective-permute-done | bytes 163872 | tf_op jit(solution)/shard_map/ppermute | solution.py:36
  94.5 1.3 %collective-permute-start.12 = (bf16[32,2560]{1,0:T(8,128)(2,1)S(1)}, bf16[32,2560]{1,0:T(8,128)(2,1)S(1)}, u32[]{:S(2)}, u32[]{:S(2)}) collective-permute-start(bf16[32,2560]{1,0:T(8,128)(2,1)S(1)} %fusion.86), channel_id=1, source_target_pairs={{8,0},{16,8},{24,16},{9,1},{17,9},{25,17},{10,2},{18,10},{26,18},{... | collective-permute-start | bytes 491528 | tf_op jit(solution)/shard_map/ppermute | solution.py:36
  95.9 5.9 %collective-permute-done.12 = bf16[32,2560]{1,0:T(8,128)(2,1)S(1)} collective-permute-done((bf16[32,2560]{1,0:T(8,128)(2,1)S(1)}, bf16[32,2560]{1,0:T(8,128)(2,1)S(1)}, u32[]{:S(2)}, u32[]{:S(2)}) %collective-permute-start.12) | collective-permute-done | bytes 163872 | tf_op jit(solution)/shard_map/ppermute | solution.py:36
  101.8 1.2 %constant_dynamic-slice_fusion = f32[4,32,2560]{2,1,0:T(8,128)} fusion(f32[7,32,2560]{2,1,0:T(8,128)S(1)} %fusion.71, s32[]{:T(128)S(6)} %select_n.32), kind=kLoop, calls=%fused_computation.121 | loop fusion | bytes 2621444 | tf_op jit(solution)/shard_map/dynamic_slice | solution.py:38
  (43 shorter events, 0.8 us)
Async XLA Ops:
  0.0 2.9 %copy-start = (bf16[1,5120,256]{2,1,0:T(8,128)(2,1)S(1)}, bf16[1,5120,256]{2,1,0:T(8,128)(2,1)}, u32[]{:S(2)}) copy-start(bf16[1,5120,256]{2,1,0:T(8,128)(2,1)} %param.14) | copy-start | bytes 7864324
  0.0 3.3 %copy-start.4 = (bf16[1,128,5120]{2,1,0:T(8,128)(2,1)S(1)}, bf16[1,128,5120]{2,1,0:T(8,128)(2,1)}, u32[]{:S(2)}) copy-start(bf16[1,128,5120]{2,1,0:T(8,128)(2,1)} %param.10) | copy-start | bytes 3932164
  3.3 10.3 %copy-start.8 = (s32[512]{0:T(512)S(1)}, s32[512]{0:T(512)}, u32[]{:S(2)}) copy-start(s32[512]{0:T(512)} %param.15) | copy-start | bytes 6148
  3.8 10.1 %collective-permute-start = (bf16[128,512]{1,0:T(8,128)(2,1)S(1)}, bf16[128,512]{1,0:T(8,128)(2,1)S(1)}, u32[]{:S(2)}, u32[]{:S(2)}) collective-permute-start(bf16[128,512]{1,0:T(8,128)(2,1)S(1)} %pad_maximum_fusion.2), channel_id=1, source_target_pairs={{0,2},{2,4},{4,6},{1,3},{3,5},{5,7},{8,10},{10,12},{12,14},{9,11},... | collective-permute-start | bytes 393224 | tf_op jit(solution)/shard_map/ppermute | solution.py:17
  8.7 6.5 %collective-permute-start.1 = (bf16[128,512]{1,0:T(8,128)(2,1)S(1)}, bf16[128,512]{1,0:T(8,128)(2,1)S(1)}, u32[]{:S(2)}, u32[]{:S(2)}) collective-permute-start(bf16[128,512]{1,0:T(8,128)(2,1)S(1)} %pad_maximum_fusion.2), channel_id=1, source_target_pairs={{0,4},{2,6},{1,5},{3,7},{8,12},{10,14},{9,13},{11,15},{16,20},{18,... | collective-permute-start | bytes 393224 | tf_op jit(solution)/shard_map/ppermute | solution.py:17
  12.1 3.8 %collective-permute-start.2 = (bf16[128,512]{1,0:T(8,128)(2,1)S(1)}, bf16[128,512]{1,0:T(8,128)(2,1)S(1)}, u32[]{:S(2)}, u32[]{:S(2)}) collective-permute-start(bf16[128,512]{1,0:T(8,128)(2,1)S(1)} %pad_maximum_fusion.2), channel_id=1, source_target_pairs={{0,6},{1,7},{8,14},{9,15},{16,22},{17,23},{24,30},{25,31}} | collective-permute-start | bytes 393224 | tf_op jit(solution)/shard_map/ppermute | solution.py:17
  16.0 1.0 copy-start.3
  17.0 1.0 copy-start.6
  20.9 1.0 copy-start.6
  33.7 13.9 %copy-start.5 = (f32[2,512,128]{1,2,0:T(8,128)S(1)}, f32[2,512,128]{1,2,0:T(8,128)}, u32[]{:S(2)}) copy-start(f32[2,512,128]{1,2,0:T(8,128)} %get-tuple-element.88) | copy-start | bytes 1572868
  35.8 7.1 %collective-permute-start.3 = (bf16[128,512]{0,1:T(8,128)(2,1)}, bf16[128,512]{0,1:T(8,128)(2,1)S(1)}, u32[]{:S(2)}, u32[]{:S(2)}) collective-permute-start(bf16[128,512]{0,1:T(8,128)(2,1)} %get-tuple-element.122), channel_id=1, source_target_pairs={{2,0},{4,2},{6,4},{3,1},{5,3},{7,5},{10,8},{12,10},{14,12},{11,9},... | collective-permute-start | bytes 393224 | tf_op jit(solution)/shard_map/ppermute | solution.py:17
  37.1 8.5 %collective-permute-start.4 = (bf16[128,512]{0,1:T(8,128)(2,1)}, bf16[128,512]{0,1:T(8,128)(2,1)S(1)}, u32[]{:S(2)}, u32[]{:S(2)}) collective-permute-start(bf16[128,512]{0,1:T(8,128)(2,1)} %get-tuple-element.124), channel_id=1, source_target_pairs={{4,0},{6,2},{5,1},{7,3},{12,8},{14,10},{13,9},{15,11},{20,16},{22,... | collective-permute-start | bytes 393224 | tf_op jit(solution)/shard_map/ppermute | solution.py:17
  38.4 9.3 %collective-permute-start.5 = (bf16[128,512]{0,1:T(8,128)(2,1)}, bf16[128,512]{0,1:T(8,128)(2,1)}, u32[]{:S(2)}, u32[]{:S(2)}) collective-permute-start(bf16[128,512]{0,1:T(8,128)(2,1)} %get-tuple-element.123), channel_id=1, source_target_pairs={{6,0},{7,1},{14,8},{15,9},{22,16},{23,17},{30,24},{31,25}} | collective-permute-start | bytes 393224 | tf_op jit(solution)/shard_map/ppermute | solution.py:17
  45.6 0.7 copy-start.7
  48.8 1.7 %copy-start.1 = (bf16[1,5120,256]{2,1,0:T(8,128)(2,1)S(1)}, bf16[1,5120,256]{2,1,0:T(8,128)(2,1)}, u32[]{:S(2)}) copy-start(bf16[1,5120,256]{2,1,0:T(8,128)(2,1)} %param.13) | copy-start | bytes 7864324
  51.9 2.4 %collective-permute-start.6 = (bf16[128,2560]{1,0:T(8,128)(2,1)}, bf16[128,2560]{1,0:T(8,128)(2,1)}, u32[]{:S(2)}, u32[]{:S(2)}) collective-permute-start(bf16[128,2560]{1,0:T(8,128)(2,1)} %fusion.39), channel_id=1, source_target_pairs={{0,1},{1,0},{2,3},{3,2},{4,5},{5,4},{6,7},{7,6},{8,9},{9,8},{10,11... | collective-permute-start | bytes 1966088 | tf_op jit(solution)/shard_map/ppermute | solution.py:155
  51.9 2.4 %copy-start.2 = (bf16[1,5120,256]{2,1,0:T(8,128)(2,1)S(1)}, bf16[1,5120,256]{2,1,0:T(8,128)(2,1)}, u32[]{:S(2)}) copy-start(bf16[1,5120,256]{2,1,0:T(8,128)(2,1)} %param.13) | copy-start | bytes 7864324
  56.8 8.1 %collective-permute-start.7 = (bf16[32,2560]{1,0:T(8,128)(2,1)S(1)}, bf16[32,2560]{1,0:T(8,128)(2,1)S(1)}, u32[]{:S(2)}, u32[]{:S(2)}) collective-permute-start(bf16[32,2560]{1,0:T(8,128)(2,1)S(1)} %fusion.87), channel_id=1, source_target_pairs={{8,0},{16,8},{24,16},{9,1},{17,9},{25,17},{10,2},{18,10},{26,18},{... | collective-permute-start | bytes 491528 | tf_op jit(solution)/shard_map/ppermute | solution.py:36
  64.9 7.3 %collective-permute-start.8 = (bf16[32,2560]{1,0:T(8,128)(2,1)S(1)}, bf16[32,2560]{1,0:T(8,128)(2,1)S(1)}, u32[]{:S(2)}, u32[]{:S(2)}) collective-permute-start(bf16[32,2560]{1,0:T(8,128)(2,1)S(1)} %fusion.82), channel_id=1, source_target_pairs={{8,0},{16,8},{24,16},{9,1},{17,9},{25,17},{10,2},{18,10},{26,18},{... | collective-permute-start | bytes 491528 | tf_op jit(solution)/shard_map/ppermute | solution.py:36
  72.2 7.2 %collective-permute-start.9 = (bf16[32,2560]{1,0:T(8,128)(2,1)S(1)}, bf16[32,2560]{1,0:T(8,128)(2,1)S(1)}, u32[]{:S(2)}, u32[]{:S(2)}) collective-permute-start(bf16[32,2560]{1,0:T(8,128)(2,1)S(1)} %fusion.83), channel_id=1, source_target_pairs={{8,0},{16,8},{24,16},{9,1},{17,9},{25,17},{10,2},{18,10},{26,18},{... | collective-permute-start | bytes 491528 | tf_op jit(solution)/shard_map/ppermute | solution.py:36
  79.5 7.2 %collective-permute-start.10 = (bf16[32,2560]{1,0:T(8,128)(2,1)S(1)}, bf16[32,2560]{1,0:T(8,128)(2,1)S(1)}, u32[]{:S(2)}, u32[]{:S(2)}) collective-permute-start(bf16[32,2560]{1,0:T(8,128)(2,1)S(1)} %fusion.84), channel_id=1, source_target_pairs={{8,0},{16,8},{24,16},{9,1},{17,9},{25,17},{10,2},{18,10},{26,18},{... | collective-permute-start | bytes 491528 | tf_op jit(solution)/shard_map/ppermute | solution.py:36
  86.8 7.7 %collective-permute-start.11 = (bf16[32,2560]{1,0:T(8,128)(2,1)S(1)}, bf16[32,2560]{1,0:T(8,128)(2,1)S(1)}, u32[]{:S(2)}, u32[]{:S(2)}) collective-permute-start(bf16[32,2560]{1,0:T(8,128)(2,1)S(1)} %fusion.85), channel_id=1, source_target_pairs={{8,0},{16,8},{24,16},{9,1},{17,9},{25,17},{10,2},{18,10},{26,18},{... | collective-permute-start | bytes 491528 | tf_op jit(solution)/shard_map/ppermute | solution.py:36
  94.5 7.2 %collective-permute-start.12 = (bf16[32,2560]{1,0:T(8,128)(2,1)S(1)}, bf16[32,2560]{1,0:T(8,128)(2,1)S(1)}, u32[]{:S(2)}, u32[]{:S(2)}) collective-permute-start(bf16[32,2560]{1,0:T(8,128)(2,1)S(1)} %fusion.86), channel_id=1, source_target_pairs={{8,0},{16,8},{24,16},{9,1},{17,9},{25,17},{10,2},{18,10},{26,18},{... | collective-permute-start | bytes 491528 | tf_op jit(solution)/shard_map/ppermute | solution.py:36

commit v4 on v3

--- a/solution.py
+++ b/solution.py
@@ -6,7 +6,7 @@
 from jax.sharding import PartitionSpec as P
 
 
-CHAIN_CHUNKS = 4
+CHAIN_CHUNKS = 2
 
 
 def shifted(x, axis, d, length, up):
@@ -82,49 +82,29 @@
     allowed = present & (col_pos <= row_pos) & ((kept == 1) | (col_pos == row_pos))
     allowed = lax.optimization_barrier(allowed)
 
-    def one_group(packed):
-        query_group, grad_group, key_group, value_group = packed
-        scores = (
-            jnp.einsum("tgd,sd->gts", query_group, key_group, preferred_element_type=jnp.float32)
-            * scaling
-        )
-        masked = jnp.where(allowed, scores, -1e30)
-        top_score = jnp.max(masked, axis=-1, keepdims=True)
-        totals = jnp.sum(
-            jnp.where(allowed, jnp.exp(masked - top_score), 0.0), axis=-1, keepdims=True
-        )
-        log_total = top_score + jnp.log(totals)
-        prob_full = jnp.where(allowed, jnp.exp(masked - log_total), 0.0)
-        prob_low = prob_full.astype(jnp.bfloat16)
-        attended = jnp.einsum(
-            "gts,sd->tgd", prob_low, value_group, preferred_element_type=jnp.float32
-        )
-        row_dots = jnp.sum(grad_group.astype(jnp.float32) * attended, axis=-1)
-        dprob = jnp.einsum(
-            "tgd,sd->gts", grad_group, value_group, preferred_element_type=jnp.float32
-        )
-        score_low = (prob_full * (dprob - jnp.transpose(row_dots, (1, 0))[..., None])).astype(
-            jnp.bfloat16
-        )
-        return (prob_low, score_low)
-
-    probs_b, dscore_b = lax.map(
-        one_group,
-        (query_major, grad_major, jnp.moveaxis(key_heads, 1, 0), jnp.moveaxis(value_heads, 1, 0)),
+    key_major = jnp.moveaxis(key_heads, 1, 0)
+    value_major = jnp.moveaxis(value_heads, 1, 0)
+    scores = (
+        jnp.einsum("ktgd,ksd->kgts", query_major, key_major, preferred_element_type=jnp.float32)
+        * scaling
     )
-
-    def per_group(packed):
-        prob_group, score_group, query_group, grad_group = packed
-        value_term = jnp.einsum(
-            "gts,tgd->sd", prob_group, grad_group, preferred_element_type=jnp.float32
-        )
-        key_term = (
-            jnp.einsum("gts,tgd->sd", score_group, query_group, preferred_element_type=jnp.float32)
-            * scaling
-        )
-        return (key_term, value_term)
-
-    key_term, value_term = lax.map(per_group, (probs_b, dscore_b, query_major, grad_major))
+    masked = jnp.where(allowed, scores, -1e30)
+    top_score = jnp.max(masked, axis=-1, keepdims=True)
+    totals = jnp.sum(jnp.where(allowed, jnp.exp(masked - top_score), 0.0), axis=-1, keepdims=True)
+    log_total = top_score + jnp.log(totals)
+    prob_full = jnp.where(allowed, jnp.exp(masked - log_total), 0.0)
+    probs_b = prob_full.astype(jnp.bfloat16)
+    attended = jnp.einsum("kgts,ksd->ktgd", probs_b, value_major, preferred_element_type=jnp.float32)
+    row_dots = jnp.sum(grad_major.astype(jnp.float32) * attended, axis=-1)
+    dprob = jnp.einsum("ktgd,ksd->kgts", grad_major, value_major, preferred_element_type=jnp.float32)
+    dscore_b = (prob_full * (dprob - jnp.transpose(row_dots, (0, 2, 1))[..., None])).astype(
+        jnp.bfloat16
+    )
+    value_term = jnp.einsum("kgts,ktgd->ksd", probs_b, grad_major, preferred_element_type=jnp.float32)
+    key_term = (
+        jnp.einsum("kgts,ktgd->ksd", dscore_b, query_major, preferred_element_type=jnp.float32)
+        * scaling
+    )
     key_flat = jnp.moveaxis(key_term, 0, 1).reshape(seq_rows, kv_cols)
     value_flat = jnp.moveaxis(value_term, 0, 1).reshape(seq_rows, kv_cols)
     terms = jnp.concatenate((key_flat, value_flat), axis=1)

time: 104 us -> 92.8 us (0.89)
  matrix products: 19.2 us -> 12.3 us
  waiting for transfers between devices: 47.8 us -> 44.4 us
  local copies, waits for them, and re-layouts: 7.72 us -> 9.14 us
  starting transfers between devices: 21.2 us -> 19.9 us
    dot_general x10 -> x4, matrix products: 11.6 us -> 5.56 us  [the longest x1 3.77 us: per_device(): jnp.einsum('kgts,ktgd->ksd', dscore_b, query_major, preferred_element_typ...]
    ppermute x6, waiting for transfers between devices: 9.26 us -> 6.58 us  [shifted(): return lax.ppermute(x, axis, perm)]
    ppermute x6 -> x4, starting transfers between devices: 7.75 us -> 5.17 us  [suffix_pipeline(): recv = lax.ppermute(acc.astype(jnp.bfloat16), axis, perm)]
    dot_general x1, matrix products: 2.79 us -> 0.51 us  [per_device(): jnp.dot(tokens, w_key[0], preferred_element_type=jnp.float32)]
    dynamic_update_slice x2 -> x0, other arithmetic: 2.14 us -> none  [per_device(): lax.map(one_group, (query_major, grad_major, jnp.moveaxis(key_heads, 1, 0...]
    another operation x0 -> x2, local copies, waits for them, and re-layouts: none -> 1.82 us  [the longest x1 0.92 us: per_device(): query_heads = query[0].reshape(tok_rows, kv_local, group_size, head_dim)]
    dynamic_update_slice x4 -> x0, local copies, waits for them, and re-layouts: 1.69 us -> none  [per_device(): lax.map(per_group, (probs_b, dscore_b, query_major, grad_major))]
    dot_general x1, matrix products: 0.51 us -> 2.02 us  [per_device(): jnp.dot(tokens, w_value[0], preferred_element_type=jnp.float32)]
  transfers between devices with their start and end apart: 13 -> 11, of which waited for: 12 -> 8; matrix products, arithmetic and copies ran while one was open for 1% -> 3% of each run, Pallas kernels for 0% -> 0%
where the time goes in v4:
time: 92.8 us; the launch traced here: 92.3 us
  waiting for transfers between devices  44.4 us (48%)
  starting transfers between devices  19.9 us (21%)
  matrix products  12.3 us (13%)
  local copies, waits for them, and re-layouts  9.14 us (10%)
  other arithmetic  6.32 us (7%)
    ppermute x4, waiting for transfers between devices, suffix_pipeline(): recv = lax.ppermute(acc.astype(jnp.bfloat16), axis, perm)  35.9 us
    ppermute x6, starting transfers between devices, shifted(): return lax.ppermute(x, axis, perm)  14.7 us
    ppermute x6, waiting for transfers between devices, shifted(): return lax.ppermute(x, axis, perm)  6.58 us
    ppermute x4, starting transfers between devices, suffix_pipeline(): recv = lax.ppermute(acc.astype(jnp.bfloat16), axis, perm)  5.17 us
    dot_general x1, matrix products, per_device(): jnp.einsum('kgts,ktgd->ksd', dscore_b, query_major, preferred_element_typ...  3.77 us
    dot_general x2, matrix products, partial_for(): lax.dot_general(grad_key, wk, contract, preferred_element_type=jnp.float32)  3.1 us
    unnamed x25, local copies, waits for them, and re-layouts  2.54 us
    dot_general x1, matrix products, per_device(): jnp.dot(tokens, w_value[0], preferred_element_type=jnp.float32)  2.02 us
  transfers between devices with their start and end apart: 11, of which 8 were waited for; matrix products, arithmetic and copies ran while one was open for 3% of the time, Pallas kernels for 0%

profile of v4, /device:TPU:0, one launch (start us, length us, event | category | flops | bytes accessed | tf_op | source)
XLA Modules:
  0.0 92.3 jit_solution(8991530508301659425)
XLA Ops:
  0.0 1.7 %copy-done = bf16[1,5120,256]{2,1,0:T(8,128)(2,1)S(1)} copy-done((bf16[1,5120,256]{2,1,0:T(8,128)(2,1)S(1)}, bf16[1,5120,256]{2,1,0:T(8,128)(2,1)}, u32[]{:S(2)}) %copy-start) | copy-done | bytes 2621464
  1.7 2.0 %fusion.37 = bf16[128,256]{1,0:T(8,128)(2,1)S(1)} fusion(bf16[1,5120,256]{2,1,0:T(8,128)(2,1)S(1)} %copy-done, bf16[1,128,5120]{2,1,0:T(8,128)(2,1)} %param.6), kind=kOutput, calls=%fused_computation.46 | convolution fusion | flops 335577088 | bytes 3997696 | tf_op jit(solution)/shard_map/dot_general | solution.py:54
  3.8 0.0 copy-done.5
  3.8 0.0 copy-start.11
  3.8 0.0 copy-start.7
  3.8 0.0 copy-start.6
  3.8 0.5 fusion.32
  4.3 0.7 pad_maximum_fusion.2
  5.0 6.5 %collective-permute-start.2 = (bf16[128,512]{1,0:T(8,128)(2,1)}, bf16[128,512]{1,0:T(8,128)(2,1)}, u32[]{:S(2)}, u32[]{:S(2)}) collective-permute-start(bf16[128,512]{1,0:T(8,128)(2,1)} %pad_maximum_fusion.2), channel_id=1, source_target_pairs={{0,6},{1,7},{8,14},{9,15},{16,22},{17,23},{24,30},{25,31}} | collective-permute-start | bytes 393224 | tf_op jit(solution)/shard_map/ppermute | solution.py:17
  11.5 1.9 %collective-permute-start.1 = (bf16[128,512]{1,0:T(8,128)(2,1)}, bf16[128,512]{1,0:T(8,128)(2,1)}, u32[]{:S(2)}, u32[]{:S(2)}) collective-permute-start(bf16[128,512]{1,0:T(8,128)(2,1)} %pad_maximum_fusion.2), channel_id=1, source_target_pairs={{0,4},{2,6},{1,5},{3,7},{8,12},{10,14},{9,13},{11,15},{16,20},{18,... | collective-permute-start | bytes 393224 | tf_op jit(solution)/shard_map/ppermute | solution.py:17
  13.4 2.5 %collective-permute-start = (bf16[128,512]{1,0:T(8,128)(2,1)}, bf16[128,512]{1,0:T(8,128)(2,1)}, u32[]{:S(2)}, u32[]{:S(2)}) collective-permute-start(bf16[128,512]{1,0:T(8,128)(2,1)} %pad_maximum_fusion.2), channel_id=1, source_target_pairs={{0,2},{2,4},{4,6},{1,3},{3,5},{5,7},{8,10},{10,12},{12,14},{9,11},... | collective-permute-start | bytes 393224 | tf_op jit(solution)/shard_map/ppermute | solution.py:17
  15.9 0.1 add_bitcast_fusion
  16.0 0.1 add_compare_fusion
  16.0 0.3 or_and_fusion
  16.3 0.9 copy.10
  17.2 0.9 copy.8
  18.2 0.0 collective-permute-done.2
  18.2 0.5 collective-permute-done.1
  18.6 0.0 collective-permute-done
  18.6 1.1 %pad_maximum_fusion.1 = bf16[512,512]{1,0:T(8,128)(2,1)S(1)} fusion(bf16[128,512]{1,0:T(8,128)(2,1)} %collective-permute-done.2, bf16[128,512]{1,0:T(8,128)(2,1)} %collective-permute-done.1, bf16[128,512]{1,0:T(8,128)(2,1)} %collective-permute-done, bf16[128,256]{1,0:T(8,128)(2,1)S(1)} %fusion.37, bf16[128,256]{1,0:T(8,128)(2,1)S(1)} %fusion.32), kind=kLoop, calls=%fused_computation.63 | loop fusion | flops 2621440 | bytes 1048576 | tf_op jit(solution)/shard_map/concatenate | solution.py:59
  19.7 0.7 fusion.82
  20.4 1.0 %reshape.106 = bf16[512,2,128]{2,1,0:T(2,128)(2,1)S(1)} reshape(bf16[512,256]{1,0:T(8,128)(2,1)} %get-tuple-element.8) | data formatting | bytes 524288 | tf_op jit(solution)/shard_map/reshape | solution.py:62
  21.4 0.9 copy.16
  22.3 0.5 fusion.83
  22.9 0.5 select_reduce_fusion
  23.4 0.6 fusion.53
  24.0 0.4 copy-done.4
  24.4 0.6 fusion.31
  25.0 0.3 copy-done.9
  25.3 3.8 %fusion.30 = f32[2,512,128]{1,2,0:T(8,128)} fusion(f32[2,5,128,512]{2,3,1,0:T(8,128)} %copy-done.4, bf16[2,512,128,1]{1,2,3,0:T(8,128)(2,1)} %copy.16, f32[2,5,128]{2,1,0:T(8,128)S(1)} %bitcast.171, f32[2,5,128]{2,1,0:T(8,128)S(1)} %log_add_fusion, pred[128,512]{0,1:T(8,128)(4,1)S(1)} %or_and_fusion, bf16[128,2,5,128]{0,3,2,1:T(8,128)(2,1)S(1)} %copy-done.9, ...), kind=kOutput, calls=%fused_computation.43 | convolution fusion | flops 338952192 | bytes 4139008 | tf_op jit(solution)/shard_map/kgts,ktgd->ksd/dot_general | solution.py:105
  29.1 1.1 %fusion.42 = bf16[512,512]{0,1:T(8,128)(2,1)S(1)} fusion(f32[512,256]{0,1:T(8,128)S(1)} %bitcast.162, f32[512,256]{0,1:T(8,128)} %bitcast.164), kind=kLoop, calls=%fused_computation.47 | loop fusion | flops 1048576 | bytes 1572864 | tf_op jit(solution)/shard_map/convert_element_type | solution.py:111
  30.2 0.8 fusion.81
  31.0 1.3 %collective-permute-start.5 = (bf16[128,512]{0,1:T(8,128)(2,1)}, bf16[128,512]{0,1:T(8,128)(2,1)S(1)}, u32[]{:S(2)}, u32[]{:S(2)}) collective-permute-start(bf16[128,512]{0,1:T(8,128)(2,1)} %get-tuple-element.6), channel_id=1, source_target_pairs={{6,0},{7,1},{14,8},{15,9},{22,16},{23,17},{30,24},{31,25}} | collective-permute-start | bytes 393224 | tf_op jit(solution)/shard_map/ppermute | solution.py:17
  32.3 1.3 %collective-permute-start.4 = (bf16[128,512]{0,1:T(8,128)(2,1)}, bf16[128,512]{0,1:T(8,128)(2,1)S(1)}, u32[]{:S(2)}, u32[]{:S(2)}) collective-permute-start(bf16[128,512]{0,1:T(8,128)(2,1)} %get-tuple-element.7), channel_id=1, source_target_pairs={{4,0},{6,2},{5,1},{7,3},{12,8},{14,10},{13,9},{15,11},{20,16},{22,... | collective-permute-start | bytes 393224 | tf_op jit(solution)/shard_map/ppermute | solution.py:17
  33.6 1.3 %collective-permute-start.3 = (bf16[128,512]{0,1:T(8,128)(2,1)S(1)}, bf16[128,512]{0,1:T(8,128)(2,1)}, u32[]{:S(2)}, u32[]{:S(2)}) collective-permute-start(bf16[128,512]{0,1:T(8,128)(2,1)S(1)} %get-tuple-element.5), channel_id=1, source_target_pairs={{2,0},{4,2},{6,4},{3,1},{5,3},{7,5},{10,8},{12,10},{14,12},{11,9},... | collective-permute-start | bytes 393224 | tf_op jit(solution)/shard_map/ppermute | solution.py:17
  34.9 0.0 copy-start.2
  34.9 4.4 %collective-permute-done.5 = bf16[128,512]{0,1:T(8,128)(2,1)S(1)} collective-permute-done((bf16[128,512]{0,1:T(8,128)(2,1)}, bf16[128,512]{0,1:T(8,128)(2,1)S(1)}, u32[]{:S(2)}, u32[]{:S(2)}) %collective-permute-start.5) | collective-permute-done | bytes 131104 | tf_op jit(solution)/shard_map/ppermute | solution.py:17
  39.3 1.7 %collective-permute-done.4 = bf16[128,512]{0,1:T(8,128)(2,1)S(1)} collective-permute-done((bf16[128,512]{0,1:T(8,128)(2,1)}, bf16[128,512]{0,1:T(8,128)(2,1)S(1)}, u32[]{:S(2)}, u32[]{:S(2)}) %collective-permute-start.4) | collective-permute-done | bytes 131104 | tf_op jit(solution)/shard_map/ppermute | solution.py:17
  41.0 0.0 collective-permute-done.3
  41.0 1.0 %fusion.62 = bf16[128,512]{0,1:T(8,128)(2,1)S(1)} fusion(f32[512,256]{0,1:T(8,128)} %bitcast.165, f32[512,256]{0,1:T(8,128)S(1)} %bitcast.163, bf16[128,512]{0,1:T(8,128)(2,1)S(1)} %collective-permute-done.5, bf16[128,512]{0,1:T(8,128)(2,1)S(1)} %collective-permute-done.4, bf16[128,512]{0,1:T(8,128)(2,1)} %collective-permute-done.3), kind=kLoop, calls=%fused_computation.76 | loop fusion | flops 524288 | bytes 1572864 | tf_op jit(solution)/shard_map/convert.1
  42.1 0.6 fusion.12
  42.6 1.4 %fusion.1 = bf16[128,2560]{1,0:T(8,128)(2,1)} fusion(f32[128,2560]{1,0:T(8,128)S(1)} %fusion.12, bf16[1,5120,256]{2,1,0:T(8,128)(2,1)S(1)} %copy-done.2, s32[]{:T(128)S(6)} %select_n.33, bf16[128,512]{0,1:T(8,128)(2,1)S(1)} %fusion.62), kind=kOutput, calls=%fused_computation.6 | convolution fusion | flops 168427520 | bytes 3342340 | tf_op jit(solution)/shard_map/dot_general | solution.py:127
  44.1 0.0 collective-permute-start.6
  44.1 0.6 fusion.15
  44.6 1.9 %collective-permute-done.6 = bf16[128,2560]{1,0:T(8,128)(2,1)} collective-permute-done((bf16[128,2560]{1,0:T(8,128)(2,1)}, bf16[128,2560]{1,0:T(8,128)(2,1)}, u32[]{:S(2)}, u32[]{:S(2)}) %collective-permute-start.6) | collective-permute-done | bytes 655392 | tf_op jit(solution)/shard_map/ppermute | solution.py:135
  46.5 1.7 %fusion = f32[128,2560]{1,0:T(8,128)S(1)} fusion(f32[128,2560]{1,0:T(8,128)S(1)} %fusion.15, bf16[128,2560]{1,0:T(8,128)(2,1)} %collective-permute-done.6, bf16[1,5120,256]{2,1,0:T(8,128)(2,1)S(1)} %copy-done.3, s32[]{:T(128)S(6)} %select_n.32, bf16[128,512]{0,1:T(8,128)(2,1)S(1)} %fusion.62), kind=kOutput, calls=%fused_computation.5 | convolution fusion | flops 168755200 | bytes 4653060 | tf_op jit(solution)/shard_map/dot_general | solution.py:127
  48.2 0.2 broadcast_in_dim.24
  48.4 1.0 %fusion.3 = f32[5,64,2560]{2,1,0:T(8,128)S(1)} fusion(s32[]{:T(128)S(6)} %select_n.34, f32[3,64,2560]{2,1,0:T(8,128)S(1)} %broadcast_in_dim.24, f32[2,64,2560]{2,1,0:T(8,128)S(1)} %bitcast.161), kind=kLoop, calls=%fused_computation.8 | loop fusion | flops 1638400 | bytes 6553604 | tf_op jit(solution)/shard_map/concatenate | solution.py:26
  49.4 1.3 %collective-permute-start.7 = (bf16[64,2560]{1,0:T(8,128)(2,1)S(1)}, bf16[64,2560]{1,0:T(8,128)(2,1)S(1)}, u32[]{:S(2)}, u32[]{:S(2)}) collective-permute-start(bf16[64,2560]{1,0:T(8,128)(2,1)S(1)} %fusion.52), channel_id=1, source_target_pairs={{8,0},{16,8},{24,16},{9,1},{17,9},{25,17},{10,2},{18,10},{26,18},{... | collective-permute-start | bytes 983048 | tf_op jit(solution)/shard_map/ppermute | solution.py:36
  50.8 10.3 %collective-permute-done.7 = bf16[64,2560]{1,0:T(8,128)(2,1)S(1)} collective-permute-done((bf16[64,2560]{1,0:T(8,128)(2,1)S(1)}, bf16[64,2560]{1,0:T(8,128)(2,1)S(1)}, u32[]{:S(2)}, u32[]{:S(2)}) %collective-permute-start.7) | collective-permute-done | bytes 327712 | tf_op jit(solution)/shard_map/ppermute | solution.py:36
  61.1 0.1 fusion.49
  61.2 1.3 %collective-permute-start.8 = (bf16[64,2560]{1,0:T(8,128)(2,1)S(1)}, bf16[64,2560]{1,0:T(8,128)(2,1)S(1)}, u32[]{:S(2)}, u32[]{:S(2)}) collective-permute-start(bf16[64,2560]{1,0:T(8,128)(2,1)S(1)} %fusion.49), channel_id=1, source_target_pairs={{8,0},{16,8},{24,16},{9,1},{17,9},{25,17},{10,2},{18,10},{26,18},{... | collective-permute-start | bytes 983048 | tf_op jit(solution)/shard_map/ppermute | solution.py:36
  62.5 0.1 bitcast_dynamic-update-slice_fusion.2
  62.5 9.4 %collective-permute-done.8 = bf16[64,2560]{1,0:T(8,128)(2,1)S(1)} collective-permute-done((bf16[64,2560]{1,0:T(8,128)(2,1)S(1)}, bf16[64,2560]{1,0:T(8,128)(2,1)S(1)}, u32[]{:S(2)}, u32[]{:S(2)}) %collective-permute-start.8) | collective-permute-done | bytes 327712 | tf_op jit(solution)/shard_map/ppermute | solution.py:36
  71.9 0.1 fusion.50
  72.0 1.3 %collective-permute-start.9 = (bf16[64,2560]{1,0:T(8,128)(2,1)S(1)}, bf16[64,2560]{1,0:T(8,128)(2,1)S(1)}, u32[]{:S(2)}, u32[]{:S(2)}) collective-permute-start(bf16[64,2560]{1,0:T(8,128)(2,1)S(1)} %fusion.50), channel_id=1, source_target_pairs={{8,0},{16,8},{24,16},{9,1},{17,9},{25,17},{10,2},{18,10},{26,18},{... | collective-permute-start | bytes 983048 | tf_op jit(solution)/shard_map/ppermute | solution.py:36
  73.3 0.1 bitcast_dynamic-update-slice_fusion.1
  73.4 8.5 %collective-permute-done.9 = bf16[64,2560]{1,0:T(8,128)(2,1)S(1)} collective-permute-done((bf16[64,2560]{1,0:T(8,128)(2,1)S(1)}, bf16[64,2560]{1,0:T(8,128)(2,1)S(1)}, u32[]{:S(2)}, u32[]{:S(2)}) %collective-permute-start.9) | collective-permute-done | bytes 327712 | tf_op jit(solution)/shard_map/ppermute | solution.py:36
  81.9 0.1 fusion.51
  82.0 1.3 %collective-permute-start.10 = (bf16[64,2560]{1,0:T(8,128)(2,1)S(1)}, bf16[64,2560]{1,0:T(8,128)(2,1)S(1)}, u32[]{:S(2)}, u32[]{:S(2)}) collective-permute-start(bf16[64,2560]{1,0:T(8,128)(2,1)S(1)} %fusion.51), channel_id=1, source_target_pairs={{8,0},{16,8},{24,16},{9,1},{17,9},{25,17},{10,2},{18,10},{26,18},{... | collective-permute-start | bytes 983048 | tf_op jit(solution)/shard_map/ppermute | solution.py:36
  83.3 0.1 bitcast_dynamic-update-slice_fusion
  83.4 7.7 %collective-permute-done.10 = bf16[64,2560]{1,0:T(8,128)(2,1)S(1)} collective-permute-done((bf16[64,2560]{1,0:T(8,128)(2,1)S(1)}, bf16[64,2560]{1,0:T(8,128)(2,1)S(1)}, u32[]{:S(2)}, u32[]{:S(2)}) %collective-permute-start.10) | collective-permute-done | bytes 327712 | tf_op jit(solution)/shard_map/ppermute | solution.py:36
  91.1 0.1 fusion.45
  91.2 1.2 %constant_dynamic-slice_fusion = f32[2,64,2560]{2,1,0:T(8,128)} fusion(f32[5,64,2560]{2,1,0:T(8,128)S(1)} %fusion.45, s32[]{:T(128)S(6)} %select_n.35), kind=kLoop, calls=%fused_computation.87 | loop fusion | bytes 2621444 | tf_op jit(solution)/shard_map/dynamic_slice | solution.py:38
  (22 shorter events, 0.1 us)
Async XLA Ops:
  0.0 1.7 %copy-start = (bf16[1,5120,256]{2,1,0:T(8,128)(2,1)S(1)}, bf16[1,5120,256]{2,1,0:T(8,128)(2,1)}, u32[]{:S(2)}) copy-start(bf16[1,5120,256]{2,1,0:T(8,128)(2,1)} %param.10) | copy-start | bytes 7864324
  0.0 3.8 %copy-start.5 = (bf16[1,128,5120]{2,1,0:T(8,128)(2,1)S(1)}, bf16[1,128,5120]{2,1,0:T(8,128)(2,1)}, u32[]{:S(2)}) copy-start(bf16[1,128,5120]{2,1,0:T(8,128)(2,1)} %param.6) | copy-start | bytes 3932164
  0.0 3.8 %copy-start.1 = (bf16[1,5120,256]{2,1,0:T(8,128)(2,1)S(1)}, bf16[1,5120,256]{2,1,0:T(8,128)(2,1)}, u32[]{:S(2)}) copy-start(bf16[1,5120,256]{2,1,0:T(8,128)(2,1)} %param.9) | copy-start | bytes 7864324
  3.8 12.2 %copy-start.11 = (s32[512]{0:T(512)S(1)}, s32[512]{0:T(512)}, u32[]{:S(2)}) copy-start(s32[512]{0:T(512)} %param.11) | copy-start | bytes 6148
  3.8 12.5 %copy-start.7 = (bf16[1,128,10,128]{3,1,2,0:T(8,128)(2,1)S(1)}, bf16[1,128,10,128]{3,1,2,0:T(8,128)(2,1)}, u32[]{:S(2)}) copy-start(bf16[1,128,10,128]{3,1,2,0:T(8,128)(2,1)} %param.8) | copy-start | bytes 983044
  3.8 13.4 %copy-start.6 = (bf16[1,128,10,128]{3,1,2,0:T(8,128)(2,1)S(1)}, bf16[1,128,10,128]{3,1,2,0:T(8,128)(2,1)}, u32[]{:S(2)}) copy-start(bf16[1,128,10,128]{3,1,2,0:T(8,128)(2,1)} %param.7) | copy-start | bytes 983044
  5.0 13.2 %collective-permute-start.2 = (bf16[128,512]{1,0:T(8,128)(2,1)}, bf16[128,512]{1,0:T(8,128)(2,1)}, u32[]{:S(2)}, u32[]{:S(2)}) collective-permute-start(bf16[128,512]{1,0:T(8,128)(2,1)} %pad_maximum_fusion.2), channel_id=1, source_target_pairs={{0,6},{1,7},{8,14},{9,15},{16,22},{17,23},{24,30},{25,31}} | collective-permute-start | bytes 393224 | tf_op jit(solution)/shard_map/ppermute | solution.py:17
  11.5 7.2 %collective-permute-start.1 = (bf16[128,512]{1,0:T(8,128)(2,1)}, bf16[128,512]{1,0:T(8,128)(2,1)}, u32[]{:S(2)}, u32[]{:S(2)}) collective-permute-start(bf16[128,512]{1,0:T(8,128)(2,1)} %pad_maximum_fusion.2), channel_id=1, source_target_pairs={{0,4},{2,6},{1,5},{3,7},{8,12},{10,14},{9,13},{11,15},{16,20},{18,... | collective-permute-start | bytes 393224 | tf_op jit(solution)/shard_map/ppermute | solution.py:17
  13.4 5.2 %collective-permute-start = (bf16[128,512]{1,0:T(8,128)(2,1)}, bf16[128,512]{1,0:T(8,128)(2,1)}, u32[]{:S(2)}, u32[]{:S(2)}) collective-permute-start(bf16[128,512]{1,0:T(8,128)(2,1)} %pad_maximum_fusion.2), channel_id=1, source_target_pairs={{0,2},{2,4},{4,6},{1,3},{3,5},{5,7},{8,10},{10,12},{12,14},{9,11},... | collective-permute-start | bytes 393224 | tf_op jit(solution)/shard_map/ppermute | solution.py:17
  22.3 1.1 %copy-start.8 = (bf16[128,2,5,128]{0,3,2,1:T(8,128)(2,1)S(1)}, bf16[128,2,5,128]{0,3,2,1:T(8,128)(2,1)}, u32[]{:S(2)}) copy-start(bf16[128,2,5,128]{0,3,2,1:T(8,128)(2,1)} %copy.10) | copy-start | bytes 983044
  22.9 1.5 %copy-start.4 = (f32[2,5,128,512]{2,3,1,0:T(8,128)}, f32[2,5,128,512]{2,3,1,0:T(8,128)S(1)}, u32[]{:S(2)}) copy-start(f32[2,5,128,512]{2,3,1,0:T(8,128)S(1)} %get-tuple-element.15) | copy-start | bytes 7864324
  22.9 1.5 %copy-start.10 = (bf16[2,512,128,1]{1,2,3,0:T(8,128)(2,1)S(1)}, bf16[2,512,128,1]{1,2,3,0:T(8,128)(2,1)}, u32[]{:S(2)}) copy-start(bf16[2,512,128,1]{1,2,3,0:T(8,128)(2,1)} %copy.16) | copy-start | bytes 786436
  24.4 1.0 %copy-start.9 = (bf16[128,2,5,128]{0,3,2,1:T(8,128)(2,1)S(1)}, bf16[128,2,5,128]{0,3,2,1:T(8,128)(2,1)}, u32[]{:S(2)}) copy-start(bf16[128,2,5,128]{0,3,2,1:T(8,128)(2,1)} %copy.10) | copy-start | bytes 983044
  31.0 8.3 %collective-permute-start.5 = (bf16[128,512]{0,1:T(8,128)(2,1)}, bf16[128,512]{0,1:T(8,128)(2,1)S(1)}, u32[]{:S(2)}, u32[]{:S(2)}) collective-permute-start(bf16[128,512]{0,1:T(8,128)(2,1)} %get-tuple-element.6), channel_id=1, source_target_pairs={{6,0},{7,1},{14,8},{15,9},{22,16},{23,17},{30,24},{31,25}} | collective-permute-start | bytes 393224 | tf_op jit(solution)/shard_map/ppermute | solution.py:17
  32.3 8.7 %collective-permute-start.4 = (bf16[128,512]{0,1:T(8,128)(2,1)}, bf16[128,512]{0,1:T(8,128)(2,1)S(1)}, u32[]{:S(2)}, u32[]{:S(2)}) collective-permute-start(bf16[128,512]{0,1:T(8,128)(2,1)} %get-tuple-element.7), channel_id=1, source_target_pairs={{4,0},{6,2},{5,1},{7,3},{12,8},{14,10},{13,9},{15,11},{20,16},{22,... | collective-permute-start | bytes 393224 | tf_op jit(solution)/shard_map/ppermute | solution.py:17
  33.6 7.4 %collective-permute-start.3 = (bf16[128,512]{0,1:T(8,128)(2,1)S(1)}, bf16[128,512]{0,1:T(8,128)(2,1)}, u32[]{:S(2)}, u32[]{:S(2)}) collective-permute-start(bf16[128,512]{0,1:T(8,128)(2,1)S(1)} %get-tuple-element.5), channel_id=1, source_target_pairs={{2,0},{4,2},{6,4},{3,1},{5,3},{7,5},{10,8},{12,10},{14,12},{11,9},... | collective-permute-start | bytes 393224 | tf_op jit(solution)/shard_map/ppermute | solution.py:17
  34.9 7.7 %copy-start.2 = (bf16[1,5120,256]{2,1,0:T(8,128)(2,1)S(1)}, bf16[1,5120,256]{2,1,0:T(8,128)(2,1)}, u32[]{:S(2)}) copy-start(bf16[1,5120,256]{2,1,0:T(8,128)(2,1)} %param.9) | copy-start | bytes 7864324
  44.1 2.4 %collective-permute-start.6 = (bf16[128,2560]{1,0:T(8,128)(2,1)}, bf16[128,2560]{1,0:T(8,128)(2,1)}, u32[]{:S(2)}, u32[]{:S(2)}) collective-permute-start(bf16[128,2560]{1,0:T(8,128)(2,1)} %fusion.1), channel_id=1, source_target_pairs={{0,1},{1,0},{2,3},{3,2},{4,5},{5,4},{6,7},{7,6},{8,9},{9,8},{10,11... | collective-permute-start | bytes 1966088 | tf_op jit(solution)/shard_map/ppermute | solution.py:135
  44.1 2.4 %copy-start.3 = (bf16[1,5120,256]{2,1,0:T(8,128)(2,1)S(1)}, bf16[1,5120,256]{2,1,0:T(8,128)(2,1)}, u32[]{:S(2)}) copy-start(bf16[1,5120,256]{2,1,0:T(8,128)(2,1)} %param.9) | copy-start | bytes 7864324
  49.4 11.6 %collective-permute-start.7 = (bf16[64,2560]{1,0:T(8,128)(2,1)S(1)}, bf16[64,2560]{1,0:T(8,128)(2,1)S(1)}, u32[]{:S(2)}, u32[]{:S(2)}) collective-permute-start(bf16[64,2560]{1,0:T(8,128)(2,1)S(1)} %fusion.52), channel_id=1, source_target_pairs={{8,0},{16,8},{24,16},{9,1},{17,9},{25,17},{10,2},{18,10},{26,18},{... | collective-permute-start | bytes 983048 | tf_op jit(solution)/shard_map/ppermute | solution.py:36
  61.2 10.8 %collective-permute-start.8 = (bf16[64,2560]{1,0:T(8,128)(2,1)S(1)}, bf16[64,2560]{1,0:T(8,128)(2,1)S(1)}, u32[]{:S(2)}, u32[]{:S(2)}) collective-permute-start(bf16[64,2560]{1,0:T(8,128)(2,1)S(1)} %fusion.49), channel_id=1, source_target_pairs={{8,0},{16,8},{24,16},{9,1},{17,9},{25,17},{10,2},{18,10},{26,18},{... | collective-permute-start | bytes 983048 | tf_op jit(solution)/shard_map/ppermute | solution.py:36
  72.0 9.9 %collective-permute-start.9 = (bf16[64,2560]{1,0:T(8,128)(2,1)S(1)}, bf16[64,2560]{1,0:T(8,128)(2,1)S(1)}, u32[]{:S(2)}, u32[]{:S(2)}) collective-permute-start(bf16[64,2560]{1,0:T(8,128)(2,1)S(1)} %fusion.50), channel_id=1, source_target_pairs={{8,0},{16,8},{24,16},{9,1},{17,9},{25,17},{10,2},{18,10},{26,18},{... | collective-permute-start | bytes 983048 | tf_op jit(solution)/shard_map/ppermute | solution.py:36
  82.0 9.1 %collective-permute-start.10 = (bf16[64,2560]{1,0:T(8,128)(2,1)S(1)}, bf16[64,2560]{1,0:T(8,128)(2,1)S(1)}, u32[]{:S(2)}, u32[]{:S(2)}) collective-permute-start(bf16[64,2560]{1,0:T(8,128)(2,1)S(1)} %fusion.51), channel_id=1, source_target_pairs={{8,0},{16,8},{24,16},{9,1},{17,9},{25,17},{10,2},{18,10},{26,18},{... | collective-permute-start | bytes 983048 | tf_op jit(solution)/shard_map/ppermute | solution.py:36

commit v5 on v4

--- a/solution.py
+++ b/solution.py
@@ -3,6 +3,7 @@
 import jax
 import jax.numpy as jnp
 from jax import lax
+from jax.experimental import pallas as pl
 from jax.sharding import PartitionSpec as P
 
 
@@ -39,6 +40,42 @@
     return mine.reshape(rows, cols)
 
 
+def attention_terms(q2, g2, kv_all, allowed_t, kv_local, group, head_dim, scaling):
+    seq_rows = kv_all.shape[0]
+    kv_cols = kv_local * head_dim
+    nt = (((1,), (1,)), ((), ()))
+
+    def kernel(q_ref, g_ref, kv_ref, m_ref, out_ref):
+        allowed = m_ref[...] > 0.5
+        for k in range(kv_local):
+            key = kv_ref[:, k * head_dim : (k + 1) * head_dim]
+            val = kv_ref[:, kv_cols + k * head_dim : kv_cols + (k + 1) * head_dim]
+            dk = jnp.zeros((seq_rows, head_dim), jnp.float32)
+            dv = jnp.zeros((seq_rows, head_dim), jnp.float32)
+            for j in range(group):
+                h = k * group + j
+                q = q_ref[:, h * head_dim : (h + 1) * head_dim]
+                gr = g_ref[:, h * head_dim : (h + 1) * head_dim]
+                s = lax.dot_general(key, q, nt, preferred_element_type=jnp.float32) * scaling
+                masked = jnp.where(allowed, s, -1e30)
+                top = jnp.max(masked, axis=0, keepdims=True)
+                tot = jnp.sum(jnp.where(allowed, jnp.exp(masked - top), 0.0), axis=0, keepdims=True)
+                log_total = top + jnp.log(tot)
+                p = jnp.where(allowed, jnp.exp(masked - log_total), 0.0)
+                pb = p.astype(jnp.bfloat16)
+                dp = lax.dot_general(val, gr, nt, preferred_element_type=jnp.float32)
+                rd = jnp.sum(pb.astype(jnp.float32) * dp, axis=0, keepdims=True)
+                ds = (p * (dp - rd)).astype(jnp.bfloat16)
+                dv = dv + jnp.dot(pb, gr, preferred_element_type=jnp.float32)
+                dk = dk + jnp.dot(ds, q, preferred_element_type=jnp.float32)
+            out_ref[:, k * head_dim : (k + 1) * head_dim] = dk * scaling
+            out_ref[:, kv_cols + k * head_dim : kv_cols + (k + 1) * head_dim] = dv
+
+    return pl.pallas_call(
+        kernel, out_shape=jax.ShapeDtypeStruct((seq_rows, 2 * kv_cols), jnp.float32)
+    )(q2, g2, kv_all, allowed_t)
+
+
 def per_device(inputs, query, grad_out, w_key, w_value, keep_mask):
     tok_rows = inputs.shape[1]
     local_heads = query.shape[2]
@@ -58,56 +95,27 @@
     blocks = [kv_own] + [shifted(kv_own, "ctx", d, ctx_len, True) for d in range(1, ctx_len)]
     kv_all = jnp.concatenate(blocks, axis=0)
     seq_rows = kv_all.shape[0]
-    key_heads = kv_all[:, :kv_cols].reshape(seq_rows, kv_local, head_dim)
-    value_heads = kv_all[:, kv_cols:].reshape(seq_rows, kv_local, head_dim)
-    query_heads = query[0].reshape(tok_rows, kv_local, group_size, head_dim)
-    grad_heads = grad_out[0].reshape(tok_rows, kv_local, group_size, head_dim)
-    query_major = jnp.moveaxis(query_heads, 1, 0)
-    grad_major = jnp.moveaxis(grad_heads, 1, 0)
     first_row = ctx_index * tok_rows
-    row_pos = first_row + jnp.arange(tok_rows, dtype=jnp.int32)[:, None]
+    row_pos = first_row + jnp.arange(tok_rows, dtype=jnp.int32)[None, :]
     blk = jnp.arange(ctx_len, dtype=jnp.int32)
     col_pos = (
         (ctx_index - blk)[:, None] * tok_rows + jnp.arange(tok_rows, dtype=jnp.int32)[None, :]
-    ).reshape(1, seq_rows)
+    ).reshape(seq_rows, 1)
     present = col_pos >= 0
     keep_blocks = keep_mask.reshape(ctx_len, tok_rows)
     kept = jnp.concatenate(
         [
-            lax.dynamic_index_in_dim(keep_blocks, jnp.maximum(ctx_index - p, 0), 0, keepdims=True)
+            lax.dynamic_index_in_dim(keep_blocks, jnp.maximum(ctx_index - p, 0), 0, keepdims=False)
             for p in range(ctx_len)
         ],
-        axis=1,
+        axis=0,
+    ).reshape(seq_rows, 1)
+    allowed_t = present & (col_pos <= row_pos) & ((kept == 1) | (col_pos == row_pos))
+    q2 = query[0].reshape(tok_rows, local_heads * head_dim)
+    g2 = grad_out[0].reshape(tok_rows, local_heads * head_dim)
+    terms = attention_terms(
+        q2, g2, kv_all, allowed_t.astype(jnp.float32), kv_local, group_size, head_dim, scaling
     )
-    allowed = present & (col_pos <= row_pos) & ((kept == 1) | (col_pos == row_pos))
-    allowed = lax.optimization_barrier(allowed)
-
-    key_major = jnp.moveaxis(key_heads, 1, 0)
-    value_major = jnp.moveaxis(value_heads, 1, 0)
-    scores = (
-        jnp.einsum("ktgd,ksd->kgts", query_major, key_major, preferred_element_type=jnp.float32)
-        * scaling
-    )
-    masked = jnp.where(allowed, scores, -1e30)
-    top_score = jnp.max(masked, axis=-1, keepdims=True)
-    totals = jnp.sum(jnp.where(allowed, jnp.exp(masked - top_score), 0.0), axis=-1, keepdims=True)
-    log_total = top_score + jnp.log(totals)
-    prob_full = jnp.where(allowed, jnp.exp(masked - log_total), 0.0)
-    probs_b = prob_full.astype(jnp.bfloat16)
-    attended = jnp.einsum("kgts,ksd->ktgd", probs_b, value_major, preferred_element_type=jnp.float32)
-    row_dots = jnp.sum(grad_major.astype(jnp.float32) * attended, axis=-1)
-    dprob = jnp.einsum("ktgd,ksd->kgts", grad_major, value_major, preferred_element_type=jnp.float32)
-    dscore_b = (prob_full * (dprob - jnp.transpose(row_dots, (0, 2, 1))[..., None])).astype(
-        jnp.bfloat16
-    )
-    value_term = jnp.einsum("kgts,ktgd->ksd", probs_b, grad_major, preferred_element_type=jnp.float32)
-    key_term = (
-        jnp.einsum("kgts,ktgd->ksd", dscore_b, query_major, preferred_element_type=jnp.float32)
-        * scaling
-    )
-    key_flat = jnp.moveaxis(key_term, 0, 1).reshape(seq_rows, kv_cols)
-    value_flat = jnp.moveaxis(value_term, 0, 1).reshape(seq_rows, kv_cols)
-    terms = jnp.concatenate((key_flat, value_flat), axis=1)
     terms_low = terms.astype(jnp.bfloat16)
     kv_grad = terms[:tok_rows]
     for d in range(1, ctx_len):

time: 92.8 us -> 90 us (0.970)
  matrix products: 12.3 us -> 5.64 us
  Pallas kernels: 0 us -> 6.29 us
  local copies, waits for them, and re-layouts: 9.14 us -> 6.49 us
    pallas_call x0 -> x1, Pallas kernels: none -> 6.29 us  [attention_terms(): pl.pallas_call(kernel, out_shape=jax.ShapeDtypeStruct((seq_rows, 2 * kv_c...]
    dot_general x4 -> x0, matrix products: 5.56 us -> none  [the longest x1 3.77 us: per_device(): jnp.einsum('kgts,ktgd->ksd', dscore_b, query_major, preferred_element_typ...]
    dot_general x2, matrix products: 3.1 us -> 1.99 us  [partial_for(): lax.dot_general(grad_key, wk, contract, preferred_element_type=jnp.float32)]
    reshape x1 -> x0, local copies, waits for them, and re-layouts: 1.01 us -> none  [per_device(): value_heads = kv_all[:, kv_cols:].reshape(seq_rows, kv_local, head_dim)]
    convert_element_type x0 -> x1, other arithmetic: none -> 0.98 us  [per_device(): allowed_t.astype(jnp.float32)]
    unnamed x25 -> x17, local copies, waits for them, and re-layouts: 2.54 us -> 3.21 us
  transfers between devices with their start and end apart: 11 -> 11, of which waited for: 8 -> 7; matrix products, arithmetic and copies ran while one was open for 3% -> 6% of each run, Pallas kernels for 0% -> 0%
where the time goes in v5:
time: 90 us; the launch traced here: 89.5 us
  waiting for transfers between devices  44 us (49%)
  starting transfers between devices  20 us (22%)
  other arithmetic  6.85 us (8%)
  local copies, waits for them, and re-layouts  6.49 us (7%)
  Pallas kernels  6.29 us (7%)
  matrix products  5.64 us (6%)
    ppermute x4, waiting for transfers between devices, suffix_pipeline(): recv = lax.ppermute(acc.astype(jnp.bfloat16), axis, perm)  35.9 us
    ppermute x6, starting transfers between devices, shifted(): return lax.ppermute(x, axis, perm)  14.8 us
    ppermute x6, waiting for transfers between devices, shifted(): return lax.ppermute(x, axis, perm)  6.37 us
    pallas_call x1, Pallas kernels, attention_terms(): pl.pallas_call(kernel, out_shape=jax.ShapeDtypeStruct((seq_rows, 2 * kv_c...  6.29 us
    ppermute x4, starting transfers between devices, suffix_pipeline(): recv = lax.ppermute(acc.astype(jnp.bfloat16), axis, perm)  5.17 us
    unnamed x17, local copies, waits for them, and re-layouts  3.21 us
    dot_general x1, matrix products, per_device(): jnp.dot(tokens, w_value[0], preferred_element_type=jnp.float32)  2.02 us
    dot_general x2, matrix products, partial_for(): lax.dot_general(grad_key, wk, contract, preferred_element_type=jnp.float32)  1.99 us
  transfers between devices with their start and end apart: 11, of which 7 were waited for; matrix products, arithmetic and copies ran while one was open for 6% of the time, Pallas kernels for 0%

profile of v5, /device:TPU:0, one launch (start us, length us, event | category | flops | bytes accessed | tf_op | source)
XLA Modules:
  0.0 89.5 jit_solution(7381521070689740683)
XLA Ops:
  0.0 0.0 copy-start
  0.0 0.0 copy-start.4
  0.0 0.0 copy-start.1
  0.0 1.7 %copy-done = bf16[1,5120,256]{2,1,0:T(8,128)(2,1)S(1)} copy-done((bf16[1,5120,256]{2,1,0:T(8,128)(2,1)S(1)}, bf16[1,5120,256]{2,1,0:T(8,128)(2,1)}, u32[]{:S(2)}) %copy-start) | copy-done | bytes 2621464
  1.7 2.0 %fusion.25 = bf16[128,256]{1,0:T(8,128)(2,1)S(1)} fusion(bf16[1,5120,256]{2,1,0:T(8,128)(2,1)S(1)} %copy-done, bf16[1,128,5120]{2,1,0:T(8,128)(2,1)} %param.6), kind=kOutput, calls=%fused_computation.26 | convolution fusion | flops 335577088 | bytes 3997696 | tf_op jit(solution)/shard_map/dot_general | solution.py:91
  3.8 0.0 copy-done.4
  3.8 0.0 copy-done.1
  3.8 0.0 copy-start.5
  3.8 0.0 copy-start.6
  3.8 0.5 fusion.20
  4.3 6.5 %collective-permute-start.2 = (bf16[128,512]{1,0:T(8,128)(2,1)S(1)}, bf16[128,512]{1,0:T(8,128)(2,1)}, u32[]{:S(2)}, u32[]{:S(2)}) collective-permute-start(bf16[128,512]{1,0:T(8,128)(2,1)S(1)} %pad_maximum_fusion.1), channel_id=1, source_target_pairs={{0,6},{1,7},{8,14},{9,15},{16,22},{17,23},{24,30},{25,31}} | collective-permute-start | bytes 393224 | tf_op jit(solution)/shard_map/ppermute | solution.py:18
  10.8 2.0 %collective-permute-start.1 = (bf16[128,512]{1,0:T(8,128)(2,1)S(1)}, bf16[128,512]{1,0:T(8,128)(2,1)}, u32[]{:S(2)}, u32[]{:S(2)}) collective-permute-start(bf16[128,512]{1,0:T(8,128)(2,1)S(1)} %pad_maximum_fusion.1), channel_id=1, source_target_pairs={{0,4},{2,6},{1,5},{3,7},{8,12},{10,14},{9,13},{11,15},{16,20},{18,... | collective-permute-start | bytes 393224 | tf_op jit(solution)/shard_map/ppermute | solution.py:18
  12.8 2.5 %collective-permute-start = (bf16[128,512]{1,0:T(8,128)(2,1)S(1)}, bf16[128,512]{1,0:T(8,128)(2,1)}, u32[]{:S(2)}, u32[]{:S(2)}) collective-permute-start(bf16[128,512]{1,0:T(8,128)(2,1)S(1)} %pad_maximum_fusion.1), channel_id=1, source_target_pairs={{0,2},{2,4},{4,6},{1,3},{3,5},{5,7},{8,10},{10,12},{12,14},{9,11},... | collective-permute-start | bytes 393224 | tf_op jit(solution)/shard_map/ppermute | solution.py:18
  15.3 0.0 copy-done.5
  15.3 0.2 copy.9
  15.5 0.9 %copy.11.q_ref = bf16[128,1280]{1,0:T(8,128)(2,1)} copy(bf16[128,1280]{0,1:T(8,128)(2,1)S(1)} %bitcast.93) | data formatting | bytes 655360 | tf_op jit(solution)/shard_map/reshape;squeeze | solution.py:114
  16.4 1.2 %copy.10 = bf16[1,128,10,128]{1,3,2,0:T(8,128)(2,1)S(1)} copy(bf16[1,128,10,128]{3,1,2,0:T(8,128)(2,1)} %param.8) | data formatting | bytes 655360 | tf_op args[2]
  17.6 0.9 %copy.12.g_ref = bf16[128,1280]{1,0:T(8,128)(2,1)} copy(bf16[128,1280]{0,1:T(8,128)(2,1)S(1)} %bitcast.94) | data formatting | bytes 655360 | tf_op jit(solution)/shard_map/reshape;squeeze | solution.py:115
  18.5 0.1 add_bitcast_fusion
  18.6 0.0 copy-done.6
  18.6 0.1 add_compare_fusion
  18.7 1.0 %and_convert_fusion.m_ref = f32[512,128]{1,0:T(8,128)} fusion(s32[128]{0:T(128)S(1)} %iota_add_fusion, s32[512]{0:T(512)S(1)} %add_bitcast_fusion, pred[512]{0:T(512)(128)(4,1)S(1)} %get-tuple-element.12, pred[512]{0:T(512)(128)(4,1)S(1)} %get-tuple-element.13), kind=kLoop, calls=%fused_computation.51 | loop fusion | flops 393216 | bytes 265728 | tf_op jit(solution)/shard_map/convert_element_type | solution.py:117
  19.7 0.0 collective-permute-done.2
  19.7 0.0 collective-permute-done.1
  19.7 0.0 collective-permute-done
  19.7 1.9 %pad_maximum_fusion.kv_ref = bf16[512,512]{1,0:T(8,128)(2,1)} fusion(bf16[128,512]{1,0:T(8,128)(2,1)} %collective-permute-done.2, bf16[128,512]{1,0:T(8,128)(2,1)} %collective-permute-done.1, bf16[128,512]{1,0:T(8,128)(2,1)} %collective-permute-done, bf16[128,256]{1,0:T(8,128)(2,1)S(1)} %fusion.25, bf16[128,256]{1,0:T(8,128)(2,1)S(1)} %fusion.20), kind=kLoop, calls=%fused_computation.42 | loop fusion | flops 2621440 | bytes 1048576 | tf_op jit(solution)/shard_map/concatenate | solution.py:96
  21.6 6.3 %shard_map.64 = f32[512,512]{1,0:T(8,128)} custom-call(bf16[128,1280]{1,0:T(8,128)(2,1)} %copy.11.q_ref, bf16[128,1280]{1,0:T(8,128)(2,1)} %copy.12.g_ref, bf16[512,512]{1,0:T(8,128)(2,1)} %pad_maximum_fusion.kv_ref, f32[512,128]{1,0:T(8,128)} %and_convert_fusion.m_ref), custom_call_target="tpu_custom_call" | custom-call | tf_op jit(solution)/shard_map/pallas_call | solution.py:74
  27.8 1.3 %convert_element_type.61 = bf16[512,512]{1,0:T(8,128)(2,1)S(1)} convert(f32[512,512]{1,0:T(8,128)} %shard_map.64) | non-fusion elementwise | flops 262144 | bytes 1572864 | tf_op jit(solution)/shard_map/convert_element_type | solution.py:119
  29.2 1.3 %collective-permute-start.5 = (bf16[128,512]{1,0:T(8,128)(2,1)S(1)}, bf16[128,512]{1,0:T(8,128)(2,1)S(1)}, u32[]{:S(2)}, u32[]{:S(2)}) collective-permute-start(bf16[128,512]{1,0:T(8,128)(2,1)S(1)} %get-tuple-element.6), channel_id=1, source_target_pairs={{6,0},{7,1},{14,8},{15,9},{22,16},{23,17},{30,24},{31,25}} | collective-permute-start | bytes 393224 | tf_op jit(solution)/shard_map/ppermute | solution.py:18
  30.5 1.3 %collective-permute-start.4 = (bf16[128,512]{1,0:T(8,128)(2,1)S(1)}, bf16[128,512]{1,0:T(8,128)(2,1)S(1)}, u32[]{:S(2)}, u32[]{:S(2)}) collective-permute-start(bf16[128,512]{1,0:T(8,128)(2,1)S(1)} %get-tuple-element.7), channel_id=1, source_target_pairs={{4,0},{6,2},{5,1},{7,3},{12,8},{14,10},{13,9},{15,11},{20,16},{22,... | collective-permute-start | bytes 393224 | tf_op jit(solution)/shard_map/ppermute | solution.py:18
  31.8 1.3 %collective-permute-start.3 = (bf16[128,512]{1,0:T(8,128)(2,1)S(1)}, bf16[128,512]{1,0:T(8,128)(2,1)S(1)}, u32[]{:S(2)}, u32[]{:S(2)}) collective-permute-start(bf16[128,512]{1,0:T(8,128)(2,1)S(1)} %get-tuple-element.5), channel_id=1, source_target_pairs={{2,0},{4,2},{6,4},{3,1},{5,3},{7,5},{10,8},{12,10},{14,12},{11,9},... | collective-permute-start | bytes 393224 | tf_op jit(solution)/shard_map/ppermute | solution.py:18
  33.1 0.0 copy-start.2
  33.1 3.8 %collective-permute-done.5 = bf16[128,512]{1,0:T(8,128)(2,1)S(1)} collective-permute-done((bf16[128,512]{1,0:T(8,128)(2,1)S(1)}, bf16[128,512]{1,0:T(8,128)(2,1)S(1)}, u32[]{:S(2)}, u32[]{:S(2)}) %collective-permute-start.5) | collective-permute-done | bytes 131104 | tf_op jit(solution)/shard_map/ppermute | solution.py:18
  36.9 2.5 %collective-permute-done.4 = bf16[128,512]{1,0:T(8,128)(2,1)S(1)} collective-permute-done((bf16[128,512]{1,0:T(8,128)(2,1)S(1)}, bf16[128,512]{1,0:T(8,128)(2,1)S(1)}, u32[]{:S(2)}, u32[]{:S(2)}) %collective-permute-start.4) | collective-permute-done | bytes 131104 | tf_op jit(solution)/shard_map/ppermute | solution.py:18
  39.5 0.0 collective-permute-done.3
  39.5 1.0 %fusion.42 = bf16[128,512]{1,0:T(8,128)(2,1)S(1)} fusion(f32[512,512]{1,0:T(8,128)} %shard_map.64, bf16[128,512]{1,0:T(8,128)(2,1)S(1)} %collective-permute-done.5, bf16[128,512]{1,0:T(8,128)(2,1)S(1)} %collective-permute-done.4, bf16[128,512]{1,0:T(8,128)(2,1)S(1)} %collective-permute-done.3), kind=kLoop, calls=%fused_computation.50 | loop fusion | flops 458752 | bytes 786432 | tf_op jit(solution)/shard_map/convert.1
  40.5 0.6 fusion.8
  41.0 0.0 copy-done.2
  41.1 1.4 %fusion.1 = bf16[128,2560]{1,0:T(8,128)(2,1)} fusion(f32[128,2560]{1,0:T(8,128)S(1)} %fusion.8, bf16[1,5120,256]{2,1,0:T(8,128)(2,1)S(1)} %copy-done.2, s32[]{:T(128)S(6)} %select_n.20, bf16[128,512]{1,0:T(8,128)(2,1)S(1)} %fusion.42), kind=kOutput, calls=%fused_computation.6 | convolution fusion | flops 168427520 | bytes 3342340 | tf_op jit(solution)/shard_map/dot_general | solution.py:135
  42.5 0.0 collective-permute-start.6
  42.5 0.0 copy-start.3
  42.5 0.6 fusion.11
  43.0 1.7 %collective-permute-done.6 = bf16[128,2560]{1,0:T(8,128)(2,1)S(1)} collective-permute-done((bf16[128,2560]{1,0:T(8,128)(2,1)}, bf16[128,2560]{1,0:T(8,128)(2,1)S(1)}, u32[]{:S(2)}, u32[]{:S(2)}) %collective-permute-start.6) | collective-permute-done | bytes 655392 | tf_op jit(solution)/shard_map/ppermute | solution.py:143
  44.8 0.0 copy-done.3
  44.8 0.6 fusion
  45.4 0.2 broadcast_in_dim.2
  45.6 1.0 %fusion.3 = f32[5,64,2560]{2,1,0:T(8,128)S(1)} fusion(s32[]{:T(128)S(6)} %select_n.21, f32[3,64,2560]{2,1,0:T(8,128)S(1)} %broadcast_in_dim.2, f32[2,64,2560]{2,1,0:T(8,128)S(1)} %bitcast.92), kind=kLoop, calls=%fused_computation.8 | loop fusion | flops 1638400 | bytes 6553604 | tf_op jit(solution)/shard_map/concatenate | solution.py:27
  46.6 1.3 %collective-permute-start.7 = (bf16[64,2560]{1,0:T(8,128)(2,1)S(1)}, bf16[64,2560]{1,0:T(8,128)(2,1)S(1)}, u32[]{:S(2)}, u32[]{:S(2)}) collective-permute-start(bf16[64,2560]{1,0:T(8,128)(2,1)S(1)} %fusion.39), channel_id=1, source_target_pairs={{8,0},{16,8},{24,16},{9,1},{17,9},{25,17},{10,2},{18,10},{26,18},{... | collective-permute-start | bytes 983048 | tf_op jit(solution)/shard_map/ppermute | solution.py:37
  48.0 10.3 %collective-permute-done.7 = bf16[64,2560]{1,0:T(8,128)(2,1)S(1)} collective-permute-done((bf16[64,2560]{1,0:T(8,128)(2,1)S(1)}, bf16[64,2560]{1,0:T(8,128)(2,1)S(1)}, u32[]{:S(2)}, u32[]{:S(2)}) %collective-permute-start.7) | collective-permute-done | bytes 327712 | tf_op jit(solution)/shard_map/ppermute | solution.py:37
  58.3 0.1 fusion.36
  58.3 1.3 %collective-permute-start.8 = (bf16[64,2560]{1,0:T(8,128)(2,1)S(1)}, bf16[64,2560]{1,0:T(8,128)(2,1)S(1)}, u32[]{:S(2)}, u32[]{:S(2)}) collective-permute-start(bf16[64,2560]{1,0:T(8,128)(2,1)S(1)} %fusion.36), channel_id=1, source_target_pairs={{8,0},{16,8},{24,16},{9,1},{17,9},{25,17},{10,2},{18,10},{26,18},{... | collective-permute-start | bytes 983048 | tf_op jit(solution)/shard_map/ppermute | solution.py:37
  59.6 0.1 bitcast_dynamic-update-slice_fusion.2
  59.7 9.4 %collective-permute-done.8 = bf16[64,2560]{1,0:T(8,128)(2,1)S(1)} collective-permute-done((bf16[64,2560]{1,0:T(8,128)(2,1)S(1)}, bf16[64,2560]{1,0:T(8,128)(2,1)S(1)}, u32[]{:S(2)}, u32[]{:S(2)}) %collective-permute-start.8) | collective-permute-done | bytes 327712 | tf_op jit(solution)/shard_map/ppermute | solution.py:37
  69.1 0.1 fusion.37
  69.2 1.3 %collective-permute-start.9 = (bf16[64,2560]{1,0:T(8,128)(2,1)S(1)}, bf16[64,2560]{1,0:T(8,128)(2,1)S(1)}, u32[]{:S(2)}, u32[]{:S(2)}) collective-permute-start(bf16[64,2560]{1,0:T(8,128)(2,1)S(1)} %fusion.37), channel_id=1, source_target_pairs={{8,0},{16,8},{24,16},{9,1},{17,9},{25,17},{10,2},{18,10},{26,18},{... | collective-permute-start | bytes 983048 | tf_op jit(solution)/shard_map/ppermute | solution.py:37
  70.5 0.1 bitcast_dynamic-update-slice_fusion.1
  70.6 8.5 %collective-permute-done.9 = bf16[64,2560]{1,0:T(8,128)(2,1)S(1)} collective-permute-done((bf16[64,2560]{1,0:T(8,128)(2,1)S(1)}, bf16[64,2560]{1,0:T(8,128)(2,1)S(1)}, u32[]{:S(2)}, u32[]{:S(2)}) %collective-permute-start.9) | collective-permute-done | bytes 327712 | tf_op jit(solution)/shard_map/ppermute | solution.py:37
  79.1 0.1 fusion.38
  79.2 1.3 %collective-permute-start.10 = (bf16[64,2560]{1,0:T(8,128)(2,1)S(1)}, bf16[64,2560]{1,0:T(8,128)(2,1)S(1)}, u32[]{:S(2)}, u32[]{:S(2)}) collective-permute-start(bf16[64,2560]{1,0:T(8,128)(2,1)S(1)} %fusion.38), channel_id=1, source_target_pairs={{8,0},{16,8},{24,16},{9,1},{17,9},{25,17},{10,2},{18,10},{26,18},{... | collective-permute-start | bytes 983048 | tf_op jit(solution)/shard_map/ppermute | solution.py:37
  80.5 0.1 bitcast_dynamic-update-slice_fusion
  80.6 7.7 %collective-permute-done.10 = bf16[64,2560]{1,0:T(8,128)(2,1)S(1)} collective-permute-done((bf16[64,2560]{1,0:T(8,128)(2,1)S(1)}, bf16[64,2560]{1,0:T(8,128)(2,1)S(1)}, u32[]{:S(2)}, u32[]{:S(2)}) %collective-permute-start.10) | collective-permute-done | bytes 327712 | tf_op jit(solution)/shard_map/ppermute | solution.py:37
  88.3 0.1 fusion.32
  88.4 1.2 %constant_dynamic-slice_fusion = f32[2,64,2560]{2,1,0:T(8,128)} fusion(f32[5,64,2560]{2,1,0:T(8,128)S(1)} %fusion.32, s32[]{:T(128)S(6)} %select_n.22), kind=kLoop, calls=%fused_computation.57 | loop fusion | bytes 2621444 | tf_op jit(solution)/shard_map/dynamic_slice | solution.py:39
  (7 shorter events, 0.1 us)
Async XLA Ops:
  0.0 1.7 %copy-start = (bf16[1,5120,256]{2,1,0:T(8,128)(2,1)S(1)}, bf16[1,5120,256]{2,1,0:T(8,128)(2,1)}, u32[]{:S(2)}) copy-start(bf16[1,5120,256]{2,1,0:T(8,128)(2,1)} %param.10) | copy-start | bytes 7864324
  0.0 3.8 %copy-start.4 = (bf16[1,128,5120]{2,1,0:T(8,128)(2,1)S(1)}, bf16[1,128,5120]{2,1,0:T(8,128)(2,1)}, u32[]{:S(2)}) copy-start(bf16[1,128,5120]{2,1,0:T(8,128)(2,1)} %param.6) | copy-start | bytes 3932164
  0.0 3.8 %copy-start.1 = (bf16[1,5120,256]{2,1,0:T(8,128)(2,1)S(1)}, bf16[1,5120,256]{2,1,0:T(8,128)(2,1)}, u32[]{:S(2)}) copy-start(bf16[1,5120,256]{2,1,0:T(8,128)(2,1)} %param.9) | copy-start | bytes 7864324
  3.8 11.5 %copy-start.5 = (bf16[1,128,10,128]{3,1,2,0:T(8,128)(2,1)S(1)}, bf16[1,128,10,128]{3,1,2,0:T(8,128)(2,1)}, u32[]{:S(2)}) copy-start(bf16[1,128,10,128]{3,1,2,0:T(8,128)(2,1)} %param.7) | copy-start | bytes 983044
  3.8 14.8 %copy-start.6 = (s32[512]{0:T(512)S(1)}, s32[512]{0:T(512)}, u32[]{:S(2)}) copy-start(s32[512]{0:T(512)} %param.11) | copy-start | bytes 6148
  4.3 15.3 %collective-permute-start.2 = (bf16[128,512]{1,0:T(8,128)(2,1)S(1)}, bf16[128,512]{1,0:T(8,128)(2,1)}, u32[]{:S(2)}, u32[]{:S(2)}) collective-permute-start(bf16[128,512]{1,0:T(8,128)(2,1)S(1)} %pad_maximum_fusion.1), channel_id=1, source_target_pairs={{0,6},{1,7},{8,14},{9,15},{16,22},{17,23},{24,30},{25,31}} | collective-permute-start | bytes 393224 | tf_op jit(solution)/shard_map/ppermute | solution.py:18
  10.8 8.9 %collective-permute-start.1 = (bf16[128,512]{1,0:T(8,128)(2,1)S(1)}, bf16[128,512]{1,0:T(8,128)(2,1)}, u32[]{:S(2)}, u32[]{:S(2)}) collective-permute-start(bf16[128,512]{1,0:T(8,128)(2,1)S(1)} %pad_maximum_fusion.1), channel_id=1, source_target_pairs={{0,4},{2,6},{1,5},{3,7},{8,12},{10,14},{9,13},{11,15},{16,20},{18,... | collective-permute-start | bytes 393224 | tf_op jit(solution)/shard_map/ppermute | solution.py:18
  12.8 6.9 %collective-permute-start = (bf16[128,512]{1,0:T(8,128)(2,1)S(1)}, bf16[128,512]{1,0:T(8,128)(2,1)}, u32[]{:S(2)}, u32[]{:S(2)}) collective-permute-start(bf16[128,512]{1,0:T(8,128)(2,1)S(1)} %pad_maximum_fusion.1), channel_id=1, source_target_pairs={{0,2},{2,4},{4,6},{1,3},{3,5},{5,7},{8,10},{10,12},{12,14},{9,11},... | collective-permute-start | bytes 393224 | tf_op jit(solution)/shard_map/ppermute | solution.py:18
  29.2 7.8 %collective-permute-start.5 = (bf16[128,512]{1,0:T(8,128)(2,1)S(1)}, bf16[128,512]{1,0:T(8,128)(2,1)S(1)}, u32[]{:S(2)}, u32[]{:S(2)}) collective-permute-start(bf16[128,512]{1,0:T(8,128)(2,1)S(1)} %get-tuple-element.6), channel_id=1, source_target_pairs={{6,0},{7,1},{14,8},{15,9},{22,16},{23,17},{30,24},{31,25}} | collective-permute-start | bytes 393224 | tf_op jit(solution)/shard_map/ppermute | solution.py:18
  30.5 9.0 %collective-permute-start.4 = (bf16[128,512]{1,0:T(8,128)(2,1)S(1)}, bf16[128,512]{1,0:T(8,128)(2,1)S(1)}, u32[]{:S(2)}, u32[]{:S(2)}) collective-permute-start(bf16[128,512]{1,0:T(8,128)(2,1)S(1)} %get-tuple-element.7), channel_id=1, source_target_pairs={{4,0},{6,2},{5,1},{7,3},{12,8},{14,10},{13,9},{15,11},{20,16},{22,... | collective-permute-start | bytes 393224 | tf_op jit(solution)/shard_map/ppermute | solution.py:18
  31.8 7.7 %collective-permute-start.3 = (bf16[128,512]{1,0:T(8,128)(2,1)S(1)}, bf16[128,512]{1,0:T(8,128)(2,1)S(1)}, u32[]{:S(2)}, u32[]{:S(2)}) collective-permute-start(bf16[128,512]{1,0:T(8,128)(2,1)S(1)} %get-tuple-element.5), channel_id=1, source_target_pairs={{2,0},{4,2},{6,4},{3,1},{5,3},{7,5},{10,8},{12,10},{14,12},{11,9},... | collective-permute-start | bytes 393224 | tf_op jit(solution)/shard_map/ppermute | solution.py:18
  33.1 8.0 %copy-start.2 = (bf16[1,5120,256]{2,1,0:T(8,128)(2,1)S(1)}, bf16[1,5120,256]{2,1,0:T(8,128)(2,1)}, u32[]{:S(2)}) copy-start(bf16[1,5120,256]{2,1,0:T(8,128)(2,1)} %param.9) | copy-start | bytes 7864324
  42.5 2.3 %collective-permute-start.6 = (bf16[128,2560]{1,0:T(8,128)(2,1)}, bf16[128,2560]{1,0:T(8,128)(2,1)S(1)}, u32[]{:S(2)}, u32[]{:S(2)}) collective-permute-start(bf16[128,2560]{1,0:T(8,128)(2,1)} %fusion.1), channel_id=1, source_target_pairs={{0,1},{1,0},{2,3},{3,2},{4,5},{5,4},{6,7},{7,6},{8,9},{9,8},{10,11... | collective-permute-start | bytes 1966088 | tf_op jit(solution)/shard_map/ppermute | solution.py:143
  42.5 2.3 %copy-start.3 = (bf16[1,5120,256]{2,1,0:T(8,128)(2,1)S(1)}, bf16[1,5120,256]{2,1,0:T(8,128)(2,1)}, u32[]{:S(2)}) copy-start(bf16[1,5120,256]{2,1,0:T(8,128)(2,1)} %param.9) | copy-start | bytes 7864324
  46.6 11.6 %collective-permute-start.7 = (bf16[64,2560]{1,0:T(8,128)(2,1)S(1)}, bf16[64,2560]{1,0:T(8,128)(2,1)S(1)}, u32[]{:S(2)}, u32[]{:S(2)}) collective-permute-start(bf16[64,2560]{1,0:T(8,128)(2,1)S(1)} %fusion.39), channel_id=1, source_target_pairs={{8,0},{16,8},{24,16},{9,1},{17,9},{25,17},{10,2},{18,10},{26,18},{... | collective-permute-start | bytes 983048 | tf_op jit(solution)/shard_map/ppermute | solution.py:37
  58.3 10.8 %collective-permute-start.8 = (bf16[64,2560]{1,0:T(8,128)(2,1)S(1)}, bf16[64,2560]{1,0:T(8,128)(2,1)S(1)}, u32[]{:S(2)}, u32[]{:S(2)}) collective-permute-start(bf16[64,2560]{1,0:T(8,128)(2,1)S(1)} %fusion.36), channel_id=1, source_target_pairs={{8,0},{16,8},{24,16},{9,1},{17,9},{25,17},{10,2},{18,10},{26,18},{... | collective-permute-start | bytes 983048 | tf_op jit(solution)/shard_map/ppermute | solution.py:37
  69.2 9.9 %collective-permute-start.9 = (bf16[64,2560]{1,0:T(8,128)(2,1)S(1)}, bf16[64,2560]{1,0:T(8,128)(2,1)S(1)}, u32[]{:S(2)}, u32[]{:S(2)}) collective-permute-start(bf16[64,2560]{1,0:T(8,128)(2,1)S(1)} %fusion.37), channel_id=1, source_target_pairs={{8,0},{16,8},{24,16},{9,1},{17,9},{25,17},{10,2},{18,10},{26,18},{... | collective-permute-start | bytes 983048 | tf_op jit(solution)/shard_map/ppermute | solution.py:37
  79.2 9.1 %collective-permute-start.10 = (bf16[64,2560]{1,0:T(8,128)(2,1)S(1)}, bf16[64,2560]{1,0:T(8,128)(2,1)S(1)}, u32[]{:S(2)}, u32[]{:S(2)}) collective-permute-start(bf16[64,2560]{1,0:T(8,128)(2,1)S(1)} %fusion.38), channel_id=1, source_target_pairs={{8,0},{16,8},{24,16},{9,1},{17,9},{25,17},{10,2},{18,10},{26,18},{... | collective-permute-start | bytes 983048 | tf_op jit(solution)/shard_map/ppermute | solution.py:37

commit v6 on v5

--- a/solution.py
+++ b/solution.py
@@ -40,22 +40,31 @@
     return mine.reshape(rows, cols)
 
 
-def attention_terms(q2, g2, kv_all, allowed_t, kv_local, group, head_dim, scaling):
-    seq_rows = kv_all.shape[0]
+def attention_terms(q3, g3, kv_blocks, lower, upper, kv_local, head_dim, scaling):
+    tok_rows = q3.shape[1]
+    group = q3.shape[0] // kv_local
+    n_blocks = len(kv_blocks)
+    seq_rows = tok_rows * n_blocks
     kv_cols = kv_local * head_dim
     nt = (((1,), (1,)), ((), ()))
 
-    def kernel(q_ref, g_ref, kv_ref, m_ref, out_ref):
-        allowed = m_ref[...] > 0.5
+    def kernel(*refs):
+        q_ref, g_ref = refs[0], refs[1]
+        kv_refs = refs[2 : 2 + n_blocks]
+        lo_ref, hi_ref, low_ref, own_ref = refs[2 + n_blocks :]
+        rows = lax.broadcasted_iota(jnp.int32, (seq_rows, tok_rows), 1)
+        allowed = (lo_ref[...] <= rows) & (rows <= hi_ref[...])
         for k in range(kv_local):
-            key = kv_ref[:, k * head_dim : (k + 1) * head_dim]
-            val = kv_ref[:, kv_cols + k * head_dim : kv_cols + (k + 1) * head_dim]
+            kcols = slice(k * head_dim, (k + 1) * head_dim)
+            vcols = slice(kv_cols + k * head_dim, kv_cols + (k + 1) * head_dim)
+            key = jnp.concatenate([r[:, kcols] for r in kv_refs], axis=0)
+            val = jnp.concatenate([r[:, vcols] for r in kv_refs], axis=0)
             dk = jnp.zeros((seq_rows, head_dim), jnp.float32)
             dv = jnp.zeros((seq_rows, head_dim), jnp.float32)
             for j in range(group):
                 h = k * group + j
-                q = q_ref[:, h * head_dim : (h + 1) * head_dim]
-                gr = g_ref[:, h * head_dim : (h + 1) * head_dim]
+                q = q_ref[h]
+                gr = g_ref[h]
                 s = lax.dot_general(key, q, nt, preferred_element_type=jnp.float32) * scaling
                 masked = jnp.where(allowed, s, -1e30)
                 top = jnp.max(masked, axis=0, keepdims=True)
@@ -68,12 +77,19 @@
                 ds = (p * (dp - rd)).astype(jnp.bfloat16)
                 dv = dv + jnp.dot(pb, gr, preferred_element_type=jnp.float32)
                 dk = dk + jnp.dot(ds, q, preferred_element_type=jnp.float32)
-            out_ref[:, k * head_dim : (k + 1) * head_dim] = dk * scaling
-            out_ref[:, kv_cols + k * head_dim : kv_cols + (k + 1) * head_dim] = dv
+            dk = dk * scaling
+            low_ref[:, kcols] = dk.astype(jnp.bfloat16)
+            low_ref[:, vcols] = dv.astype(jnp.bfloat16)
+            own_ref[:, kcols] = dk[:tok_rows]
+            own_ref[:, vcols] = dv[:tok_rows]
 
     return pl.pallas_call(
-        kernel, out_shape=jax.ShapeDtypeStruct((seq_rows, 2 * kv_cols), jnp.float32)
-    )(q2, g2, kv_all, allowed_t)
+        kernel,
+        out_shape=(
+            jax.ShapeDtypeStruct((seq_rows, 2 * kv_cols), jnp.bfloat16),
+            jax.ShapeDtypeStruct((tok_rows, 2 * kv_cols), jnp.float32),
+        ),
+    )(q3, g3, *kv_blocks, lower, upper)
 
 
 def per_device(inputs, query, grad_out, w_key, w_value, keep_mask):
@@ -93,15 +109,12 @@
     )
     kv_own = jnp.concatenate((key_rows, value_rows), axis=1)
     blocks = [kv_own] + [shifted(kv_own, "ctx", d, ctx_len, True) for d in range(1, ctx_len)]
-    kv_all = jnp.concatenate(blocks, axis=0)
-    seq_rows = kv_all.shape[0]
+    seq_rows = tok_rows * ctx_len
     first_row = ctx_index * tok_rows
-    row_pos = first_row + jnp.arange(tok_rows, dtype=jnp.int32)[None, :]
     blk = jnp.arange(ctx_len, dtype=jnp.int32)
     col_pos = (
         (ctx_index - blk)[:, None] * tok_rows + jnp.arange(tok_rows, dtype=jnp.int32)[None, :]
     ).reshape(seq_rows, 1)
-    present = col_pos >= 0
     keep_blocks = keep_mask.reshape(ctx_len, tok_rows)
     kept = jnp.concatenate(
         [
@@ -110,14 +123,14 @@
         ],
         axis=0,
     ).reshape(seq_rows, 1)
-    allowed_t = present & (col_pos <= row_pos) & ((kept == 1) | (col_pos == row_pos))
-    q2 = query[0].reshape(tok_rows, local_heads * head_dim)
-    g2 = grad_out[0].reshape(tok_rows, local_heads * head_dim)
-    terms = attention_terms(
-        q2, g2, kv_all, allowed_t.astype(jnp.float32), kv_local, group_size, head_dim, scaling
+    never = jnp.iinfo(jnp.int32).max
+    lower = jnp.where(col_pos >= 0, col_pos - first_row, never)
+    upper = jnp.where(kept == 1, never, col_pos - first_row)
+    q3 = jnp.transpose(query[0], (1, 0, 2))
+    g3 = jnp.transpose(grad_out[0], (1, 0, 2))
+    terms_low, kv_grad = attention_terms(
+        q3, g3, blocks, lower, upper, kv_local, head_dim, scaling
     )
-    terms_low = terms.astype(jnp.bfloat16)
-    kv_grad = terms[:tok_rows]
     for d in range(1, ctx_len):
         part = terms_low[d * tok_rows : (d + 1) * tok_rows]
         kv_grad = kv_grad + shifted(part, "ctx", d, ctx_len, False).astype(jnp.float32)

time: 90 us -> 84.6 us (0.940)
  other arithmetic: 6.85 us -> 3.6 us
  starting transfers between devices: 20 us -> 18.6 us
  local copies, waits for them, and re-layouts: 6.49 us -> 5.46 us
    convert_element_type x2 -> x0, other arithmetic: 2.27 us -> none  [the longest x1 1.29 us: per_device(): terms_low = terms.astype(jnp.bfloat16)]
    concatenate x1 -> x0, other arithmetic: 1.86 us -> none  [per_device(): kv_all = jnp.concatenate(blocks, axis=0)]
    another operation x2 -> x0, local copies, waits for them, and re-layouts: 1.85 us -> none  [the longest x1 0.94 us: per_device(): g2 = grad_out[0].reshape(tok_rows, local_heads * head_dim)]
    ppermute x6, starting transfers between devices: 14.8 us -> 13.5 us  [shifted(): return lax.ppermute(x, axis, perm)]
    slice x1, local copies, waits for them, and re-layouts: 0.03 us -> 1.06 us  [per_device(): part = terms_low[d * tok_rows:(d + 1) * tok_rows]]
    unnamed x17 -> x23, local copies, waits for them, and re-layouts: 3.21 us -> 2.65 us
  transfers between devices with their start and end apart: 11 -> 11, of which waited for: 7 -> 9; matrix products, arithmetic and copies ran while one was open for 6% -> 3% of each run, Pallas kernels for 0% -> 0%
where the time goes in v6:
time: 84.6 us; the launch traced here: 84.2 us
  waiting for transfers between devices  44.3 us (52%)
  starting transfers between devices  18.6 us (22%)
  Pallas kernels  6.26 us (7%)
  matrix products  5.64 us (7%)
  local copies, waits for them, and re-layouts  5.46 us (6%)
  other arithmetic  3.6 us (4%)
    ppermute x4, waiting for transfers between devices, suffix_pipeline(): recv = lax.ppermute(acc.astype(jnp.bfloat16), axis, perm)  35.9 us
    ppermute x6, starting transfers between devices, shifted(): return lax.ppermute(x, axis, perm)  13.5 us
    ppermute x6, waiting for transfers between devices, shifted(): return lax.ppermute(x, axis, perm)  6.63 us
    pallas_call x1, Pallas kernels, attention_terms(): pl.pallas_call(kernel, out_shape=(jax.ShapeDtypeStruct((seq_rows, 2 * kv_...  6.26 us
    ppermute x4, starting transfers between devices, suffix_pipeline(): recv = lax.ppermute(acc.astype(jnp.bfloat16), axis, perm)  5.17 us
    unnamed x23, local copies, waits for them, and re-layouts  2.65 us
    dot_general x1, matrix products, per_device(): jnp.dot(tokens, w_value[0], preferred_element_type=jnp.float32)  2.02 us
    dot_general x2, matrix products, partial_for(): lax.dot_general(grad_key, wk, contract, preferred_element_type=jnp.float32)  1.99 us
  transfers between devices with their start and end apart: 11, of which 9 were waited for; matrix products, arithmetic and copies ran while one was open for 3% of the time, Pallas kernels for 0%

profile of v6, /device:TPU:0, one launch (start us, length us, event | category | flops | bytes accessed | tf_op | source)
XLA Modules:
  0.0 84.2 jit_solution(17040834476568755416)
XLA Ops:
  0.0 0.0 copy-start
  0.0 0.0 copy-start.4
  0.0 0.0 copy-start.1
  0.0 1.7 %copy-done = bf16[1,5120,256]{2,1,0:T(8,128)(2,1)S(1)} copy-done((bf16[1,5120,256]{2,1,0:T(8,128)(2,1)S(1)}, bf16[1,5120,256]{2,1,0:T(8,128)(2,1)}, u32[]{:S(2)}) %copy-start) | copy-done | bytes 2621464
  1.7 2.0 %fusion.25 = bf16[128,256]{1,0:T(8,128)(2,1)S(1)} fusion(bf16[1,5120,256]{2,1,0:T(8,128)(2,1)S(1)} %copy-done, bf16[1,128,5120]{2,1,0:T(8,128)(2,1)} %param.6), kind=kOutput, calls=%fused_computation.26 | convolution fusion | flops 335577088 | bytes 3997696 | tf_op jit(solution)/shard_map/dot_general | solution.py:107
  3.8 0.0 copy-done.4
  3.8 0.0 copy-done.1
  3.8 0.0 copy-start.9
  3.8 0.5 fusion.20
  4.3 0.0 copy-start.5
  4.3 4.9 %collective-permute-start = (bf16[128,512]{1,0:T(8,128)(2,1)S(1)}, bf16[128,512]{1,0:T(8,128)(2,1)S(1)}, u32[]{:S(2)}, u32[]{:S(2)}) collective-permute-start(bf16[128,512]{1,0:T(8,128)(2,1)S(1)} %pad_maximum_fusion.refs_2_), channel_id=1, source_target_pairs={{0,2},{2,4},{4,6},{1,3},{3,5},{5,7},{8,10},{10,12},{12,14},{9,11},... | collective-permute-start | bytes 393224 | tf_op jit(solution)/shard_map/ppermute | solution.py:18
  9.2 3.4 %collective-permute-start.1 = (bf16[128,512]{1,0:T(8,128)(2,1)S(1)}, bf16[128,512]{1,0:T(8,128)(2,1)S(1)}, u32[]{:S(2)}, u32[]{:S(2)}) collective-permute-start(bf16[128,512]{1,0:T(8,128)(2,1)S(1)} %pad_maximum_fusion.refs_2_), channel_id=1, source_target_pairs={{0,4},{2,6},{1,5},{3,7},{8,12},{10,14},{9,13},{11,15},{16,20},{18,... | collective-permute-start | bytes 393224 | tf_op jit(solution)/shard_map/ppermute | solution.py:18
  12.7 1.3 %collective-permute-start.2 = (bf16[128,512]{1,0:T(8,128)(2,1)S(1)}, bf16[128,512]{1,0:T(8,128)(2,1)S(1)}, u32[]{:S(2)}, u32[]{:S(2)}) collective-permute-start(bf16[128,512]{1,0:T(8,128)(2,1)S(1)} %pad_maximum_fusion.refs_2_), channel_id=1, source_target_pairs={{0,6},{1,7},{8,14},{9,15},{16,22},{17,23},{24,30},{25,31}} | collective-permute-start | bytes 393224 | tf_op jit(solution)/shard_map/ppermute | solution.py:18
  14.0 0.0 copy-done.9
  14.0 0.2 copy.25
  14.2 0.1 fusion.50
  14.3 0.1 fusion.48
  14.4 0.2 copy.24
  14.6 0.2 copy.28
  14.8 0.9 %broadcast_select_fusion = (s32[512,1]{1,0:T(8,128)}, s32[512,1]{1,0:T(8,128)}) fusion(pred[512,1]{1,0:T(8,128)(4,1)S(1)} %copy.25, s32[512,1]{1,0:T(8,128)S(1)} %copy.24, pred[1,512]{0,1:T(8,128)(4,1)S(1)} %copy.28), kind=kLoop, calls=%fused_computation.49 | loop fusion | flops 1024 | bytes 7168 | tf_op jit(solution)/shard_map/jit(_where)/select_n | solution.py:128
  15.6 0.0 collective-permute-done.refs_3_
  15.6 0.0 copy-start.6
  15.6 0.1 collective-permute-done.1.refs_4_
  15.7 0.8 collective-permute-done.2.refs_5_
  16.5 0.0 copy-done.5
  16.5 0.0 copy-done.6
  16.5 0.0 copy-done.7
  16.5 0.6 copy-done.8
  17.1 6.3 %shard_map.64 = (bf16[512,512]{1,0:T(8,128)(2,1)}, f32[128,512]{1,0:T(8,128)}) custom-call(bf16[10,128,128]{2,1,0:T(8,128)(2,1)} %bitcast.102, bf16[10,128,128]{2,1,0:T(8,128)(2,1)} %bitcast.103, bf16[128,512]{1,0:T(8,128)(2,1)} %copy-done.5, bf16[128,512]{1,0:T(8,128)(2,1)} %copy-done.6, bf16[128,512]{1,0:T(8,128)(2,1)} %copy-done.7, ...), custom_call_target="tpu_custom_call" | custom-call | tf_op jit(solution)/shard_map/pallas_call | solution.py:86
  23.4 1.1 %fusion.55 = (bf16[128,512]{1,0:T(8,128)(2,1)S(1)}, bf16[128,512]{1,0:T(8,128)(2,1)S(1)}, bf16[128,512]{1,0:T(8,128)(2,1)S(1)}) fusion(bf16[512,512]{1,0:T(8,128)(2,1)} %get-tuple-element.8), kind=kLoop, calls=%fused_computation.74 | loop fusion | bytes 786432 | tf_op jit(solution)/shard_map/slice | solution.py:135
  24.4 1.3 %collective-permute-start.5 = (bf16[128,512]{1,0:T(8,128)(2,1)S(1)}, bf16[128,512]{1,0:T(8,128)(2,1)S(1)}, u32[]{:S(2)}, u32[]{:S(2)}) collective-permute-start(bf16[128,512]{1,0:T(8,128)(2,1)S(1)} %get-tuple-element.10), channel_id=1, source_target_pairs={{6,0},{7,1},{14,8},{15,9},{22,16},{23,17},{30,24},{31,25}} | collective-permute-start | bytes 393224 | tf_op jit(solution)/shard_map/ppermute | solution.py:18
  25.7 1.3 %collective-permute-start.4 = (bf16[128,512]{1,0:T(8,128)(2,1)S(1)}, bf16[128,512]{1,0:T(8,128)(2,1)S(1)}, u32[]{:S(2)}, u32[]{:S(2)}) collective-permute-start(bf16[128,512]{1,0:T(8,128)(2,1)S(1)} %get-tuple-element.11), channel_id=1, source_target_pairs={{4,0},{6,2},{5,1},{7,3},{12,8},{14,10},{13,9},{15,11},{20,16},{22,... | collective-permute-start | bytes 393224 | tf_op jit(solution)/shard_map/ppermute | solution.py:18
  27.0 1.3 %collective-permute-start.3 = (bf16[128,512]{1,0:T(8,128)(2,1)S(1)}, bf16[128,512]{1,0:T(8,128)(2,1)S(1)}, u32[]{:S(2)}, u32[]{:S(2)}) collective-permute-start(bf16[128,512]{1,0:T(8,128)(2,1)S(1)} %get-tuple-element.9), channel_id=1, source_target_pairs={{2,0},{4,2},{6,4},{3,1},{5,3},{7,5},{10,8},{12,10},{14,12},{11,9},... | collective-permute-start | bytes 393224 | tf_op jit(solution)/shard_map/ppermute | solution.py:18
  28.3 0.0 copy-start.2
  28.4 4.1 %collective-permute-done.5 = bf16[128,512]{1,0:T(8,128)(2,1)S(1)} collective-permute-done((bf16[128,512]{1,0:T(8,128)(2,1)S(1)}, bf16[128,512]{1,0:T(8,128)(2,1)S(1)}, u32[]{:S(2)}, u32[]{:S(2)}) %collective-permute-start.5) | collective-permute-done | bytes 131104 | tf_op jit(solution)/shard_map/ppermute | solution.py:18
  32.4 1.7 %collective-permute-done.4 = bf16[128,512]{1,0:T(8,128)(2,1)S(1)} collective-permute-done((bf16[128,512]{1,0:T(8,128)(2,1)S(1)}, bf16[128,512]{1,0:T(8,128)(2,1)S(1)}, u32[]{:S(2)}, u32[]{:S(2)}) %collective-permute-start.4) | collective-permute-done | bytes 131104 | tf_op jit(solution)/shard_map/ppermute | solution.py:18
  34.1 0.0 collective-permute-done.3
  34.1 1.0 %add_convert_fusion = bf16[128,512]{1,0:T(8,128)(2,1)S(1)} fusion(bf16[128,512]{1,0:T(8,128)(2,1)S(1)} %collective-permute-done.5, bf16[128,512]{1,0:T(8,128)(2,1)S(1)} %collective-permute-done.4, f32[128,512]{1,0:T(8,128)} %get-tuple-element.7, bf16[128,512]{1,0:T(8,128)(2,1)S(1)} %collective-permute-done.3), kind=kLoop, calls=%fused_computation.46 | loop fusion | flops 458752 | bytes 786432 | tf_op jit(solution)/shard_map/convert.1
  35.2 0.6 fusion.8
  35.7 0.0 copy-done.2
  35.7 1.4 %fusion.1 = bf16[128,2560]{1,0:T(8,128)(2,1)} fusion(f32[128,2560]{1,0:T(8,128)S(1)} %fusion.8, bf16[1,5120,256]{2,1,0:T(8,128)(2,1)S(1)} %copy-done.2, s32[]{:T(128)S(6)} %select_n.30, bf16[128,512]{1,0:T(8,128)(2,1)S(1)} %add_convert_fusion), kind=kOutput, calls=%fused_computation.6 | convolution fusion | flops 168427520 | bytes 3342340 | tf_op jit(solution)/shard_map/dot_general | solution.py:148
  37.1 0.0 collective-permute-start.6
  37.1 0.6 fusion.11
  37.7 1.7 %collective-permute-done.6 = bf16[128,2560]{1,0:T(8,128)(2,1)S(1)} collective-permute-done((bf16[128,2560]{1,0:T(8,128)(2,1)}, bf16[128,2560]{1,0:T(8,128)(2,1)S(1)}, u32[]{:S(2)}, u32[]{:S(2)}) %collective-permute-start.6) | collective-permute-done | bytes 655392 | tf_op jit(solution)/shard_map/ppermute | solution.py:156
  39.5 0.0 copy-done.3
  39.5 0.6 fusion
  40.0 0.2 broadcast_in_dim.12
  40.3 1.0 %fusion.3 = f32[5,64,2560]{2,1,0:T(8,128)S(1)} fusion(s32[]{:T(128)S(6)} %select_n.31, f32[3,64,2560]{2,1,0:T(8,128)S(1)} %broadcast_in_dim.12, f32[2,64,2560]{2,1,0:T(8,128)S(1)} %bitcast.101), kind=kLoop, calls=%fused_computation.8 | loop fusion | flops 1638400 | bytes 6553604 | tf_op jit(solution)/shard_map/concatenate | solution.py:27
  41.3 1.3 %collective-permute-start.7 = (bf16[64,2560]{1,0:T(8,128)(2,1)S(1)}, bf16[64,2560]{1,0:T(8,128)(2,1)S(1)}, u32[]{:S(2)}, u32[]{:S(2)}) collective-permute-start(bf16[64,2560]{1,0:T(8,128)(2,1)S(1)} %fusion.39), channel_id=1, source_target_pairs={{8,0},{16,8},{24,16},{9,1},{17,9},{25,17},{10,2},{18,10},{26,18},{... | collective-permute-start | bytes 983048 | tf_op jit(solution)/shard_map/ppermute | solution.py:37
  42.6 10.3 %collective-permute-done.7 = bf16[64,2560]{1,0:T(8,128)(2,1)S(1)} collective-permute-done((bf16[64,2560]{1,0:T(8,128)(2,1)S(1)}, bf16[64,2560]{1,0:T(8,128)(2,1)S(1)}, u32[]{:S(2)}, u32[]{:S(2)}) %collective-permute-start.7) | collective-permute-done | bytes 327712 | tf_op jit(solution)/shard_map/ppermute | solution.py:37
  52.9 0.1 fusion.36
  53.0 1.3 %collective-permute-start.8 = (bf16[64,2560]{1,0:T(8,128)(2,1)S(1)}, bf16[64,2560]{1,0:T(8,128)(2,1)S(1)}, u32[]{:S(2)}, u32[]{:S(2)}) collective-permute-start(bf16[64,2560]{1,0:T(8,128)(2,1)S(1)} %fusion.36), channel_id=1, source_target_pairs={{8,0},{16,8},{24,16},{9,1},{17,9},{25,17},{10,2},{18,10},{26,18},{... | collective-permute-start | bytes 983048 | tf_op jit(solution)/shard_map/ppermute | solution.py:37
  54.3 0.1 bitcast_dynamic-update-slice_fusion.2
  54.4 9.4 %collective-permute-done.8 = bf16[64,2560]{1,0:T(8,128)(2,1)S(1)} collective-permute-done((bf16[64,2560]{1,0:T(8,128)(2,1)S(1)}, bf16[64,2560]{1,0:T(8,128)(2,1)S(1)}, u32[]{:S(2)}, u32[]{:S(2)}) %collective-permute-start.8) | collective-permute-done | bytes 327712 | tf_op jit(solution)/shard_map/ppermute | solution.py:37
  63.8 0.1 fusion.37
  63.9 1.3 %collective-permute-start.9 = (bf16[64,2560]{1,0:T(8,128)(2,1)S(1)}, bf16[64,2560]{1,0:T(8,128)(2,1)S(1)}, u32[]{:S(2)}, u32[]{:S(2)}) collective-permute-start(bf16[64,2560]{1,0:T(8,128)(2,1)S(1)} %fusion.37), channel_id=1, source_target_pairs={{8,0},{16,8},{24,16},{9,1},{17,9},{25,17},{10,2},{18,10},{26,18},{... | collective-permute-start | bytes 983048 | tf_op jit(solution)/shard_map/ppermute | solution.py:37
  65.2 0.1 bitcast_dynamic-update-slice_fusion.1
  65.3 8.5 %collective-permute-done.9 = bf16[64,2560]{1,0:T(8,128)(2,1)S(1)} collective-permute-done((bf16[64,2560]{1,0:T(8,128)(2,1)S(1)}, bf16[64,2560]{1,0:T(8,128)(2,1)S(1)}, u32[]{:S(2)}, u32[]{:S(2)}) %collective-permute-start.9) | collective-permute-done | bytes 327712 | tf_op jit(solution)/shard_map/ppermute | solution.py:37
  73.8 0.1 fusion.38
  73.9 1.3 %collective-permute-start.10 = (bf16[64,2560]{1,0:T(8,128)(2,1)S(1)}, bf16[64,2560]{1,0:T(8,128)(2,1)S(1)}, u32[]{:S(2)}, u32[]{:S(2)}) collective-permute-start(bf16[64,2560]{1,0:T(8,128)(2,1)S(1)} %fusion.38), channel_id=1, source_target_pairs={{8,0},{16,8},{24,16},{9,1},{17,9},{25,17},{10,2},{18,10},{26,18},{... | collective-permute-start | bytes 983048 | tf_op jit(solution)/shard_map/ppermute | solution.py:37
  75.2 0.1 bitcast_dynamic-update-slice_fusion
  75.3 7.7 %collective-permute-done.10 = bf16[64,2560]{1,0:T(8,128)(2,1)S(1)} collective-permute-done((bf16[64,2560]{1,0:T(8,128)(2,1)S(1)}, bf16[64,2560]{1,0:T(8,128)(2,1)S(1)}, u32[]{:S(2)}, u32[]{:S(2)}) %collective-permute-start.10) | collective-permute-done | bytes 327712 | tf_op jit(solution)/shard_map/ppermute | solution.py:37
  83.0 0.1 fusion.32
  83.0 1.2 %constant_dynamic-slice_fusion = f32[2,64,2560]{2,1,0:T(8,128)} fusion(f32[5,64,2560]{2,1,0:T(8,128)S(1)} %fusion.32, s32[]{:T(128)S(6)} %select_n.32), kind=kLoop, calls=%fused_computation.55 | loop fusion | bytes 2621444 | tf_op jit(solution)/shard_map/dynamic_slice | solution.py:39
  (10 shorter events, 0.1 us)
Async XLA Ops:
  0.0 1.7 %copy-start = (bf16[1,5120,256]{2,1,0:T(8,128)(2,1)S(1)}, bf16[1,5120,256]{2,1,0:T(8,128)(2,1)}, u32[]{:S(2)}) copy-start(bf16[1,5120,256]{2,1,0:T(8,128)(2,1)} %param.10) | copy-start | bytes 7864324
  0.0 3.8 %copy-start.4 = (bf16[1,128,5120]{2,1,0:T(8,128)(2,1)S(1)}, bf16[1,128,5120]{2,1,0:T(8,128)(2,1)}, u32[]{:S(2)}) copy-start(bf16[1,128,5120]{2,1,0:T(8,128)(2,1)} %param.6) | copy-start | bytes 3932164
  0.0 3.8 %copy-start.1 = (bf16[1,5120,256]{2,1,0:T(8,128)(2,1)S(1)}, bf16[1,5120,256]{2,1,0:T(8,128)(2,1)}, u32[]{:S(2)}) copy-start(bf16[1,5120,256]{2,1,0:T(8,128)(2,1)} %param.9) | copy-start | bytes 7864324
  3.8 10.2 %copy-start.9 = (s32[512]{0:T(512)S(1)}, s32[512]{0:T(512)}, u32[]{:S(2)}) copy-start(s32[512]{0:T(512)} %param.11) | copy-start | bytes 6148
  4.3 12.1 %copy-start.5 = (bf16[128,512]{1,0:T(8,128)(2,1)}, bf16[128,512]{1,0:T(8,128)(2,1)S(1)}, u32[]{:S(2)}) copy-start(bf16[128,512]{1,0:T(8,128)(2,1)S(1)} %pad_maximum_fusion.refs_2_) | copy-start | bytes 393220
  4.3 11.3 %collective-permute-start = (bf16[128,512]{1,0:T(8,128)(2,1)S(1)}, bf16[128,512]{1,0:T(8,128)(2,1)S(1)}, u32[]{:S(2)}, u32[]{:S(2)}) collective-permute-start(bf16[128,512]{1,0:T(8,128)(2,1)S(1)} %pad_maximum_fusion.refs_2_), channel_id=1, source_target_pairs={{0,2},{2,4},{4,6},{1,3},{3,5},{5,7},{8,10},{10,12},{12,14},{9,11},... | collective-permute-start | bytes 393224 | tf_op jit(solution)/shard_map/ppermute | solution.py:18
  9.2 6.5 %collective-permute-start.1 = (bf16[128,512]{1,0:T(8,128)(2,1)S(1)}, bf16[128,512]{1,0:T(8,128)(2,1)S(1)}, u32[]{:S(2)}, u32[]{:S(2)}) collective-permute-start(bf16[128,512]{1,0:T(8,128)(2,1)S(1)} %pad_maximum_fusion.refs_2_), channel_id=1, source_target_pairs={{0,4},{2,6},{1,5},{3,7},{8,12},{10,14},{9,13},{11,15},{16,20},{18,... | collective-permute-start | bytes 393224 | tf_op jit(solution)/shard_map/ppermute | solution.py:18
  12.7 3.8 %collective-permute-start.2 = (bf16[128,512]{1,0:T(8,128)(2,1)S(1)}, bf16[128,512]{1,0:T(8,128)(2,1)S(1)}, u32[]{:S(2)}, u32[]{:S(2)}) collective-permute-start(bf16[128,512]{1,0:T(8,128)(2,1)S(1)} %pad_maximum_fusion.refs_2_), channel_id=1, source_target_pairs={{0,6},{1,7},{8,14},{9,15},{16,22},{17,23},{24,30},{25,31}} | collective-permute-start | bytes 393224 | tf_op jit(solution)/shard_map/ppermute | solution.py:18
  15.6 0.8 %copy-start.6 = (bf16[128,512]{1,0:T(8,128)(2,1)}, bf16[128,512]{1,0:T(8,128)(2,1)S(1)}, u32[]{:S(2)}) copy-start(bf16[128,512]{1,0:T(8,128)(2,1)S(1)} %collective-permute-done.refs_3_) | copy-start | bytes 393220
  15.7 0.8 copy-start.7
  16.5 0.6 copy-start.8
  24.4 8.0 %collective-permute-start.5 = (bf16[128,512]{1,0:T(8,128)(2,1)S(1)}, bf16[128,512]{1,0:T(8,128)(2,1)S(1)}, u32[]{:S(2)}, u32[]{:S(2)}) collective-permute-start(bf16[128,512]{1,0:T(8,128)(2,1)S(1)} %get-tuple-element.10), channel_id=1, source_target_pairs={{6,0},{7,1},{14,8},{15,9},{22,16},{23,17},{30,24},{31,25}} | collective-permute-start | bytes 393224 | tf_op jit(solution)/shard_map/ppermute | solution.py:18
  25.7 8.4 %collective-permute-start.4 = (bf16[128,512]{1,0:T(8,128)(2,1)S(1)}, bf16[128,512]{1,0:T(8,128)(2,1)S(1)}, u32[]{:S(2)}, u32[]{:S(2)}) collective-permute-start(bf16[128,512]{1,0:T(8,128)(2,1)S(1)} %get-tuple-element.11), channel_id=1, source_target_pairs={{4,0},{6,2},{5,1},{7,3},{12,8},{14,10},{13,9},{15,11},{20,16},{22,... | collective-permute-start | bytes 393224 | tf_op jit(solution)/shard_map/ppermute | solution.py:18
  27.0 7.1 %collective-permute-start.3 = (bf16[128,512]{1,0:T(8,128)(2,1)S(1)}, bf16[128,512]{1,0:T(8,128)(2,1)S(1)}, u32[]{:S(2)}, u32[]{:S(2)}) collective-permute-start(bf16[128,512]{1,0:T(8,128)(2,1)S(1)} %get-tuple-element.9), channel_id=1, source_target_pairs={{2,0},{4,2},{6,4},{3,1},{5,3},{7,5},{10,8},{12,10},{14,12},{11,9},... | collective-permute-start | bytes 393224 | tf_op jit(solution)/shard_map/ppermute | solution.py:18
  28.3 7.4 %copy-start.2 = (bf16[1,5120,256]{2,1,0:T(8,128)(2,1)S(1)}, bf16[1,5120,256]{2,1,0:T(8,128)(2,1)}, u32[]{:S(2)}) copy-start(bf16[1,5120,256]{2,1,0:T(8,128)(2,1)} %param.9) | copy-start | bytes 7864324
  37.1 2.3 %collective-permute-start.6 = (bf16[128,2560]{1,0:T(8,128)(2,1)}, bf16[128,2560]{1,0:T(8,128)(2,1)S(1)}, u32[]{:S(2)}, u32[]{:S(2)}) collective-permute-start(bf16[128,2560]{1,0:T(8,128)(2,1)} %fusion.1), channel_id=1, source_target_pairs={{0,1},{1,0},{2,3},{3,2},{4,5},{5,4},{6,7},{7,6},{8,9},{9,8},{10,11... | collective-permute-start | bytes 1966088 | tf_op jit(solution)/shard_map/ppermute | solution.py:156
  37.1 2.3 %copy-start.3 = (bf16[1,5120,256]{2,1,0:T(8,128)(2,1)S(1)}, bf16[1,5120,256]{2,1,0:T(8,128)(2,1)}, u32[]{:S(2)}) copy-start(bf16[1,5120,256]{2,1,0:T(8,128)(2,1)} %param.9) | copy-start | bytes 7864324
  41.3 11.6 %collective-permute-start.7 = (bf16[64,2560]{1,0:T(8,128)(2,1)S(1)}, bf16[64,2560]{1,0:T(8,128)(2,1)S(1)}, u32[]{:S(2)}, u32[]{:S(2)}) collective-permute-start(bf16[64,2560]{1,0:T(8,128)(2,1)S(1)} %fusion.39), channel_id=1, source_target_pairs={{8,0},{16,8},{24,16},{9,1},{17,9},{25,17},{10,2},{18,10},{26,18},{... | collective-permute-start | bytes 983048 | tf_op jit(solution)/shard_map/ppermute | solution.py:37
  53.0 10.8 %collective-permute-start.8 = (bf16[64,2560]{1,0:T(8,128)(2,1)S(1)}, bf16[64,2560]{1,0:T(8,128)(2,1)S(1)}, u32[]{:S(2)}, u32[]{:S(2)}) collective-permute-start(bf16[64,2560]{1,0:T(8,128)(2,1)S(1)} %fusion.36), channel_id=1, source_target_pairs={{8,0},{16,8},{24,16},{9,1},{17,9},{25,17},{10,2},{18,10},{26,18},{... | collective-permute-start | bytes 983048 | tf_op jit(solution)/shard_map/ppermute | solution.py:37
  63.9 9.9 %collective-permute-start.9 = (bf16[64,2560]{1,0:T(8,128)(2,1)S(1)}, bf16[64,2560]{1,0:T(8,128)(2,1)S(1)}, u32[]{:S(2)}, u32[]{:S(2)}) collective-permute-start(bf16[64,2560]{1,0:T(8,128)(2,1)S(1)} %fusion.37), channel_id=1, source_target_pairs={{8,0},{16,8},{24,16},{9,1},{17,9},{25,17},{10,2},{18,10},{26,18},{... | collective-permute-start | bytes 983048 | tf_op jit(solution)/shard_map/ppermute | solution.py:37
  73.9 9.1 %collective-permute-start.10 = (bf16[64,2560]{1,0:T(8,128)(2,1)S(1)}, bf16[64,2560]{1,0:T(8,128)(2,1)S(1)}, u32[]{:S(2)}, u32[]{:S(2)}) collective-permute-start(bf16[64,2560]{1,0:T(8,128)(2,1)S(1)} %fusion.38), channel_id=1, source_target_pairs={{8,0},{16,8},{24,16},{9,1},{17,9},{25,17},{10,2},{18,10},{26,18},{... | collective-permute-start | bytes 983048 | tf_op jit(solution)/shard_map/ppermute | solution.py:37

commit v7 on v6

--- a/solution.py
+++ b/solution.py
@@ -27,13 +27,13 @@
     padded = jnp.concatenate((pad, chunks, pad), axis=0)
     steps = n_chunks + length - 1
     ordered = lax.dynamic_slice_in_dim(padded, index, steps, axis=0)
-    perm = [(i, i - 1) for i in range(1, length)]
     recv = jnp.zeros((height, cols), jnp.bfloat16)
     done = []
     for tau in range(steps):
         acc = ordered[tau] + recv.astype(jnp.float32)
         done.append(acc)
-        if tau < steps - 1:
+        perm = [(i, i - 1) for i in range(1, length) if 0 <= tau - (length - 1 - i) < n_chunks]
+        if perm:
             recv = lax.ppermute(acc.astype(jnp.bfloat16), axis, perm)
     stacked = jnp.stack(done, axis=0)
     mine = lax.dynamic_slice_in_dim(stacked, length - 1 - index, n_chunks, axis=0)

time: 84.6 us -> 85.1 us (level)
  waiting for transfers between devices: 44.3 us -> 46 us
  starting transfers between devices: 18.6 us -> 17.4 us
    ppermute x4, waiting for transfers between devices: 35.9 us -> 37.6 us  [suffix_pipeline(): recv = lax.ppermute(acc.astype(jnp.bfloat16), axis, perm)]
    ppermute x4, starting transfers between devices: 5.17 us -> 3.95 us  [suffix_pipeline(): recv = lax.ppermute(acc.astype(jnp.bfloat16), axis, perm)]
  transfers between devices with their start and end apart: 11 -> 11, of which waited for: 9 -> 7; matrix products, arithmetic and copies ran while one was open for 3% -> 3% of each run, Pallas kernels for 0% -> 0%
where the time goes in v7:
time: 85.1 us; the launch traced here: 84.7 us
  waiting for transfers between devices  46 us (54%)
  starting transfers between devices  17.4 us (20%)
  Pallas kernels  6.26 us (7%)
  matrix products  5.64 us (7%)
  local copies, waits for them, and re-layouts  5.46 us (6%)
  other arithmetic  3.6 us (4%)
    ppermute x4, waiting for transfers between devices, suffix_pipeline(): recv = lax.ppermute(acc.astype(jnp.bfloat16), axis, perm)  37.6 us
    ppermute x6, starting transfers between devices, shifted(): return lax.ppermute(x, axis, perm)  13.5 us
    ppermute x6, waiting for transfers between devices, shifted(): return lax.ppermute(x, axis, perm)  6.63 us
    pallas_call x1, Pallas kernels, attention_terms(): pl.pallas_call(kernel, out_shape=(jax.ShapeDtypeStruct((seq_rows, 2 * kv_...  6.26 us
    ppermute x4, starting transfers between devices, suffix_pipeline(): recv = lax.ppermute(acc.astype(jnp.bfloat16), axis, perm)  3.95 us
    unnamed x23, local copies, waits for them, and re-layouts  2.65 us
    dot_general x1, matrix products, per_device(): jnp.dot(tokens, w_value[0], preferred_element_type=jnp.float32)  2.02 us
    dot_general x2, matrix products, partial_for(): lax.dot_general(grad_key, wk, contract, preferred_element_type=jnp.float32)  1.99 us
  transfers between devices with their start and end apart: 11, of which 7 were waited for; matrix products, arithmetic and copies ran while one was open for 3% of the time, Pallas kernels for 0%

profile of v7, /device:TPU:0, one launch (start us, length us, event | category | flops | bytes accessed | tf_op | source)
XLA Modules:
  0.0 84.7 jit_solution(11116456319744063390)
XLA Ops:
  0.0 0.0 copy-start
  0.0 0.0 copy-start.4
  0.0 0.0 copy-start.1
  0.0 1.7 %copy-done = bf16[1,5120,256]{2,1,0:T(8,128)(2,1)S(1)} copy-done((bf16[1,5120,256]{2,1,0:T(8,128)(2,1)S(1)}, bf16[1,5120,256]{2,1,0:T(8,128)(2,1)}, u32[]{:S(2)}) %copy-start) | copy-done | bytes 2621464
  1.7 2.0 %fusion.25 = bf16[128,256]{1,0:T(8,128)(2,1)S(1)} fusion(bf16[1,5120,256]{2,1,0:T(8,128)(2,1)S(1)} %copy-done, bf16[1,128,5120]{2,1,0:T(8,128)(2,1)} %param.6), kind=kOutput, calls=%fused_computation.26 | convolution fusion | flops 335577088 | bytes 3997696 | tf_op jit(solution)/shard_map/dot_general | solution.py:107
  3.8 0.0 copy-done.4
  3.8 0.0 copy-done.1
  3.8 0.0 copy-start.9
  3.8 0.5 fusion.20
  4.3 0.0 copy-start.5
  4.3 4.9 %collective-permute-start = (bf16[128,512]{1,0:T(8,128)(2,1)S(1)}, bf16[128,512]{1,0:T(8,128)(2,1)S(1)}, u32[]{:S(2)}, u32[]{:S(2)}) collective-permute-start(bf16[128,512]{1,0:T(8,128)(2,1)S(1)} %pad_maximum_fusion.refs_2_), channel_id=1, source_target_pairs={{0,2},{2,4},{4,6},{1,3},{3,5},{5,7},{8,10},{10,12},{12,14},{9,11},... | collective-permute-start | bytes 393224 | tf_op jit(solution)/shard_map/ppermute | solution.py:18
  9.2 3.4 %collective-permute-start.1 = (bf16[128,512]{1,0:T(8,128)(2,1)S(1)}, bf16[128,512]{1,0:T(8,128)(2,1)S(1)}, u32[]{:S(2)}, u32[]{:S(2)}) collective-permute-start(bf16[128,512]{1,0:T(8,128)(2,1)S(1)} %pad_maximum_fusion.refs_2_), channel_id=1, source_target_pairs={{0,4},{2,6},{1,5},{3,7},{8,12},{10,14},{9,13},{11,15},{16,20},{18,... | collective-permute-start | bytes 393224 | tf_op jit(solution)/shard_map/ppermute | solution.py:18
  12.7 1.3 %collective-permute-start.2 = (bf16[128,512]{1,0:T(8,128)(2,1)S(1)}, bf16[128,512]{1,0:T(8,128)(2,1)S(1)}, u32[]{:S(2)}, u32[]{:S(2)}) collective-permute-start(bf16[128,512]{1,0:T(8,128)(2,1)S(1)} %pad_maximum_fusion.refs_2_), channel_id=1, source_target_pairs={{0,6},{1,7},{8,14},{9,15},{16,22},{17,23},{24,30},{25,31}} | collective-permute-start | bytes 393224 | tf_op jit(solution)/shard_map/ppermute | solution.py:18
  14.0 0.0 copy-done.9
  14.0 0.2 copy.25
  14.2 0.1 fusion.50
  14.3 0.1 fusion.48
  14.4 0.2 copy.24
  14.6 0.2 copy.28
  14.8 0.9 %broadcast_select_fusion = (s32[512,1]{1,0:T(8,128)}, s32[512,1]{1,0:T(8,128)}) fusion(pred[512,1]{1,0:T(8,128)(4,1)S(1)} %copy.25, s32[512,1]{1,0:T(8,128)S(1)} %copy.24, pred[1,512]{0,1:T(8,128)(4,1)S(1)} %copy.28), kind=kLoop, calls=%fused_computation.49 | loop fusion | flops 1024 | bytes 7168 | tf_op jit(solution)/shard_map/jit(_where)/select_n | solution.py:128
  15.6 0.0 collective-permute-done.refs_3_
  15.6 0.0 copy-start.6
  15.6 0.1 collective-permute-done.1.refs_4_
  15.7 0.8 collective-permute-done.2.refs_5_
  16.5 0.0 copy-done.5
  16.5 0.0 copy-done.6
  16.5 0.0 copy-done.7
  16.5 0.6 copy-done.8
  17.1 6.3 %shard_map.64 = (bf16[512,512]{1,0:T(8,128)(2,1)}, f32[128,512]{1,0:T(8,128)}) custom-call(bf16[10,128,128]{2,1,0:T(8,128)(2,1)} %bitcast.102, bf16[10,128,128]{2,1,0:T(8,128)(2,1)} %bitcast.103, bf16[128,512]{1,0:T(8,128)(2,1)} %copy-done.5, bf16[128,512]{1,0:T(8,128)(2,1)} %copy-done.6, bf16[128,512]{1,0:T(8,128)(2,1)} %copy-done.7, ...), custom_call_target="tpu_custom_call" | custom-call | tf_op jit(solution)/shard_map/pallas_call | solution.py:86
  23.4 1.1 %fusion.55 = (bf16[128,512]{1,0:T(8,128)(2,1)S(1)}, bf16[128,512]{1,0:T(8,128)(2,1)S(1)}, bf16[128,512]{1,0:T(8,128)(2,1)S(1)}) fusion(bf16[512,512]{1,0:T(8,128)(2,1)} %get-tuple-element.8), kind=kLoop, calls=%fused_computation.74 | loop fusion | bytes 786432 | tf_op jit(solution)/shard_map/slice | solution.py:135
  24.4 1.3 %collective-permute-start.5 = (bf16[128,512]{1,0:T(8,128)(2,1)S(1)}, bf16[128,512]{1,0:T(8,128)(2,1)S(1)}, u32[]{:S(2)}, u32[]{:S(2)}) collective-permute-start(bf16[128,512]{1,0:T(8,128)(2,1)S(1)} %get-tuple-element.10), channel_id=1, source_target_pairs={{6,0},{7,1},{14,8},{15,9},{22,16},{23,17},{30,24},{31,25}} | collective-permute-start | bytes 393224 | tf_op jit(solution)/shard_map/ppermute | solution.py:18
  25.7 1.3 %collective-permute-start.4 = (bf16[128,512]{1,0:T(8,128)(2,1)S(1)}, bf16[128,512]{1,0:T(8,128)(2,1)S(1)}, u32[]{:S(2)}, u32[]{:S(2)}) collective-permute-start(bf16[128,512]{1,0:T(8,128)(2,1)S(1)} %get-tuple-element.11), channel_id=1, source_target_pairs={{4,0},{6,2},{5,1},{7,3},{12,8},{14,10},{13,9},{15,11},{20,16},{22,... | collective-permute-start | bytes 393224 | tf_op jit(solution)/shard_map/ppermute | solution.py:18
  27.0 1.3 %collective-permute-start.3 = (bf16[128,512]{1,0:T(8,128)(2,1)S(1)}, bf16[128,512]{1,0:T(8,128)(2,1)S(1)}, u32[]{:S(2)}, u32[]{:S(2)}) collective-permute-start(bf16[128,512]{1,0:T(8,128)(2,1)S(1)} %get-tuple-element.9), channel_id=1, source_target_pairs={{2,0},{4,2},{6,4},{3,1},{5,3},{7,5},{10,8},{12,10},{14,12},{11,9},... | collective-permute-start | bytes 393224 | tf_op jit(solution)/shard_map/ppermute | solution.py:18
  28.3 0.0 copy-start.2
  28.4 4.1 %collective-permute-done.5 = bf16[128,512]{1,0:T(8,128)(2,1)S(1)} collective-permute-done((bf16[128,512]{1,0:T(8,128)(2,1)S(1)}, bf16[128,512]{1,0:T(8,128)(2,1)S(1)}, u32[]{:S(2)}, u32[]{:S(2)}) %collective-permute-start.5) | collective-permute-done | bytes 131104 | tf_op jit(solution)/shard_map/ppermute | solution.py:18
  32.4 1.7 %collective-permute-done.4 = bf16[128,512]{1,0:T(8,128)(2,1)S(1)} collective-permute-done((bf16[128,512]{1,0:T(8,128)(2,1)S(1)}, bf16[128,512]{1,0:T(8,128)(2,1)S(1)}, u32[]{:S(2)}, u32[]{:S(2)}) %collective-permute-start.4) | collective-permute-done | bytes 131104 | tf_op jit(solution)/shard_map/ppermute | solution.py:18
  34.1 0.0 collective-permute-done.3
  34.1 1.0 %add_convert_fusion = bf16[128,512]{1,0:T(8,128)(2,1)S(1)} fusion(bf16[128,512]{1,0:T(8,128)(2,1)S(1)} %collective-permute-done.5, bf16[128,512]{1,0:T(8,128)(2,1)S(1)} %collective-permute-done.4, f32[128,512]{1,0:T(8,128)} %get-tuple-element.7, bf16[128,512]{1,0:T(8,128)(2,1)S(1)} %collective-permute-done.3), kind=kLoop, calls=%fused_computation.46 | loop fusion | flops 458752 | bytes 786432 | tf_op jit(solution)/shard_map/convert.1
  35.2 0.6 fusion.8
  35.7 0.0 copy-done.2
  35.7 1.4 %fusion.1 = bf16[128,2560]{1,0:T(8,128)(2,1)} fusion(f32[128,2560]{1,0:T(8,128)S(1)} %fusion.8, bf16[1,5120,256]{2,1,0:T(8,128)(2,1)S(1)} %copy-done.2, s32[]{:T(128)S(6)} %select_n.30, bf16[128,512]{1,0:T(8,128)(2,1)S(1)} %add_convert_fusion), kind=kOutput, calls=%fused_computation.6 | convolution fusion | flops 168427520 | bytes 3342340 | tf_op jit(solution)/shard_map/dot_general | solution.py:148
  37.1 0.0 collective-permute-start.6
  37.1 0.6 fusion.11
  37.7 1.7 %collective-permute-done.6 = bf16[128,2560]{1,0:T(8,128)(2,1)S(1)} collective-permute-done((bf16[128,2560]{1,0:T(8,128)(2,1)}, bf16[128,2560]{1,0:T(8,128)(2,1)S(1)}, u32[]{:S(2)}, u32[]{:S(2)}) %collective-permute-start.6) | collective-permute-done | bytes 655392 | tf_op jit(solution)/shard_map/ppermute | solution.py:156
  39.5 0.0 copy-done.3
  39.5 0.6 fusion
  40.0 0.2 broadcast_in_dim.12
  40.3 1.0 %fusion.3 = f32[5,64,2560]{2,1,0:T(8,128)S(1)} fusion(s32[]{:T(128)S(6)} %select_n.31, f32[3,64,2560]{2,1,0:T(8,128)S(1)} %broadcast_in_dim.12, f32[2,64,2560]{2,1,0:T(8,128)S(1)} %bitcast.101), kind=kLoop, calls=%fused_computation.8 | loop fusion | flops 1638400 | bytes 6553604 | tf_op jit(solution)/shard_map/concatenate | solution.py:27
  41.3 0.7 collective-permute-start.7
  42.0 0.0 collective-permute-done.7
  42.0 0.1 fusion.36
  42.1 0.7 collective-permute-start.8
  42.8 0.1 bitcast_dynamic-update-slice_fusion.2
  42.9 0.0 collective-permute-done.8
  42.9 0.1 fusion.37
  43.0 1.3 %collective-permute-start.9 = (bf16[64,2560]{1,0:T(8,128)(2,1)S(1)}, bf16[64,2560]{1,0:T(8,128)(2,1)S(1)}, u32[]{:S(2)}, u32[]{:S(2)}) collective-permute-start(bf16[64,2560]{1,0:T(8,128)(2,1)S(1)} %fusion.37), channel_id=1, source_target_pairs={{8,0},{16,8},{9,1},{17,9},{10,2},{18,10},{11,3},{19,11},{12,4},{20... | collective-permute-start | bytes 983048 | tf_op jit(solution)/shard_map/ppermute | solution.py:37
  44.3 0.1 bitcast_dynamic-update-slice_fusion.1
  44.4 29.4 %collective-permute-done.9 = bf16[64,2560]{1,0:T(8,128)(2,1)S(1)} collective-permute-done((bf16[64,2560]{1,0:T(8,128)(2,1)S(1)}, bf16[64,2560]{1,0:T(8,128)(2,1)S(1)}, u32[]{:S(2)}, u32[]{:S(2)}) %collective-permute-start.9) | collective-permute-done | bytes 327712 | tf_op jit(solution)/shard_map/ppermute | solution.py:37
  73.8 0.1 fusion.38
  73.9 1.3 %collective-permute-start.10 = (bf16[64,2560]{1,0:T(8,128)(2,1)S(1)}, bf16[64,2560]{1,0:T(8,128)(2,1)S(1)}, u32[]{:S(2)}, u32[]{:S(2)}) collective-permute-start(bf16[64,2560]{1,0:T(8,128)(2,1)S(1)} %fusion.38), channel_id=1, source_target_pairs={{8,0},{9,1},{10,2},{11,3},{12,4},{13,5},{14,6},{15,7}} | collective-permute-start | bytes 983048 | tf_op jit(solution)/shard_map/ppermute | solution.py:37
  75.2 0.1 bitcast_dynamic-update-slice_fusion
  75.2 8.2 %collective-permute-done.10 = bf16[64,2560]{1,0:T(8,128)(2,1)S(1)} collective-permute-done((bf16[64,2560]{1,0:T(8,128)(2,1)S(1)}, bf16[64,2560]{1,0:T(8,128)(2,1)S(1)}, u32[]{:S(2)}, u32[]{:S(2)}) %collective-permute-start.10) | collective-permute-done | bytes 327712 | tf_op jit(solution)/shard_map/ppermute | solution.py:37
  83.5 0.1 fusion.32
  83.6 1.2 %constant_dynamic-slice_fusion = f32[2,64,2560]{2,1,0:T(8,128)} fusion(f32[5,64,2560]{2,1,0:T(8,128)S(1)} %fusion.32, s32[]{:T(128)S(6)} %select_n.32), kind=kLoop, calls=%fused_computation.55 | loop fusion | bytes 2621444 | tf_op jit(solution)/shard_map/dynamic_slice | solution.py:39
  (10 shorter events, 0.1 us)
Async XLA Ops:
  0.0 1.7 %copy-start = (bf16[1,5120,256]{2,1,0:T(8,128)(2,1)S(1)}, bf16[1,5120,256]{2,1,0:T(8,128)(2,1)}, u32[]{:S(2)}) copy-start(bf16[1,5120,256]{2,1,0:T(8,128)(2,1)} %param.10) | copy-start | bytes 7864324
  0.0 3.8 %copy-start.4 = (bf16[1,128,5120]{2,1,0:T(8,128)(2,1)S(1)}, bf16[1,128,5120]{2,1,0:T(8,128)(2,1)}, u32[]{:S(2)}) copy-start(bf16[1,128,5120]{2,1,0:T(8,128)(2,1)} %param.6) | copy-start | bytes 3932164
  0.0 3.8 %copy-start.1 = (bf16[1,5120,256]{2,1,0:T(8,128)(2,1)S(1)}, bf16[1,5120,256]{2,1,0:T(8,128)(2,1)}, u32[]{:S(2)}) copy-start(bf16[1,5120,256]{2,1,0:T(8,128)(2,1)} %param.9) | copy-start | bytes 7864324
  3.8 10.2 %copy-start.9 = (s32[512]{0:T(512)S(1)}, s32[512]{0:T(512)}, u32[]{:S(2)}) copy-start(s32[512]{0:T(512)} %param.11) | copy-start | bytes 6148
  4.3 12.1 %copy-start.5 = (bf16[128,512]{1,0:T(8,128)(2,1)}, bf16[128,512]{1,0:T(8,128)(2,1)S(1)}, u32[]{:S(2)}) copy-start(bf16[128,512]{1,0:T(8,128)(2,1)S(1)} %pad_maximum_fusion.refs_2_) | copy-start | bytes 393220
  4.3 11.3 %collective-permute-start = (bf16[128,512]{1,0:T(8,128)(2,1)S(1)}, bf16[128,512]{1,0:T(8,128)(2,1)S(1)}, u32[]{:S(2)}, u32[]{:S(2)}) collective-permute-start(bf16[128,512]{1,0:T(8,128)(2,1)S(1)} %pad_maximum_fusion.refs_2_), channel_id=1, source_target_pairs={{0,2},{2,4},{4,6},{1,3},{3,5},{5,7},{8,10},{10,12},{12,14},{9,11},... | collective-permute-start | bytes 393224 | tf_op jit(solution)/shard_map/ppermute | solution.py:18
  9.2 6.5 %collective-permute-start.1 = (bf16[128,512]{1,0:T(8,128)(2,1)S(1)}, bf16[128,512]{1,0:T(8,128)(2,1)S(1)}, u32[]{:S(2)}, u32[]{:S(2)}) collective-permute-start(bf16[128,512]{1,0:T(8,128)(2,1)S(1)} %pad_maximum_fusion.refs_2_), channel_id=1, source_target_pairs={{0,4},{2,6},{1,5},{3,7},{8,12},{10,14},{9,13},{11,15},{16,20},{18,... | collective-permute-start | bytes 393224 | tf_op jit(solution)/shard_map/ppermute | solution.py:18
  12.7 3.8 %collective-permute-start.2 = (bf16[128,512]{1,0:T(8,128)(2,1)S(1)}, bf16[128,512]{1,0:T(8,128)(2,1)S(1)}, u32[]{:S(2)}, u32[]{:S(2)}) collective-permute-start(bf16[128,512]{1,0:T(8,128)(2,1)S(1)} %pad_maximum_fusion.refs_2_), channel_id=1, source_target_pairs={{0,6},{1,7},{8,14},{9,15},{16,22},{17,23},{24,30},{25,31}} | collective-permute-start | bytes 393224 | tf_op jit(solution)/shard_map/ppermute | solution.py:18
  15.6 0.8 %copy-start.6 = (bf16[128,512]{1,0:T(8,128)(2,1)}, bf16[128,512]{1,0:T(8,128)(2,1)S(1)}, u32[]{:S(2)}) copy-start(bf16[128,512]{1,0:T(8,128)(2,1)S(1)} %collective-permute-done.refs_3_) | copy-start | bytes 393220
  15.7 0.8 copy-start.7
  16.5 0.6 copy-start.8
  24.4 8.0 %collective-permute-start.5 = (bf16[128,512]{1,0:T(8,128)(2,1)S(1)}, bf16[128,512]{1,0:T(8,128)(2,1)S(1)}, u32[]{:S(2)}, u32[]{:S(2)}) collective-permute-start(bf16[128,512]{1,0:T(8,128)(2,1)S(1)} %get-tuple-element.10), channel_id=1, source_target_pairs={{6,0},{7,1},{14,8},{15,9},{22,16},{23,17},{30,24},{31,25}} | collective-permute-start | bytes 393224 | tf_op jit(solution)/shard_map/ppermute | solution.py:18
  25.7 8.4 %collective-permute-start.4 = (bf16[128,512]{1,0:T(8,128)(2,1)S(1)}, bf16[128,512]{1,0:T(8,128)(2,1)S(1)}, u32[]{:S(2)}, u32[]{:S(2)}) collective-permute-start(bf16[128,512]{1,0:T(8,128)(2,1)S(1)} %get-tuple-element.11), channel_id=1, source_target_pairs={{4,0},{6,2},{5,1},{7,3},{12,8},{14,10},{13,9},{15,11},{20,16},{22,... | collective-permute-start | bytes 393224 | tf_op jit(solution)/shard_map/ppermute | solution.py:18
  27.0 7.1 %collective-permute-start.3 = (bf16[128,512]{1,0:T(8,128)(2,1)S(1)}, bf16[128,512]{1,0:T(8,128)(2,1)S(1)}, u32[]{:S(2)}, u32[]{:S(2)}) collective-permute-start(bf16[128,512]{1,0:T(8,128)(2,1)S(1)} %get-tuple-element.9), channel_id=1, source_target_pairs={{2,0},{4,2},{6,4},{3,1},{5,3},{7,5},{10,8},{12,10},{14,12},{11,9},... | collective-permute-start | bytes 393224 | tf_op jit(solution)/shard_map/ppermute | solution.py:18
  28.3 7.4 %copy-start.2 = (bf16[1,5120,256]{2,1,0:T(8,128)(2,1)S(1)}, bf16[1,5120,256]{2,1,0:T(8,128)(2,1)}, u32[]{:S(2)}) copy-start(bf16[1,5120,256]{2,1,0:T(8,128)(2,1)} %param.9) | copy-start | bytes 7864324
  37.1 2.3 %collective-permute-start.6 = (bf16[128,2560]{1,0:T(8,128)(2,1)}, bf16[128,2560]{1,0:T(8,128)(2,1)S(1)}, u32[]{:S(2)}, u32[]{:S(2)}) collective-permute-start(bf16[128,2560]{1,0:T(8,128)(2,1)} %fusion.1), channel_id=1, source_target_pairs={{0,1},{1,0},{2,3},{3,2},{4,5},{5,4},{6,7},{7,6},{8,9},{9,8},{10,11... | collective-permute-start | bytes 1966088 | tf_op jit(solution)/shard_map/ppermute | solution.py:156
  37.1 2.3 %copy-start.3 = (bf16[1,5120,256]{2,1,0:T(8,128)(2,1)S(1)}, bf16[1,5120,256]{2,1,0:T(8,128)(2,1)}, u32[]{:S(2)}) copy-start(bf16[1,5120,256]{2,1,0:T(8,128)(2,1)} %param.9) | copy-start | bytes 7864324
  41.3 0.7 collective-permute-start.7
  42.1 0.8 collective-permute-start.8
  43.0 30.8 %collective-permute-start.9 = (bf16[64,2560]{1,0:T(8,128)(2,1)S(1)}, bf16[64,2560]{1,0:T(8,128)(2,1)S(1)}, u32[]{:S(2)}, u32[]{:S(2)}) collective-permute-start(bf16[64,2560]{1,0:T(8,128)(2,1)S(1)} %fusion.37), channel_id=1, source_target_pairs={{8,0},{16,8},{9,1},{17,9},{10,2},{18,10},{11,3},{19,11},{12,4},{20... | collective-permute-start | bytes 983048 | tf_op jit(solution)/shard_map/ppermute | solution.py:37
  73.9 9.6 %collective-permute-start.10 = (bf16[64,2560]{1,0:T(8,128)(2,1)S(1)}, bf16[64,2560]{1,0:T(8,128)(2,1)S(1)}, u32[]{:S(2)}, u32[]{:S(2)}) collective-permute-start(bf16[64,2560]{1,0:T(8,128)(2,1)S(1)} %fusion.38), channel_id=1, source_target_pairs={{8,0},{9,1},{10,2},{11,3},{12,4},{13,5},{14,6},{15,7}} | collective-permute-start | bytes 983048 | tf_op jit(solution)/shard_map/ppermute | solution.py:37

commit v8 on v7

--- a/solution.py
+++ b/solution.py
@@ -18,26 +18,26 @@
     return lax.ppermute(x, axis, perm)
 
 
-def suffix_pipeline(own, axis, n_chunks):
+def suffix_pipeline(chunks, axis):
     length, index = (lax.axis_size(axis), lax.axis_index(axis))
-    rows, cols = own.shape
-    height = rows // n_chunks
-    chunks = own.reshape(n_chunks, height, cols)
-    pad = jnp.zeros((length - 1, height, cols), own.dtype)
-    padded = jnp.concatenate((pad, chunks, pad), axis=0)
+    n_chunks = len(chunks)
+    height, cols = chunks[0].shape
     steps = n_chunks + length - 1
-    ordered = lax.dynamic_slice_in_dim(padded, index, steps, axis=0)
     recv = jnp.zeros((height, cols), jnp.bfloat16)
     done = []
     for tau in range(steps):
-        acc = ordered[tau] + recv.astype(jnp.float32)
+        which = tau - (length - 1 - index)
+        own = jnp.zeros((height, cols), jnp.float32)
+        for k in range(max(0, tau - length + 1), min(tau, n_chunks - 1) + 1):
+            own = jnp.where(which == k, chunks[k], own)
+        acc = own + recv.astype(jnp.float32)
         done.append(acc)
         perm = [(i, i - 1) for i in range(1, length) if 0 <= tau - (length - 1 - i) < n_chunks]
         if perm:
             recv = lax.ppermute(acc.astype(jnp.bfloat16), axis, perm)
     stacked = jnp.stack(done, axis=0)
     mine = lax.dynamic_slice_in_dim(stacked, length - 1 - index, n_chunks, axis=0)
-    return mine.reshape(rows, cols)
+    return mine.reshape(n_chunks * height, cols)
 
 
 def attention_terms(q3, g3, kv_blocks, lower, upper, kv_local, head_dim, scaling):
@@ -131,33 +131,39 @@
     terms_low, kv_grad = attention_terms(
         q3, g3, blocks, lower, upper, kv_local, head_dim, scaling
     )
-    for d in range(1, ctx_len):
-        part = terms_low[d * tok_rows : (d + 1) * tok_rows]
-        kv_grad = kv_grad + shifted(part, "ctx", d, ctx_len, False).astype(jnp.float32)
-    grad_key = kv_grad[:, :kv_cols].astype(jnp.bfloat16)
-    grad_value = kv_grad[:, kv_cols:].astype(jnp.bfloat16)
     contract = (((1,), (1,)), ((), ()))
     head_len = lax.axis_size("head")
     head_index = lax.axis_index("head")
     out_cols = w_key.shape[1] // head_len
+    height = tok_rows // CHAIN_CHUNKS
 
-    def partial_for(b):
+    def partial_for(b, grad_key, grad_value):
         start = b * out_cols
         wk = lax.dynamic_slice_in_dim(w_key[0], start, out_cols, axis=0)
         wv = lax.dynamic_slice_in_dim(w_value[0], start, out_cols, axis=0)
         part = lax.dot_general(grad_key, wk, contract, preferred_element_type=jnp.float32)
         return part + lax.dot_general(grad_value, wv, contract, preferred_element_type=jnp.float32)
 
-    received = []
-    for d in range(1, head_len):
-        target = lax.rem(head_index + d, head_len)
-        send = partial_for(target).astype(jnp.bfloat16)
-        perm = [(h, (h + d) % head_len) for h in range(head_len)]
-        received.append(lax.ppermute(send, "head", perm))
-    reduced = partial_for(head_index)
-    for got in received:
-        reduced = reduced + got.astype(jnp.float32)
-    result = suffix_pipeline(reduced, "segment", CHAIN_CHUNKS)
+    chunks = []
+    for c in range(CHAIN_CHUNKS):
+        lo_row = c * height
+        chunk_grad = kv_grad[lo_row : lo_row + height]
+        for d in range(1, ctx_len):
+            part = terms_low[d * tok_rows + lo_row : d * tok_rows + lo_row + height]
+            chunk_grad = chunk_grad + shifted(part, "ctx", d, ctx_len, False).astype(jnp.float32)
+        grad_key = chunk_grad[:, :kv_cols].astype(jnp.bfloat16)
+        grad_value = chunk_grad[:, kv_cols:].astype(jnp.bfloat16)
+        received = []
+        for d in range(1, head_len):
+            target = lax.rem(head_index + d, head_len)
+            send = partial_for(target, grad_key, grad_value).astype(jnp.bfloat16)
+            perm = [(h, (h + d) % head_len) for h in range(head_len)]
+            received.append(lax.ppermute(send, "head", perm))
+        reduced = partial_for(head_index, grad_key, grad_value)
+        for got in received:
+            reduced = reduced + got.astype(jnp.float32)
+        chunks.append(reduced)
+    result = suffix_pipeline(chunks, "segment")
     return result[None]
 
 

time: 85.1 us -> 98 us (1.15)
  matrix products: 5.64 us -> 13.7 us
  waiting for transfers between devices: 46 us -> 38.2 us
  other arithmetic: 3.6 us -> 9.64 us
  starting transfers between devices: 17.4 us -> 23.2 us
    ppermute x4, waiting for transfers between devices: 37.6 us -> 32 us  [suffix_pipeline(): recv = lax.ppermute(acc.astype(jnp.bfloat16), axis, perm)]
    ppermute x6 -> x9, starting transfers between devices: 13.5 us -> 17.3 us  [shifted(): return lax.ppermute(x, axis, perm)]
    dot_general x2 -> x4, matrix products: 1.99 us -> 5.68 us  [partial_for(): lax.dot_general(grad_key, wk, contract, preferred_element_type=jnp.float32)]
    convert_element_type x3 -> x4, other arithmetic: 0.24 us -> 3.81 us  [suffix_pipeline(): recv = lax.ppermute(acc.astype(jnp.bfloat16), axis, perm)]
    dot_general x2 -> x4, matrix products: 1.12 us -> 4.68 us  [partial_for(): lax.dot_general(grad_value, wv, contract, preferred_element_type=jnp.floa...]
    unnamed x4 -> x3, other arithmetic: 0.32 us -> 2.94 us
    ppermute x1 -> x2, waiting for transfers between devices: 1.74 us -> 0.01 us  [per_device(): received.append(lax.ppermute(send, 'head', perm))]
    ppermute x4, starting transfers between devices: 3.95 us -> 5.36 us  [suffix_pipeline(): recv = lax.ppermute(acc.astype(jnp.bfloat16), axis, perm)]
  transfers between devices with their start and end apart: 11 -> 15, of which waited for: 7 -> 8; matrix products, arithmetic and copies ran while one was open for 3% -> 11% of each run, Pallas kernels for 0% -> 0%
where the time goes in v8:
time: 98 us; the launch traced here: 97.4 us
  waiting for transfers between devices  38.2 us (39%)
  starting transfers between devices  23.2 us (24%)
  matrix products  13.7 us (14%)
  other arithmetic  9.64 us (10%)
  Pallas kernels  6.26 us (6%)
  local copies, waits for them, and re-layouts  6.03 us (6%)
    ppermute x4, waiting for transfers between devices, suffix_pipeline(): recv = lax.ppermute(acc.astype(jnp.bfloat16), axis, perm)  32 us
    ppermute x9, starting transfers between devices, shifted(): return lax.ppermute(x, axis, perm)  17.3 us
    pallas_call x1, Pallas kernels, attention_terms(): pl.pallas_call(kernel, out_shape=(jax.ShapeDtypeStruct((seq_rows, 2 * kv_...  6.26 us
    ppermute x9, waiting for transfers between devices, shifted(): return lax.ppermute(x, axis, perm)  6.24 us
    dot_general x4, matrix products, partial_for(): lax.dot_general(grad_key, wk, contract, preferred_element_type=jnp.float32)  5.68 us
    ppermute x4, starting transfers between devices, suffix_pipeline(): recv = lax.ppermute(acc.astype(jnp.bfloat16), axis, perm)  5.36 us
    dot_general x4, matrix products, partial_for(): lax.dot_general(grad_value, wv, contract, preferred_element_type=jnp.floa...  4.68 us
    convert_element_type x4, other arithmetic, suffix_pipeline(): recv = lax.ppermute(acc.astype(jnp.bfloat16), axis, perm)  3.81 us
  transfers between devices with their start and end apart: 15, of which 8 were waited for; matrix products, arithmetic and copies ran while one was open for 11% of the time, Pallas kernels for 0%

profile of v8, /device:TPU:0, one launch (start us, length us, event | category | flops | bytes accessed | tf_op | source)
XLA Modules:
  0.0 97.4 jit_solution(12446925332094767927)
XLA Ops:
  0.0 0.0 copy-start
  0.0 2.8 %fusion.35 = bf16[128,256]{1,0:T(8,128)(2,1)S(1)} fusion(bf16[1,5120,256]{2,1,0:T(8,128)(2,1)} %param.10, bf16[1,128,5120]{2,1,0:T(8,128)(2,1)} %param.6), kind=kOutput, calls=%fused_computation.35 | convolution fusion | flops 335577088 | bytes 3997696 | tf_op jit(solution)/shard_map/dot_general | solution.py:107
  2.8 0.1 copy-done
  2.9 0.4 copy-done.4
  3.3 0.5 fusion.30
  3.8 4.9 %collective-permute-start = (bf16[128,512]{1,0:T(8,128)(2,1)S(1)}, bf16[128,512]{1,0:T(8,128)(2,1)S(1)}, u32[]{:S(2)}, u32[]{:S(2)}) collective-permute-start(bf16[128,512]{1,0:T(8,128)(2,1)S(1)} %pad_maximum_fusion.refs_2_), channel_id=1, source_target_pairs={{0,2},{2,4},{4,6},{1,3},{3,5},{5,7},{8,10},{10,12},{12,14},{9,11},... | collective-permute-start | bytes 393224 | tf_op jit(solution)/shard_map/ppermute | solution.py:18
  8.7 3.4 %collective-permute-start.1 = (bf16[128,512]{1,0:T(8,128)(2,1)S(1)}, bf16[128,512]{1,0:T(8,128)(2,1)S(1)}, u32[]{:S(2)}, u32[]{:S(2)}) collective-permute-start(bf16[128,512]{1,0:T(8,128)(2,1)S(1)} %pad_maximum_fusion.refs_2_), channel_id=1, source_target_pairs={{0,4},{2,6},{1,5},{3,7},{8,12},{10,14},{9,13},{11,15},{16,20},{18,... | collective-permute-start | bytes 393224 | tf_op jit(solution)/shard_map/ppermute | solution.py:18
  12.2 1.3 %collective-permute-start.2 = (bf16[128,512]{1,0:T(8,128)(2,1)S(1)}, bf16[128,512]{1,0:T(8,128)(2,1)S(1)}, u32[]{:S(2)}, u32[]{:S(2)}) collective-permute-start(bf16[128,512]{1,0:T(8,128)(2,1)S(1)} %pad_maximum_fusion.refs_2_), channel_id=1, source_target_pairs={{0,6},{1,7},{8,14},{9,15},{16,22},{17,23},{24,30},{25,31}} | collective-permute-start | bytes 393224 | tf_op jit(solution)/shard_map/ppermute | solution.py:18
  13.5 0.2 copy.25
  13.7 0.1 fusion.61
  13.8 0.1 fusion.59
  13.9 0.2 copy.24
  14.0 0.2 copy.28
  14.2 0.9 broadcast_select_fusion
  15.1 0.0 collective-permute-done.refs_3_
  15.1 0.1 collective-permute-done.1.refs_4_
  15.2 0.8 collective-permute-done.2.refs_5_
  16.0 0.0 copy-done.7
  16.0 0.6 copy-done.8
  16.6 6.3 %shard_map.64 = (bf16[512,512]{1,0:T(8,128)(2,1)}, f32[128,512]{1,0:T(8,128)}) custom-call(bf16[10,128,128]{2,1,0:T(8,128)(2,1)} %bitcast.78, bf16[10,128,128]{2,1,0:T(8,128)(2,1)} %bitcast.79, bf16[128,512]{1,0:T(8,128)(2,1)} %copy-done.5, bf16[128,512]{1,0:T(8,128)(2,1)} %copy-done.6, bf16[128,512]{1,0:T(8,128)(2,1)} %copy-done.7, ...), custom_call_target="tpu_custom_call" | custom-call | tf_op jit(solution)/shard_map/pallas_call | solution.py:86
  22.9 1.0 %fusion.66 = (bf16[64,512]{1,0:T(8,128)(2,1)S(1)}, bf16[64,512]{1,0:T(8,128)(2,1)S(1)}, bf16[64,512]{1,0:T(8,128)(2,1)S(1)}, bf16[64,512]{1,0:T(8,128)(2,1)S(1)}...) fusion(bf16[512,512]{1,0:T(8,128)(2,1)} %get-tuple-element.8), kind=kLoop, calls=%fused_computation.85 | loop fusion | bytes 786432 | tf_op jit(solution)/shard_map/slice | solution.py:152
  23.9 1.3 %collective-permute-start.9 = (bf16[64,512]{1,0:T(8,128)(2,1)S(1)}, bf16[64,512]{1,0:T(8,128)(2,1)S(1)}, u32[]{:S(2)}, u32[]{:S(2)}) collective-permute-start(bf16[64,512]{1,0:T(8,128)(2,1)S(1)} %get-tuple-element.10), channel_id=1, source_target_pairs={{6,0},{7,1},{14,8},{15,9},{22,16},{23,17},{30,24},{31,25}} | collective-permute-start | bytes 196616 | tf_op jit(solution)/shard_map/ppermute | solution.py:18
  25.2 1.3 %collective-permute-start.8 = (bf16[64,512]{1,0:T(8,128)(2,1)S(1)}, bf16[64,512]{1,0:T(8,128)(2,1)S(1)}, u32[]{:S(2)}, u32[]{:S(2)}) collective-permute-start(bf16[64,512]{1,0:T(8,128)(2,1)S(1)} %get-tuple-element.11), channel_id=1, source_target_pairs={{4,0},{6,2},{5,1},{7,3},{12,8},{14,10},{13,9},{15,11},{20,16},{22,... | collective-permute-start | bytes 196616 | tf_op jit(solution)/shard_map/ppermute | solution.py:18
  26.5 1.3 %collective-permute-start.7 = (bf16[64,512]{1,0:T(8,128)(2,1)S(1)}, bf16[64,512]{1,0:T(8,128)(2,1)S(1)}, u32[]{:S(2)}, u32[]{:S(2)}) collective-permute-start(bf16[64,512]{1,0:T(8,128)(2,1)S(1)} %get-tuple-element.9), channel_id=1, source_target_pairs={{2,0},{4,2},{6,4},{3,1},{5,3},{7,5},{10,8},{12,10},{14,12},{11,9},... | collective-permute-start | bytes 196616 | tf_op jit(solution)/shard_map/ppermute | solution.py:18
  27.8 1.3 %collective-permute-start.5 = (bf16[64,512]{1,0:T(8,128)(2,1)S(1)}, bf16[64,512]{1,0:T(8,128)(2,1)S(1)}, u32[]{:S(2)}, u32[]{:S(2)}) collective-permute-start(bf16[64,512]{1,0:T(8,128)(2,1)S(1)} %get-tuple-element.12), channel_id=1, source_target_pairs={{6,0},{7,1},{14,8},{15,9},{22,16},{23,17},{30,24},{31,25}} | collective-permute-start | bytes 196616 | tf_op jit(solution)/shard_map/ppermute | solution.py:18
  29.1 1.3 %collective-permute-start.4 = (bf16[64,512]{1,0:T(8,128)(2,1)S(1)}, bf16[64,512]{1,0:T(8,128)(2,1)S(1)}, u32[]{:S(2)}, u32[]{:S(2)}) collective-permute-start(bf16[64,512]{1,0:T(8,128)(2,1)S(1)} %get-tuple-element.13), channel_id=1, source_target_pairs={{4,0},{6,2},{5,1},{7,3},{12,8},{14,10},{13,9},{15,11},{20,16},{22,... | collective-permute-start | bytes 196616 | tf_op jit(solution)/shard_map/ppermute | solution.py:18
  30.4 0.6 collective-permute-done.9
  31.0 1.3 %collective-permute-start.3 = (bf16[64,512]{1,0:T(8,128)(2,1)S(1)}, bf16[64,512]{1,0:T(8,128)(2,1)S(1)}, u32[]{:S(2)}, u32[]{:S(2)}) collective-permute-start(bf16[64,512]{1,0:T(8,128)(2,1)S(1)} %get-tuple-element.14), channel_id=1, source_target_pairs={{2,0},{4,2},{6,4},{3,1},{5,3},{7,5},{10,8},{12,10},{14,12},{11,9},... | collective-permute-start | bytes 196616 | tf_op jit(solution)/shard_map/ppermute | solution.py:18
  32.3 0.0 copy-start.3
  32.3 0.0 collective-permute-done.8
  32.3 0.3 collective-permute-done.7
  32.7 4.0 %collective-permute-done.5 = bf16[64,512]{1,0:T(8,128)(2,1)S(1)} collective-permute-done((bf16[64,512]{1,0:T(8,128)(2,1)S(1)}, bf16[64,512]{1,0:T(8,128)(2,1)S(1)}, u32[]{:S(2)}, u32[]{:S(2)}) %collective-permute-start.5) | collective-permute-done | bytes 65568 | tf_op jit(solution)/shard_map/ppermute | solution.py:18
  36.7 0.0 collective-permute-done.4
  36.7 0.5 collective-permute-done.3
  37.1 1.0 %add_convert_fusion = (bf16[64,512]{1,0:T(8,128)(2,1)S(1)}, bf16[64,512]{1,0:T(8,128)(2,1)S(1)}) fusion(bf16[64,512]{1,0:T(8,128)(2,1)S(1)} %collective-permute-done.9, bf16[64,512]{1,0:T(8,128)(2,1)S(1)} %collective-permute-done.8, bf16[64,512]{1,0:T(8,128)(2,1)S(1)} %collective-permute-done.7, f32[128,512]{1,0:T(8,128)} %get-tuple-element.7, ...), kind=kLoop, calls=%fused_computation.47 | loop fusion | flops 458752 | bytes 786432 | tf_op jit(solution)/shard_map/convert.1
  38.2 1.8 %fusion.10 = f32[64,2560]{1,0:T(8,128)S(1)} fusion(bf16[1,5120,256]{2,1,0:T(8,128)(2,1)} %param.10, s32[]{:T(128)S(6)} %select_n.82, bf16[64,512]{1,0:T(8,128)(2,1)S(1)} %get-tuple-element.16), kind=kOutput, calls=%fused_computation.14 | convolution fusion | flops 83886080 | bytes 1998852 | tf_op jit(solution)/shard_map/dot_general | solution.py:145
  40.0 0.5 fusion.2
  40.5 0.1 collective-permute-start.6
  40.6 0.5 fusion.8
  41.1 1.3 %fusion.3 = bf16[64,2560]{1,0:T(8,128)(2,1)} fusion(f32[64,2560]{1,0:T(8,128)S(1)} %fusion.8, bf16[1,5120,256]{2,1,0:T(8,128)(2,1)S(1)} %copy-done, s32[]{:T(128)S(6)} %select_n.82, bf16[64,512]{1,0:T(8,128)(2,1)S(1)} %get-tuple-element.15), kind=kOutput, calls=%fused_computation.7 | convolution fusion | flops 84213760 | bytes 2326532 | tf_op jit(solution)/shard_map/dot_general | solution.py:144
  42.4 0.5 collective-permute-start.10
  42.9 0.5 fusion.16
  43.4 0.0 collective-permute-done.6
  43.4 1.4 %bitcast_dynamic-update-slice_fusion.4 = (f32[5,64,2560]{2,1,0:T(8,128)}, f32[64,2560]{1,0:T(8,128)S(1)}) fusion(pred[]{:T(512)S(6)} %eq.38, bf16[64,2560]{1,0:T(8,128)(2,1)S(1)} %collective-permute-done.6, f32[64,2560]{1,0:T(8,128)S(1)} %fusion.16, bf16[1,5120,256]{2,1,0:T(8,128)(2,1)S(1)} %copy-done, s32[]{:T(128)S(6)} %select_n.81, ...), kind=kOutput, calls=%fused_computation.40 | convolution fusion | flops 84541440 | bytes 3637253 | tf_op jit(solution)/shard_map/dot_general | solution.py:144
  44.8 0.8 select_convert_fusion
  45.5 1.4 %collective-permute-start.11 = (bf16[64,2560]{1,0:T(8,128)(2,1)}, bf16[64,2560]{1,0:T(8,128)(2,1)}, u32[]{:S(2)}, u32[]{:S(2)}) collective-permute-start(bf16[64,2560]{1,0:T(8,128)(2,1)} %select_convert_fusion), channel_id=1, source_target_pairs={{24,16},{25,17},{26,18},{27,19},{28,20},{29,21},{30,22},{31,23}} | collective-permute-start | bytes 983048 | tf_op jit(solution)/shard_map/ppermute | solution.py:37
  46.9 1.8 %fusion.14 = f32[64,2560]{1,0:T(8,128)S(1)} fusion(bf16[1,5120,256]{2,1,0:T(8,128)(2,1)} %param.10, s32[]{:T(128)S(6)} %select_n.81, bf16[64,512]{1,0:T(8,128)(2,1)S(1)} %get-tuple-element.15), kind=kOutput, calls=%fused_computation.18 | convolution fusion | flops 83886080 | bytes 1998852 | tf_op jit(solution)/shard_map/dot_general | solution.py:145
  48.7 0.0 collective-permute-done.10
  48.7 0.0 collective-permute-done.11
  48.8 2.5 %bitcast_dynamic-update-slice_fusion.3 = (f32[5,64,2560]{2,1,0:T(8,128)}, f32[64,2560]{1,0:T(8,128)S(1)}) fusion(f32[5,64,2560]{2,1,0:T(8,128)} %get-tuple-element.23, bf16[64,2560]{1,0:T(8,128)(2,1)} %collective-permute-done.11, f32[64,2560]{1,0:T(8,128)S(1)} %get-tuple-element.24, pred[]{:T(512)S(6)} %eq.42, pred[]{:T(512)S(6)} %eq.41, ...), kind=kOutput, calls=%fused_computation.39 | convolution fusion | flops 85032960 | bytes 4620294 | tf_op jit(solution)/shard_map/dot_general | solution.py:144
  51.3 0.8 copy-done.1
  52.1 1.8 %fusion.40 = bf16[64,2560]{1,0:T(8,128)(2,1)} fusion(bf16[64,2560]{1,0:T(8,128)(2,1)} %collective-permute-done.11, f32[64,2560]{1,0:T(8,128)S(1)} %get-tuple-element.26, f32[64,2560]{1,0:T(8,128)S(1)} %get-tuple-element.24, pred[]{:T(512)S(6)} %eq.42, pred[]{:T(512)S(6)} %eq.41), kind=kLoop, calls=%fused_computation.50 | loop fusion | flops 819200 | bytes 1966082 | tf_op jit(solution)/shard_map/convert_element_type | solution.py:37
  53.9 1.4 %collective-permute-start.12 = (bf16[64,2560]{1,0:T(8,128)(2,1)}, bf16[64,2560]{1,0:T(8,128)(2,1)}, u32[]{:S(2)}, u32[]{:S(2)}) collective-permute-start(bf16[64,2560]{1,0:T(8,128)(2,1)} %fusion.40), channel_id=1, source_target_pairs={{16,8},{24,16},{17,9},{25,17},{18,10},{26,18},{19,11},{27,19},{20,... | collective-permute-start | bytes 983048 | tf_op jit(solution)/shard_map/ppermute | solution.py:37
  55.3 0.0 collective-permute-done.12
  55.3 1.1 %fusion.41 = bf16[64,2560]{1,0:T(8,128)(2,1)S(1)} fusion(bf16[64,2560]{1,0:T(8,128)(2,1)} %collective-permute-done.12, f32[64,2560]{1,0:T(8,128)} %copy-done.1, f32[64,2560]{1,0:T(8,128)S(1)} %get-tuple-element.24, pred[]{:T(512)S(6)} %eq.44, pred[]{:T(512)S(6)} %eq.43), kind=kLoop, calls=%fused_computation.51 | loop fusion | flops 819200 | bytes 1966082 | tf_op jit(solution)/shard_map/convert_element_type | solution.py:37
  56.5 1.3 %collective-permute-start.13 = (bf16[64,2560]{1,0:T(8,128)(2,1)S(1)}, bf16[64,2560]{1,0:T(8,128)(2,1)S(1)}, u32[]{:S(2)}, u32[]{:S(2)}) collective-permute-start(bf16[64,2560]{1,0:T(8,128)(2,1)S(1)} %fusion.41), channel_id=1, source_target_pairs={{8,0},{16,8},{9,1},{17,9},{10,2},{18,10},{11,3},{19,11},{12,4},{20... | collective-permute-start | bytes 983048 | tf_op jit(solution)/shard_map/ppermute | solution.py:37
  57.8 1.9 %bitcast_dynamic-update-slice_fusion.2 = f32[5,64,2560]{2,1,0:T(8,128)} fusion(f32[5,64,2560]{2,1,0:T(8,128)} %get-tuple-element.25, bf16[64,2560]{1,0:T(8,128)(2,1)} %collective-permute-done.12, f32[64,2560]{1,0:T(8,128)} %copy-done.1, f32[64,2560]{1,0:T(8,128)S(1)} %get-tuple-element.24, pred[]{:T(512)S(6)} %eq.44, pred[]{:T(512)S(6)} %eq.43), kind=kLoop, calls=%fused_computation.38 | loop fusion | flops 655360 | bytes 2293762
  59.7 24.7 %collective-permute-done.13 = bf16[64,2560]{1,0:T(8,128)(2,1)S(1)} collective-permute-done((bf16[64,2560]{1,0:T(8,128)(2,1)S(1)}, bf16[64,2560]{1,0:T(8,128)(2,1)S(1)}, u32[]{:S(2)}, u32[]{:S(2)}) %collective-permute-start.13) | collective-permute-done | bytes 327712 | tf_op jit(solution)/shard_map/ppermute | solution.py:37
  84.4 0.1 fusion.42
  84.5 1.3 %collective-permute-start.14 = (bf16[64,2560]{1,0:T(8,128)(2,1)S(1)}, bf16[64,2560]{1,0:T(8,128)(2,1)S(1)}, u32[]{:S(2)}, u32[]{:S(2)}) collective-permute-start(bf16[64,2560]{1,0:T(8,128)(2,1)S(1)} %fusion.42), channel_id=1, source_target_pairs={{8,0},{9,1},{10,2},{11,3},{12,4},{13,5},{14,6},{15,7}} | collective-permute-start | bytes 983048 | tf_op jit(solution)/shard_map/ppermute | solution.py:37
  85.8 0.9 bitcast_dynamic-update-slice_fusion.1
  86.7 7.3 %collective-permute-done.14 = bf16[64,2560]{1,0:T(8,128)(2,1)S(1)} collective-permute-done((bf16[64,2560]{1,0:T(8,128)(2,1)S(1)}, bf16[64,2560]{1,0:T(8,128)(2,1)S(1)}, u32[]{:S(2)}, u32[]{:S(2)}) %collective-permute-start.14) | collective-permute-done | bytes 327712 | tf_op jit(solution)/shard_map/ppermute | solution.py:37
  94.0 0.9 bitcast_dynamic-update-slice_fusion
  94.9 2.5 %constant_dynamic-slice_fusion = f32[2,64,2560]{2,1,0:T(8,128)} fusion(f32[5,64,2560]{2,1,0:T(8,128)} %bitcast_dynamic-update-slice_fusion, s32[]{:T(128)S(6)} %select_n.98), kind=kLoop, calls=%fused_computation.66 | loop fusion | bytes 2621444 | tf_op jit(solution)/shard_map/dynamic_slice | solution.py:39
  (18 shorter events, 0.1 us)
Async XLA Ops:
  0.0 2.9 %copy-start = (bf16[1,5120,256]{2,1,0:T(8,128)(2,1)S(1)}, bf16[1,5120,256]{2,1,0:T(8,128)(2,1)}, u32[]{:S(2)}) copy-start(bf16[1,5120,256]{2,1,0:T(8,128)(2,1)} %param.9) | copy-start | bytes 7864324
  0.0 3.3 %copy-start.4 = (bf16[1,128,5120]{2,1,0:T(8,128)(2,1)S(1)}, bf16[1,128,5120]{2,1,0:T(8,128)(2,1)}, u32[]{:S(2)}) copy-start(bf16[1,128,5120]{2,1,0:T(8,128)(2,1)} %param.6) | copy-start | bytes 3932164
  3.3 10.2 %copy-start.9 = (s32[512]{0:T(512)S(1)}, s32[512]{0:T(512)}, u32[]{:S(2)}) copy-start(s32[512]{0:T(512)} %param.11) | copy-start | bytes 6148
  3.8 12.1 %copy-start.5 = (bf16[128,512]{1,0:T(8,128)(2,1)}, bf16[128,512]{1,0:T(8,128)(2,1)S(1)}, u32[]{:S(2)}) copy-start(bf16[128,512]{1,0:T(8,128)(2,1)S(1)} %pad_maximum_fusion.refs_2_) | copy-start | bytes 393220
  3.8 11.3 %collective-permute-start = (bf16[128,512]{1,0:T(8,128)(2,1)S(1)}, bf16[128,512]{1,0:T(8,128)(2,1)S(1)}, u32[]{:S(2)}, u32[]{:S(2)}) collective-permute-start(bf16[128,512]{1,0:T(8,128)(2,1)S(1)} %pad_maximum_fusion.refs_2_), channel_id=1, source_target_pairs={{0,2},{2,4},{4,6},{1,3},{3,5},{5,7},{8,10},{10,12},{12,14},{9,11},... | collective-permute-start | bytes 393224 | tf_op jit(solution)/shard_map/ppermute | solution.py:18
  8.7 6.5 %collective-permute-start.1 = (bf16[128,512]{1,0:T(8,128)(2,1)S(1)}, bf16[128,512]{1,0:T(8,128)(2,1)S(1)}, u32[]{:S(2)}, u32[]{:S(2)}) collective-permute-start(bf16[128,512]{1,0:T(8,128)(2,1)S(1)} %pad_maximum_fusion.refs_2_), channel_id=1, source_target_pairs={{0,4},{2,6},{1,5},{3,7},{8,12},{10,14},{9,13},{11,15},{16,20},{18,... | collective-permute-start | bytes 393224 | tf_op jit(solution)/shard_map/ppermute | solution.py:18
  12.2 3.8 %collective-permute-start.2 = (bf16[128,512]{1,0:T(8,128)(2,1)S(1)}, bf16[128,512]{1,0:T(8,128)(2,1)S(1)}, u32[]{:S(2)}, u32[]{:S(2)}) collective-permute-start(bf16[128,512]{1,0:T(8,128)(2,1)S(1)} %pad_maximum_fusion.refs_2_), channel_id=1, source_target_pairs={{0,6},{1,7},{8,14},{9,15},{16,22},{17,23},{24,30},{25,31}} | collective-permute-start | bytes 393224 | tf_op jit(solution)/shard_map/ppermute | solution.py:18
  15.1 0.8 copy-start.6
  15.2 0.8 copy-start.7
  16.0 0.6 copy-start.8
  23.9 7.1 %collective-permute-start.9 = (bf16[64,512]{1,0:T(8,128)(2,1)S(1)}, bf16[64,512]{1,0:T(8,128)(2,1)S(1)}, u32[]{:S(2)}, u32[]{:S(2)}) collective-permute-start(bf16[64,512]{1,0:T(8,128)(2,1)S(1)} %get-tuple-element.10), channel_id=1, source_target_pairs={{6,0},{7,1},{14,8},{15,9},{22,16},{23,17},{30,24},{31,25}} | collective-permute-start | bytes 196616 | tf_op jit(solution)/shard_map/ppermute | solution.py:18
  25.2 7.1 %collective-permute-start.8 = (bf16[64,512]{1,0:T(8,128)(2,1)S(1)}, bf16[64,512]{1,0:T(8,128)(2,1)S(1)}, u32[]{:S(2)}, u32[]{:S(2)}) collective-permute-start(bf16[64,512]{1,0:T(8,128)(2,1)S(1)} %get-tuple-element.11), channel_id=1, source_target_pairs={{4,0},{6,2},{5,1},{7,3},{12,8},{14,10},{13,9},{15,11},{20,16},{22,... | collective-permute-start | bytes 196616 | tf_op jit(solution)/shard_map/ppermute | solution.py:18
  26.5 6.2 %collective-permute-start.7 = (bf16[64,512]{1,0:T(8,128)(2,1)S(1)}, bf16[64,512]{1,0:T(8,128)(2,1)S(1)}, u32[]{:S(2)}, u32[]{:S(2)}) collective-permute-start(bf16[64,512]{1,0:T(8,128)(2,1)S(1)} %get-tuple-element.9), channel_id=1, source_target_pairs={{2,0},{4,2},{6,4},{3,1},{5,3},{7,5},{10,8},{12,10},{14,12},{11,9},... | collective-permute-start | bytes 196616 | tf_op jit(solution)/shard_map/ppermute | solution.py:18
  27.8 8.9 %collective-permute-start.5 = (bf16[64,512]{1,0:T(8,128)(2,1)S(1)}, bf16[64,512]{1,0:T(8,128)(2,1)S(1)}, u32[]{:S(2)}, u32[]{:S(2)}) collective-permute-start(bf16[64,512]{1,0:T(8,128)(2,1)S(1)} %get-tuple-element.12), channel_id=1, source_target_pairs={{6,0},{7,1},{14,8},{15,9},{22,16},{23,17},{30,24},{31,25}} | collective-permute-start | bytes 196616 | tf_op jit(solution)/shard_map/ppermute | solution.py:18
  29.1 7.6 %collective-permute-start.4 = (bf16[64,512]{1,0:T(8,128)(2,1)S(1)}, bf16[64,512]{1,0:T(8,128)(2,1)S(1)}, u32[]{:S(2)}, u32[]{:S(2)}) collective-permute-start(bf16[64,512]{1,0:T(8,128)(2,1)S(1)} %get-tuple-element.13), channel_id=1, source_target_pairs={{4,0},{6,2},{5,1},{7,3},{12,8},{14,10},{13,9},{15,11},{20,16},{22,... | collective-permute-start | bytes 196616 | tf_op jit(solution)/shard_map/ppermute | solution.py:18
  31.0 6.1 %collective-permute-start.3 = (bf16[64,512]{1,0:T(8,128)(2,1)S(1)}, bf16[64,512]{1,0:T(8,128)(2,1)S(1)}, u32[]{:S(2)}, u32[]{:S(2)}) collective-permute-start(bf16[64,512]{1,0:T(8,128)(2,1)S(1)} %get-tuple-element.14), channel_id=1, source_target_pairs={{2,0},{4,2},{6,4},{3,1},{5,3},{7,5},{10,8},{12,10},{14,12},{11,9},... | collective-permute-start | bytes 196616 | tf_op jit(solution)/shard_map/ppermute | solution.py:18
  32.3 8.3 %copy-start.3 = (bf16[1,5120,256]{2,1,0:T(8,128)(2,1)S(1)}, bf16[1,5120,256]{2,1,0:T(8,128)(2,1)}, u32[]{:S(2)}) copy-start(bf16[1,5120,256]{2,1,0:T(8,128)(2,1)} %param.10) | copy-start | bytes 7864324
  40.5 2.9 %collective-permute-start.6 = (bf16[64,2560]{1,0:T(8,128)(2,1)S(1)}, bf16[64,2560]{1,0:T(8,128)(2,1)S(1)}, u32[]{:S(2)}, u32[]{:S(2)}) collective-permute-start(bf16[64,2560]{1,0:T(8,128)(2,1)S(1)} %fusion.2), channel_id=1, source_target_pairs={{0,1},{1,0},{2,3},{3,2},{4,5},{5,4},{6,7},{7,6},{8,9},{9,8},{10,11... | collective-permute-start | bytes 983048 | tf_op jit(solution)/shard_map/ppermute | solution.py:161
  42.4 6.3 %collective-permute-start.10 = (bf16[64,2560]{1,0:T(8,128)(2,1)}, bf16[64,2560]{1,0:T(8,128)(2,1)}, u32[]{:S(2)}, u32[]{:S(2)}) collective-permute-start(bf16[64,2560]{1,0:T(8,128)(2,1)} %fusion.3), channel_id=1, source_target_pairs={{0,1},{1,0},{2,3},{3,2},{4,5},{5,4},{6,7},{7,6},{8,9},{9,8},{10,11... | collective-permute-start | bytes 983048 | tf_op jit(solution)/shard_map/ppermute | solution.py:161
  45.5 3.2 %collective-permute-start.11 = (bf16[64,2560]{1,0:T(8,128)(2,1)}, bf16[64,2560]{1,0:T(8,128)(2,1)}, u32[]{:S(2)}, u32[]{:S(2)}) collective-permute-start(bf16[64,2560]{1,0:T(8,128)(2,1)} %select_convert_fusion), channel_id=1, source_target_pairs={{24,16},{25,17},{26,18},{27,19},{28,20},{29,21},{30,22},{31,23}} | collective-permute-start | bytes 983048 | tf_op jit(solution)/shard_map/ppermute | solution.py:37
  51.3 0.8 copy-start.1
  53.9 1.4 %collective-permute-start.12 = (bf16[64,2560]{1,0:T(8,128)(2,1)}, bf16[64,2560]{1,0:T(8,128)(2,1)}, u32[]{:S(2)}, u32[]{:S(2)}) collective-permute-start(bf16[64,2560]{1,0:T(8,128)(2,1)} %fusion.40), channel_id=1, source_target_pairs={{16,8},{24,16},{17,9},{25,17},{18,10},{26,18},{19,11},{27,19},{20,... | collective-permute-start | bytes 983048 | tf_op jit(solution)/shard_map/ppermute | solution.py:37
  55.3 29.1 %copy-start.2 = (f32[64,2560]{1,0:T(8,128)S(1)}, f32[64,2560]{1,0:T(8,128)}, u32[]{:S(2)}) copy-start(f32[64,2560]{1,0:T(8,128)} %copy-done.1) | copy-start | bytes 1966084
  56.5 27.9 %collective-permute-start.13 = (bf16[64,2560]{1,0:T(8,128)(2,1)S(1)}, bf16[64,2560]{1,0:T(8,128)(2,1)S(1)}, u32[]{:S(2)}, u32[]{:S(2)}) collective-permute-start(bf16[64,2560]{1,0:T(8,128)(2,1)S(1)} %fusion.41), channel_id=1, source_target_pairs={{8,0},{16,8},{9,1},{17,9},{10,2},{18,10},{11,3},{19,11},{12,4},{20... | collective-permute-start | bytes 983048 | tf_op jit(solution)/shard_map/ppermute | solution.py:37
  84.5 9.5 %collective-permute-start.14 = (bf16[64,2560]{1,0:T(8,128)(2,1)S(1)}, bf16[64,2560]{1,0:T(8,128)(2,1)S(1)}, u32[]{:S(2)}, u32[]{:S(2)}) collective-permute-start(bf16[64,2560]{1,0:T(8,128)(2,1)S(1)} %fusion.42), channel_id=1, source_target_pairs={{8,0},{9,1},{10,2},{11,3},{12,4},{13,5},{14,6},{15,7}} | collective-permute-start | bytes 983048 | tf_op jit(solution)/shard_map/ppermute | solution.py:37

commit v9 on v7

--- a/solution.py
+++ b/solution.py
@@ -131,9 +131,13 @@
     terms_low, kv_grad = attention_terms(
         q3, g3, blocks, lower, upper, kv_local, head_dim, scaling
     )
-    for d in range(1, ctx_len):
-        part = terms_low[d * tok_rows : (d + 1) * tok_rows]
-        kv_grad = kv_grad + shifted(part, "ctx", d, ctx_len, False).astype(jnp.float32)
+    low_blocks = terms_low.reshape(ctx_len, tok_rows, terms_low.shape[1])
+    targets = jnp.arange(ctx_len, dtype=jnp.int32)
+    pick = ctx_index - targets
+    outgoing = jnp.take(low_blocks, jnp.clip(pick, 0, ctx_len - 1), axis=0)
+    outgoing = jnp.where(((pick >= 1))[:, None, None], outgoing, jnp.zeros_like(outgoing))
+    incoming = lax.all_to_all(outgoing, "ctx", 0, 0, tiled=True)
+    kv_grad = kv_grad + jnp.sum(incoming.astype(jnp.float32), axis=0)
     grad_key = kv_grad[:, :kv_cols].astype(jnp.bfloat16)
     grad_value = kv_grad[:, kv_cols:].astype(jnp.bfloat16)
     contract = (((1,), (1,)), ((), ()))

time: 85.1 us -> 87.8 us (1.032)
    all_to_all x0 -> x1, waiting for transfers between devices: none -> 6.63 us  [per_device(): incoming = lax.all_to_all(outgoing, 'ctx', 0, 0, tiled=True)]
    ppermute x6 -> x3, waiting for transfers between devices: 6.63 us -> 0.79 us  [shifted(): return lax.ppermute(x, axis, perm)]
    all_to_all x0 -> x1, starting transfers between devices: none -> 4.61 us  [per_device(): incoming = lax.all_to_all(outgoing, 'ctx', 0, 0, tiled=True)]
    ppermute x6 -> x3, starting transfers between devices: 13.5 us -> 9.6 us  [shifted(): return lax.ppermute(x, axis, perm)]
    gather x0 -> x1, local copies, waits for them, and re-layouts: none -> 1.66 us  [per_device(): outgoing = jnp.take(low_blocks, jnp.clip(pick, 0, ctx_len - 1), axis=0)]
    slice x1 -> x0, local copies, waits for them, and re-layouts: 1.06 us -> none  [per_device(): part = terms_low[d * tok_rows:(d + 1) * tok_rows]]
    another operation x1, other arithmetic: 1.01 us -> 0.04 us
    select_n x0 -> x2, other arithmetic: none -> 0.93 us  [the longest x1 0.92 us: per_device(): jnp.where((pick >= 1)[:, None, None], outgoing, jnp.zeros_like(outgoing))]
  transfers between devices with their start and end apart: 11 -> 9, of which waited for: 7 -> 5; matrix products, arithmetic and copies ran while one was open for 3% -> 3% of each run, Pallas kernels for 0% -> 0%
where the time goes in v9:
time: 87.8 us; the launch traced here: 87.4 us
  waiting for transfers between devices  46.8 us (53%)
  starting transfers between devices  18.2 us (21%)
  matrix products  6.41 us (7%)
  Pallas kernels  6.26 us (7%)
  local copies, waits for them, and re-layouts  5.84 us (7%)
  other arithmetic  3.64 us (4%)
    ppermute x4, waiting for transfers between devices, suffix_pipeline(): recv = lax.ppermute(acc.astype(jnp.bfloat16), axis, perm)  37.6 us
    ppermute x3, starting transfers between devices, shifted(): return lax.ppermute(x, axis, perm)  9.6 us
    all_to_all x1, waiting for transfers between devices, per_device(): incoming = lax.all_to_all(outgoing, 'ctx', 0, 0, tiled=True)  6.63 us
    pallas_call x1, Pallas kernels, attention_terms(): pl.pallas_call(kernel, out_shape=(jax.ShapeDtypeStruct((seq_rows, 2 * kv_...  6.26 us
    all_to_all x1, starting transfers between devices, per_device(): incoming = lax.all_to_all(outgoing, 'ctx', 0, 0, tiled=True)  4.61 us
    ppermute x4, starting transfers between devices, suffix_pipeline(): recv = lax.ppermute(acc.astype(jnp.bfloat16), axis, perm)  3.95 us
    dot_general x1, matrix products, per_device(): jnp.dot(tokens, w_value[0], preferred_element_type=jnp.float32)  2.79 us
    unnamed x23, local copies, waits for them, and re-layouts  2.43 us
  transfers between devices with their start and end apart: 9, of which 5 were waited for; matrix products, arithmetic and copies ran while one was open for 3% of the time, Pallas kernels for 0%

profile of v9, /device:TPU:0, one launch (start us, length us, event | category | flops | bytes accessed | tf_op | source)
XLA Modules:
  0.0 87.4 jit_solution(13735662537941705325)
XLA Ops:
  0.0 0.0 copy-start
  0.0 0.0 copy-start.3
  0.0 2.8 %fusion.26 = bf16[128,256]{1,0:T(8,128)(2,1)S(1)} fusion(bf16[1,5120,256]{2,1,0:T(8,128)(2,1)} %param.10, bf16[1,128,5120]{2,1,0:T(8,128)(2,1)} %param.6), kind=kOutput, calls=%fused_computation.27 | convolution fusion | flops 335577088 | bytes 3997696 | tf_op jit(solution)/shard_map/dot_general | solution.py:107
  2.8 0.1 copy-done
  2.9 0.4 copy-done.3
  3.3 0.0 copy-start.9
  3.3 0.5 fusion.21
  3.8 0.0 copy-start.4
  3.8 4.9 %collective-permute-start = (bf16[128,512]{1,0:T(8,128)(2,1)S(1)}, bf16[128,512]{1,0:T(8,128)(2,1)S(1)}, u32[]{:S(2)}, u32[]{:S(2)}) collective-permute-start(bf16[128,512]{1,0:T(8,128)(2,1)S(1)} %pad_maximum_fusion.refs_2_), channel_id=1, source_target_pairs={{0,2},{2,4},{4,6},{1,3},{3,5},{5,7},{8,10},{10,12},{12,14},{9,11},... | collective-permute-start | bytes 393224 | tf_op jit(solution)/shard_map/ppermute | solution.py:18
  8.7 3.4 %collective-permute-start.1 = (bf16[128,512]{1,0:T(8,128)(2,1)S(1)}, bf16[128,512]{1,0:T(8,128)(2,1)S(1)}, u32[]{:S(2)}, u32[]{:S(2)}) collective-permute-start(bf16[128,512]{1,0:T(8,128)(2,1)S(1)} %pad_maximum_fusion.refs_2_), channel_id=1, source_target_pairs={{0,4},{2,6},{1,5},{3,7},{8,12},{10,14},{9,13},{11,15},{16,20},{18,... | collective-permute-start | bytes 393224 | tf_op jit(solution)/shard_map/ppermute | solution.py:18
  12.2 1.3 %collective-permute-start.2 = (bf16[128,512]{1,0:T(8,128)(2,1)S(1)}, bf16[128,512]{1,0:T(8,128)(2,1)S(1)}, u32[]{:S(2)}, u32[]{:S(2)}) collective-permute-start(bf16[128,512]{1,0:T(8,128)(2,1)S(1)} %pad_maximum_fusion.refs_2_), channel_id=1, source_target_pairs={{0,6},{1,7},{8,14},{9,15},{16,22},{17,23},{24,30},{25,31}} | collective-permute-start | bytes 393224 | tf_op jit(solution)/shard_map/ppermute | solution.py:18
  13.5 0.0 copy-done.9
  13.6 0.2 copy.25
  13.7 0.1 fusion.51
  13.8 0.1 fusion.49
  13.9 0.2 copy.24
  14.1 0.2 copy.28
  14.3 0.9 broadcast_select_fusion
  15.1 0.0 collective-permute-done.refs_3_
  15.2 0.0 copy-start.6
  15.2 0.0 collective-permute-done.1.refs_4_
  15.2 0.0 copy-start.7
  15.2 0.8 collective-permute-done.2.refs_5_
  16.0 0.0 copy-start.8
  16.0 0.0 copy-done.4
  16.0 0.0 copy-done.6
  16.0 0.0 copy-done.7
  16.0 0.6 copy-done.8
  16.6 6.3 %shard_map.64 = (bf16[512,512]{1,0:T(8,128)(2,1)}, f32[128,512]{1,0:T(8,128)}) custom-call(bf16[10,128,128]{2,1,0:T(8,128)(2,1)} %bitcast.108, bf16[10,128,128]{2,1,0:T(8,128)(2,1)} %bitcast.109, bf16[128,512]{1,0:T(8,128)(2,1)} %copy-done.4, bf16[128,512]{1,0:T(8,128)(2,1)} %copy-done.6, bf16[128,512]{1,0:T(8,128)(2,1)} %copy-done.7, ...), custom_call_target="tpu_custom_call" | custom-call | tf_op jit(solution)/shard_map/pallas_call | solution.py:86
  22.9 0.0 copy-start.5
  22.9 1.7 %gather_fusion = bf16[4,128,512]{2,1,0:T(8,128)(2,1)S(1)} fusion(bf16[4,128,512]{2,1,0:T(8,128)(2,1)} %bitcast.107, s32[1024]{0:T(1024)S(1)} %pad_clamp_fusion), kind=kCustom, calls=%fused_computation | custom fusion | bytes 1048592 | tf_op jit(solution)/shard_map/jit(_take)/gather | solution.py:137
  24.5 0.9 %select_select_fusion = bf16[4,128,512]{2,1,0:T(8,128)(2,1)} fusion(bf16[4,128,512]{2,1,0:T(8,128)(2,1)S(1)} %gather_fusion, pred[4]{0:T(512)(128)(4,1)S(1)} %get-tuple-element.15, pred[4]{0:T(512)(128)(4,1)S(1)} %get-tuple-element.16), kind=kLoop, calls=%fused_computation.44 | loop fusion | flops 524288 | bytes 1048584 | tf_op jit(solution)/shard_map/jit(_where)/select_n | solution.py:138
  25.4 4.6 %all-to-all-start = ((bf16[4,128,512]{2,1,0:T(8,128)(2,1)}), bf16[4,128,512]{2,1,0:T(8,128)(2,1)S(1)}, u32[]{:S(2)}, u32[]{:S(2)}) async-start(bf16[4,128,512]{2,1,0:T(8,128)(2,1)} %select_select_fusion), calls=%async_computation | async-start | bytes 1048576 | tf_op jit(solution)/shard_map/all_to_all | solution.py:139
  30.1 6.6 %all-to-all-done = bf16[4,128,512]{2,1,0:T(8,128)(2,1)S(1)} async-done(((bf16[4,128,512]{2,1,0:T(8,128)(2,1)}), bf16[4,128,512]{2,1,0:T(8,128)(2,1)S(1)}, u32[]{:S(2)}, u32[]{:S(2)}) %all-to-all-start) | async-done | bytes 524320 | tf_op jit(solution)/shard_map/all_to_all | solution.py:139
  36.7 0.0 copy-start.1
  36.7 0.1 convert_reduce_fusion
  36.8 0.0 copy-done.5
  36.8 0.6 fusion.8
  37.4 1.0 %copy-done.1 = bf16[1,5120,256]{2,1,0:T(8,128)(2,1)S(1)} copy-done((bf16[1,5120,256]{2,1,0:T(8,128)(2,1)S(1)}, bf16[1,5120,256]{2,1,0:T(8,128)(2,1)}, u32[]{:S(2)}) %copy-start.1) | copy-done | bytes 2621464
  38.4 1.4 %fusion = bf16[128,2560]{1,0:T(8,128)(2,1)} fusion(f32[128,2560]{1,0:T(8,128)S(1)} %fusion.8, bf16[1,5120,256]{2,1,0:T(8,128)(2,1)S(1)} %copy-done.1, s32[]{:T(128)S(6)} %select_n.58, bf16[128,512]{1,0:T(8,128)(2,1)S(1)} %add_convert_fusion), kind=kOutput, calls=%fused_computation.6 | convolution fusion | flops 168427520 | bytes 3342340 | tf_op jit(solution)/shard_map/dot_general | solution.py:153
  39.8 0.0 collective-permute-start.3
  39.8 0.0 copy-start.2
  39.8 0.6 fusion.11
  40.4 1.7 %collective-permute-done.3 = bf16[128,2560]{1,0:T(8,128)(2,1)S(1)} collective-permute-done((bf16[128,2560]{1,0:T(8,128)(2,1)}, bf16[128,2560]{1,0:T(8,128)(2,1)S(1)}, u32[]{:S(2)}, u32[]{:S(2)}) %collective-permute-start.3) | collective-permute-done | bytes 655392 | tf_op jit(solution)/shard_map/ppermute | solution.py:160
  42.1 0.0 copy-done.2
  42.2 0.6 convert_add_fusion
  42.7 0.2 broadcast_in_dim.34
  42.9 1.0 %fusion.2 = f32[5,64,2560]{2,1,0:T(8,128)S(1)} fusion(s32[]{:T(128)S(6)} %select_n.59, f32[3,64,2560]{2,1,0:T(8,128)S(1)} %broadcast_in_dim.34, f32[2,64,2560]{2,1,0:T(8,128)S(1)} %bitcast.106), kind=kLoop, calls=%fused_computation.8 | loop fusion | flops 1638400 | bytes 6553604 | tf_op jit(solution)/shard_map/concatenate | solution.py:27
  44.0 0.7 collective-permute-start.4
  44.7 0.0 collective-permute-done.4
  44.7 0.1 fusion.37
  44.8 0.7 collective-permute-start.5
  45.5 0.1 bitcast_dynamic-update-slice_fusion.2
  45.6 0.0 collective-permute-done.5
  45.6 0.1 fusion.38
  45.7 1.3 %collective-permute-start.6 = (bf16[64,2560]{1,0:T(8,128)(2,1)S(1)}, bf16[64,2560]{1,0:T(8,128)(2,1)S(1)}, u32[]{:S(2)}, u32[]{:S(2)}) collective-permute-start(bf16[64,2560]{1,0:T(8,128)(2,1)S(1)} %fusion.38), channel_id=1, source_target_pairs={{8,0},{16,8},{9,1},{17,9},{10,2},{18,10},{11,3},{19,11},{12,4},{20... | collective-permute-start | bytes 983048 | tf_op jit(solution)/shard_map/ppermute | solution.py:37
  47.0 0.1 bitcast_dynamic-update-slice_fusion.1
  47.1 29.4 %collective-permute-done.6 = bf16[64,2560]{1,0:T(8,128)(2,1)S(1)} collective-permute-done((bf16[64,2560]{1,0:T(8,128)(2,1)S(1)}, bf16[64,2560]{1,0:T(8,128)(2,1)S(1)}, u32[]{:S(2)}, u32[]{:S(2)}) %collective-permute-start.6) | collective-permute-done | bytes 327712 | tf_op jit(solution)/shard_map/ppermute | solution.py:37
  76.5 0.1 fusion.39
  76.5 1.3 %collective-permute-start.7 = (bf16[64,2560]{1,0:T(8,128)(2,1)S(1)}, bf16[64,2560]{1,0:T(8,128)(2,1)S(1)}, u32[]{:S(2)}, u32[]{:S(2)}) collective-permute-start(bf16[64,2560]{1,0:T(8,128)(2,1)S(1)} %fusion.39), channel_id=1, source_target_pairs={{8,0},{9,1},{10,2},{11,3},{12,4},{13,5},{14,6},{15,7}} | collective-permute-start | bytes 983048 | tf_op jit(solution)/shard_map/ppermute | solution.py:37
  77.8 0.1 bitcast_dynamic-update-slice_fusion
  77.9 8.2 %collective-permute-done.7 = bf16[64,2560]{1,0:T(8,128)(2,1)S(1)} collective-permute-done((bf16[64,2560]{1,0:T(8,128)(2,1)S(1)}, bf16[64,2560]{1,0:T(8,128)(2,1)S(1)}, u32[]{:S(2)}, u32[]{:S(2)}) %collective-permute-start.7) | collective-permute-done | bytes 327712 | tf_op jit(solution)/shard_map/ppermute | solution.py:37
  86.2 0.1 fusion.33
  86.3 1.2 %constant_dynamic-slice_fusion = f32[2,64,2560]{2,1,0:T(8,128)} fusion(f32[5,64,2560]{2,1,0:T(8,128)S(1)} %fusion.33, s32[]{:T(128)S(6)} %select_n.60), kind=kLoop, calls=%fused_computation.59 | loop fusion | bytes 2621444 | tf_op jit(solution)/shard_map/dynamic_slice | solution.py:39
  (11 shorter events, 0.2 us)
Async XLA Ops:
  0.0 2.9 %copy-start = (bf16[1,5120,256]{2,1,0:T(8,128)(2,1)S(1)}, bf16[1,5120,256]{2,1,0:T(8,128)(2,1)}, u32[]{:S(2)}) copy-start(bf16[1,5120,256]{2,1,0:T(8,128)(2,1)} %param.9) | copy-start | bytes 7864324
  0.0 3.3 %copy-start.3 = (bf16[1,128,5120]{2,1,0:T(8,128)(2,1)S(1)}, bf16[1,128,5120]{2,1,0:T(8,128)(2,1)}, u32[]{:S(2)}) copy-start(bf16[1,128,5120]{2,1,0:T(8,128)(2,1)} %param.6) | copy-start | bytes 3932164
  3.3 10.2 %copy-start.9 = (s32[512]{0:T(512)S(1)}, s32[512]{0:T(512)}, u32[]{:S(2)}) copy-start(s32[512]{0:T(512)} %param.11) | copy-start | bytes 6148
  3.8 12.1 %copy-start.4 = (bf16[128,512]{1,0:T(8,128)(2,1)}, bf16[128,512]{1,0:T(8,128)(2,1)S(1)}, u32[]{:S(2)}) copy-start(bf16[128,512]{1,0:T(8,128)(2,1)S(1)} %pad_maximum_fusion.refs_2_) | copy-start | bytes 393220
  3.8 11.3 %collective-permute-start = (bf16[128,512]{1,0:T(8,128)(2,1)S(1)}, bf16[128,512]{1,0:T(8,128)(2,1)S(1)}, u32[]{:S(2)}, u32[]{:S(2)}) collective-permute-start(bf16[128,512]{1,0:T(8,128)(2,1)S(1)} %pad_maximum_fusion.refs_2_), channel_id=1, source_target_pairs={{0,2},{2,4},{4,6},{1,3},{3,5},{5,7},{8,10},{10,12},{12,14},{9,11},... | collective-permute-start | bytes 393224 | tf_op jit(solution)/shard_map/ppermute | solution.py:18
  8.7 6.5 %collective-permute-start.1 = (bf16[128,512]{1,0:T(8,128)(2,1)S(1)}, bf16[128,512]{1,0:T(8,128)(2,1)S(1)}, u32[]{:S(2)}, u32[]{:S(2)}) collective-permute-start(bf16[128,512]{1,0:T(8,128)(2,1)S(1)} %pad_maximum_fusion.refs_2_), channel_id=1, source_target_pairs={{0,4},{2,6},{1,5},{3,7},{8,12},{10,14},{9,13},{11,15},{16,20},{18,... | collective-permute-start | bytes 393224 | tf_op jit(solution)/shard_map/ppermute | solution.py:18
  12.2 3.8 %collective-permute-start.2 = (bf16[128,512]{1,0:T(8,128)(2,1)S(1)}, bf16[128,512]{1,0:T(8,128)(2,1)S(1)}, u32[]{:S(2)}, u32[]{:S(2)}) collective-permute-start(bf16[128,512]{1,0:T(8,128)(2,1)S(1)} %pad_maximum_fusion.refs_2_), channel_id=1, source_target_pairs={{0,6},{1,7},{8,14},{9,15},{16,22},{17,23},{24,30},{25,31}} | collective-permute-start | bytes 393224 | tf_op jit(solution)/shard_map/ppermute | solution.py:18
  15.2 0.8 copy-start.6
  15.2 0.8 copy-start.7
  16.0 0.6 copy-start.8
  22.9 13.9 %copy-start.5 = (f32[128,512]{1,0:T(8,128)S(1)}, f32[128,512]{1,0:T(8,128)}, u32[]{:S(2)}) copy-start(f32[128,512]{1,0:T(8,128)} %get-tuple-element.7) | copy-start | bytes 786436
  25.4 11.2 %all-to-all-start = ((bf16[4,128,512]{2,1,0:T(8,128)(2,1)}), bf16[4,128,512]{2,1,0:T(8,128)(2,1)S(1)}, u32[]{:S(2)}, u32[]{:S(2)}) async-start(bf16[4,128,512]{2,1,0:T(8,128)(2,1)} %select_select_fusion), calls=%async_computation | async-start | bytes 1048576 | tf_op jit(solution)/shard_map/all_to_all | solution.py:139
  36.7 1.7 %copy-start.1 = (bf16[1,5120,256]{2,1,0:T(8,128)(2,1)S(1)}, bf16[1,5120,256]{2,1,0:T(8,128)(2,1)}, u32[]{:S(2)}) copy-start(bf16[1,5120,256]{2,1,0:T(8,128)(2,1)} %param.10) | copy-start | bytes 7864324
  39.8 2.3 %collective-permute-start.3 = (bf16[128,2560]{1,0:T(8,128)(2,1)}, bf16[128,2560]{1,0:T(8,128)(2,1)S(1)}, u32[]{:S(2)}, u32[]{:S(2)}) collective-permute-start(bf16[128,2560]{1,0:T(8,128)(2,1)} %fusion), channel_id=1, source_target_pairs={{0,1},{1,0},{2,3},{3,2},{4,5},{5,4},{6,7},{7,6},{8,9},{9,8},{10,11... | collective-permute-start | bytes 1966088 | tf_op jit(solution)/shard_map/ppermute | solution.py:160
  39.8 2.3 %copy-start.2 = (bf16[1,5120,256]{2,1,0:T(8,128)(2,1)S(1)}, bf16[1,5120,256]{2,1,0:T(8,128)(2,1)}, u32[]{:S(2)}) copy-start(bf16[1,5120,256]{2,1,0:T(8,128)(2,1)} %param.10) | copy-start | bytes 7864324
  44.0 0.7 collective-permute-start.4
  44.8 0.8 collective-permute-start.5
  45.7 30.8 %collective-permute-start.6 = (bf16[64,2560]{1,0:T(8,128)(2,1)S(1)}, bf16[64,2560]{1,0:T(8,128)(2,1)S(1)}, u32[]{:S(2)}, u32[]{:S(2)}) collective-permute-start(bf16[64,2560]{1,0:T(8,128)(2,1)S(1)} %fusion.38), channel_id=1, source_target_pairs={{8,0},{16,8},{9,1},{17,9},{10,2},{18,10},{11,3},{19,11},{12,4},{20... | collective-permute-start | bytes 983048 | tf_op jit(solution)/shard_map/ppermute | solution.py:37
  76.5 9.6 %collective-permute-start.7 = (bf16[64,2560]{1,0:T(8,128)(2,1)S(1)}, bf16[64,2560]{1,0:T(8,128)(2,1)S(1)}, u32[]{:S(2)}, u32[]{:S(2)}) collective-permute-start(bf16[64,2560]{1,0:T(8,128)(2,1)S(1)} %fusion.39), channel_id=1, source_target_pairs={{8,0},{9,1},{10,2},{11,3},{12,4},{13,5},{14,6},{15,7}} | collective-permute-start | bytes 983048 | tf_op jit(solution)/shard_map/ppermute | solution.py:37

commit v10 on v7

--- a/solution.py
+++ b/solution.py
@@ -7,7 +7,7 @@
 from jax.sharding import PartitionSpec as P
 
 
-CHAIN_CHUNKS = 2
+CHAIN_CHUNKS = 4
 
 
 def shifted(x, axis, d, length, up):
@@ -23,21 +23,19 @@
     rows, cols = own.shape
     height = rows // n_chunks
     chunks = own.reshape(n_chunks, height, cols)
-    pad = jnp.zeros((length - 1, height, cols), own.dtype)
-    padded = jnp.concatenate((pad, chunks, pad), axis=0)
-    steps = n_chunks + length - 1
-    ordered = lax.dynamic_slice_in_dim(padded, index, steps, axis=0)
-    recv = jnp.zeros((height, cols), jnp.bfloat16)
-    done = []
-    for tau in range(steps):
-        acc = ordered[tau] + recv.astype(jnp.float32)
-        done.append(acc)
-        perm = [(i, i - 1) for i in range(1, length) if 0 <= tau - (length - 1 - i) < n_chunks]
-        if perm:
-            recv = lax.ppermute(acc.astype(jnp.bfloat16), axis, perm)
-    stacked = jnp.stack(done, axis=0)
-    mine = lax.dynamic_slice_in_dim(stacked, length - 1 - index, n_chunks, axis=0)
-    return mine.reshape(rows, cols)
+    partial = [chunks[k] for k in range(n_chunks)]
+    history = [[chunks[k]] for k in range(n_chunks)]
+    for hop in range(1, length):
+        for k in range(n_chunks):
+            sender = length - hop
+            got = lax.ppermute(partial[k].astype(jnp.bfloat16), axis, [(sender, sender - 1)])
+            partial[k] = chunks[k] + got.astype(jnp.float32)
+            history[k].append(partial[k])
+    out = [
+        lax.dynamic_index_in_dim(jnp.stack(history[k], axis=0), length - 1 - index, 0, keepdims=False)
+        for k in range(n_chunks)
+    ]
+    return jnp.concatenate(out, axis=0)
 
 
 def attention_terms(q3, g3, kv_blocks, lower, upper, kv_local, head_dim, scaling):

time: 85.1 us -> 100 us (1.18)
  starting transfers between devices: 17.4 us -> 24.6 us
  other arithmetic: 3.6 us -> 8.76 us
  waiting for transfers between devices: 46 us -> 47.4 us
    ppermute x4 -> x12, starting transfers between devices: 3.95 us -> 11.2 us  [suffix_pipeline(): lax.ppermute(partial[k].astype(jnp.bfloat16), axis, [(sender, sender - 1)])]
    convert_element_type x3, other arithmetic: 0.24 us -> 4.09 us  [suffix_pipeline(): partial[k].astype(jnp.bfloat16)]
    ppermute x6, waiting for transfers between devices: 6.63 us -> 9.08 us  [shifted(): return lax.ppermute(x, axis, perm)]
    unnamed x23 -> x42, local copies, waits for them, and re-layouts: 2.65 us -> 4.75 us
    dynamic_slice x1 -> x0, local copies, waits for them, and re-layouts: 1.16 us -> none  [suffix_pipeline(): lax.dynamic_slice_in_dim(stacked, length - 1 - index, n_chunks, axis=0)]
    broadcast_in_dim x0 -> x1, other arithmetic: none -> 1.15 us  [per_device(): return result[None]]
    ppermute x4 -> x12, waiting for transfers between devices: 37.6 us -> 36.6 us  [suffix_pipeline(): lax.ppermute(partial[k].astype(jnp.bfloat16), axis, [(sender, sender - 1)])]
  transfers between devices with their start and end apart: 11 -> 19, of which waited for: 7 -> 9; matrix products, arithmetic and copies ran while one was open for 3% -> 4% of each run, Pallas kernels for 0% -> 0%
where the time goes in v10:
time: 100 us; the launch traced here: 99.5 us
  waiting for transfers between devices  47.4 us (47%)
  starting transfers between devices  24.6 us (25%)
  other arithmetic  8.76 us (9%)
  Pallas kernels  6.26 us (6%)
  local copies, waits for them, and re-layouts  6.23 us (6%)
  matrix products  5.63 us (6%)
    ppermute x12, waiting for transfers between devices, suffix_pipeline(): lax.ppermute(partial[k].astype(jnp.bfloat16), axis, [(sender, sender - 1)])  36.6 us
    ppermute x6, starting transfers between devices, shifted(): return lax.ppermute(x, axis, perm)  13.5 us
    ppermute x12, starting transfers between devices, suffix_pipeline(): lax.ppermute(partial[k].astype(jnp.bfloat16), axis, [(sender, sender - 1)])  11.2 us
    ppermute x6, waiting for transfers between devices, shifted(): return lax.ppermute(x, axis, perm)  9.08 us
    pallas_call x1, Pallas kernels, attention_terms(): pl.pallas_call(kernel, out_shape=(jax.ShapeDtypeStruct((seq_rows, 2 * kv_...  6.26 us
    unnamed x42, local copies, waits for them, and re-layouts  4.75 us
    convert_element_type x3, other arithmetic, suffix_pipeline(): partial[k].astype(jnp.bfloat16)  4.09 us
    dot_general x1, matrix products, per_device(): jnp.dot(tokens, w_value[0], preferred_element_type=jnp.float32)  2.02 us
  transfers between devices with their start and end apart: 19, of which 9 were waited for; matrix products, arithmetic and copies ran while one was open for 4% of the time, Pallas kernels for 0%

profile of v10, /device:TPU:0, one launch (start us, length us, event | category | flops | bytes accessed | tf_op | source)
XLA Modules:
  0.0 99.5 jit_solution(1659073137511300937)
XLA Ops:
  0.0 1.7 %copy-done = bf16[1,5120,256]{2,1,0:T(8,128)(2,1)S(1)} copy-done((bf16[1,5120,256]{2,1,0:T(8,128)(2,1)S(1)}, bf16[1,5120,256]{2,1,0:T(8,128)(2,1)}, u32[]{:S(2)}) %copy-start) | copy-done | bytes 2621464
  1.7 2.0 %fusion.23 = bf16[128,256]{1,0:T(8,128)(2,1)S(1)} fusion(bf16[1,5120,256]{2,1,0:T(8,128)(2,1)S(1)} %copy-done, bf16[1,128,5120]{2,1,0:T(8,128)(2,1)} %param.6), kind=kOutput, calls=%fused_computation.38 | convolution fusion | flops 335577088 | bytes 3997696 | tf_op jit(solution)/shard_map/dot_general | solution.py:105
  3.8 0.0 copy-start.19
  3.8 0.5 fusion.18
  4.3 5.8 %collective-permute-start.2 = (bf16[128,512]{1,0:T(8,128)(2,1)S(1)}, bf16[128,512]{1,0:T(8,128)(2,1)S(1)}, u32[]{:S(2)}, u32[]{:S(2)}) collective-permute-start(bf16[128,512]{1,0:T(8,128)(2,1)S(1)} %pad_maximum_fusion.refs_2_), channel_id=1, source_target_pairs={{0,6},{1,7},{8,14},{9,15},{16,22},{17,23},{24,30},{25,31}} | collective-permute-start | bytes 393224 | tf_op jit(solution)/shard_map/ppermute | solution.py:18
  10.2 1.3 %collective-permute-start.1 = (bf16[128,512]{1,0:T(8,128)(2,1)S(1)}, bf16[128,512]{1,0:T(8,128)(2,1)S(1)}, u32[]{:S(2)}, u32[]{:S(2)}) collective-permute-start(bf16[128,512]{1,0:T(8,128)(2,1)S(1)} %pad_maximum_fusion.refs_2_), channel_id=1, source_target_pairs={{0,4},{2,6},{1,5},{3,7},{8,12},{10,14},{9,13},{11,15},{16,20},{18,... | collective-permute-start | bytes 393224 | tf_op jit(solution)/shard_map/ppermute | solution.py:18
  11.5 2.5 %collective-permute-start = (bf16[128,512]{1,0:T(8,128)(2,1)S(1)}, bf16[128,512]{1,0:T(8,128)(2,1)S(1)}, u32[]{:S(2)}, u32[]{:S(2)}) collective-permute-start(bf16[128,512]{1,0:T(8,128)(2,1)S(1)} %pad_maximum_fusion.refs_2_), channel_id=1, source_target_pairs={{0,2},{2,4},{4,6},{1,3},{3,5},{5,7},{8,10},{10,12},{12,14},{9,11},... | collective-permute-start | bytes 393224 | tf_op jit(solution)/shard_map/ppermute | solution.py:18
  14.0 0.1 fusion.70
  14.1 0.1 fusion.68
  14.1 0.2 copy.28
  14.4 0.2 copy.25
  14.6 0.1 copy.24
  14.7 0.9 broadcast_select_fusion
  15.6 0.0 collective-permute-done.2.refs_5_
  15.6 1.4 %collective-permute-done.1.refs_4_ = bf16[128,512]{1,0:T(8,128)(2,1)S(1)} collective-permute-done((bf16[128,512]{1,0:T(8,128)(2,1)S(1)}, bf16[128,512]{1,0:T(8,128)(2,1)S(1)}, u32[]{:S(2)}, u32[]{:S(2)}) %collective-permute-start.1) | collective-permute-done | bytes 131104 | tf_op jit(solution)/shard_map/ppermute | solution.py:18
  17.1 0.6 copy-done.17
  17.7 0.1 copy-done.18
  17.7 6.3 %shard_map.64 = (bf16[512,512]{1,0:T(8,128)(2,1)}, f32[128,512]{1,0:T(8,128)}) custom-call(bf16[10,128,128]{2,1,0:T(8,128)(2,1)} %bitcast.97, bf16[10,128,128]{2,1,0:T(8,128)(2,1)} %bitcast.98, bf16[128,512]{1,0:T(8,128)(2,1)} %copy-done.15, bf16[128,512]{1,0:T(8,128)(2,1)} %copy-done.18, bf16[128,512]{1,0:T(8,128)(2,1)} %copy-done.17, ...), custom_call_target="tpu_custom_call" | custom-call | tf_op jit(solution)/shard_map/pallas_call | solution.py:84
  24.0 1.1 %fusion.76 = (bf16[128,512]{1,0:T(8,128)(2,1)S(1)}, bf16[128,512]{1,0:T(8,128)(2,1)S(1)}, bf16[128,512]{1,0:T(8,128)(2,1)S(1)}) fusion(bf16[512,512]{1,0:T(8,128)(2,1)} %get-tuple-element.8), kind=kLoop, calls=%fused_computation.119 | loop fusion | bytes 786432 | tf_op jit(solution)/shard_map/slice | solution.py:133
  25.0 1.3 %collective-permute-start.3 = (bf16[128,512]{1,0:T(8,128)(2,1)S(1)}, bf16[128,512]{1,0:T(8,128)(2,1)S(1)}, u32[]{:S(2)}, u32[]{:S(2)}) collective-permute-start(bf16[128,512]{1,0:T(8,128)(2,1)S(1)} %get-tuple-element.46), channel_id=1, source_target_pairs={{2,0},{4,2},{6,4},{3,1},{5,3},{7,5},{10,8},{12,10},{14,12},{11,9},... | collective-permute-start | bytes 393224 | tf_op jit(solution)/shard_map/ppermute | solution.py:18
  26.3 1.3 %collective-permute-start.5 = (bf16[128,512]{1,0:T(8,128)(2,1)S(1)}, bf16[128,512]{1,0:T(8,128)(2,1)S(1)}, u32[]{:S(2)}, u32[]{:S(2)}) collective-permute-start(bf16[128,512]{1,0:T(8,128)(2,1)S(1)} %get-tuple-element.47), channel_id=1, source_target_pairs={{6,0},{7,1},{14,8},{15,9},{22,16},{23,17},{30,24},{31,25}} | collective-permute-start | bytes 393224 | tf_op jit(solution)/shard_map/ppermute | solution.py:18
  27.6 1.3 %collective-permute-start.4 = (bf16[128,512]{1,0:T(8,128)(2,1)S(1)}, bf16[128,512]{1,0:T(8,128)(2,1)S(1)}, u32[]{:S(2)}, u32[]{:S(2)}) collective-permute-start(bf16[128,512]{1,0:T(8,128)(2,1)S(1)} %get-tuple-element.48), channel_id=1, source_target_pairs={{4,0},{6,2},{5,1},{7,3},{12,8},{14,10},{13,9},{15,11},{20,16},{22,... | collective-permute-start | bytes 393224 | tf_op jit(solution)/shard_map/ppermute | solution.py:18
  29.0 3.0 %collective-permute-done.3 = bf16[128,512]{1,0:T(8,128)(2,1)S(1)} collective-permute-done((bf16[128,512]{1,0:T(8,128)(2,1)S(1)}, bf16[128,512]{1,0:T(8,128)(2,1)S(1)}, u32[]{:S(2)}, u32[]{:S(2)}) %collective-permute-start.3) | collective-permute-done | bytes 131104 | tf_op jit(solution)/shard_map/ppermute | solution.py:18
  31.9 3.4 %collective-permute-done.5 = bf16[128,512]{1,0:T(8,128)(2,1)S(1)} collective-permute-done((bf16[128,512]{1,0:T(8,128)(2,1)S(1)}, bf16[128,512]{1,0:T(8,128)(2,1)S(1)}, u32[]{:S(2)}, u32[]{:S(2)}) %collective-permute-start.5) | collective-permute-done | bytes 131104 | tf_op jit(solution)/shard_map/ppermute | solution.py:18
  35.3 1.3 %collective-permute-done.4 = bf16[128,512]{1,0:T(8,128)(2,1)S(1)} collective-permute-done((bf16[128,512]{1,0:T(8,128)(2,1)S(1)}, bf16[128,512]{1,0:T(8,128)(2,1)S(1)}, u32[]{:S(2)}, u32[]{:S(2)}) %collective-permute-start.4) | collective-permute-done | bytes 131104 | tf_op jit(solution)/shard_map/ppermute | solution.py:18
  36.6 1.0 %add_convert_fusion = bf16[128,512]{1,0:T(8,128)(2,1)S(1)} fusion(bf16[128,512]{1,0:T(8,128)(2,1)S(1)} %collective-permute-done.5, bf16[128,512]{1,0:T(8,128)(2,1)S(1)} %collective-permute-done.4, f32[128,512]{1,0:T(8,128)} %get-tuple-element.7, bf16[128,512]{1,0:T(8,128)(2,1)S(1)} %collective-permute-done.3), kind=kLoop, calls=%fused_computation.67 | loop fusion | flops 458752 | bytes 786432 | tf_op jit(solution)/shard_map/convert.1
  37.6 0.0 copy-start.3
  37.6 0.6 fusion.6
  38.2 1.2 %copy-done.3 = bf16[1,5120,256]{2,1,0:T(8,128)(2,1)S(1)} copy-done((bf16[1,5120,256]{2,1,0:T(8,128)(2,1)S(1)}, bf16[1,5120,256]{2,1,0:T(8,128)(2,1)}, u32[]{:S(2)}) %copy-start.3) | copy-done | bytes 2621464
  39.4 1.4 %fusion.1 = bf16[128,2560]{1,0:T(8,128)(2,1)} fusion(f32[128,2560]{1,0:T(8,128)S(1)} %fusion.6, bf16[1,5120,256]{2,1,0:T(8,128)(2,1)S(1)} %copy-done.3, s32[]{:T(128)S(6)} %select_n.31, bf16[128,512]{1,0:T(8,128)(2,1)S(1)} %add_convert_fusion), kind=kOutput, calls=%fused_computation.3 | convolution fusion | flops 168427520 | bytes 3342340 | tf_op jit(solution)/shard_map/dot_general | solution.py:146
  40.8 0.0 collective-permute-start.6
  40.8 0.6 fusion.9
  41.3 1.7 %collective-permute-done.6 = bf16[128,2560]{1,0:T(8,128)(2,1)S(1)} collective-permute-done((bf16[128,2560]{1,0:T(8,128)(2,1)}, bf16[128,2560]{1,0:T(8,128)(2,1)S(1)}, u32[]{:S(2)}, u32[]{:S(2)}) %collective-permute-start.6) | collective-permute-done | bytes 655392 | tf_op jit(solution)/shard_map/ppermute | solution.py:154
  43.1 0.6 fusion
  43.7 0.0 copy-start.1
  43.7 0.1 fusion.75
  43.8 0.7 collective-permute-start.7
  44.4 0.7 collective-permute-start.10
  45.1 0.7 collective-permute-start.13
  45.8 0.7 collective-permute-start.16
  46.5 0.0 collective-permute-done.10
  46.5 1.0 %fusion.44 = (bf16[32,2560]{1,0:T(8,128)(2,1)S(1)}, f32[1,32,2560]{2,1,0:T(8,128)}, f32[1,32,2560]{2,1,0:T(8,128)}, bf16[32,2560]{1,0:T(8,128)(2,1)S(1)}, f32[1,...) fusion(bf16[32,2560]{1,0:T(8,128)(2,1)S(1)} %collective-permute-done.7, f32[128,2560]{1,0:T(8,128)S(1)} %fusion, ...), kind=kLoop, calls=%fused_computation.77 | loop fusion | flops 737280 | bytes 2949120 | tf_op jit(solution)/shard_map/convert_element_type | solution.py:31
  47.5 0.7 collective-permute-start.8
  48.2 0.7 collective-permute-start.14
  48.9 0.7 collective-permute-start.11
  49.6 1.5 %fusion.46 = (bf16[32,2560]{1,0:T(8,128)(2,1)}, f32[1,32,2560]{2,1,0:T(8,128)}, f32[1,32,2560]{2,1,0:T(8,128)S(1)}, bf16[32,2560]{1,0:T(8,128)(2,1)}, f32[1,32,2...) fusion(bf16[32,2560]{1,0:T(8,128)(2,1)S(1)} %collective-permute, ...), kind=kLoop, calls=%fused_computation.79 | loop fusion | flops 983040 | bytes 5242880 | tf_op jit(solution)/shard_map/convert_element_type | solution.py:31
  51.1 1.3 %collective-permute-start.9 = (bf16[32,2560]{1,0:T(8,128)(2,1)}, bf16[32,2560]{1,0:T(8,128)(2,1)}, u32[]{:S(2)}, u32[]{:S(2)}) collective-permute-start(bf16[32,2560]{1,0:T(8,128)(2,1)} %get-tuple-element.9), channel_id=1, source_target_pairs={{8,0},{9,1},{10,2},{11,3},{12,4},{13,5},{14,6},{15,7}} | collective-permute-start | bytes 491528 | tf_op jit(solution)/shard_map/ppermute | solution.py:31
  52.4 1.3 %collective-permute-start.17 = (bf16[32,2560]{1,0:T(8,128)(2,1)}, bf16[32,2560]{1,0:T(8,128)(2,1)}, u32[]{:S(2)}, u32[]{:S(2)}) collective-permute-start(bf16[32,2560]{1,0:T(8,128)(2,1)} %get-tuple-element.27), channel_id=1, source_target_pairs={{16,8},{17,9},{18,10},{19,11},{20,12},{21,13},{22,14},{23,15}} | collective-permute-start | bytes 491528 | tf_op jit(solution)/shard_map/ppermute | solution.py:31
  53.7 1.3 %collective-permute-start.15 = (bf16[32,2560]{1,0:T(8,128)(2,1)}, bf16[32,2560]{1,0:T(8,128)(2,1)}, u32[]{:S(2)}, u32[]{:S(2)}) collective-permute-start(bf16[32,2560]{1,0:T(8,128)(2,1)} %get-tuple-element.29), channel_id=1, source_target_pairs={{8,0},{9,1},{10,2},{11,3},{12,4},{13,5},{14,6},{15,7}} | collective-permute-start | bytes 491528 | tf_op jit(solution)/shard_map/ppermute | solution.py:31
  55.0 1.3 %collective-permute-start.12 = (bf16[32,2560]{1,0:T(8,128)(2,1)S(1)}, bf16[32,2560]{1,0:T(8,128)(2,1)}, u32[]{:S(2)}, u32[]{:S(2)}) collective-permute-start(bf16[32,2560]{1,0:T(8,128)(2,1)S(1)} %get-tuple-element.31), channel_id=1, source_target_pairs={{8,0},{9,1},{10,2},{11,3},{12,4},{13,5},{14,6},{15,7}} | collective-permute-start | bytes 491528 | tf_op jit(solution)/shard_map/ppermute | solution.py:31
  56.4 26.4 %collective-permute-done.9 = bf16[32,2560]{1,0:T(8,128)(2,1)} collective-permute-done((bf16[32,2560]{1,0:T(8,128)(2,1)}, bf16[32,2560]{1,0:T(8,128)(2,1)}, u32[]{:S(2)}, u32[]{:S(2)}) %collective-permute-start.9) | collective-permute-done | bytes 163872 | tf_op jit(solution)/shard_map/ppermute | solution.py:31
  82.7 3.6 %collective-permute-done.15 = bf16[32,2560]{1,0:T(8,128)(2,1)} collective-permute-done((bf16[32,2560]{1,0:T(8,128)(2,1)}, bf16[32,2560]{1,0:T(8,128)(2,1)}, u32[]{:S(2)}, u32[]{:S(2)}) %collective-permute-start.15) | collective-permute-done | bytes 163872 | tf_op jit(solution)/shard_map/ppermute | solution.py:31
  86.4 2.0 %collective-permute-done.12 = bf16[32,2560]{1,0:T(8,128)(2,1)} collective-permute-done((bf16[32,2560]{1,0:T(8,128)(2,1)S(1)}, bf16[32,2560]{1,0:T(8,128)(2,1)}, u32[]{:S(2)}, u32[]{:S(2)}) %collective-permute-start.12) | collective-permute-done | bytes 163872 | tf_op jit(solution)/shard_map/ppermute | solution.py:31
  88.4 1.6 %fusion.58 = (bf16[32,2560]{1,0:T(8,128)(2,1)S(1)}, f32[1,32,2560]{2,1,0:T(8,128)S(1)}, f32[1,32,2560]{2,1,0:T(8,128)S(1)}, f32[1,32,2560]{2,1,0:T(8,128)S(1)}, f32[1,32,2560]{2,1,0:T(8,128)S(1)}) fusion(bf16[32,2560]{1,0:T(8,128)(2,1)} %collective-permute-done.17, f32[128,2560]{1,0:T(8,128)} %copy-done.1, bf16[32,2560]{1,0:T(8,128)(2,1)} %collective-permute-done.9, ...), kind=kLoop, calls=%fused_computation.91 | loop fusion | flops 737280 | bytes 3440640 | tf_op jit(solution)/shard_map/convert_element_type | solution.py:31
  90.0 1.3 %collective-permute-start.18 = (bf16[32,2560]{1,0:T(8,128)(2,1)S(1)}, bf16[32,2560]{1,0:T(8,128)(2,1)S(1)}, u32[]{:S(2)}, u32[]{:S(2)}) collective-permute-start(bf16[32,2560]{1,0:T(8,128)(2,1)S(1)} %get-tuple-element.21), channel_id=1, source_target_pairs={{8,0},{9,1},{10,2},{11,3},{12,4},{13,5},{14,6},{15,7}} | collective-permute-start | bytes 491528 | tf_op jit(solution)/shard_map/ppermute | solution.py:31
  91.4 0.2 fusion.35
  91.6 0.7 copy-done.6
  92.3 0.1 copy-done.7
  92.4 0.1 copy-done.12
  92.5 0.1 fusion.43
  92.6 4.6 %collective-permute-done.18 = bf16[32,2560]{1,0:T(8,128)(2,1)S(1)} collective-permute-done((bf16[32,2560]{1,0:T(8,128)(2,1)S(1)}, bf16[32,2560]{1,0:T(8,128)(2,1)S(1)}, u32[]{:S(2)}, u32[]{:S(2)}) %collective-permute-start.18) | collective-permute-done | bytes 163872 | tf_op jit(solution)/shard_map/ppermute | solution.py:31
  97.2 1.0 %add_bitcast_fusion = f32[1,32,2560]{2,1,0:T(8,128)S(1)} fusion(bf16[32,2560]{1,0:T(8,128)(2,1)S(1)} %collective-permute-done.18, f32[128,2560]{1,0:T(8,128)} %copy-done.1), kind=kLoop, calls=%fused_computation.55 | loop fusion | flops 163840 | bytes 819200 | tf_op jit(solution)/shard_map/stack | solution.py:35
  98.2 0.1 fusion.31
  98.3 1.1 %maximum_bitcast_fusion = f32[1,128,2560]{2,1,0:T(8,128)} fusion(f32[32,2560]{1,0:T(8,128)S(1)} %fusion.31, f32[32,2560]{1,0:T(8,128)S(1)} %get-tuple-element.55, f32[32,2560]{1,0:T(8,128)S(1)} %get-tuple-element.56, f32[32,2560]{1,0:T(8,128)S(1)} %fusion.43), kind=kLoop, calls=%fused_computation.24 | loop fusion | flops 983040 | bytes 2621440 | tf_op jit(solution)/shard_map/broadcast_in_dim | solution.py:159
  (43 shorter events, 0.1 us)
Async XLA Ops:
  0.0 1.7 %copy-start = (bf16[1,5120,256]{2,1,0:T(8,128)(2,1)S(1)}, bf16[1,5120,256]{2,1,0:T(8,128)(2,1)}, u32[]{:S(2)}) copy-start(bf16[1,5120,256]{2,1,0:T(8,128)(2,1)} %param.10) | copy-start | bytes 7864324
  0.0 3.8 %copy-start.5 = (bf16[1,128,5120]{2,1,0:T(8,128)(2,1)S(1)}, bf16[1,128,5120]{2,1,0:T(8,128)(2,1)}, u32[]{:S(2)}) copy-start(bf16[1,128,5120]{2,1,0:T(8,128)(2,1)} %param.6) | copy-start | bytes 3932164
  0.0 3.8 %copy-start.2 = (bf16[1,5120,256]{2,1,0:T(8,128)(2,1)S(1)}, bf16[1,5120,256]{2,1,0:T(8,128)(2,1)}, u32[]{:S(2)}) copy-start(bf16[1,5120,256]{2,1,0:T(8,128)(2,1)} %param.9) | copy-start | bytes 7864324
  3.8 10.6 %copy-start.19 = (s32[512]{0:T(512)S(1)}, s32[512]{0:T(512)}, u32[]{:S(2)}) copy-start(s32[512]{0:T(512)} %param.11) | copy-start | bytes 6148
  4.3 12.7 %copy-start.15 = (bf16[128,512]{1,0:T(8,128)(2,1)}, bf16[128,512]{1,0:T(8,128)(2,1)S(1)}, u32[]{:S(2)}) copy-start(bf16[128,512]{1,0:T(8,128)(2,1)S(1)} %pad_maximum_fusion.refs_2_) | copy-start | bytes 393220
  4.3 11.3 %collective-permute-start.2 = (bf16[128,512]{1,0:T(8,128)(2,1)S(1)}, bf16[128,512]{1,0:T(8,128)(2,1)S(1)}, u32[]{:S(2)}, u32[]{:S(2)}) collective-permute-start(bf16[128,512]{1,0:T(8,128)(2,1)S(1)} %pad_maximum_fusion.refs_2_), channel_id=1, source_target_pairs={{0,6},{1,7},{8,14},{9,15},{16,22},{17,23},{24,30},{25,31}} | collective-permute-start | bytes 393224 | tf_op jit(solution)/shard_map/ppermute | solution.py:18
  10.2 6.8 %collective-permute-start.1 = (bf16[128,512]{1,0:T(8,128)(2,1)S(1)}, bf16[128,512]{1,0:T(8,128)(2,1)S(1)}, u32[]{:S(2)}, u32[]{:S(2)}) collective-permute-start(bf16[128,512]{1,0:T(8,128)(2,1)S(1)} %pad_maximum_fusion.refs_2_), channel_id=1, source_target_pairs={{0,4},{2,6},{1,5},{3,7},{8,12},{10,14},{9,13},{11,15},{16,20},{18,... | collective-permute-start | bytes 393224 | tf_op jit(solution)/shard_map/ppermute | solution.py:18
  11.5 5.5 %collective-permute-start = (bf16[128,512]{1,0:T(8,128)(2,1)S(1)}, bf16[128,512]{1,0:T(8,128)(2,1)S(1)}, u32[]{:S(2)}, u32[]{:S(2)}) collective-permute-start(bf16[128,512]{1,0:T(8,128)(2,1)S(1)} %pad_maximum_fusion.refs_2_), channel_id=1, source_target_pairs={{0,2},{2,4},{4,6},{1,3},{3,5},{5,7},{8,10},{10,12},{12,14},{9,11},... | collective-permute-start | bytes 393224 | tf_op jit(solution)/shard_map/ppermute | solution.py:18
  15.6 1.4 %copy-start.16 = (bf16[128,512]{1,0:T(8,128)(2,1)}, bf16[128,512]{1,0:T(8,128)(2,1)S(1)}, u32[]{:S(2)}) copy-start(bf16[128,512]{1,0:T(8,128)(2,1)S(1)} %collective-permute-done.2.refs_5_) | copy-start | bytes 393220
  17.0 0.6 copy-start.17
  17.0 0.7 copy-start.18
  25.0 6.9 %collective-permute-start.3 = (bf16[128,512]{1,0:T(8,128)(2,1)S(1)}, bf16[128,512]{1,0:T(8,128)(2,1)S(1)}, u32[]{:S(2)}, u32[]{:S(2)}) collective-permute-start(bf16[128,512]{1,0:T(8,128)(2,1)S(1)} %get-tuple-element.46), channel_id=1, source_target_pairs={{2,0},{4,2},{6,4},{3,1},{5,3},{7,5},{10,8},{12,10},{14,12},{11,9},... | collective-permute-start | bytes 393224 | tf_op jit(solution)/shard_map/ppermute | solution.py:18
  26.3 9.0 %collective-permute-start.5 = (bf16[128,512]{1,0:T(8,128)(2,1)S(1)}, bf16[128,512]{1,0:T(8,128)(2,1)S(1)}, u32[]{:S(2)}, u32[]{:S(2)}) collective-permute-start(bf16[128,512]{1,0:T(8,128)(2,1)S(1)} %get-tuple-element.47), channel_id=1, source_target_pairs={{6,0},{7,1},{14,8},{15,9},{22,16},{23,17},{30,24},{31,25}} | collective-permute-start | bytes 393224 | tf_op jit(solution)/shard_map/ppermute | solution.py:18
  27.6 9.0 %collective-permute-start.4 = (bf16[128,512]{1,0:T(8,128)(2,1)S(1)}, bf16[128,512]{1,0:T(8,128)(2,1)S(1)}, u32[]{:S(2)}, u32[]{:S(2)}) collective-permute-start(bf16[128,512]{1,0:T(8,128)(2,1)S(1)} %get-tuple-element.48), channel_id=1, source_target_pairs={{4,0},{6,2},{5,1},{7,3},{12,8},{14,10},{13,9},{15,11},{20,16},{22,... | collective-permute-start | bytes 393224 | tf_op jit(solution)/shard_map/ppermute | solution.py:18
  37.6 1.7 %copy-start.3 = (bf16[1,5120,256]{2,1,0:T(8,128)(2,1)S(1)}, bf16[1,5120,256]{2,1,0:T(8,128)(2,1)}, u32[]{:S(2)}) copy-start(bf16[1,5120,256]{2,1,0:T(8,128)(2,1)} %param.9) | copy-start | bytes 7864324
  40.8 2.3 %collective-permute-start.6 = (bf16[128,2560]{1,0:T(8,128)(2,1)}, bf16[128,2560]{1,0:T(8,128)(2,1)S(1)}, u32[]{:S(2)}, u32[]{:S(2)}) collective-permute-start(bf16[128,2560]{1,0:T(8,128)(2,1)} %fusion.1), channel_id=1, source_target_pairs={{0,1},{1,0},{2,3},{3,2},{4,5},{5,4},{6,7},{7,6},{8,9},{9,8},{10,11... | collective-permute-start | bytes 1966088 | tf_op jit(solution)/shard_map/ppermute | solution.py:154
  40.8 2.3 %copy-start.4 = (bf16[1,5120,256]{2,1,0:T(8,128)(2,1)S(1)}, bf16[1,5120,256]{2,1,0:T(8,128)(2,1)}, u32[]{:S(2)}) copy-start(bf16[1,5120,256]{2,1,0:T(8,128)(2,1)} %param.9) | copy-start | bytes 7864324
  43.7 5.9 %copy-start.1 = (f32[128,2560]{1,0:T(8,128)}, f32[128,2560]{1,0:T(8,128)S(1)}, u32[]{:S(2)}) copy-start(f32[128,2560]{1,0:T(8,128)S(1)} %fusion) | copy-start | bytes 3932164
  43.8 2.7 %collective-permute-start.7 = (bf16[32,2560]{1,0:T(8,128)(2,1)S(1)}, bf16[32,2560]{1,0:T(8,128)(2,1)S(1)}, u32[]{:S(2)}, u32[]{:S(2)}) collective-permute-start(bf16[32,2560]{1,0:T(8,128)(2,1)S(1)} %get-tuple-element.40), channel_id=1, source_target_pairs={{24,16},{25,17},{26,18},{27,19},{28,20},{29,21},{30,22},{31,23}} | collective-permute-start | bytes 491528 | tf_op jit(solution)/shard_map/ppermute | solution.py:31
  44.4 2.0 %collective-permute-start.10 = (bf16[32,2560]{1,0:T(8,128)(2,1)S(1)}, bf16[32,2560]{1,0:T(8,128)(2,1)S(1)}, u32[]{:S(2)}, u32[]{:S(2)}) collective-permute-start(bf16[32,2560]{1,0:T(8,128)(2,1)S(1)} %get-tuple-element.41), channel_id=1, source_target_pairs={{24,16},{25,17},{26,18},{27,19},{28,20},{29,21},{30,22},{31,23}} | collective-permute-start | bytes 491528 | tf_op jit(solution)/shard_map/ppermute | solution.py:31
  45.1 1.4 %collective-permute-start.13 = (bf16[32,2560]{1,0:T(8,128)(2,1)S(1)}, bf16[32,2560]{1,0:T(8,128)(2,1)S(1)}, u32[]{:S(2)}, u32[]{:S(2)}) collective-permute-start(bf16[32,2560]{1,0:T(8,128)(2,1)S(1)} %get-tuple-element.42), channel_id=1, source_target_pairs={{24,16},{25,17},{26,18},{27,19},{28,20},{29,21},{30,22},{31,23}} | collective-permute-start | bytes 491528 | tf_op jit(solution)/shard_map/ppermute | solution.py:31
  45.8 3.8 %collective-permute-start.16 = (bf16[32,2560]{1,0:T(8,128)(2,1)S(1)}, bf16[32,2560]{1,0:T(8,128)(2,1)S(1)}, u32[]{:S(2)}, u32[]{:S(2)}) collective-permute-start(bf16[32,2560]{1,0:T(8,128)(2,1)S(1)} %get-tuple-element.43), channel_id=1, source_target_pairs={{24,16},{25,17},{26,18},{27,19},{28,20},{29,21},{30,22},{31,23}} | collective-permute-start | bytes 491528 | tf_op jit(solution)/shard_map/ppermute | solution.py:31
  47.5 2.0 %collective-permute-start.8 = (bf16[32,2560]{1,0:T(8,128)(2,1)S(1)}, bf16[32,2560]{1,0:T(8,128)(2,1)S(1)}, u32[]{:S(2)}, u32[]{:S(2)}) collective-permute-start(bf16[32,2560]{1,0:T(8,128)(2,1)S(1)} %get-tuple-element.11), channel_id=1, source_target_pairs={{16,8},{17,9},{18,10},{19,11},{20,12},{21,13},{22,14},{23,15}} | collective-permute-start | bytes 491528 | tf_op jit(solution)/shard_map/ppermute | solution.py:31
  48.2 1.4 %collective-permute-start.14 = (bf16[32,2560]{1,0:T(8,128)(2,1)S(1)}, bf16[32,2560]{1,0:T(8,128)(2,1)S(1)}, u32[]{:S(2)}, u32[]{:S(2)}) collective-permute-start(bf16[32,2560]{1,0:T(8,128)(2,1)S(1)} %get-tuple-element.37), channel_id=1, source_target_pairs={{16,8},{17,9},{18,10},{19,11},{20,12},{21,13},{22,14},{23,15}} | collective-permute-start | bytes 491528 | tf_op jit(solution)/shard_map/ppermute | solution.py:31
  48.9 0.7 collective-permute-start.11
  51.1 31.6 %collective-permute-start.9 = (bf16[32,2560]{1,0:T(8,128)(2,1)}, bf16[32,2560]{1,0:T(8,128)(2,1)}, u32[]{:S(2)}, u32[]{:S(2)}) collective-permute-start(bf16[32,2560]{1,0:T(8,128)(2,1)} %get-tuple-element.9), channel_id=1, source_target_pairs={{8,0},{9,1},{10,2},{11,3},{12,4},{13,5},{14,6},{15,7}} | collective-permute-start | bytes 491528 | tf_op jit(solution)/shard_map/ppermute | solution.py:31
  52.4 30.3 %collective-permute-start.17 = (bf16[32,2560]{1,0:T(8,128)(2,1)}, bf16[32,2560]{1,0:T(8,128)(2,1)}, u32[]{:S(2)}, u32[]{:S(2)}) collective-permute-start(bf16[32,2560]{1,0:T(8,128)(2,1)} %get-tuple-element.27), channel_id=1, source_target_pairs={{16,8},{17,9},{18,10},{19,11},{20,12},{21,13},{22,14},{23,15}} | collective-permute-start | bytes 491528 | tf_op jit(solution)/shard_map/ppermute | solution.py:31
  53.7 32.7 %collective-permute-start.15 = (bf16[32,2560]{1,0:T(8,128)(2,1)}, bf16[32,2560]{1,0:T(8,128)(2,1)}, u32[]{:S(2)}, u32[]{:S(2)}) collective-permute-start(bf16[32,2560]{1,0:T(8,128)(2,1)} %get-tuple-element.29), channel_id=1, source_target_pairs={{8,0},{9,1},{10,2},{11,3},{12,4},{13,5},{14,6},{15,7}} | collective-permute-start | bytes 491528 | tf_op jit(solution)/shard_map/ppermute | solution.py:31
  55.0 33.4 %collective-permute-start.12 = (bf16[32,2560]{1,0:T(8,128)(2,1)S(1)}, bf16[32,2560]{1,0:T(8,128)(2,1)}, u32[]{:S(2)}, u32[]{:S(2)}) collective-permute-start(bf16[32,2560]{1,0:T(8,128)(2,1)S(1)} %get-tuple-element.31), channel_id=1, source_target_pairs={{8,0},{9,1},{10,2},{11,3},{12,4},{13,5},{14,6},{15,7}} | collective-permute-start | bytes 491528 | tf_op jit(solution)/shard_map/ppermute | solution.py:31
  56.3 35.0 %copy-start.8 = (f32[1,32,2560]{2,1,0:T(8,128)S(1)}, f32[1,32,2560]{2,1,0:T(8,128)}, u32[]{:S(2)}) copy-start(f32[1,32,2560]{2,1,0:T(8,128)} %get-tuple-element.28) | copy-start | bytes 983044
  56.3 35.0 %copy-start.9 = (f32[1,32,2560]{2,1,0:T(8,128)S(1)}, f32[1,32,2560]{2,1,0:T(8,128)}, u32[]{:S(2)}) copy-start(f32[1,32,2560]{2,1,0:T(8,128)} %get-tuple-element.30) | copy-start | bytes 983044
  56.3 35.0 %copy-start.10 = (f32[1,32,2560]{2,1,0:T(8,128)S(1)}, f32[1,32,2560]{2,1,0:T(8,128)}, u32[]{:S(2)}) copy-start(f32[1,32,2560]{2,1,0:T(8,128)} %get-tuple-element.33) | copy-start | bytes 983044
  56.3 35.0 %copy-start.11 = (f32[1,32,2560]{2,1,0:T(8,128)S(1)}, f32[1,32,2560]{2,1,0:T(8,128)}, u32[]{:S(2)}) copy-start(f32[1,32,2560]{2,1,0:T(8,128)} %get-tuple-element.34) | copy-start | bytes 983044
  56.3 35.0 %copy-start.13 = (f32[1,32,2560]{2,1,0:T(8,128)S(1)}, f32[1,32,2560]{2,1,0:T(8,128)}, u32[]{:S(2)}) copy-start(f32[1,32,2560]{2,1,0:T(8,128)} %get-tuple-element.36) | copy-start | bytes 983044
  56.3 35.0 %copy-start.14 = (f32[1,32,2560]{2,1,0:T(8,128)S(1)}, f32[1,32,2560]{2,1,0:T(8,128)}, u32[]{:S(2)}) copy-start(f32[1,32,2560]{2,1,0:T(8,128)} %get-tuple-element.38) | copy-start | bytes 983044
  90.0 7.2 %collective-permute-start.18 = (bf16[32,2560]{1,0:T(8,128)(2,1)S(1)}, bf16[32,2560]{1,0:T(8,128)(2,1)S(1)}, u32[]{:S(2)}, u32[]{:S(2)}) collective-permute-start(bf16[32,2560]{1,0:T(8,128)(2,1)S(1)} %get-tuple-element.21), channel_id=1, source_target_pairs={{8,0},{9,1},{10,2},{11,3},{12,4},{13,5},{14,6},{15,7}} | collective-permute-start | bytes 491528 | tf_op jit(solution)/shard_map/ppermute | solution.py:31
  91.4 1.0 copy-start.6
  91.4 1.1 %copy-start.7 = (f32[1,32,2560]{2,1,0:T(8,128)S(1)}, f32[1,32,2560]{2,1,0:T(8,128)}, u32[]{:S(2)}) copy-start(f32[1,32,2560]{2,1,0:T(8,128)} %get-tuple-element.35) | copy-start | bytes 983044
  91.4 1.2 %copy-start.12 = (f32[1,32,2560]{2,1,0:T(8,128)S(1)}, f32[1,32,2560]{2,1,0:T(8,128)}, u32[]{:S(2)}) copy-start(f32[1,32,2560]{2,1,0:T(8,128)} %get-tuple-element.12) | copy-start | bytes 983044

commit v11 on v6

--- a/solution.py
+++ b/solution.py
@@ -68,9 +68,9 @@
                 s = lax.dot_general(key, q, nt, preferred_element_type=jnp.float32) * scaling
                 masked = jnp.where(allowed, s, -1e30)
                 top = jnp.max(masked, axis=0, keepdims=True)
-                tot = jnp.sum(jnp.where(allowed, jnp.exp(masked - top), 0.0), axis=0, keepdims=True)
-                log_total = top + jnp.log(tot)
-                p = jnp.where(allowed, jnp.exp(masked - log_total), 0.0)
+                e = jnp.where(allowed, jnp.exp(masked - top), 0.0)
+                tot = jnp.sum(e, axis=0, keepdims=True)
+                p = e * (1.0 / tot)
                 pb = p.astype(jnp.bfloat16)
                 dp = lax.dot_general(val, gr, nt, preferred_element_type=jnp.float32)
                 rd = jnp.sum(pb.astype(jnp.float32) * dp, axis=0, keepdims=True)
@@ -108,7 +108,8 @@
         jnp.bfloat16
     )
     kv_own = jnp.concatenate((key_rows, value_rows), axis=1)
-    blocks = [kv_own] + [shifted(kv_own, "ctx", d, ctx_len, True) for d in range(1, ctx_len)]
+    later = {d: shifted(kv_own, "ctx", d, ctx_len, True) for d in range(ctx_len - 1, 0, -1)}
+    blocks = [kv_own] + [later[d] for d in range(1, ctx_len)]
     seq_rows = tok_rows * ctx_len
     first_row = ctx_index * tok_rows
     blk = jnp.arange(ctx_len, dtype=jnp.int32)

time: 84.6 us -> 84.2 us (level)
  no operation moved by 1% of the time
where the time goes in v11:
time: 84.2 us; the launch traced here: 83.8 us
  waiting for transfers between devices  44.3 us (53%)
  starting transfers between devices  18.6 us (22%)
  Pallas kernels  5.89 us (7%)
  matrix products  5.64 us (7%)
  local copies, waits for them, and re-layouts  5.46 us (6%)
  other arithmetic  3.6 us (4%)
    ppermute x4, waiting for transfers between devices, suffix_pipeline(): recv = lax.ppermute(acc.astype(jnp.bfloat16), axis, perm)  35.9 us
    ppermute x6, starting transfers between devices, shifted(): return lax.ppermute(x, axis, perm)  13.5 us
    ppermute x6, waiting for transfers between devices, shifted(): return lax.ppermute(x, axis, perm)  6.62 us
    pallas_call x1, Pallas kernels, attention_terms(): pl.pallas_call(kernel, out_shape=(jax.ShapeDtypeStruct((seq_rows, 2 * kv_...  5.89 us
    ppermute x4, starting transfers between devices, suffix_pipeline(): recv = lax.ppermute(acc.astype(jnp.bfloat16), axis, perm)  5.17 us
    unnamed x23, local copies, waits for them, and re-layouts  2.65 us
    dot_general x1, matrix products, per_device(): jnp.dot(tokens, w_value[0], preferred_element_type=jnp.float32)  2.02 us
    dot_general x2, matrix products, partial_for(): lax.dot_general(grad_key, wk, contract, preferred_element_type=jnp.float32)  1.99 us
  transfers between devices with their start and end apart: 11, of which 9 were waited for; matrix products, arithmetic and copies ran while one was open for 3% of the time, Pallas kernels for 0%

profile of v11, /device:TPU:0, one launch (start us, length us, event | category | flops | bytes accessed | tf_op | source)
XLA Modules:
  0.0 83.8 jit_solution(2518447540799030902)
XLA Ops:
  0.0 0.0 copy-start
  0.0 0.0 copy-start.4
  0.0 0.0 copy-start.1
  0.0 1.7 %copy-done = bf16[1,5120,256]{2,1,0:T(8,128)(2,1)S(1)} copy-done((bf16[1,5120,256]{2,1,0:T(8,128)(2,1)S(1)}, bf16[1,5120,256]{2,1,0:T(8,128)(2,1)}, u32[]{:S(2)}) %copy-start) | copy-done | bytes 2621464
  1.7 2.0 %fusion.25 = bf16[128,256]{1,0:T(8,128)(2,1)S(1)} fusion(bf16[1,5120,256]{2,1,0:T(8,128)(2,1)S(1)} %copy-done, bf16[1,128,5120]{2,1,0:T(8,128)(2,1)} %param.6), kind=kOutput, calls=%fused_computation.26 | convolution fusion | flops 335577088 | bytes 3997696 | tf_op jit(solution)/shard_map/dot_general | solution.py:107
  3.8 0.0 copy-done.4
  3.8 0.0 copy-done.1
  3.8 0.0 copy-start.9
  3.8 0.5 fusion.20
  4.3 0.0 copy-start.5
  4.3 4.9 %collective-permute-start = (bf16[128,512]{1,0:T(8,128)(2,1)S(1)}, bf16[128,512]{1,0:T(8,128)(2,1)S(1)}, u32[]{:S(2)}, u32[]{:S(2)}) collective-permute-start(bf16[128,512]{1,0:T(8,128)(2,1)S(1)} %pad_maximum_fusion.refs_2_), channel_id=1, source_target_pairs={{0,2},{2,4},{4,6},{1,3},{3,5},{5,7},{8,10},{10,12},{12,14},{9,11},... | collective-permute-start | bytes 393224 | tf_op jit(solution)/shard_map/ppermute | solution.py:18
  9.2 3.4 %collective-permute-start.1 = (bf16[128,512]{1,0:T(8,128)(2,1)S(1)}, bf16[128,512]{1,0:T(8,128)(2,1)S(1)}, u32[]{:S(2)}, u32[]{:S(2)}) collective-permute-start(bf16[128,512]{1,0:T(8,128)(2,1)S(1)} %pad_maximum_fusion.refs_2_), channel_id=1, source_target_pairs={{0,4},{2,6},{1,5},{3,7},{8,12},{10,14},{9,13},{11,15},{16,20},{18,... | collective-permute-start | bytes 393224 | tf_op jit(solution)/shard_map/ppermute | solution.py:18
  12.7 1.3 %collective-permute-start.2 = (bf16[128,512]{1,0:T(8,128)(2,1)S(1)}, bf16[128,512]{1,0:T(8,128)(2,1)S(1)}, u32[]{:S(2)}, u32[]{:S(2)}) collective-permute-start(bf16[128,512]{1,0:T(8,128)(2,1)S(1)} %pad_maximum_fusion.refs_2_), channel_id=1, source_target_pairs={{0,6},{1,7},{8,14},{9,15},{16,22},{17,23},{24,30},{25,31}} | collective-permute-start | bytes 393224 | tf_op jit(solution)/shard_map/ppermute | solution.py:18
  14.0 0.0 copy-done.9
  14.0 0.2 copy.25
  14.2 0.1 fusion.50
  14.3 0.1 fusion.48
  14.4 0.2 copy.24
  14.6 0.2 copy.28
  14.8 0.9 %broadcast_select_fusion = (s32[512,1]{1,0:T(8,128)}, s32[512,1]{1,0:T(8,128)}) fusion(pred[512,1]{1,0:T(8,128)(4,1)S(1)} %copy.25, s32[512,1]{1,0:T(8,128)S(1)} %copy.24, pred[1,512]{0,1:T(8,128)(4,1)S(1)} %copy.28), kind=kLoop, calls=%fused_computation.49 | loop fusion | flops 1024 | bytes 7168 | tf_op jit(solution)/shard_map/jit(_where)/select_n | solution.py:129
  15.6 0.0 collective-permute-done.refs_3_
  15.6 0.0 copy-start.6
  15.6 0.1 collective-permute-done.1.refs_4_
  15.7 0.8 collective-permute-done.2.refs_5_
  16.5 0.0 copy-done.5
  16.5 0.0 copy-done.6
  16.5 0.0 copy-done.7
  16.5 0.6 copy-done.8
  17.1 5.9 %shard_map.64 = (bf16[512,512]{1,0:T(8,128)(2,1)}, f32[128,512]{1,0:T(8,128)}) custom-call(bf16[10,128,128]{2,1,0:T(8,128)(2,1)} %bitcast.102, bf16[10,128,128]{2,1,0:T(8,128)(2,1)} %bitcast.103, bf16[128,512]{1,0:T(8,128)(2,1)} %copy-done.5, bf16[128,512]{1,0:T(8,128)(2,1)} %copy-done.6, bf16[128,512]{1,0:T(8,128)(2,1)} %copy-done.7, ...), custom_call_target="tpu_custom_call" | custom-call | tf_op jit(solution)/shard_map/pallas_call | solution.py:86
  23.0 1.1 %fusion.55 = (bf16[128,512]{1,0:T(8,128)(2,1)S(1)}, bf16[128,512]{1,0:T(8,128)(2,1)S(1)}, bf16[128,512]{1,0:T(8,128)(2,1)S(1)}) fusion(bf16[512,512]{1,0:T(8,128)(2,1)} %get-tuple-element.8), kind=kLoop, calls=%fused_computation.74 | loop fusion | bytes 786432 | tf_op jit(solution)/shard_map/slice | solution.py:136
  24.1 1.3 %collective-permute-start.5 = (bf16[128,512]{1,0:T(8,128)(2,1)S(1)}, bf16[128,512]{1,0:T(8,128)(2,1)S(1)}, u32[]{:S(2)}, u32[]{:S(2)}) collective-permute-start(bf16[128,512]{1,0:T(8,128)(2,1)S(1)} %get-tuple-element.10), channel_id=1, source_target_pairs={{6,0},{7,1},{14,8},{15,9},{22,16},{23,17},{30,24},{31,25}} | collective-permute-start | bytes 393224 | tf_op jit(solution)/shard_map/ppermute | solution.py:18
  25.4 1.3 %collective-permute-start.4 = (bf16[128,512]{1,0:T(8,128)(2,1)S(1)}, bf16[128,512]{1,0:T(8,128)(2,1)S(1)}, u32[]{:S(2)}, u32[]{:S(2)}) collective-permute-start(bf16[128,512]{1,0:T(8,128)(2,1)S(1)} %get-tuple-element.11), channel_id=1, source_target_pairs={{4,0},{6,2},{5,1},{7,3},{12,8},{14,10},{13,9},{15,11},{20,16},{22,... | collective-permute-start | bytes 393224 | tf_op jit(solution)/shard_map/ppermute | solution.py:18
  26.7 1.3 %collective-permute-start.3 = (bf16[128,512]{1,0:T(8,128)(2,1)S(1)}, bf16[128,512]{1,0:T(8,128)(2,1)S(1)}, u32[]{:S(2)}, u32[]{:S(2)}) collective-permute-start(bf16[128,512]{1,0:T(8,128)(2,1)S(1)} %get-tuple-element.9), channel_id=1, source_target_pairs={{2,0},{4,2},{6,4},{3,1},{5,3},{7,5},{10,8},{12,10},{14,12},{11,9},... | collective-permute-start | bytes 393224 | tf_op jit(solution)/shard_map/ppermute | solution.py:18
  28.0 0.0 copy-start.2
  28.0 4.1 %collective-permute-done.5 = bf16[128,512]{1,0:T(8,128)(2,1)S(1)} collective-permute-done((bf16[128,512]{1,0:T(8,128)(2,1)S(1)}, bf16[128,512]{1,0:T(8,128)(2,1)S(1)}, u32[]{:S(2)}, u32[]{:S(2)}) %collective-permute-start.5) | collective-permute-done | bytes 131104 | tf_op jit(solution)/shard_map/ppermute | solution.py:18
  32.1 1.7 %collective-permute-done.4 = bf16[128,512]{1,0:T(8,128)(2,1)S(1)} collective-permute-done((bf16[128,512]{1,0:T(8,128)(2,1)S(1)}, bf16[128,512]{1,0:T(8,128)(2,1)S(1)}, u32[]{:S(2)}, u32[]{:S(2)}) %collective-permute-start.4) | collective-permute-done | bytes 131104 | tf_op jit(solution)/shard_map/ppermute | solution.py:18
  33.8 0.0 collective-permute-done.3
  33.8 1.0 %add_convert_fusion = bf16[128,512]{1,0:T(8,128)(2,1)S(1)} fusion(bf16[128,512]{1,0:T(8,128)(2,1)S(1)} %collective-permute-done.5, bf16[128,512]{1,0:T(8,128)(2,1)S(1)} %collective-permute-done.4, f32[128,512]{1,0:T(8,128)} %get-tuple-element.7, bf16[128,512]{1,0:T(8,128)(2,1)S(1)} %collective-permute-done.3), kind=kLoop, calls=%fused_computation.46 | loop fusion | flops 458752 | bytes 786432 | tf_op jit(solution)/shard_map/convert.1
  34.8 0.6 fusion.8
  35.4 0.0 copy-done.2
  35.4 1.4 %fusion.1 = bf16[128,2560]{1,0:T(8,128)(2,1)} fusion(f32[128,2560]{1,0:T(8,128)S(1)} %fusion.8, bf16[1,5120,256]{2,1,0:T(8,128)(2,1)S(1)} %copy-done.2, s32[]{:T(128)S(6)} %select_n.30, bf16[128,512]{1,0:T(8,128)(2,1)S(1)} %add_convert_fusion), kind=kOutput, calls=%fused_computation.6 | convolution fusion | flops 168427520 | bytes 3342340 | tf_op jit(solution)/shard_map/dot_general | solution.py:149
  36.8 0.0 collective-permute-start.6
  36.8 0.6 fusion.11
  37.3 1.7 %collective-permute-done.6 = bf16[128,2560]{1,0:T(8,128)(2,1)S(1)} collective-permute-done((bf16[128,2560]{1,0:T(8,128)(2,1)}, bf16[128,2560]{1,0:T(8,128)(2,1)S(1)}, u32[]{:S(2)}, u32[]{:S(2)}) %collective-permute-start.6) | collective-permute-done | bytes 655392 | tf_op jit(solution)/shard_map/ppermute | solution.py:157
  39.1 0.0 copy-done.3
  39.1 0.6 fusion
  39.7 0.2 broadcast_in_dim.12
  39.9 1.0 %fusion.3 = f32[5,64,2560]{2,1,0:T(8,128)S(1)} fusion(s32[]{:T(128)S(6)} %select_n.31, f32[3,64,2560]{2,1,0:T(8,128)S(1)} %broadcast_in_dim.12, f32[2,64,2560]{2,1,0:T(8,128)S(1)} %bitcast.101), kind=kLoop, calls=%fused_computation.8 | loop fusion | flops 1638400 | bytes 6553604 | tf_op jit(solution)/shard_map/concatenate | solution.py:27
  40.9 1.3 %collective-permute-start.7 = (bf16[64,2560]{1,0:T(8,128)(2,1)S(1)}, bf16[64,2560]{1,0:T(8,128)(2,1)S(1)}, u32[]{:S(2)}, u32[]{:S(2)}) collective-permute-start(bf16[64,2560]{1,0:T(8,128)(2,1)S(1)} %fusion.39), channel_id=1, source_target_pairs={{8,0},{16,8},{24,16},{9,1},{17,9},{25,17},{10,2},{18,10},{26,18},{... | collective-permute-start | bytes 983048 | tf_op jit(solution)/shard_map/ppermute | solution.py:37
  42.3 10.3 %collective-permute-done.7 = bf16[64,2560]{1,0:T(8,128)(2,1)S(1)} collective-permute-done((bf16[64,2560]{1,0:T(8,128)(2,1)S(1)}, bf16[64,2560]{1,0:T(8,128)(2,1)S(1)}, u32[]{:S(2)}, u32[]{:S(2)}) %collective-permute-start.7) | collective-permute-done | bytes 327712 | tf_op jit(solution)/shard_map/ppermute | solution.py:37
  52.6 0.1 fusion.36
  52.6 1.3 %collective-permute-start.8 = (bf16[64,2560]{1,0:T(8,128)(2,1)S(1)}, bf16[64,2560]{1,0:T(8,128)(2,1)S(1)}, u32[]{:S(2)}, u32[]{:S(2)}) collective-permute-start(bf16[64,2560]{1,0:T(8,128)(2,1)S(1)} %fusion.36), channel_id=1, source_target_pairs={{8,0},{16,8},{24,16},{9,1},{17,9},{25,17},{10,2},{18,10},{26,18},{... | collective-permute-start | bytes 983048 | tf_op jit(solution)/shard_map/ppermute | solution.py:37
  53.9 0.1 bitcast_dynamic-update-slice_fusion.2
  54.0 9.4 %collective-permute-done.8 = bf16[64,2560]{1,0:T(8,128)(2,1)S(1)} collective-permute-done((bf16[64,2560]{1,0:T(8,128)(2,1)S(1)}, bf16[64,2560]{1,0:T(8,128)(2,1)S(1)}, u32[]{:S(2)}, u32[]{:S(2)}) %collective-permute-start.8) | collective-permute-done | bytes 327712 | tf_op jit(solution)/shard_map/ppermute | solution.py:37
  63.4 0.1 fusion.37
  63.5 1.3 %collective-permute-start.9 = (bf16[64,2560]{1,0:T(8,128)(2,1)S(1)}, bf16[64,2560]{1,0:T(8,128)(2,1)S(1)}, u32[]{:S(2)}, u32[]{:S(2)}) collective-permute-start(bf16[64,2560]{1,0:T(8,128)(2,1)S(1)} %fusion.37), channel_id=1, source_target_pairs={{8,0},{16,8},{24,16},{9,1},{17,9},{25,17},{10,2},{18,10},{26,18},{... | collective-permute-start | bytes 983048 | tf_op jit(solution)/shard_map/ppermute | solution.py:37
  64.8 0.1 bitcast_dynamic-update-slice_fusion.1
  64.9 8.5 %collective-permute-done.9 = bf16[64,2560]{1,0:T(8,128)(2,1)S(1)} collective-permute-done((bf16[64,2560]{1,0:T(8,128)(2,1)S(1)}, bf16[64,2560]{1,0:T(8,128)(2,1)S(1)}, u32[]{:S(2)}, u32[]{:S(2)}) %collective-permute-start.9) | collective-permute-done | bytes 327712 | tf_op jit(solution)/shard_map/ppermute | solution.py:37
  73.4 0.1 fusion.38
  73.5 1.3 %collective-permute-start.10 = (bf16[64,2560]{1,0:T(8,128)(2,1)S(1)}, bf16[64,2560]{1,0:T(8,128)(2,1)S(1)}, u32[]{:S(2)}, u32[]{:S(2)}) collective-permute-start(bf16[64,2560]{1,0:T(8,128)(2,1)S(1)} %fusion.38), channel_id=1, source_target_pairs={{8,0},{16,8},{24,16},{9,1},{17,9},{25,17},{10,2},{18,10},{26,18},{... | collective-permute-start | bytes 983048 | tf_op jit(solution)/shard_map/ppermute | solution.py:37
  74.8 0.1 bitcast_dynamic-update-slice_fusion
  74.9 7.7 %collective-permute-done.10 = bf16[64,2560]{1,0:T(8,128)(2,1)S(1)} collective-permute-done((bf16[64,2560]{1,0:T(8,128)(2,1)S(1)}, bf16[64,2560]{1,0:T(8,128)(2,1)S(1)}, u32[]{:S(2)}, u32[]{:S(2)}) %collective-permute-start.10) | collective-permute-done | bytes 327712 | tf_op jit(solution)/shard_map/ppermute | solution.py:37
  82.6 0.1 fusion.32
  82.7 1.2 %constant_dynamic-slice_fusion = f32[2,64,2560]{2,1,0:T(8,128)} fusion(f32[5,64,2560]{2,1,0:T(8,128)S(1)} %fusion.32, s32[]{:T(128)S(6)} %select_n.32), kind=kLoop, calls=%fused_computation.55 | loop fusion | bytes 2621444 | tf_op jit(solution)/shard_map/dynamic_slice | solution.py:39
  (10 shorter events, 0.1 us)
Async XLA Ops:
  0.0 1.7 %copy-start = (bf16[1,5120,256]{2,1,0:T(8,128)(2,1)S(1)}, bf16[1,5120,256]{2,1,0:T(8,128)(2,1)}, u32[]{:S(2)}) copy-start(bf16[1,5120,256]{2,1,0:T(8,128)(2,1)} %param.10) | copy-start | bytes 7864324
  0.0 3.8 %copy-start.4 = (bf16[1,128,5120]{2,1,0:T(8,128)(2,1)S(1)}, bf16[1,128,5120]{2,1,0:T(8,128)(2,1)}, u32[]{:S(2)}) copy-start(bf16[1,128,5120]{2,1,0:T(8,128)(2,1)} %param.6) | copy-start | bytes 3932164
  0.0 3.8 %copy-start.1 = (bf16[1,5120,256]{2,1,0:T(8,128)(2,1)S(1)}, bf16[1,5120,256]{2,1,0:T(8,128)(2,1)}, u32[]{:S(2)}) copy-start(bf16[1,5120,256]{2,1,0:T(8,128)(2,1)} %param.9) | copy-start | bytes 7864324
  3.8 10.2 %copy-start.9 = (s32[512]{0:T(512)S(1)}, s32[512]{0:T(512)}, u32[]{:S(2)}) copy-start(s32[512]{0:T(512)} %param.11) | copy-start | bytes 6148
  4.3 12.1 %copy-start.5 = (bf16[128,512]{1,0:T(8,128)(2,1)}, bf16[128,512]{1,0:T(8,128)(2,1)S(1)}, u32[]{:S(2)}) copy-start(bf16[128,512]{1,0:T(8,128)(2,1)S(1)} %pad_maximum_fusion.refs_2_) | copy-start | bytes 393220
  4.3 11.3 %collective-permute-start = (bf16[128,512]{1,0:T(8,128)(2,1)S(1)}, bf16[128,512]{1,0:T(8,128)(2,1)S(1)}, u32[]{:S(2)}, u32[]{:S(2)}) collective-permute-start(bf16[128,512]{1,0:T(8,128)(2,1)S(1)} %pad_maximum_fusion.refs_2_), channel_id=1, source_target_pairs={{0,2},{2,4},{4,6},{1,3},{3,5},{5,7},{8,10},{10,12},{12,14},{9,11},... | collective-permute-start | bytes 393224 | tf_op jit(solution)/shard_map/ppermute | solution.py:18
  9.2 6.5 %collective-permute-start.1 = (bf16[128,512]{1,0:T(8,128)(2,1)S(1)}, bf16[128,512]{1,0:T(8,128)(2,1)S(1)}, u32[]{:S(2)}, u32[]{:S(2)}) collective-permute-start(bf16[128,512]{1,0:T(8,128)(2,1)S(1)} %pad_maximum_fusion.refs_2_), channel_id=1, source_target_pairs={{0,4},{2,6},{1,5},{3,7},{8,12},{10,14},{9,13},{11,15},{16,20},{18,... | collective-permute-start | bytes 393224 | tf_op jit(solution)/shard_map/ppermute | solution.py:18
  12.7 3.8 %collective-permute-start.2 = (bf16[128,512]{1,0:T(8,128)(2,1)S(1)}, bf16[128,512]{1,0:T(8,128)(2,1)S(1)}, u32[]{:S(2)}, u32[]{:S(2)}) collective-permute-start(bf16[128,512]{1,0:T(8,128)(2,1)S(1)} %pad_maximum_fusion.refs_2_), channel_id=1, source_target_pairs={{0,6},{1,7},{8,14},{9,15},{16,22},{17,23},{24,30},{25,31}} | collective-permute-start | bytes 393224 | tf_op jit(solution)/shard_map/ppermute | solution.py:18
  15.6 0.8 %copy-start.6 = (bf16[128,512]{1,0:T(8,128)(2,1)}, bf16[128,512]{1,0:T(8,128)(2,1)S(1)}, u32[]{:S(2)}) copy-start(bf16[128,512]{1,0:T(8,128)(2,1)S(1)} %collective-permute-done.refs_3_) | copy-start | bytes 393220
  15.7 0.8 copy-start.7
  16.5 0.6 copy-start.8
  24.1 8.0 %collective-permute-start.5 = (bf16[128,512]{1,0:T(8,128)(2,1)S(1)}, bf16[128,512]{1,0:T(8,128)(2,1)S(1)}, u32[]{:S(2)}, u32[]{:S(2)}) collective-permute-start(bf16[128,512]{1,0:T(8,128)(2,1)S(1)} %get-tuple-element.10), channel_id=1, source_target_pairs={{6,0},{7,1},{14,8},{15,9},{22,16},{23,17},{30,24},{31,25}} | collective-permute-start | bytes 393224 | tf_op jit(solution)/shard_map/ppermute | solution.py:18
  25.4 8.4 %collective-permute-start.4 = (bf16[128,512]{1,0:T(8,128)(2,1)S(1)}, bf16[128,512]{1,0:T(8,128)(2,1)S(1)}, u32[]{:S(2)}, u32[]{:S(2)}) collective-permute-start(bf16[128,512]{1,0:T(8,128)(2,1)S(1)} %get-tuple-element.11), channel_id=1, source_target_pairs={{4,0},{6,2},{5,1},{7,3},{12,8},{14,10},{13,9},{15,11},{20,16},{22,... | collective-permute-start | bytes 393224 | tf_op jit(solution)/shard_map/ppermute | solution.py:18
  26.7 7.1 %collective-permute-start.3 = (bf16[128,512]{1,0:T(8,128)(2,1)S(1)}, bf16[128,512]{1,0:T(8,128)(2,1)S(1)}, u32[]{:S(2)}, u32[]{:S(2)}) collective-permute-start(bf16[128,512]{1,0:T(8,128)(2,1)S(1)} %get-tuple-element.9), channel_id=1, source_target_pairs={{2,0},{4,2},{6,4},{3,1},{5,3},{7,5},{10,8},{12,10},{14,12},{11,9},... | collective-permute-start | bytes 393224 | tf_op jit(solution)/shard_map/ppermute | solution.py:18
  28.0 7.4 %copy-start.2 = (bf16[1,5120,256]{2,1,0:T(8,128)(2,1)S(1)}, bf16[1,5120,256]{2,1,0:T(8,128)(2,1)}, u32[]{:S(2)}) copy-start(bf16[1,5120,256]{2,1,0:T(8,128)(2,1)} %param.9) | copy-start | bytes 7864324
  36.8 2.3 %collective-permute-start.6 = (bf16[128,2560]{1,0:T(8,128)(2,1)}, bf16[128,2560]{1,0:T(8,128)(2,1)S(1)}, u32[]{:S(2)}, u32[]{:S(2)}) collective-permute-start(bf16[128,2560]{1,0:T(8,128)(2,1)} %fusion.1), channel_id=1, source_target_pairs={{0,1},{1,0},{2,3},{3,2},{4,5},{5,4},{6,7},{7,6},{8,9},{9,8},{10,11... | collective-permute-start | bytes 1966088 | tf_op jit(solution)/shard_map/ppermute | solution.py:157
  36.8 2.3 %copy-start.3 = (bf16[1,5120,256]{2,1,0:T(8,128)(2,1)S(1)}, bf16[1,5120,256]{2,1,0:T(8,128)(2,1)}, u32[]{:S(2)}) copy-start(bf16[1,5120,256]{2,1,0:T(8,128)(2,1)} %param.9) | copy-start | bytes 7864324
  40.9 11.6 %collective-permute-start.7 = (bf16[64,2560]{1,0:T(8,128)(2,1)S(1)}, bf16[64,2560]{1,0:T(8,128)(2,1)S(1)}, u32[]{:S(2)}, u32[]{:S(2)}) collective-permute-start(bf16[64,2560]{1,0:T(8,128)(2,1)S(1)} %fusion.39), channel_id=1, source_target_pairs={{8,0},{16,8},{24,16},{9,1},{17,9},{25,17},{10,2},{18,10},{26,18},{... | collective-permute-start | bytes 983048 | tf_op jit(solution)/shard_map/ppermute | solution.py:37
  52.6 10.8 %collective-permute-start.8 = (bf16[64,2560]{1,0:T(8,128)(2,1)S(1)}, bf16[64,2560]{1,0:T(8,128)(2,1)S(1)}, u32[]{:S(2)}, u32[]{:S(2)}) collective-permute-start(bf16[64,2560]{1,0:T(8,128)(2,1)S(1)} %fusion.36), channel_id=1, source_target_pairs={{8,0},{16,8},{24,16},{9,1},{17,9},{25,17},{10,2},{18,10},{26,18},{... | collective-permute-start | bytes 983048 | tf_op jit(solution)/shard_map/ppermute | solution.py:37
  63.5 9.9 %collective-permute-start.9 = (bf16[64,2560]{1,0:T(8,128)(2,1)S(1)}, bf16[64,2560]{1,0:T(8,128)(2,1)S(1)}, u32[]{:S(2)}, u32[]{:S(2)}) collective-permute-start(bf16[64,2560]{1,0:T(8,128)(2,1)S(1)} %fusion.37), channel_id=1, source_target_pairs={{8,0},{16,8},{24,16},{9,1},{17,9},{25,17},{10,2},{18,10},{26,18},{... | collective-permute-start | bytes 983048 | tf_op jit(solution)/shard_map/ppermute | solution.py:37
  73.5 9.1 %collective-permute-start.10 = (bf16[64,2560]{1,0:T(8,128)(2,1)S(1)}, bf16[64,2560]{1,0:T(8,128)(2,1)S(1)}, u32[]{:S(2)}, u32[]{:S(2)}) collective-permute-start(bf16[64,2560]{1,0:T(8,128)(2,1)S(1)} %fusion.38), channel_id=1, source_target_pairs={{8,0},{16,8},{24,16},{9,1},{17,9},{25,17},{10,2},{18,10},{26,18},{... | collective-permute-start | bytes 983048 | tf_op jit(solution)/shard_map/ppermute | solution.py:37

commit v12 on v11

--- a/solution.py
+++ b/solution.py
@@ -7,7 +7,7 @@
 from jax.sharding import PartitionSpec as P
 
 
-CHAIN_CHUNKS = 2
+CHAIN_CHUNKS = 4
 
 
 def shifted(x, axis, d, length, up):
@@ -27,13 +27,13 @@
     padded = jnp.concatenate((pad, chunks, pad), axis=0)
     steps = n_chunks + length - 1
     ordered = lax.dynamic_slice_in_dim(padded, index, steps, axis=0)
-    perm = [(i, i - 1) for i in range(1, length)]
     recv = jnp.zeros((height, cols), jnp.bfloat16)
     done = []
     for tau in range(steps):
         acc = ordered[tau] + recv.astype(jnp.float32)
         done.append(acc)
-        if tau < steps - 1:
+        perm = [(i, i - 1) for i in range(1, length) if 0 <= tau - (length - 1 - i) < n_chunks]
+        if perm:
             recv = lax.ppermute(acc.astype(jnp.bfloat16), axis, perm)
     stacked = jnp.stack(done, axis=0)
     mine = lax.dynamic_slice_in_dim(stacked, length - 1 - index, n_chunks, axis=0)

time: 84.2 us -> 85.8 us (1.019)
  starting transfers between devices: 18.6 us -> 20 us
  waiting for transfers between devices: 44.3 us -> 45.2 us
    ppermute x4 -> x6, starting transfers between devices: 5.17 us -> 6.51 us  [suffix_pipeline(): recv = lax.ppermute(acc.astype(jnp.bfloat16), axis, perm)]
    ppermute x4 -> x6, waiting for transfers between devices: 35.9 us -> 36.9 us  [suffix_pipeline(): recv = lax.ppermute(acc.astype(jnp.bfloat16), axis, perm)]
  transfers between devices with their start and end apart: 11 -> 13, of which waited for: 9 -> 9; matrix products, arithmetic and copies ran while one was open for 3% -> 3% of each run, Pallas kernels for 0% -> 0%
where the time goes in v12:
time: 85.8 us; the launch traced here: 85.4 us
  waiting for transfers between devices  45.2 us (53%)
  starting transfers between devices  20 us (23%)
  Pallas kernels  5.89 us (7%)
  matrix products  5.63 us (7%)
  local copies, waits for them, and re-layouts  5.3 us (6%)
  other arithmetic  2.98 us (3%)
    ppermute x6, waiting for transfers between devices, suffix_pipeline(): recv = lax.ppermute(acc.astype(jnp.bfloat16), axis, perm)  36.9 us
    ppermute x6, starting transfers between devices, shifted(): return lax.ppermute(x, axis, perm)  13.5 us
    ppermute x6, waiting for transfers between devices, shifted(): return lax.ppermute(x, axis, perm)  6.63 us
    ppermute x6, starting transfers between devices, suffix_pipeline(): recv = lax.ppermute(acc.astype(jnp.bfloat16), axis, perm)  6.51 us
    pallas_call x1, Pallas kernels, attention_terms(): pl.pallas_call(kernel, out_shape=(jax.ShapeDtypeStruct((seq_rows, 2 * kv_...  5.89 us
    unnamed x23, local copies, waits for them, and re-layouts  2.64 us
    dot_general x1, matrix products, per_device(): jnp.dot(tokens, w_value[0], preferred_element_type=jnp.float32)  2.02 us
    dot_general x2, matrix products, partial_for(): lax.dot_general(grad_key, wk, contract, preferred_element_type=jnp.float32)  1.99 us
  transfers between devices with their start and end apart: 13, of which 9 were waited for; matrix products, arithmetic and copies ran while one was open for 3% of the time, Pallas kernels for 0%

profile of v12, /device:TPU:0, one launch (start us, length us, event | category | flops | bytes accessed | tf_op | source)
XLA Modules:
  0.0 85.4 jit_solution(1267199401760155068)
XLA Ops:
  0.0 0.0 copy-start
  0.0 0.0 copy-start.4
  0.0 0.0 copy-start.1
  0.0 1.7 %copy-done = bf16[1,5120,256]{2,1,0:T(8,128)(2,1)S(1)} copy-done((bf16[1,5120,256]{2,1,0:T(8,128)(2,1)S(1)}, bf16[1,5120,256]{2,1,0:T(8,128)(2,1)}, u32[]{:S(2)}) %copy-start) | copy-done | bytes 2621464
  1.7 2.0 %fusion.25 = bf16[128,256]{1,0:T(8,128)(2,1)S(1)} fusion(bf16[1,5120,256]{2,1,0:T(8,128)(2,1)S(1)} %copy-done, bf16[1,128,5120]{2,1,0:T(8,128)(2,1)} %param.6), kind=kOutput, calls=%fused_computation.26 | convolution fusion | flops 335577088 | bytes 3997696 | tf_op jit(solution)/shard_map/dot_general | solution.py:107
  3.8 0.0 copy-done.4
  3.8 0.0 copy-done.1
  3.8 0.0 copy-start.9
  3.8 0.5 fusion.20
  4.3 0.0 copy-start.5
  4.3 4.9 %collective-permute-start = (bf16[128,512]{1,0:T(8,128)(2,1)S(1)}, bf16[128,512]{1,0:T(8,128)(2,1)S(1)}, u32[]{:S(2)}, u32[]{:S(2)}) collective-permute-start(bf16[128,512]{1,0:T(8,128)(2,1)S(1)} %pad_maximum_fusion.refs_2_), channel_id=1, source_target_pairs={{0,2},{2,4},{4,6},{1,3},{3,5},{5,7},{8,10},{10,12},{12,14},{9,11},... | collective-permute-start | bytes 393224 | tf_op jit(solution)/shard_map/ppermute | solution.py:18
  9.2 3.4 %collective-permute-start.1 = (bf16[128,512]{1,0:T(8,128)(2,1)S(1)}, bf16[128,512]{1,0:T(8,128)(2,1)S(1)}, u32[]{:S(2)}, u32[]{:S(2)}) collective-permute-start(bf16[128,512]{1,0:T(8,128)(2,1)S(1)} %pad_maximum_fusion.refs_2_), channel_id=1, source_target_pairs={{0,4},{2,6},{1,5},{3,7},{8,12},{10,14},{9,13},{11,15},{16,20},{18,... | collective-permute-start | bytes 393224 | tf_op jit(solution)/shard_map/ppermute | solution.py:18
  12.7 1.3 %collective-permute-start.2 = (bf16[128,512]{1,0:T(8,128)(2,1)S(1)}, bf16[128,512]{1,0:T(8,128)(2,1)S(1)}, u32[]{:S(2)}, u32[]{:S(2)}) collective-permute-start(bf16[128,512]{1,0:T(8,128)(2,1)S(1)} %pad_maximum_fusion.refs_2_), channel_id=1, source_target_pairs={{0,6},{1,7},{8,14},{9,15},{16,22},{17,23},{24,30},{25,31}} | collective-permute-start | bytes 393224 | tf_op jit(solution)/shard_map/ppermute | solution.py:18
  14.0 0.0 copy-done.9
  14.0 0.2 copy.25
  14.2 0.1 fusion.54
  14.3 0.1 fusion.52
  14.4 0.2 copy.24
  14.6 0.2 copy.28
  14.8 0.9 %broadcast_select_fusion = (s32[512,1]{1,0:T(8,128)}, s32[512,1]{1,0:T(8,128)}) fusion(pred[512,1]{1,0:T(8,128)(4,1)S(1)} %copy.25, s32[512,1]{1,0:T(8,128)S(1)} %copy.24, pred[1,512]{0,1:T(8,128)(4,1)S(1)} %copy.28), kind=kLoop, calls=%fused_computation.57 | loop fusion | flops 1024 | bytes 7168 | tf_op jit(solution)/shard_map/jit(_where)/select_n | solution.py:129
  15.6 0.0 collective-permute-done.refs_3_
  15.6 0.0 copy-start.6
  15.6 0.1 collective-permute-done.1.refs_4_
  15.7 0.0 copy-start.7
  15.7 0.8 collective-permute-done.2.refs_5_
  16.5 0.0 copy-start.8
  16.5 0.0 copy-done.5
  16.5 0.0 copy-done.6
  16.5 0.0 copy-done.7
  16.5 0.6 copy-done.8
  17.1 5.9 %shard_map.64 = (bf16[512,512]{1,0:T(8,128)(2,1)}, f32[128,512]{1,0:T(8,128)}) custom-call(bf16[10,128,128]{2,1,0:T(8,128)(2,1)} %bitcast.122, bf16[10,128,128]{2,1,0:T(8,128)(2,1)} %bitcast.123, bf16[128,512]{1,0:T(8,128)(2,1)} %copy-done.5, bf16[128,512]{1,0:T(8,128)(2,1)} %copy-done.6, bf16[128,512]{1,0:T(8,128)(2,1)} %copy-done.7, ...), custom_call_target="tpu_custom_call" | custom-call | tf_op jit(solution)/shard_map/pallas_call | solution.py:86
  23.0 1.1 %fusion.59 = (bf16[128,512]{1,0:T(8,128)(2,1)S(1)}, bf16[128,512]{1,0:T(8,128)(2,1)S(1)}, bf16[128,512]{1,0:T(8,128)(2,1)S(1)}) fusion(bf16[512,512]{1,0:T(8,128)(2,1)} %get-tuple-element.8), kind=kLoop, calls=%fused_computation.82 | loop fusion | bytes 786432 | tf_op jit(solution)/shard_map/slice | solution.py:136
  24.1 1.3 %collective-permute-start.5 = (bf16[128,512]{1,0:T(8,128)(2,1)S(1)}, bf16[128,512]{1,0:T(8,128)(2,1)S(1)}, u32[]{:S(2)}, u32[]{:S(2)}) collective-permute-start(bf16[128,512]{1,0:T(8,128)(2,1)S(1)} %get-tuple-element.10), channel_id=1, source_target_pairs={{6,0},{7,1},{14,8},{15,9},{22,16},{23,17},{30,24},{31,25}} | collective-permute-start | bytes 393224 | tf_op jit(solution)/shard_map/ppermute | solution.py:18
  25.4 1.3 %collective-permute-start.4 = (bf16[128,512]{1,0:T(8,128)(2,1)S(1)}, bf16[128,512]{1,0:T(8,128)(2,1)S(1)}, u32[]{:S(2)}, u32[]{:S(2)}) collective-permute-start(bf16[128,512]{1,0:T(8,128)(2,1)S(1)} %get-tuple-element.11), channel_id=1, source_target_pairs={{4,0},{6,2},{5,1},{7,3},{12,8},{14,10},{13,9},{15,11},{20,16},{22,... | collective-permute-start | bytes 393224 | tf_op jit(solution)/shard_map/ppermute | solution.py:18
  26.7 1.3 %collective-permute-start.3 = (bf16[128,512]{1,0:T(8,128)(2,1)S(1)}, bf16[128,512]{1,0:T(8,128)(2,1)S(1)}, u32[]{:S(2)}, u32[]{:S(2)}) collective-permute-start(bf16[128,512]{1,0:T(8,128)(2,1)S(1)} %get-tuple-element.9), channel_id=1, source_target_pairs={{2,0},{4,2},{6,4},{3,1},{5,3},{7,5},{10,8},{12,10},{14,12},{11,9},... | collective-permute-start | bytes 393224 | tf_op jit(solution)/shard_map/ppermute | solution.py:18
  28.0 0.0 copy-start.2
  28.0 4.1 %collective-permute-done.5 = bf16[128,512]{1,0:T(8,128)(2,1)S(1)} collective-permute-done((bf16[128,512]{1,0:T(8,128)(2,1)S(1)}, bf16[128,512]{1,0:T(8,128)(2,1)S(1)}, u32[]{:S(2)}, u32[]{:S(2)}) %collective-permute-start.5) | collective-permute-done | bytes 131104 | tf_op jit(solution)/shard_map/ppermute | solution.py:18
  32.1 1.7 %collective-permute-done.4 = bf16[128,512]{1,0:T(8,128)(2,1)S(1)} collective-permute-done((bf16[128,512]{1,0:T(8,128)(2,1)S(1)}, bf16[128,512]{1,0:T(8,128)(2,1)S(1)}, u32[]{:S(2)}, u32[]{:S(2)}) %collective-permute-start.4) | collective-permute-done | bytes 131104 | tf_op jit(solution)/shard_map/ppermute | solution.py:18
  33.8 0.0 collective-permute-done.3
  33.8 1.0 %add_convert_fusion = bf16[128,512]{1,0:T(8,128)(2,1)S(1)} fusion(bf16[128,512]{1,0:T(8,128)(2,1)S(1)} %collective-permute-done.5, bf16[128,512]{1,0:T(8,128)(2,1)S(1)} %collective-permute-done.4, f32[128,512]{1,0:T(8,128)} %get-tuple-element.7, bf16[128,512]{1,0:T(8,128)(2,1)S(1)} %collective-permute-done.3), kind=kLoop, calls=%fused_computation.48 | loop fusion | flops 458752 | bytes 786432 | tf_op jit(solution)/shard_map/convert.1
  34.8 0.6 fusion.8
  35.4 0.0 copy-done.2
  35.4 1.4 %fusion.1 = bf16[128,2560]{1,0:T(8,128)(2,1)} fusion(f32[128,2560]{1,0:T(8,128)S(1)} %fusion.8, bf16[1,5120,256]{2,1,0:T(8,128)(2,1)S(1)} %copy-done.2, s32[]{:T(128)S(6)} %select_n.30, bf16[128,512]{1,0:T(8,128)(2,1)S(1)} %add_convert_fusion), kind=kOutput, calls=%fused_computation.3 | convolution fusion | flops 168427520 | bytes 3342340 | tf_op jit(solution)/shard_map/dot_general | solution.py:149
  36.8 0.0 collective-permute-start.6
  36.8 0.0 copy-start.3
  36.8 0.6 fusion.11
  37.3 1.7 %collective-permute-done.6 = bf16[128,2560]{1,0:T(8,128)(2,1)S(1)} collective-permute-done((bf16[128,2560]{1,0:T(8,128)(2,1)}, bf16[128,2560]{1,0:T(8,128)(2,1)S(1)}, u32[]{:S(2)}, u32[]{:S(2)}) %collective-permute-start.6) | collective-permute-done | bytes 655392 | tf_op jit(solution)/shard_map/ppermute | solution.py:157
  39.1 0.0 copy-done.3
  39.1 0.6 fusion
  39.7 0.1 broadcast_in_dim.12
  39.8 0.6 fusion.7
  40.4 0.7 collective-permute-start.7
  41.1 0.0 collective-permute-done.7
  41.2 0.7 collective-permute-start.8
  41.9 0.0 collective-permute-done.8
  41.9 1.3 %collective-permute-start.9 = (bf16[32,2560]{1,0:T(8,128)(2,1)S(1)}, bf16[32,2560]{1,0:T(8,128)(2,1)S(1)}, u32[]{:S(2)}, u32[]{:S(2)}) collective-permute-start(bf16[32,2560]{1,0:T(8,128)(2,1)S(1)} %fusion.39), channel_id=1, source_target_pairs={{8,0},{16,8},{24,16},{9,1},{17,9},{25,17},{10,2},{18,10},{26,18},{... | collective-permute-start | bytes 491528 | tf_op jit(solution)/shard_map/ppermute | solution.py:37
  43.3 19.2 %collective-permute-done.9 = bf16[32,2560]{1,0:T(8,128)(2,1)S(1)} collective-permute-done((bf16[32,2560]{1,0:T(8,128)(2,1)S(1)}, bf16[32,2560]{1,0:T(8,128)(2,1)S(1)}, u32[]{:S(2)}, u32[]{:S(2)}) %collective-permute-start.9) | collective-permute-done | bytes 163872 | tf_op jit(solution)/shard_map/ppermute | solution.py:37
  62.5 1.3 %collective-permute-start.10 = (bf16[32,2560]{1,0:T(8,128)(2,1)S(1)}, bf16[32,2560]{1,0:T(8,128)(2,1)S(1)}, u32[]{:S(2)}, u32[]{:S(2)}) collective-permute-start(bf16[32,2560]{1,0:T(8,128)(2,1)S(1)} %fusion.40), channel_id=1, source_target_pairs={{8,0},{16,8},{24,16},{9,1},{17,9},{25,17},{10,2},{18,10},{26,18},{... | collective-permute-start | bytes 491528 | tf_op jit(solution)/shard_map/ppermute | solution.py:37
  63.9 5.9 %collective-permute-done.10 = bf16[32,2560]{1,0:T(8,128)(2,1)S(1)} collective-permute-done((bf16[32,2560]{1,0:T(8,128)(2,1)S(1)}, bf16[32,2560]{1,0:T(8,128)(2,1)S(1)}, u32[]{:S(2)}, u32[]{:S(2)}) %collective-permute-start.10) | collective-permute-done | bytes 163872 | tf_op jit(solution)/shard_map/ppermute | solution.py:37
  69.8 1.3 %collective-permute-start.11 = (bf16[32,2560]{1,0:T(8,128)(2,1)S(1)}, bf16[32,2560]{1,0:T(8,128)(2,1)S(1)}, u32[]{:S(2)}, u32[]{:S(2)}) collective-permute-start(bf16[32,2560]{1,0:T(8,128)(2,1)S(1)} %fusion.41), channel_id=1, source_target_pairs={{8,0},{16,8},{9,1},{17,9},{10,2},{18,10},{11,3},{19,11},{12,4},{20... | collective-permute-start | bytes 491528 | tf_op jit(solution)/shard_map/ppermute | solution.py:37
  71.1 5.9 %collective-permute-done.11 = bf16[32,2560]{1,0:T(8,128)(2,1)S(1)} collective-permute-done((bf16[32,2560]{1,0:T(8,128)(2,1)S(1)}, bf16[32,2560]{1,0:T(8,128)(2,1)S(1)}, u32[]{:S(2)}, u32[]{:S(2)}) %collective-permute-start.11) | collective-permute-done | bytes 163872 | tf_op jit(solution)/shard_map/ppermute | solution.py:37
  77.0 1.3 %collective-permute-start.12 = (bf16[32,2560]{1,0:T(8,128)(2,1)S(1)}, bf16[32,2560]{1,0:T(8,128)(2,1)S(1)}, u32[]{:S(2)}, u32[]{:S(2)}) collective-permute-start(bf16[32,2560]{1,0:T(8,128)(2,1)S(1)} %fusion.42), channel_id=1, source_target_pairs={{8,0},{9,1},{10,2},{11,3},{12,4},{13,5},{14,6},{15,7}} | collective-permute-start | bytes 491528 | tf_op jit(solution)/shard_map/ppermute | solution.py:37
  78.4 5.9 %collective-permute-done.12 = bf16[32,2560]{1,0:T(8,128)(2,1)S(1)} collective-permute-done((bf16[32,2560]{1,0:T(8,128)(2,1)S(1)}, bf16[32,2560]{1,0:T(8,128)(2,1)S(1)}, u32[]{:S(2)}, u32[]{:S(2)}) %collective-permute-start.12) | collective-permute-done | bytes 163872 | tf_op jit(solution)/shard_map/ppermute | solution.py:37
  84.3 1.2 %constant_dynamic-slice_fusion = f32[4,32,2560]{2,1,0:T(8,128)} fusion(f32[7,32,2560]{2,1,0:T(8,128)S(1)} %fusion.32, s32[]{:T(128)S(6)} %select_n.32), kind=kLoop, calls=%fused_computation.63 | loop fusion | bytes 2621444 | tf_op jit(solution)/shard_map/dynamic_slice | solution.py:39
  (18 shorter events, 0.4 us)
Async XLA Ops:
  0.0 1.7 %copy-start = (bf16[1,5120,256]{2,1,0:T(8,128)(2,1)S(1)}, bf16[1,5120,256]{2,1,0:T(8,128)(2,1)}, u32[]{:S(2)}) copy-start(bf16[1,5120,256]{2,1,0:T(8,128)(2,1)} %param.10) | copy-start | bytes 7864324
  0.0 3.8 %copy-start.4 = (bf16[1,128,5120]{2,1,0:T(8,128)(2,1)S(1)}, bf16[1,128,5120]{2,1,0:T(8,128)(2,1)}, u32[]{:S(2)}) copy-start(bf16[1,128,5120]{2,1,0:T(8,128)(2,1)} %param.6) | copy-start | bytes 3932164
  0.0 3.8 %copy-start.1 = (bf16[1,5120,256]{2,1,0:T(8,128)(2,1)S(1)}, bf16[1,5120,256]{2,1,0:T(8,128)(2,1)}, u32[]{:S(2)}) copy-start(bf16[1,5120,256]{2,1,0:T(8,128)(2,1)} %param.9) | copy-start | bytes 7864324
  3.8 10.2 %copy-start.9 = (s32[512]{0:T(512)S(1)}, s32[512]{0:T(512)}, u32[]{:S(2)}) copy-start(s32[512]{0:T(512)} %param.11) | copy-start | bytes 6148
  4.3 12.1 %copy-start.5 = (bf16[128,512]{1,0:T(8,128)(2,1)}, bf16[128,512]{1,0:T(8,128)(2,1)S(1)}, u32[]{:S(2)}) copy-start(bf16[128,512]{1,0:T(8,128)(2,1)S(1)} %pad_maximum_fusion.refs_2_) | copy-start | bytes 393220
  4.3 11.3 %collective-permute-start = (bf16[128,512]{1,0:T(8,128)(2,1)S(1)}, bf16[128,512]{1,0:T(8,128)(2,1)S(1)}, u32[]{:S(2)}, u32[]{:S(2)}) collective-permute-start(bf16[128,512]{1,0:T(8,128)(2,1)S(1)} %pad_maximum_fusion.refs_2_), channel_id=1, source_target_pairs={{0,2},{2,4},{4,6},{1,3},{3,5},{5,7},{8,10},{10,12},{12,14},{9,11},... | collective-permute-start | bytes 393224 | tf_op jit(solution)/shard_map/ppermute | solution.py:18
  9.2 6.5 %collective-permute-start.1 = (bf16[128,512]{1,0:T(8,128)(2,1)S(1)}, bf16[128,512]{1,0:T(8,128)(2,1)S(1)}, u32[]{:S(2)}, u32[]{:S(2)}) collective-permute-start(bf16[128,512]{1,0:T(8,128)(2,1)S(1)} %pad_maximum_fusion.refs_2_), channel_id=1, source_target_pairs={{0,4},{2,6},{1,5},{3,7},{8,12},{10,14},{9,13},{11,15},{16,20},{18,... | collective-permute-start | bytes 393224 | tf_op jit(solution)/shard_map/ppermute | solution.py:18
  12.7 3.8 %collective-permute-start.2 = (bf16[128,512]{1,0:T(8,128)(2,1)S(1)}, bf16[128,512]{1,0:T(8,128)(2,1)S(1)}, u32[]{:S(2)}, u32[]{:S(2)}) collective-permute-start(bf16[128,512]{1,0:T(8,128)(2,1)S(1)} %pad_maximum_fusion.refs_2_), channel_id=1, source_target_pairs={{0,6},{1,7},{8,14},{9,15},{16,22},{17,23},{24,30},{25,31}} | collective-permute-start | bytes 393224 | tf_op jit(solution)/shard_map/ppermute | solution.py:18
  15.6 0.9 %copy-start.6 = (bf16[128,512]{1,0:T(8,128)(2,1)}, bf16[128,512]{1,0:T(8,128)(2,1)S(1)}, u32[]{:S(2)}) copy-start(bf16[128,512]{1,0:T(8,128)(2,1)S(1)} %collective-permute-done.refs_3_) | copy-start | bytes 393220
  15.7 0.8 copy-start.7
  16.5 0.7 copy-start.8
  24.1 8.0 %collective-permute-start.5 = (bf16[128,512]{1,0:T(8,128)(2,1)S(1)}, bf16[128,512]{1,0:T(8,128)(2,1)S(1)}, u32[]{:S(2)}, u32[]{:S(2)}) collective-permute-start(bf16[128,512]{1,0:T(8,128)(2,1)S(1)} %get-tuple-element.10), channel_id=1, source_target_pairs={{6,0},{7,1},{14,8},{15,9},{22,16},{23,17},{30,24},{31,25}} | collective-permute-start | bytes 393224 | tf_op jit(solution)/shard_map/ppermute | solution.py:18
  25.4 8.4 %collective-permute-start.4 = (bf16[128,512]{1,0:T(8,128)(2,1)S(1)}, bf16[128,512]{1,0:T(8,128)(2,1)S(1)}, u32[]{:S(2)}, u32[]{:S(2)}) collective-permute-start(bf16[128,512]{1,0:T(8,128)(2,1)S(1)} %get-tuple-element.11), channel_id=1, source_target_pairs={{4,0},{6,2},{5,1},{7,3},{12,8},{14,10},{13,9},{15,11},{20,16},{22,... | collective-permute-start | bytes 393224 | tf_op jit(solution)/shard_map/ppermute | solution.py:18
  26.7 7.1 %collective-permute-start.3 = (bf16[128,512]{1,0:T(8,128)(2,1)S(1)}, bf16[128,512]{1,0:T(8,128)(2,1)S(1)}, u32[]{:S(2)}, u32[]{:S(2)}) collective-permute-start(bf16[128,512]{1,0:T(8,128)(2,1)S(1)} %get-tuple-element.9), channel_id=1, source_target_pairs={{2,0},{4,2},{6,4},{3,1},{5,3},{7,5},{10,8},{12,10},{14,12},{11,9},... | collective-permute-start | bytes 393224 | tf_op jit(solution)/shard_map/ppermute | solution.py:18
  28.0 7.4 %copy-start.2 = (bf16[1,5120,256]{2,1,0:T(8,128)(2,1)S(1)}, bf16[1,5120,256]{2,1,0:T(8,128)(2,1)}, u32[]{:S(2)}) copy-start(bf16[1,5120,256]{2,1,0:T(8,128)(2,1)} %param.9) | copy-start | bytes 7864324
  36.8 2.3 %collective-permute-start.6 = (bf16[128,2560]{1,0:T(8,128)(2,1)}, bf16[128,2560]{1,0:T(8,128)(2,1)S(1)}, u32[]{:S(2)}, u32[]{:S(2)}) collective-permute-start(bf16[128,2560]{1,0:T(8,128)(2,1)} %fusion.1), channel_id=1, source_target_pairs={{0,1},{1,0},{2,3},{3,2},{4,5},{5,4},{6,7},{7,6},{8,9},{9,8},{10,11... | collective-permute-start | bytes 1966088 | tf_op jit(solution)/shard_map/ppermute | solution.py:157
  36.8 2.3 %copy-start.3 = (bf16[1,5120,256]{2,1,0:T(8,128)(2,1)S(1)}, bf16[1,5120,256]{2,1,0:T(8,128)(2,1)}, u32[]{:S(2)}) copy-start(bf16[1,5120,256]{2,1,0:T(8,128)(2,1)} %param.9) | copy-start | bytes 7864324
  40.4 0.7 collective-permute-start.7
  41.2 0.7 collective-permute-start.8
  41.9 20.6 %collective-permute-start.9 = (bf16[32,2560]{1,0:T(8,128)(2,1)S(1)}, bf16[32,2560]{1,0:T(8,128)(2,1)S(1)}, u32[]{:S(2)}, u32[]{:S(2)}) collective-permute-start(bf16[32,2560]{1,0:T(8,128)(2,1)S(1)} %fusion.39), channel_id=1, source_target_pairs={{8,0},{16,8},{24,16},{9,1},{17,9},{25,17},{10,2},{18,10},{26,18},{... | collective-permute-start | bytes 491528 | tf_op jit(solution)/shard_map/ppermute | solution.py:37
  62.5 7.2 %collective-permute-start.10 = (bf16[32,2560]{1,0:T(8,128)(2,1)S(1)}, bf16[32,2560]{1,0:T(8,128)(2,1)S(1)}, u32[]{:S(2)}, u32[]{:S(2)}) collective-permute-start(bf16[32,2560]{1,0:T(8,128)(2,1)S(1)} %fusion.40), channel_id=1, source_target_pairs={{8,0},{16,8},{24,16},{9,1},{17,9},{25,17},{10,2},{18,10},{26,18},{... | collective-permute-start | bytes 491528 | tf_op jit(solution)/shard_map/ppermute | solution.py:37
  69.8 7.2 %collective-permute-start.11 = (bf16[32,2560]{1,0:T(8,128)(2,1)S(1)}, bf16[32,2560]{1,0:T(8,128)(2,1)S(1)}, u32[]{:S(2)}, u32[]{:S(2)}) collective-permute-start(bf16[32,2560]{1,0:T(8,128)(2,1)S(1)} %fusion.41), channel_id=1, source_target_pairs={{8,0},{16,8},{9,1},{17,9},{10,2},{18,10},{11,3},{19,11},{12,4},{20... | collective-permute-start | bytes 491528 | tf_op jit(solution)/shard_map/ppermute | solution.py:37
  77.0 7.2 %collective-permute-start.12 = (bf16[32,2560]{1,0:T(8,128)(2,1)S(1)}, bf16[32,2560]{1,0:T(8,128)(2,1)S(1)}, u32[]{:S(2)}, u32[]{:S(2)}) collective-permute-start(bf16[32,2560]{1,0:T(8,128)(2,1)S(1)} %fusion.42), channel_id=1, source_target_pairs={{8,0},{9,1},{10,2},{11,3},{12,4},{13,5},{14,6},{15,7}} | collective-permute-start | bytes 491528 | tf_op jit(solution)/shard_map/ppermute | solution.py:37

commit v13 on v11

--- a/solution.py
+++ b/solution.py
@@ -51,7 +51,8 @@
     def kernel(*refs):
         q_ref, g_ref = refs[0], refs[1]
         kv_refs = refs[2 : 2 + n_blocks]
-        lo_ref, hi_ref, low_ref, own_ref = refs[2 + n_blocks :]
+        lo_ref, hi_ref, own_ref = refs[2 + n_blocks : 5 + n_blocks]
+        send_refs = refs[5 + n_blocks :]
         rows = lax.broadcasted_iota(jnp.int32, (seq_rows, tok_rows), 1)
         allowed = (lo_ref[...] <= rows) & (rows <= hi_ref[...])
         for k in range(kv_local):
@@ -78,16 +79,17 @@
                 dv = dv + jnp.dot(pb, gr, preferred_element_type=jnp.float32)
                 dk = dk + jnp.dot(ds, q, preferred_element_type=jnp.float32)
             dk = dk * scaling
-            low_ref[:, kcols] = dk.astype(jnp.bfloat16)
-            low_ref[:, vcols] = dv.astype(jnp.bfloat16)
             own_ref[:, kcols] = dk[:tok_rows]
             own_ref[:, vcols] = dv[:tok_rows]
+            for p, send_ref in enumerate(send_refs, start=1):
+                send_ref[:, kcols] = dk[p * tok_rows : (p + 1) * tok_rows].astype(jnp.bfloat16)
+                send_ref[:, vcols] = dv[p * tok_rows : (p + 1) * tok_rows].astype(jnp.bfloat16)
 
     return pl.pallas_call(
         kernel,
-        out_shape=(
-            jax.ShapeDtypeStruct((seq_rows, 2 * kv_cols), jnp.bfloat16),
-            jax.ShapeDtypeStruct((tok_rows, 2 * kv_cols), jnp.float32),
+        out_shape=(jax.ShapeDtypeStruct((tok_rows, 2 * kv_cols), jnp.float32),)
+        + tuple(
+            jax.ShapeDtypeStruct((tok_rows, 2 * kv_cols), jnp.bfloat16) for _ in range(n_blocks - 1)
         ),
     )(q3, g3, *kv_blocks, lower, upper)
 
@@ -129,11 +131,9 @@
     upper = jnp.where(kept == 1, never, col_pos - first_row)
     q3 = jnp.transpose(query[0], (1, 0, 2))
     g3 = jnp.transpose(grad_out[0], (1, 0, 2))
-    terms_low, kv_grad = attention_terms(
-        q3, g3, blocks, lower, upper, kv_local, head_dim, scaling
-    )
+    kv_grad, *parts = attention_terms(q3, g3, blocks, lower, upper, kv_local, head_dim, scaling)
     for d in range(1, ctx_len):
-        part = terms_low[d * tok_rows : (d + 1) * tok_rows]
+        part = parts[d - 1]
         kv_grad = kv_grad + shifted(part, "ctx", d, ctx_len, False).astype(jnp.float32)
     grad_key = kv_grad[:, :kv_cols].astype(jnp.bfloat16)
     grad_value = kv_grad[:, kv_cols:].astype(jnp.bfloat16)

time: 84.2 us -> 83.3 us (0.989)
  local copies, waits for them, and re-layouts: 5.46 us -> 4.4 us
    slice x1 -> x0, local copies, waits for them, and re-layouts: 1.06 us -> none  [per_device(): part = terms_low[d * tok_rows:(d + 1) * tok_rows]]
where the time goes in v13:
time: 83.3 us; the launch traced here: 82.9 us
  waiting for transfers between devices  44.5 us (53%)
  starting transfers between devices  18.6 us (22%)
  Pallas kernels  5.86 us (7%)
  matrix products  5.63 us (7%)
  local copies, waits for them, and re-layouts  4.4 us (5%)
  other arithmetic  3.57 us (4%)
    ppermute x4, waiting for transfers between devices, suffix_pipeline(): recv = lax.ppermute(acc.astype(jnp.bfloat16), axis, perm)  35.9 us
    ppermute x6, starting transfers between devices, shifted(): return lax.ppermute(x, axis, perm)  13.5 us
    ppermute x6, waiting for transfers between devices, shifted(): return lax.ppermute(x, axis, perm)  6.86 us
    pallas_call x1, Pallas kernels, attention_terms(): pl.pallas_call(kernel, out_shape=(jax.ShapeDtypeStruct((tok_rows, 2 * kv_...  5.86 us
    ppermute x4, starting transfers between devices, suffix_pipeline(): recv = lax.ppermute(acc.astype(jnp.bfloat16), axis, perm)  5.17 us
    unnamed x23, local copies, waits for them, and re-layouts  2.65 us
    dot_general x1, matrix products, per_device(): jnp.dot(tokens, w_value[0], preferred_element_type=jnp.float32)  2.02 us
    dot_general x2, matrix products, partial_for(): lax.dot_general(grad_key, wk, contract, preferred_element_type=jnp.float32)  1.99 us
  transfers between devices with their start and end apart: 11, of which 9 were waited for; matrix products, arithmetic and copies ran while one was open for 3% of the time, Pallas kernels for 0%

profile of v13, /device:TPU:0, one launch (start us, length us, event | category | flops | bytes accessed | tf_op | source)
XLA Modules:
  0.0 82.9 jit_solution(14160365460739477615)
XLA Ops:
  0.0 0.0 copy-start
  0.0 0.0 copy-start.4
  0.0 0.0 copy-start.1
  0.0 1.7 %copy-done = bf16[1,5120,256]{2,1,0:T(8,128)(2,1)S(1)} copy-done((bf16[1,5120,256]{2,1,0:T(8,128)(2,1)S(1)}, bf16[1,5120,256]{2,1,0:T(8,128)(2,1)}, u32[]{:S(2)}) %copy-start) | copy-done | bytes 2621464
  1.7 2.0 %fusion.25 = bf16[128,256]{1,0:T(8,128)(2,1)S(1)} fusion(bf16[1,5120,256]{2,1,0:T(8,128)(2,1)S(1)} %copy-done, bf16[1,128,5120]{2,1,0:T(8,128)(2,1)} %param.6), kind=kOutput, calls=%fused_computation.26 | convolution fusion | flops 335577088 | bytes 3997696 | tf_op jit(solution)/shard_map/dot_general | solution.py:109
  3.8 0.0 copy-done.4
  3.8 0.0 copy-done.1
  3.8 0.0 copy-start.9
  3.8 0.5 fusion.20
  4.3 0.0 copy-start.5
  4.3 4.9 %collective-permute-start = (bf16[128,512]{1,0:T(8,128)(2,1)S(1)}, bf16[128,512]{1,0:T(8,128)(2,1)S(1)}, u32[]{:S(2)}, u32[]{:S(2)}) collective-permute-start(bf16[128,512]{1,0:T(8,128)(2,1)S(1)} %pad_maximum_fusion.refs_2_), channel_id=1, source_target_pairs={{0,2},{2,4},{4,6},{1,3},{3,5},{5,7},{8,10},{10,12},{12,14},{9,11},... | collective-permute-start | bytes 393224 | tf_op jit(solution)/shard_map/ppermute | solution.py:18
  9.2 3.4 %collective-permute-start.1 = (bf16[128,512]{1,0:T(8,128)(2,1)S(1)}, bf16[128,512]{1,0:T(8,128)(2,1)S(1)}, u32[]{:S(2)}, u32[]{:S(2)}) collective-permute-start(bf16[128,512]{1,0:T(8,128)(2,1)S(1)} %pad_maximum_fusion.refs_2_), channel_id=1, source_target_pairs={{0,4},{2,6},{1,5},{3,7},{8,12},{10,14},{9,13},{11,15},{16,20},{18,... | collective-permute-start | bytes 393224 | tf_op jit(solution)/shard_map/ppermute | solution.py:18
  12.7 1.3 %collective-permute-start.2 = (bf16[128,512]{1,0:T(8,128)(2,1)S(1)}, bf16[128,512]{1,0:T(8,128)(2,1)S(1)}, u32[]{:S(2)}, u32[]{:S(2)}) collective-permute-start(bf16[128,512]{1,0:T(8,128)(2,1)S(1)} %pad_maximum_fusion.refs_2_), channel_id=1, source_target_pairs={{0,6},{1,7},{8,14},{9,15},{16,22},{17,23},{24,30},{25,31}} | collective-permute-start | bytes 393224 | tf_op jit(solution)/shard_map/ppermute | solution.py:18
  14.0 0.0 copy-done.9
  14.0 0.2 copy.25
  14.2 0.1 fusion.50
  14.3 0.1 fusion.48
  14.4 0.2 copy.24
  14.6 0.2 copy.28
  14.8 0.8 %broadcast_select_fusion = (s32[512,1]{1,0:T(8,128)}, s32[512,1]{1,0:T(8,128)}) fusion(pred[512,1]{1,0:T(8,128)(4,1)S(1)} %copy.25, s32[512,1]{1,0:T(8,128)S(1)} %copy.24, pred[1,512]{0,1:T(8,128)(4,1)S(1)} %copy.28), kind=kLoop, calls=%fused_computation.49 | loop fusion | flops 1024 | bytes 7168 | tf_op jit(solution)/shard_map/jit(_where)/select_n | solution.py:131
  15.6 0.0 collective-permute-done.refs_3_
  15.6 0.0 copy-start.6
  15.6 0.1 collective-permute-done.1.refs_4_
  15.7 0.0 copy-start.7
  15.7 0.8 collective-permute-done.2.refs_5_
  16.5 0.0 copy-done.5
  16.5 0.0 copy-done.6
  16.5 0.0 copy-done.7
  16.5 0.6 copy-done.8
  17.1 5.9 %shard_map.64 = (f32[128,512]{1,0:T(8,128)}, bf16[128,512]{1,0:T(8,128)(2,1)}, bf16[128,512]{1,0:T(8,128)(2,1)}, bf16[128,512]{1,0:T(8,128)(2,1)}) custom-call(bf16[10,128,128]{2,1,0:T(8,128)(2,1)} %bitcast.102, bf16[10,128,128]{2,1,0:T(8,128)(2,1)} %bitcast.103, bf16[128,512]{1,0:T(8,128)(2,1)} %copy-done.5, bf16[128,512]{1,0:T(8,128)(2,1)} %copy-done.6, ...), custom_call_target="tpu_custom_call" | custom-call | tf_op jit(solution)/shard_map/pallas_call | solution.py:88
  23.0 1.3 %collective-permute-start.5 = (bf16[128,512]{1,0:T(8,128)(2,1)}, bf16[128,512]{1,0:T(8,128)(2,1)S(1)}, u32[]{:S(2)}, u32[]{:S(2)}) collective-permute-start(bf16[128,512]{1,0:T(8,128)(2,1)} %get-tuple-element.12), channel_id=1, source_target_pairs={{6,0},{7,1},{14,8},{15,9},{22,16},{23,17},{30,24},{31,25}} | collective-permute-start | bytes 393224 | tf_op jit(solution)/shard_map/ppermute | solution.py:18
  24.3 1.3 %collective-permute-start.4 = (bf16[128,512]{1,0:T(8,128)(2,1)}, bf16[128,512]{1,0:T(8,128)(2,1)S(1)}, u32[]{:S(2)}, u32[]{:S(2)}) collective-permute-start(bf16[128,512]{1,0:T(8,128)(2,1)} %get-tuple-element.11), channel_id=1, source_target_pairs={{4,0},{6,2},{5,1},{7,3},{12,8},{14,10},{13,9},{15,11},{20,16},{22,... | collective-permute-start | bytes 393224 | tf_op jit(solution)/shard_map/ppermute | solution.py:18
  25.6 1.3 %collective-permute-start.3 = (bf16[128,512]{1,0:T(8,128)(2,1)}, bf16[128,512]{1,0:T(8,128)(2,1)S(1)}, u32[]{:S(2)}, u32[]{:S(2)}) collective-permute-start(bf16[128,512]{1,0:T(8,128)(2,1)} %get-tuple-element.10), channel_id=1, source_target_pairs={{2,0},{4,2},{6,4},{3,1},{5,3},{7,5},{10,8},{12,10},{14,12},{11,9},... | collective-permute-start | bytes 393224 | tf_op jit(solution)/shard_map/ppermute | solution.py:18
  26.9 0.0 copy-start.2
  26.9 4.3 %collective-permute-done.5 = bf16[128,512]{1,0:T(8,128)(2,1)S(1)} collective-permute-done((bf16[128,512]{1,0:T(8,128)(2,1)}, bf16[128,512]{1,0:T(8,128)(2,1)S(1)}, u32[]{:S(2)}, u32[]{:S(2)}) %collective-permute-start.5) | collective-permute-done | bytes 131104 | tf_op jit(solution)/shard_map/ppermute | solution.py:18
  31.2 1.7 %collective-permute-done.4 = bf16[128,512]{1,0:T(8,128)(2,1)S(1)} collective-permute-done((bf16[128,512]{1,0:T(8,128)(2,1)}, bf16[128,512]{1,0:T(8,128)(2,1)S(1)}, u32[]{:S(2)}, u32[]{:S(2)}) %collective-permute-start.4) | collective-permute-done | bytes 131104 | tf_op jit(solution)/shard_map/ppermute | solution.py:18
  32.9 0.0 collective-permute-done.3
  32.9 1.0 %add_convert_fusion = bf16[128,512]{1,0:T(8,128)(2,1)S(1)} fusion(bf16[128,512]{1,0:T(8,128)(2,1)S(1)} %collective-permute-done.5, bf16[128,512]{1,0:T(8,128)(2,1)S(1)} %collective-permute-done.4, f32[128,512]{1,0:T(8,128)} %get-tuple-element.9, bf16[128,512]{1,0:T(8,128)(2,1)S(1)} %collective-permute-done.3), kind=kLoop, calls=%fused_computation.46 | loop fusion | flops 458752 | bytes 786432 | tf_op jit(solution)/shard_map/convert.1
  33.9 0.6 fusion.8
  34.5 0.0 copy-done.2
  34.5 1.4 %fusion.1 = bf16[128,2560]{1,0:T(8,128)(2,1)} fusion(f32[128,2560]{1,0:T(8,128)S(1)} %fusion.8, bf16[1,5120,256]{2,1,0:T(8,128)(2,1)S(1)} %copy-done.2, s32[]{:T(128)S(6)} %select_n.30, bf16[128,512]{1,0:T(8,128)(2,1)S(1)} %add_convert_fusion), kind=kOutput, calls=%fused_computation.6 | convolution fusion | flops 168427520 | bytes 3342340 | tf_op jit(solution)/shard_map/dot_general | solution.py:149
  35.9 0.0 collective-permute-start.6
  35.9 0.6 fusion.11
  36.4 1.7 %collective-permute-done.6 = bf16[128,2560]{1,0:T(8,128)(2,1)S(1)} collective-permute-done((bf16[128,2560]{1,0:T(8,128)(2,1)}, bf16[128,2560]{1,0:T(8,128)(2,1)S(1)}, u32[]{:S(2)}, u32[]{:S(2)}) %collective-permute-start.6) | collective-permute-done | bytes 655392 | tf_op jit(solution)/shard_map/ppermute | solution.py:157
  38.2 0.0 copy-done.3
  38.2 0.6 fusion
  38.8 0.2 broadcast_in_dim.12
  39.0 1.0 %fusion.3 = f32[5,64,2560]{2,1,0:T(8,128)S(1)} fusion(s32[]{:T(128)S(6)} %select_n.31, f32[3,64,2560]{2,1,0:T(8,128)S(1)} %broadcast_in_dim.12, f32[2,64,2560]{2,1,0:T(8,128)S(1)} %bitcast.101), kind=kLoop, calls=%fused_computation.8 | loop fusion | flops 1638400 | bytes 6553604 | tf_op jit(solution)/shard_map/concatenate | solution.py:27
  40.0 1.3 %collective-permute-start.7 = (bf16[64,2560]{1,0:T(8,128)(2,1)S(1)}, bf16[64,2560]{1,0:T(8,128)(2,1)S(1)}, u32[]{:S(2)}, u32[]{:S(2)}) collective-permute-start(bf16[64,2560]{1,0:T(8,128)(2,1)S(1)} %fusion.39), channel_id=1, source_target_pairs={{8,0},{16,8},{24,16},{9,1},{17,9},{25,17},{10,2},{18,10},{26,18},{... | collective-permute-start | bytes 983048 | tf_op jit(solution)/shard_map/ppermute | solution.py:37
  41.4 10.3 %collective-permute-done.7 = bf16[64,2560]{1,0:T(8,128)(2,1)S(1)} collective-permute-done((bf16[64,2560]{1,0:T(8,128)(2,1)S(1)}, bf16[64,2560]{1,0:T(8,128)(2,1)S(1)}, u32[]{:S(2)}, u32[]{:S(2)}) %collective-permute-start.7) | collective-permute-done | bytes 327712 | tf_op jit(solution)/shard_map/ppermute | solution.py:37
  51.7 0.1 fusion.36
  51.8 1.3 %collective-permute-start.8 = (bf16[64,2560]{1,0:T(8,128)(2,1)S(1)}, bf16[64,2560]{1,0:T(8,128)(2,1)S(1)}, u32[]{:S(2)}, u32[]{:S(2)}) collective-permute-start(bf16[64,2560]{1,0:T(8,128)(2,1)S(1)} %fusion.36), channel_id=1, source_target_pairs={{8,0},{16,8},{24,16},{9,1},{17,9},{25,17},{10,2},{18,10},{26,18},{... | collective-permute-start | bytes 983048 | tf_op jit(solution)/shard_map/ppermute | solution.py:37
  53.1 0.1 bitcast_dynamic-update-slice_fusion.2
  53.1 9.4 %collective-permute-done.8 = bf16[64,2560]{1,0:T(8,128)(2,1)S(1)} collective-permute-done((bf16[64,2560]{1,0:T(8,128)(2,1)S(1)}, bf16[64,2560]{1,0:T(8,128)(2,1)S(1)}, u32[]{:S(2)}, u32[]{:S(2)}) %collective-permute-start.8) | collective-permute-done | bytes 327712 | tf_op jit(solution)/shard_map/ppermute | solution.py:37
  62.5 0.1 fusion.37
  62.6 1.3 %collective-permute-start.9 = (bf16[64,2560]{1,0:T(8,128)(2,1)S(1)}, bf16[64,2560]{1,0:T(8,128)(2,1)S(1)}, u32[]{:S(2)}, u32[]{:S(2)}) collective-permute-start(bf16[64,2560]{1,0:T(8,128)(2,1)S(1)} %fusion.37), channel_id=1, source_target_pairs={{8,0},{16,8},{24,16},{9,1},{17,9},{25,17},{10,2},{18,10},{26,18},{... | collective-permute-start | bytes 983048 | tf_op jit(solution)/shard_map/ppermute | solution.py:37
  63.9 0.1 bitcast_dynamic-update-slice_fusion.1
  64.0 8.5 %collective-permute-done.9 = bf16[64,2560]{1,0:T(8,128)(2,1)S(1)} collective-permute-done((bf16[64,2560]{1,0:T(8,128)(2,1)S(1)}, bf16[64,2560]{1,0:T(8,128)(2,1)S(1)}, u32[]{:S(2)}, u32[]{:S(2)}) %collective-permute-start.9) | collective-permute-done | bytes 327712 | tf_op jit(solution)/shard_map/ppermute | solution.py:37
  72.5 0.1 fusion.38
  72.6 1.3 %collective-permute-start.10 = (bf16[64,2560]{1,0:T(8,128)(2,1)S(1)}, bf16[64,2560]{1,0:T(8,128)(2,1)S(1)}, u32[]{:S(2)}, u32[]{:S(2)}) collective-permute-start(bf16[64,2560]{1,0:T(8,128)(2,1)S(1)} %fusion.38), channel_id=1, source_target_pairs={{8,0},{16,8},{24,16},{9,1},{17,9},{25,17},{10,2},{18,10},{26,18},{... | collective-permute-start | bytes 983048 | tf_op jit(solution)/shard_map/ppermute | solution.py:37
  73.9 0.1 bitcast_dynamic-update-slice_fusion
  74.0 7.7 %collective-permute-done.10 = bf16[64,2560]{1,0:T(8,128)(2,1)S(1)} collective-permute-done((bf16[64,2560]{1,0:T(8,128)(2,1)S(1)}, bf16[64,2560]{1,0:T(8,128)(2,1)S(1)}, u32[]{:S(2)}, u32[]{:S(2)}) %collective-permute-start.10) | collective-permute-done | bytes 327712 | tf_op jit(solution)/shard_map/ppermute | solution.py:37
  81.7 0.1 fusion.32
  81.8 1.2 %constant_dynamic-slice_fusion = f32[2,64,2560]{2,1,0:T(8,128)} fusion(f32[5,64,2560]{2,1,0:T(8,128)S(1)} %fusion.32, s32[]{:T(128)S(6)} %select_n.32), kind=kLoop, calls=%fused_computation.55 | loop fusion | bytes 2621444 | tf_op jit(solution)/shard_map/dynamic_slice | solution.py:39
  (9 shorter events, 0.1 us)
Async XLA Ops:
  0.0 1.7 %copy-start = (bf16[1,5120,256]{2,1,0:T(8,128)(2,1)S(1)}, bf16[1,5120,256]{2,1,0:T(8,128)(2,1)}, u32[]{:S(2)}) copy-start(bf16[1,5120,256]{2,1,0:T(8,128)(2,1)} %param.10) | copy-start | bytes 7864324
  0.0 3.8 %copy-start.4 = (bf16[1,128,5120]{2,1,0:T(8,128)(2,1)S(1)}, bf16[1,128,5120]{2,1,0:T(8,128)(2,1)}, u32[]{:S(2)}) copy-start(bf16[1,128,5120]{2,1,0:T(8,128)(2,1)} %param.6) | copy-start | bytes 3932164
  0.0 3.8 %copy-start.1 = (bf16[1,5120,256]{2,1,0:T(8,128)(2,1)S(1)}, bf16[1,5120,256]{2,1,0:T(8,128)(2,1)}, u32[]{:S(2)}) copy-start(bf16[1,5120,256]{2,1,0:T(8,128)(2,1)} %param.9) | copy-start | bytes 7864324
  3.8 10.2 %copy-start.9 = (s32[512]{0:T(512)S(1)}, s32[512]{0:T(512)}, u32[]{:S(2)}) copy-start(s32[512]{0:T(512)} %param.11) | copy-start | bytes 6148
  4.3 12.1 %copy-start.5 = (bf16[128,512]{1,0:T(8,128)(2,1)}, bf16[128,512]{1,0:T(8,128)(2,1)S(1)}, u32[]{:S(2)}) copy-start(bf16[128,512]{1,0:T(8,128)(2,1)S(1)} %pad_maximum_fusion.refs_2_) | copy-start | bytes 393220
  4.3 11.3 %collective-permute-start = (bf16[128,512]{1,0:T(8,128)(2,1)S(1)}, bf16[128,512]{1,0:T(8,128)(2,1)S(1)}, u32[]{:S(2)}, u32[]{:S(2)}) collective-permute-start(bf16[128,512]{1,0:T(8,128)(2,1)S(1)} %pad_maximum_fusion.refs_2_), channel_id=1, source_target_pairs={{0,2},{2,4},{4,6},{1,3},{3,5},{5,7},{8,10},{10,12},{12,14},{9,11},... | collective-permute-start | bytes 393224 | tf_op jit(solution)/shard_map/ppermute | solution.py:18
  9.2 6.5 %collective-permute-start.1 = (bf16[128,512]{1,0:T(8,128)(2,1)S(1)}, bf16[128,512]{1,0:T(8,128)(2,1)S(1)}, u32[]{:S(2)}, u32[]{:S(2)}) collective-permute-start(bf16[128,512]{1,0:T(8,128)(2,1)S(1)} %pad_maximum_fusion.refs_2_), channel_id=1, source_target_pairs={{0,4},{2,6},{1,5},{3,7},{8,12},{10,14},{9,13},{11,15},{16,20},{18,... | collective-permute-start | bytes 393224 | tf_op jit(solution)/shard_map/ppermute | solution.py:18
  12.7 3.8 %collective-permute-start.2 = (bf16[128,512]{1,0:T(8,128)(2,1)S(1)}, bf16[128,512]{1,0:T(8,128)(2,1)S(1)}, u32[]{:S(2)}, u32[]{:S(2)}) collective-permute-start(bf16[128,512]{1,0:T(8,128)(2,1)S(1)} %pad_maximum_fusion.refs_2_), channel_id=1, source_target_pairs={{0,6},{1,7},{8,14},{9,15},{16,22},{17,23},{24,30},{25,31}} | collective-permute-start | bytes 393224 | tf_op jit(solution)/shard_map/ppermute | solution.py:18
  15.6 0.9 %copy-start.6 = (bf16[128,512]{1,0:T(8,128)(2,1)}, bf16[128,512]{1,0:T(8,128)(2,1)S(1)}, u32[]{:S(2)}) copy-start(bf16[128,512]{1,0:T(8,128)(2,1)S(1)} %collective-permute-done.refs_3_) | copy-start | bytes 393220
  15.7 0.8 copy-start.7
  16.5 0.6 copy-start.8
  23.0 8.2 %collective-permute-start.5 = (bf16[128,512]{1,0:T(8,128)(2,1)}, bf16[128,512]{1,0:T(8,128)(2,1)S(1)}, u32[]{:S(2)}, u32[]{:S(2)}) collective-permute-start(bf16[128,512]{1,0:T(8,128)(2,1)} %get-tuple-element.12), channel_id=1, source_target_pairs={{6,0},{7,1},{14,8},{15,9},{22,16},{23,17},{30,24},{31,25}} | collective-permute-start | bytes 393224 | tf_op jit(solution)/shard_map/ppermute | solution.py:18
  24.3 8.6 %collective-permute-start.4 = (bf16[128,512]{1,0:T(8,128)(2,1)}, bf16[128,512]{1,0:T(8,128)(2,1)S(1)}, u32[]{:S(2)}, u32[]{:S(2)}) collective-permute-start(bf16[128,512]{1,0:T(8,128)(2,1)} %get-tuple-element.11), channel_id=1, source_target_pairs={{4,0},{6,2},{5,1},{7,3},{12,8},{14,10},{13,9},{15,11},{20,16},{22,... | collective-permute-start | bytes 393224 | tf_op jit(solution)/shard_map/ppermute | solution.py:18
  25.6 7.3 %collective-permute-start.3 = (bf16[128,512]{1,0:T(8,128)(2,1)}, bf16[128,512]{1,0:T(8,128)(2,1)S(1)}, u32[]{:S(2)}, u32[]{:S(2)}) collective-permute-start(bf16[128,512]{1,0:T(8,128)(2,1)} %get-tuple-element.10), channel_id=1, source_target_pairs={{2,0},{4,2},{6,4},{3,1},{5,3},{7,5},{10,8},{12,10},{14,12},{11,9},... | collective-permute-start | bytes 393224 | tf_op jit(solution)/shard_map/ppermute | solution.py:18
  26.9 7.6 %copy-start.2 = (bf16[1,5120,256]{2,1,0:T(8,128)(2,1)S(1)}, bf16[1,5120,256]{2,1,0:T(8,128)(2,1)}, u32[]{:S(2)}) copy-start(bf16[1,5120,256]{2,1,0:T(8,128)(2,1)} %param.9) | copy-start | bytes 7864324
  35.9 2.3 %collective-permute-start.6 = (bf16[128,2560]{1,0:T(8,128)(2,1)}, bf16[128,2560]{1,0:T(8,128)(2,1)S(1)}, u32[]{:S(2)}, u32[]{:S(2)}) collective-permute-start(bf16[128,2560]{1,0:T(8,128)(2,1)} %fusion.1), channel_id=1, source_target_pairs={{0,1},{1,0},{2,3},{3,2},{4,5},{5,4},{6,7},{7,6},{8,9},{9,8},{10,11... | collective-permute-start | bytes 1966088 | tf_op jit(solution)/shard_map/ppermute | solution.py:157
  35.9 2.3 %copy-start.3 = (bf16[1,5120,256]{2,1,0:T(8,128)(2,1)S(1)}, bf16[1,5120,256]{2,1,0:T(8,128)(2,1)}, u32[]{:S(2)}) copy-start(bf16[1,5120,256]{2,1,0:T(8,128)(2,1)} %param.9) | copy-start | bytes 7864324
  40.0 11.6 %collective-permute-start.7 = (bf16[64,2560]{1,0:T(8,128)(2,1)S(1)}, bf16[64,2560]{1,0:T(8,128)(2,1)S(1)}, u32[]{:S(2)}, u32[]{:S(2)}) collective-permute-start(bf16[64,2560]{1,0:T(8,128)(2,1)S(1)} %fusion.39), channel_id=1, source_target_pairs={{8,0},{16,8},{24,16},{9,1},{17,9},{25,17},{10,2},{18,10},{26,18},{... | collective-permute-start | bytes 983048 | tf_op jit(solution)/shard_map/ppermute | solution.py:37
  51.8 10.8 %collective-permute-start.8 = (bf16[64,2560]{1,0:T(8,128)(2,1)S(1)}, bf16[64,2560]{1,0:T(8,128)(2,1)S(1)}, u32[]{:S(2)}, u32[]{:S(2)}) collective-permute-start(bf16[64,2560]{1,0:T(8,128)(2,1)S(1)} %fusion.36), channel_id=1, source_target_pairs={{8,0},{16,8},{24,16},{9,1},{17,9},{25,17},{10,2},{18,10},{26,18},{... | collective-permute-start | bytes 983048 | tf_op jit(solution)/shard_map/ppermute | solution.py:37
  62.6 9.9 %collective-permute-start.9 = (bf16[64,2560]{1,0:T(8,128)(2,1)S(1)}, bf16[64,2560]{1,0:T(8,128)(2,1)S(1)}, u32[]{:S(2)}, u32[]{:S(2)}) collective-permute-start(bf16[64,2560]{1,0:T(8,128)(2,1)S(1)} %fusion.37), channel_id=1, source_target_pairs={{8,0},{16,8},{24,16},{9,1},{17,9},{25,17},{10,2},{18,10},{26,18},{... | collective-permute-start | bytes 983048 | tf_op jit(solution)/shard_map/ppermute | solution.py:37
  72.6 9.1 %collective-permute-start.10 = (bf16[64,2560]{1,0:T(8,128)(2,1)S(1)}, bf16[64,2560]{1,0:T(8,128)(2,1)S(1)}, u32[]{:S(2)}, u32[]{:S(2)}) collective-permute-start(bf16[64,2560]{1,0:T(8,128)(2,1)S(1)} %fusion.38), channel_id=1, source_target_pairs={{8,0},{16,8},{24,16},{9,1},{17,9},{25,17},{10,2},{18,10},{26,18},{... | collective-permute-start | bytes 983048 | tf_op jit(solution)/shard_map/ppermute | solution.py:37

commit v14 on v13

--- a/solution.py
+++ b/solution.py
@@ -23,21 +23,20 @@
     rows, cols = own.shape
     height = rows // n_chunks
     chunks = own.reshape(n_chunks, height, cols)
-    pad = jnp.zeros((length - 1, height, cols), own.dtype)
-    padded = jnp.concatenate((pad, chunks, pad), axis=0)
     steps = n_chunks + length - 1
-    ordered = lax.dynamic_slice_in_dim(padded, index, steps, axis=0)
-    perm = [(i, i - 1) for i in range(1, length)]
     recv = jnp.zeros((height, cols), jnp.bfloat16)
-    done = []
+    out = jnp.zeros((n_chunks, height, cols), jnp.float32)
     for tau in range(steps):
-        acc = ordered[tau] + recv.astype(jnp.float32)
-        done.append(acc)
-        if tau < steps - 1:
+        which = tau - (length - 1 - index)
+        at = jnp.clip(which, 0, n_chunks - 1)
+        acc = lax.dynamic_index_in_dim(chunks, at, 0, keepdims=False) + recv.astype(jnp.float32)
+        perm = [(i, i - 1) for i in range(1, length) if 0 <= tau - (length - 1 - i) < n_chunks]
+        if perm:
             recv = lax.ppermute(acc.astype(jnp.bfloat16), axis, perm)
-    stacked = jnp.stack(done, axis=0)
-    mine = lax.dynamic_slice_in_dim(stacked, length - 1 - index, n_chunks, axis=0)
-    return mine.reshape(rows, cols)
+        valid = (which >= 0) & (which < n_chunks)
+        cur = lax.dynamic_index_in_dim(out, at, 0, keepdims=False)
+        out = lax.dynamic_update_index_in_dim(out, jnp.where(valid, acc, cur), at, 0)
+    return out.reshape(rows, cols)
 
 
 def attention_terms(q3, g3, kv_blocks, lower, upper, kv_local, head_dim, scaling):

time: 83.3 us -> 83.7 us (level)
  starting transfers between devices: 18.6 us -> 17.4 us
  waiting for transfers between devices: 44.5 us -> 45.7 us
  local copies, waits for them, and re-layouts: 4.4 us -> 5.56 us
    unnamed x23 -> x24, local copies, waits for them, and re-layouts: 2.65 us -> 4.83 us
    ppermute x4, starting transfers between devices: 5.17 us -> 3.95 us  [suffix_pipeline(): recv = lax.ppermute(acc.astype(jnp.bfloat16), axis, perm)]
    ppermute x4, waiting for transfers between devices: 35.9 us -> 37.1 us  [suffix_pipeline(): recv = lax.ppermute(acc.astype(jnp.bfloat16), axis, perm)]
    concatenate x1 -> x0, other arithmetic: 0.99 us -> none  [suffix_pipeline(): padded = jnp.concatenate((pad, chunks, pad), axis=0)]
    dynamic_slice x1 -> x4, local copies, waits for them, and re-layouts: 1.16 us -> 0.21 us  [suffix_pipeline(): cur = lax.dynamic_index_in_dim(out, at, 0, keepdims=False)]
  transfers between devices with their start and end apart: 11 -> 11, of which waited for: 9 -> 7; matrix products, arithmetic and copies ran while one was open for 3% -> 3% of each run, Pallas kernels for 0% -> 0%
where the time goes in v14:
time: 83.7 us; the launch traced here: 83.4 us
  waiting for transfers between devices  45.7 us (55%)
  starting transfers between devices  17.4 us (21%)
  Pallas kernels  5.88 us (7%)
  matrix products  5.63 us (7%)
  local copies, waits for them, and re-layouts  5.56 us (7%)
  other arithmetic  2.81 us (3%)
    ppermute x4, waiting for transfers between devices, suffix_pipeline(): recv = lax.ppermute(acc.astype(jnp.bfloat16), axis, perm)  37.1 us
    ppermute x6, starting transfers between devices, shifted(): return lax.ppermute(x, axis, perm)  13.5 us
    ppermute x6, waiting for transfers between devices, shifted(): return lax.ppermute(x, axis, perm)  6.85 us
    pallas_call x1, Pallas kernels, attention_terms(): pl.pallas_call(kernel, out_shape=(jax.ShapeDtypeStruct((tok_rows, 2 * kv_...  5.88 us
    unnamed x24, local copies, waits for them, and re-layouts  4.83 us
    ppermute x4, starting transfers between devices, suffix_pipeline(): recv = lax.ppermute(acc.astype(jnp.bfloat16), axis, perm)  3.95 us
    dot_general x1, matrix products, per_device(): jnp.dot(tokens, w_value[0], preferred_element_type=jnp.float32)  2.02 us
    dot_general x2, matrix products, partial_for(): lax.dot_general(grad_key, wk, contract, preferred_element_type=jnp.float32)  1.98 us
  transfers between devices with their start and end apart: 11, of which 7 were waited for; matrix products, arithmetic and copies ran while one was open for 3% of the time, Pallas kernels for 0%

profile of v14, /device:TPU:0, one launch (start us, length us, event | category | flops | bytes accessed | tf_op | source)
XLA Modules:
  0.0 83.4 jit_solution(13816099401920970076)
XLA Ops:
  0.0 0.0 copy-start
  0.0 1.7 %copy-done = bf16[1,5120,256]{2,1,0:T(8,128)(2,1)S(1)} copy-done((bf16[1,5120,256]{2,1,0:T(8,128)(2,1)S(1)}, bf16[1,5120,256]{2,1,0:T(8,128)(2,1)}, u32[]{:S(2)}) %copy-start) | copy-done | bytes 2621464
  1.7 2.0 %fusion.23 = bf16[128,256]{1,0:T(8,128)(2,1)S(1)} fusion(bf16[1,5120,256]{2,1,0:T(8,128)(2,1)S(1)} %copy-done, bf16[1,128,5120]{2,1,0:T(8,128)(2,1)} %param.6), kind=kOutput, calls=%fused_computation.21 | convolution fusion | flops 335577088 | bytes 3997696 | tf_op jit(solution)/shard_map/dot_general | solution.py:108
  3.8 0.0 copy-done.5
  3.8 0.0 copy-done.2
  3.8 0.0 copy-start.10
  3.8 0.5 fusion.18
  4.3 0.0 copy-start.6
  4.3 4.9 %collective-permute-start = (bf16[128,512]{1,0:T(8,128)(2,1)S(1)}, bf16[128,512]{1,0:T(8,128)(2,1)S(1)}, u32[]{:S(2)}, u32[]{:S(2)}) collective-permute-start(bf16[128,512]{1,0:T(8,128)(2,1)S(1)} %pad_maximum_fusion.refs_2_), channel_id=1, source_target_pairs={{0,2},{2,4},{4,6},{1,3},{3,5},{5,7},{8,10},{10,12},{12,14},{9,11},... | collective-permute-start | bytes 393224 | tf_op jit(solution)/shard_map/ppermute | solution.py:18
  9.2 3.4 %collective-permute-start.1 = (bf16[128,512]{1,0:T(8,128)(2,1)S(1)}, bf16[128,512]{1,0:T(8,128)(2,1)S(1)}, u32[]{:S(2)}, u32[]{:S(2)}) collective-permute-start(bf16[128,512]{1,0:T(8,128)(2,1)S(1)} %pad_maximum_fusion.refs_2_), channel_id=1, source_target_pairs={{0,4},{2,6},{1,5},{3,7},{8,12},{10,14},{9,13},{11,15},{16,20},{18,... | collective-permute-start | bytes 393224 | tf_op jit(solution)/shard_map/ppermute | solution.py:18
  12.7 1.3 %collective-permute-start.2 = (bf16[128,512]{1,0:T(8,128)(2,1)S(1)}, bf16[128,512]{1,0:T(8,128)(2,1)S(1)}, u32[]{:S(2)}, u32[]{:S(2)}) collective-permute-start(bf16[128,512]{1,0:T(8,128)(2,1)S(1)} %pad_maximum_fusion.refs_2_), channel_id=1, source_target_pairs={{0,6},{1,7},{8,14},{9,15},{16,22},{17,23},{24,30},{25,31}} | collective-permute-start | bytes 393224 | tf_op jit(solution)/shard_map/ppermute | solution.py:18
  14.0 0.0 copy-done.10
  14.0 0.2 copy.25
  14.2 0.1 fusion.42
  14.3 0.1 fusion.40
  14.4 0.2 copy.24
  14.6 0.2 copy.28
  14.8 0.9 %broadcast_select_fusion = (s32[512,1]{1,0:T(8,128)}, s32[512,1]{1,0:T(8,128)}) fusion(pred[512,1]{1,0:T(8,128)(4,1)S(1)} %copy.25, s32[512,1]{1,0:T(8,128)S(1)} %copy.24, pred[1,512]{0,1:T(8,128)(4,1)S(1)} %copy.28), kind=kLoop, calls=%fused_computation.43 | loop fusion | flops 1024 | bytes 7168 | tf_op jit(solution)/shard_map/jit(_where)/select_n | solution.py:130
  15.6 0.0 collective-permute-done.refs_3_
  15.6 0.1 collective-permute-done.1.refs_4_
  15.7 0.8 collective-permute-done.2.refs_5_
  16.5 0.0 copy-done.6
  16.5 0.0 copy-done.7
  16.5 0.0 copy-done.8
  16.5 0.6 copy-done.9
  17.1 5.9 %shard_map.64 = (f32[128,512]{1,0:T(8,128)}, bf16[128,512]{1,0:T(8,128)(2,1)}, bf16[128,512]{1,0:T(8,128)(2,1)}, bf16[128,512]{1,0:T(8,128)(2,1)}) custom-call(bf16[10,128,128]{2,1,0:T(8,128)(2,1)} %bitcast.114, bf16[10,128,128]{2,1,0:T(8,128)(2,1)} %bitcast.115, bf16[128,512]{1,0:T(8,128)(2,1)} %copy-done.6, bf16[128,512]{1,0:T(8,128)(2,1)} %copy-done.7, ...), custom_call_target="tpu_custom_call" | custom-call | tf_op jit(solution)/shard_map/pallas_call | solution.py:87
  23.0 1.3 %collective-permute-start.5 = (bf16[128,512]{1,0:T(8,128)(2,1)}, bf16[128,512]{1,0:T(8,128)(2,1)S(1)}, u32[]{:S(2)}, u32[]{:S(2)}) collective-permute-start(bf16[128,512]{1,0:T(8,128)(2,1)} %get-tuple-element.12), channel_id=1, source_target_pairs={{6,0},{7,1},{14,8},{15,9},{22,16},{23,17},{30,24},{31,25}} | collective-permute-start | bytes 393224 | tf_op jit(solution)/shard_map/ppermute | solution.py:18
  24.3 1.3 %collective-permute-start.4 = (bf16[128,512]{1,0:T(8,128)(2,1)}, bf16[128,512]{1,0:T(8,128)(2,1)S(1)}, u32[]{:S(2)}, u32[]{:S(2)}) collective-permute-start(bf16[128,512]{1,0:T(8,128)(2,1)} %get-tuple-element.11), channel_id=1, source_target_pairs={{4,0},{6,2},{5,1},{7,3},{12,8},{14,10},{13,9},{15,11},{20,16},{22,... | collective-permute-start | bytes 393224 | tf_op jit(solution)/shard_map/ppermute | solution.py:18
  25.6 1.3 %collective-permute-start.3 = (bf16[128,512]{1,0:T(8,128)(2,1)}, bf16[128,512]{1,0:T(8,128)(2,1)S(1)}, u32[]{:S(2)}, u32[]{:S(2)}) collective-permute-start(bf16[128,512]{1,0:T(8,128)(2,1)} %get-tuple-element.10), channel_id=1, source_target_pairs={{2,0},{4,2},{6,4},{3,1},{5,3},{7,5},{10,8},{12,10},{14,12},{11,9},... | collective-permute-start | bytes 393224 | tf_op jit(solution)/shard_map/ppermute | solution.py:18
  26.9 4.3 %collective-permute-done.5 = bf16[128,512]{1,0:T(8,128)(2,1)S(1)} collective-permute-done((bf16[128,512]{1,0:T(8,128)(2,1)}, bf16[128,512]{1,0:T(8,128)(2,1)S(1)}, u32[]{:S(2)}, u32[]{:S(2)}) %collective-permute-start.5) | collective-permute-done | bytes 131104 | tf_op jit(solution)/shard_map/ppermute | solution.py:18
  31.2 1.7 %collective-permute-done.4 = bf16[128,512]{1,0:T(8,128)(2,1)S(1)} collective-permute-done((bf16[128,512]{1,0:T(8,128)(2,1)}, bf16[128,512]{1,0:T(8,128)(2,1)S(1)}, u32[]{:S(2)}, u32[]{:S(2)}) %collective-permute-start.4) | collective-permute-done | bytes 131104 | tf_op jit(solution)/shard_map/ppermute | solution.py:18
  32.9 0.0 collective-permute-done.3
  32.9 1.0 %add_convert_fusion = bf16[128,512]{1,0:T(8,128)(2,1)S(1)} fusion(bf16[128,512]{1,0:T(8,128)(2,1)S(1)} %collective-permute-done.5, bf16[128,512]{1,0:T(8,128)(2,1)S(1)} %collective-permute-done.4, f32[128,512]{1,0:T(8,128)} %get-tuple-element.9, bf16[128,512]{1,0:T(8,128)(2,1)S(1)} %collective-permute-done.3), kind=kLoop, calls=%fused_computation.40 | loop fusion | flops 458752 | bytes 786432 | tf_op jit(solution)/shard_map/convert.1
  33.9 0.0 copy-start.3
  33.9 0.6 fusion.6
  34.5 1.2 %copy-done.3 = bf16[1,5120,256]{2,1,0:T(8,128)(2,1)S(1)} copy-done((bf16[1,5120,256]{2,1,0:T(8,128)(2,1)S(1)}, bf16[1,5120,256]{2,1,0:T(8,128)(2,1)}, u32[]{:S(2)}) %copy-start.3) | copy-done | bytes 2621464
  35.7 1.4 %fusion.1 = bf16[128,2560]{1,0:T(8,128)(2,1)} fusion(f32[128,2560]{1,0:T(8,128)S(1)} %fusion.6, bf16[1,5120,256]{2,1,0:T(8,128)(2,1)S(1)} %copy-done.3, s32[]{:T(128)S(6)} %select_n.75, bf16[128,512]{1,0:T(8,128)(2,1)S(1)} %add_convert_fusion), kind=kOutput, calls=%fused_computation.3 | convolution fusion | flops 168427520 | bytes 3342340 | tf_op jit(solution)/shard_map/dot_general | solution.py:148
  37.1 0.0 collective-permute-start.6
  37.1 0.6 fusion.9
  37.6 1.7 %collective-permute-done.6 = bf16[128,2560]{1,0:T(8,128)(2,1)S(1)} collective-permute-done((bf16[128,2560]{1,0:T(8,128)(2,1)}, bf16[128,2560]{1,0:T(8,128)(2,1)S(1)}, u32[]{:S(2)}, u32[]{:S(2)}) %collective-permute-start.6) | collective-permute-done | bytes 655392 | tf_op jit(solution)/shard_map/ppermute | solution.py:156
  39.4 0.6 fusion
  40.0 0.7 collective-permute-start.7
  40.7 0.1 broadcast_in_dim.28
  40.8 0.1 select_dynamic-update-slice_fusion
  40.9 0.1 constant_dynamic-slice_fusion.3
  41.0 0.0 collective-permute-done.7
  41.0 0.1 fusion.28
  41.0 0.7 collective-permute-start.8
  41.7 0.1 bitcast_dynamic-update-slice_fusion.3
  41.9 0.1 constant_dynamic-slice_fusion.2
  41.9 0.0 collective-permute-done.8
  41.9 0.1 fusion.29
  42.0 1.3 %collective-permute-start.9 = (bf16[64,2560]{1,0:T(8,128)(2,1)S(1)}, bf16[64,2560]{1,0:T(8,128)(2,1)S(1)}, u32[]{:S(2)}, u32[]{:S(2)}) collective-permute-start(bf16[64,2560]{1,0:T(8,128)(2,1)S(1)} %fusion.29), channel_id=1, source_target_pairs={{8,0},{16,8},{9,1},{17,9},{10,2},{18,10},{11,3},{19,11},{12,4},{20... | collective-permute-start | bytes 983048 | tf_op jit(solution)/shard_map/ppermute | solution.py:35
  43.3 0.1 bitcast_dynamic-update-slice_fusion.2
  43.4 0.1 constant_dynamic-slice_fusion.1
  43.5 29.0 %collective-permute-done.9 = bf16[64,2560]{1,0:T(8,128)(2,1)S(1)} collective-permute-done((bf16[64,2560]{1,0:T(8,128)(2,1)S(1)}, bf16[64,2560]{1,0:T(8,128)(2,1)S(1)}, u32[]{:S(2)}, u32[]{:S(2)}) %collective-permute-start.9) | collective-permute-done | bytes 327712 | tf_op jit(solution)/shard_map/ppermute | solution.py:35
  72.5 0.1 fusion.30
  72.6 1.3 %collective-permute-start.10 = (bf16[64,2560]{1,0:T(8,128)(2,1)S(1)}, bf16[64,2560]{1,0:T(8,128)(2,1)S(1)}, u32[]{:S(2)}, u32[]{:S(2)}) collective-permute-start(bf16[64,2560]{1,0:T(8,128)(2,1)S(1)} %fusion.30), channel_id=1, source_target_pairs={{8,0},{9,1},{10,2},{11,3},{12,4},{13,5},{14,6},{15,7}} | collective-permute-start | bytes 983048 | tf_op jit(solution)/shard_map/ppermute | solution.py:35
  73.9 0.1 bitcast_dynamic-update-slice_fusion.1
  74.0 0.1 constant_dynamic-slice_fusion
  74.0 8.1 %collective-permute-done.10 = bf16[64,2560]{1,0:T(8,128)(2,1)S(1)} collective-permute-done((bf16[64,2560]{1,0:T(8,128)(2,1)S(1)}, bf16[64,2560]{1,0:T(8,128)(2,1)S(1)}, u32[]{:S(2)}, u32[]{:S(2)}) %collective-permute-start.10) | collective-permute-done | bytes 327712 | tf_op jit(solution)/shard_map/ppermute | solution.py:35
  82.2 0.1 bitcast_dynamic-update-slice_fusion
  82.3 0.0 copy-start.1
  82.3 1.0 %copy-done.1 = f32[2,64,2560]{2,1,0:T(8,128)} copy-done((f32[2,64,2560]{2,1,0:T(8,128)}, f32[2,64,2560]{2,1,0:T(8,128)S(1)}, u32[]{:S(2)}) %copy-start.1) | copy-done | bytes 1310744
  (13 shorter events, 0.1 us)
Async XLA Ops:
  0.0 1.7 %copy-start = (bf16[1,5120,256]{2,1,0:T(8,128)(2,1)S(1)}, bf16[1,5120,256]{2,1,0:T(8,128)(2,1)}, u32[]{:S(2)}) copy-start(bf16[1,5120,256]{2,1,0:T(8,128)(2,1)} %param.10) | copy-start | bytes 7864324
  0.0 3.8 %copy-start.5 = (bf16[1,128,5120]{2,1,0:T(8,128)(2,1)S(1)}, bf16[1,128,5120]{2,1,0:T(8,128)(2,1)}, u32[]{:S(2)}) copy-start(bf16[1,128,5120]{2,1,0:T(8,128)(2,1)} %param.6) | copy-start | bytes 3932164
  0.0 3.8 %copy-start.2 = (bf16[1,5120,256]{2,1,0:T(8,128)(2,1)S(1)}, bf16[1,5120,256]{2,1,0:T(8,128)(2,1)}, u32[]{:S(2)}) copy-start(bf16[1,5120,256]{2,1,0:T(8,128)(2,1)} %param.9) | copy-start | bytes 7864324
  3.8 10.2 %copy-start.10 = (s32[512]{0:T(512)S(1)}, s32[512]{0:T(512)}, u32[]{:S(2)}) copy-start(s32[512]{0:T(512)} %param.11) | copy-start | bytes 6148
  4.3 12.1 %copy-start.6 = (bf16[128,512]{1,0:T(8,128)(2,1)}, bf16[128,512]{1,0:T(8,128)(2,1)S(1)}, u32[]{:S(2)}) copy-start(bf16[128,512]{1,0:T(8,128)(2,1)S(1)} %pad_maximum_fusion.refs_2_) | copy-start | bytes 393220
  4.3 11.3 %collective-permute-start = (bf16[128,512]{1,0:T(8,128)(2,1)S(1)}, bf16[128,512]{1,0:T(8,128)(2,1)S(1)}, u32[]{:S(2)}, u32[]{:S(2)}) collective-permute-start(bf16[128,512]{1,0:T(8,128)(2,1)S(1)} %pad_maximum_fusion.refs_2_), channel_id=1, source_target_pairs={{0,2},{2,4},{4,6},{1,3},{3,5},{5,7},{8,10},{10,12},{12,14},{9,11},... | collective-permute-start | bytes 393224 | tf_op jit(solution)/shard_map/ppermute | solution.py:18
  9.2 6.5 %collective-permute-start.1 = (bf16[128,512]{1,0:T(8,128)(2,1)S(1)}, bf16[128,512]{1,0:T(8,128)(2,1)S(1)}, u32[]{:S(2)}, u32[]{:S(2)}) collective-permute-start(bf16[128,512]{1,0:T(8,128)(2,1)S(1)} %pad_maximum_fusion.refs_2_), channel_id=1, source_target_pairs={{0,4},{2,6},{1,5},{3,7},{8,12},{10,14},{9,13},{11,15},{16,20},{18,... | collective-permute-start | bytes 393224 | tf_op jit(solution)/shard_map/ppermute | solution.py:18
  12.7 3.8 %collective-permute-start.2 = (bf16[128,512]{1,0:T(8,128)(2,1)S(1)}, bf16[128,512]{1,0:T(8,128)(2,1)S(1)}, u32[]{:S(2)}, u32[]{:S(2)}) collective-permute-start(bf16[128,512]{1,0:T(8,128)(2,1)S(1)} %pad_maximum_fusion.refs_2_), channel_id=1, source_target_pairs={{0,6},{1,7},{8,14},{9,15},{16,22},{17,23},{24,30},{25,31}} | collective-permute-start | bytes 393224 | tf_op jit(solution)/shard_map/ppermute | solution.py:18
  15.6 0.9 %copy-start.7 = (bf16[128,512]{1,0:T(8,128)(2,1)}, bf16[128,512]{1,0:T(8,128)(2,1)S(1)}, u32[]{:S(2)}) copy-start(bf16[128,512]{1,0:T(8,128)(2,1)S(1)} %collective-permute-done.refs_3_) | copy-start | bytes 393220
  15.7 0.8 copy-start.8
  16.5 0.7 copy-start.9
  23.0 8.2 %collective-permute-start.5 = (bf16[128,512]{1,0:T(8,128)(2,1)}, bf16[128,512]{1,0:T(8,128)(2,1)S(1)}, u32[]{:S(2)}, u32[]{:S(2)}) collective-permute-start(bf16[128,512]{1,0:T(8,128)(2,1)} %get-tuple-element.12), channel_id=1, source_target_pairs={{6,0},{7,1},{14,8},{15,9},{22,16},{23,17},{30,24},{31,25}} | collective-permute-start | bytes 393224 | tf_op jit(solution)/shard_map/ppermute | solution.py:18
  24.3 8.6 %collective-permute-start.4 = (bf16[128,512]{1,0:T(8,128)(2,1)}, bf16[128,512]{1,0:T(8,128)(2,1)S(1)}, u32[]{:S(2)}, u32[]{:S(2)}) collective-permute-start(bf16[128,512]{1,0:T(8,128)(2,1)} %get-tuple-element.11), channel_id=1, source_target_pairs={{4,0},{6,2},{5,1},{7,3},{12,8},{14,10},{13,9},{15,11},{20,16},{22,... | collective-permute-start | bytes 393224 | tf_op jit(solution)/shard_map/ppermute | solution.py:18
  25.6 7.3 %collective-permute-start.3 = (bf16[128,512]{1,0:T(8,128)(2,1)}, bf16[128,512]{1,0:T(8,128)(2,1)S(1)}, u32[]{:S(2)}, u32[]{:S(2)}) collective-permute-start(bf16[128,512]{1,0:T(8,128)(2,1)} %get-tuple-element.10), channel_id=1, source_target_pairs={{2,0},{4,2},{6,4},{3,1},{5,3},{7,5},{10,8},{12,10},{14,12},{11,9},... | collective-permute-start | bytes 393224 | tf_op jit(solution)/shard_map/ppermute | solution.py:18
  33.9 1.7 %copy-start.3 = (bf16[1,5120,256]{2,1,0:T(8,128)(2,1)S(1)}, bf16[1,5120,256]{2,1,0:T(8,128)(2,1)}, u32[]{:S(2)}) copy-start(bf16[1,5120,256]{2,1,0:T(8,128)(2,1)} %param.9) | copy-start | bytes 7864324
  37.1 2.3 %collective-permute-start.6 = (bf16[128,2560]{1,0:T(8,128)(2,1)}, bf16[128,2560]{1,0:T(8,128)(2,1)S(1)}, u32[]{:S(2)}, u32[]{:S(2)}) collective-permute-start(bf16[128,2560]{1,0:T(8,128)(2,1)} %fusion.1), channel_id=1, source_target_pairs={{0,1},{1,0},{2,3},{3,2},{4,5},{5,4},{6,7},{7,6},{8,9},{9,8},{10,11... | collective-permute-start | bytes 1966088 | tf_op jit(solution)/shard_map/ppermute | solution.py:156
  37.1 2.3 %copy-start.4 = (bf16[1,5120,256]{2,1,0:T(8,128)(2,1)S(1)}, bf16[1,5120,256]{2,1,0:T(8,128)(2,1)}, u32[]{:S(2)}) copy-start(bf16[1,5120,256]{2,1,0:T(8,128)(2,1)} %param.9) | copy-start | bytes 7864324
  40.0 0.9 %collective-permute-start.7 = (bf16[64,2560]{1,0:T(8,128)(2,1)S(1)}, bf16[64,2560]{1,0:T(8,128)(2,1)S(1)}, u32[]{:S(2)}, u32[]{:S(2)}) collective-permute-start(bf16[64,2560]{1,0:T(8,128)(2,1)S(1)} %fusion.31), channel_id=1, source_target_pairs={{24,16},{25,17},{26,18},{27,19},{28,20},{29,21},{30,22},{31,23}} | collective-permute-start | bytes 983048 | tf_op jit(solution)/shard_map/ppermute | solution.py:35
  41.0 0.9 %collective-permute-start.8 = (bf16[64,2560]{1,0:T(8,128)(2,1)S(1)}, bf16[64,2560]{1,0:T(8,128)(2,1)S(1)}, u32[]{:S(2)}, u32[]{:S(2)}) collective-permute-start(bf16[64,2560]{1,0:T(8,128)(2,1)S(1)} %fusion.28), channel_id=1, source_target_pairs={{16,8},{24,16},{17,9},{25,17},{18,10},{26,18},{19,11},{27,19},{20,... | collective-permute-start | bytes 983048 | tf_op jit(solution)/shard_map/ppermute | solution.py:35
  42.0 30.5 %collective-permute-start.9 = (bf16[64,2560]{1,0:T(8,128)(2,1)S(1)}, bf16[64,2560]{1,0:T(8,128)(2,1)S(1)}, u32[]{:S(2)}, u32[]{:S(2)}) collective-permute-start(bf16[64,2560]{1,0:T(8,128)(2,1)S(1)} %fusion.29), channel_id=1, source_target_pairs={{8,0},{16,8},{9,1},{17,9},{10,2},{18,10},{11,3},{19,11},{12,4},{20... | collective-permute-start | bytes 983048 | tf_op jit(solution)/shard_map/ppermute | solution.py:35
  72.6 9.6 %collective-permute-start.10 = (bf16[64,2560]{1,0:T(8,128)(2,1)S(1)}, bf16[64,2560]{1,0:T(8,128)(2,1)S(1)}, u32[]{:S(2)}, u32[]{:S(2)}) collective-permute-start(bf16[64,2560]{1,0:T(8,128)(2,1)S(1)} %fusion.30), channel_id=1, source_target_pairs={{8,0},{9,1},{10,2},{11,3},{12,4},{13,5},{14,6},{15,7}} | collective-permute-start | bytes 983048 | tf_op jit(solution)/shard_map/ppermute | solution.py:35
  82.3 1.1 %copy-start.1 = (f32[2,64,2560]{2,1,0:T(8,128)}, f32[2,64,2560]{2,1,0:T(8,128)S(1)}, u32[]{:S(2)}) copy-start(f32[2,64,2560]{2,1,0:T(8,128)S(1)} %bitcast_dynamic-update-slice_fusion) | copy-start | bytes 3932164

commit v15 on v13

--- a/solution.py
+++ b/solution.py
@@ -135,29 +135,33 @@
     for d in range(1, ctx_len):
         part = parts[d - 1]
         kv_grad = kv_grad + shifted(part, "ctx", d, ctx_len, False).astype(jnp.float32)
-    grad_key = kv_grad[:, :kv_cols].astype(jnp.bfloat16)
-    grad_value = kv_grad[:, kv_cols:].astype(jnp.bfloat16)
+    grads_low = kv_grad.astype(jnp.bfloat16)
     contract = (((1,), (1,)), ((), ()))
     head_len = lax.axis_size("head")
     head_index = lax.axis_index("head")
     out_cols = w_key.shape[1] // head_len
 
-    def partial_for(b):
+    def rows_of(b):
         start = b * out_cols
         wk = lax.dynamic_slice_in_dim(w_key[0], start, out_cols, axis=0)
         wv = lax.dynamic_slice_in_dim(w_value[0], start, out_cols, axis=0)
-        part = lax.dot_general(grad_key, wk, contract, preferred_element_type=jnp.float32)
-        return part + lax.dot_general(grad_value, wv, contract, preferred_element_type=jnp.float32)
+        return wk, wv
 
-    received = []
+    def product(grads, wk, wv):
+        part = lax.dot_general(grads[:, :kv_cols], wk, contract, preferred_element_type=jnp.float32)
+        return part + lax.dot_general(
+            grads[:, kv_cols:], wv, contract, preferred_element_type=jnp.float32
+        )
+
+    sources = []
     for d in range(1, head_len):
-        target = lax.rem(head_index + d, head_len)
-        send = partial_for(target).astype(jnp.bfloat16)
         perm = [(h, (h + d) % head_len) for h in range(head_len)]
-        received.append(lax.ppermute(send, "head", perm))
-    reduced = partial_for(head_index)
-    for got in received:
-        reduced = reduced + got.astype(jnp.float32)
+        wk, wv = rows_of(lax.rem(head_index + d, head_len))
+        weights = lax.ppermute(jnp.concatenate((wk, wv), axis=1), "head", perm)
+        sources.append((lax.ppermute(grads_low, "head", perm), weights))
+    reduced = product(grads_low, *rows_of(head_index))
+    for grads, weights in sources:
+        reduced = reduced + product(grads, weights[:, :kv_cols], weights[:, kv_cols:])
     result = suffix_pipeline(reduced, "segment", CHAIN_CHUNKS)
     return result[None]
 

time: 83.3 us -> 88.4 us (1.061)
  matrix products: 5.63 us -> 7.37 us
  other arithmetic: 3.57 us -> 5.3 us
  local copies, waits for them, and re-layouts: 4.4 us -> 5.66 us
    dot_general x4, matrix products: 3.11 us -> 6.35 us  [the longest x2 3.75 us: product(): lax.dot_general(grads[:, kv_cols:], wv, contract, preferred_element_type=...]
    dynamic_slice x0 -> x1, local copies, waits for them, and re-layouts: none -> 1.98 us  [rows_of(): wv = lax.dynamic_slice_in_dim(w_value[0], start, out_cols, axis=0)]
    ppermute x1 -> x2, waiting for transfers between devices: 1.74 us -> 0.01 us  [the longest x1 0.01 us: per_device(): sources.append((lax.ppermute(grads_low, 'head', perm), weights))]
    concatenate x0 -> x1, other arithmetic: none -> 1.72 us  [per_device(): weights = lax.ppermute(jnp.concatenate((wk, wv), axis=1), 'head', perm)]
    dot_general x1, matrix products: 2.02 us -> 0.51 us  [per_device(): jnp.dot(tokens, w_value[0], preferred_element_type=jnp.float32)]
    ppermute x4, waiting for transfers between devices: 35.9 us -> 37.4 us  [suffix_pipeline(): recv = lax.ppermute(acc.astype(jnp.bfloat16), axis, perm)]
    another operation x1 -> x0, other arithmetic: 1.01 us -> none
    convert_element_type x0 -> x1, other arithmetic: none -> 1.01 us  [per_device(): grads_low = kv_grad.astype(jnp.bfloat16)]
  transfers between devices with their start and end apart: 11 -> 12, of which waited for: 9 -> 8; matrix products, arithmetic and copies ran while one was open for 3% -> 7% of each run, Pallas kernels for 0% -> 7%
where the time goes in v15:
time: 88.4 us; the launch traced here: 87.9 us
  waiting for transfers between devices  44.2 us (50%)
  starting transfers between devices  19.2 us (22%)
  matrix products  7.37 us (8%)
  Pallas kernels  5.85 us (7%)
  local copies, waits for them, and re-layouts  5.66 us (6%)
  other arithmetic  5.3 us (6%)
    ppermute x4, waiting for transfers between devices, suffix_pipeline(): recv = lax.ppermute(acc.astype(jnp.bfloat16), axis, perm)  37.4 us
    ppermute x6, starting transfers between devices, shifted(): return lax.ppermute(x, axis, perm)  13.5 us
    ppermute x6, waiting for transfers between devices, shifted(): return lax.ppermute(x, axis, perm)  6.86 us
    pallas_call x1, Pallas kernels, attention_terms(): pl.pallas_call(kernel, out_shape=(jax.ShapeDtypeStruct((tok_rows, 2 * kv_...  5.85 us
    ppermute x4, starting transfers between devices, suffix_pipeline(): recv = lax.ppermute(acc.astype(jnp.bfloat16), axis, perm)  5.17 us
    dot_general x2, matrix products, product(): lax.dot_general(grads[:, kv_cols:], wv, contract, preferred_element_type=...  3.75 us
    dot_general x2, matrix products, product(): lax.dot_general(grads[:, :kv_cols], wk, contract, preferred_element_type=...  2.59 us
    dynamic_slice x1, local copies, waits for them, and re-layouts, rows_of(): wv = lax.dynamic_slice_in_dim(w_value[0], start, out_cols, axis=0)  1.98 us
  transfers between devices with their start and end apart: 12, of which 8 were waited for; matrix products, arithmetic and copies ran while one was open for 7% of the time, Pallas kernels for 7%

profile of v15, /device:TPU:0, one launch (start us, length us, event | category | flops | bytes accessed | tf_op | source)
XLA Modules:
  0.0 87.9 jit_solution(3474461352444780239)
XLA Ops:
  0.0 0.0 copy-start
  0.0 2.0 %dynamic-slice_bitcast_fusion = (bf16[2560,256]{1,0:T(8,128)(2,1)S(1)}, bf16[2560,256]{1,0:T(8,128)(2,1)S(1)}) fusion(bf16[1,5120,256]{2,1,0:T(8,128)(2,1)} %param.10, s32[]{:T(128)S(6)} %select_n.30, bf16[1,5120,256]{2,1,0:T(8,128)(2,1)} %param.9), kind=kLoop, calls=%fused_computation.21 | loop fusion | bytes 5242884 | tf_op jit(solution)/shard_map/dynamic_slice | solution.py:147
  2.0 0.0 copy-start.1
  2.0 1.7 %pad_maximum_fusion = bf16[2560,512]{1,0:T(8,128)(2,1)} fusion(bf16[2560,256]{1,0:T(8,128)(2,1)S(1)} %get-tuple-element.19, bf16[2560,256]{1,0:T(8,128)(2,1)S(1)} %get-tuple-element.20), kind=kLoop, calls=%fused_computation.8 | loop fusion | flops 5242880 | bytes 5242880 | tf_op jit(solution)/shard_map/concatenate | solution.py:160
  3.7 0.0 copy-start.2
  3.7 0.5 collective-permute-start.7
  4.2 0.0 copy-done
  4.2 0.5 copy-done.1
  4.7 0.5 fusion.22
  5.2 0.4 copy-done.2
  5.7 0.5 fusion.17
  6.2 0.0 copy-start.4
  6.2 4.9 %collective-permute-start = (bf16[128,512]{1,0:T(8,128)(2,1)S(1)}, bf16[128,512]{1,0:T(8,128)(2,1)S(1)}, u32[]{:S(2)}, u32[]{:S(2)}) collective-permute-start(bf16[128,512]{1,0:T(8,128)(2,1)S(1)} %pad_maximum_fusion.1.refs_2_), channel_id=1, source_target_pairs={{0,2},{2,4},{4,6},{1,3},{3,5},{5,7},{8,10},{10,12},{12,14},{9,11},... | collective-permute-start | bytes 393224 | tf_op jit(solution)/shard_map/ppermute | solution.py:18
  11.1 3.4 %collective-permute-start.1 = (bf16[128,512]{1,0:T(8,128)(2,1)S(1)}, bf16[128,512]{1,0:T(8,128)(2,1)S(1)}, u32[]{:S(2)}, u32[]{:S(2)}) collective-permute-start(bf16[128,512]{1,0:T(8,128)(2,1)S(1)} %pad_maximum_fusion.1.refs_2_), channel_id=1, source_target_pairs={{0,4},{2,6},{1,5},{3,7},{8,12},{10,14},{9,13},{11,15},{16,20},{18,... | collective-permute-start | bytes 393224 | tf_op jit(solution)/shard_map/ppermute | solution.py:18
  14.5 1.3 %collective-permute-start.2 = (bf16[128,512]{1,0:T(8,128)(2,1)S(1)}, bf16[128,512]{1,0:T(8,128)(2,1)S(1)}, u32[]{:S(2)}, u32[]{:S(2)}) collective-permute-start(bf16[128,512]{1,0:T(8,128)(2,1)S(1)} %pad_maximum_fusion.1.refs_2_), channel_id=1, source_target_pairs={{0,6},{1,7},{8,14},{9,15},{16,22},{17,23},{24,30},{25,31}} | collective-permute-start | bytes 393224 | tf_op jit(solution)/shard_map/ppermute | solution.py:18
  15.8 0.0 copy-done.8
  15.9 0.2 copy.25
  16.1 0.1 fusion.43
  16.2 0.1 copy.24
  16.3 0.1 fusion.45
  16.4 0.2 copy.28
  16.6 0.9 broadcast_select_fusion
  17.5 0.0 collective-permute-done.refs_3_
  17.5 0.1 collective-permute-done.1.refs_4_
  17.6 0.8 collective-permute-done.2.refs_5_
  18.3 0.0 copy-done.4
  18.3 0.0 copy-done.5
  18.3 0.0 copy-done.6
  18.3 0.6 copy-done.7
  19.0 5.9 %shard_map.64 = (f32[128,512]{1,0:T(8,128)}, bf16[128,512]{1,0:T(8,128)(2,1)}, bf16[128,512]{1,0:T(8,128)(2,1)}, bf16[128,512]{1,0:T(8,128)(2,1)}) custom-call(bf16[10,128,128]{2,1,0:T(8,128)(2,1)} %bitcast.100, bf16[10,128,128]{2,1,0:T(8,128)(2,1)} %bitcast.101, bf16[128,512]{1,0:T(8,128)(2,1)} %copy-done.4, bf16[128,512]{1,0:T(8,128)(2,1)} %copy-done.5, ...), custom_call_target="tpu_custom_call" | custom-call | tf_op jit(solution)/shard_map/pallas_call | solution.py:88
  24.8 1.3 %collective-permute-start.5 = (bf16[128,512]{1,0:T(8,128)(2,1)}, bf16[128,512]{1,0:T(8,128)(2,1)S(1)}, u32[]{:S(2)}, u32[]{:S(2)}) collective-permute-start(bf16[128,512]{1,0:T(8,128)(2,1)} %get-tuple-element.12), channel_id=1, source_target_pairs={{6,0},{7,1},{14,8},{15,9},{22,16},{23,17},{30,24},{31,25}} | collective-permute-start | bytes 393224 | tf_op jit(solution)/shard_map/ppermute | solution.py:18
  26.1 1.3 %collective-permute-start.4 = (bf16[128,512]{1,0:T(8,128)(2,1)}, bf16[128,512]{1,0:T(8,128)(2,1)S(1)}, u32[]{:S(2)}, u32[]{:S(2)}) collective-permute-start(bf16[128,512]{1,0:T(8,128)(2,1)} %get-tuple-element.11), channel_id=1, source_target_pairs={{4,0},{6,2},{5,1},{7,3},{12,8},{14,10},{13,9},{15,11},{20,16},{22,... | collective-permute-start | bytes 393224 | tf_op jit(solution)/shard_map/ppermute | solution.py:18
  27.4 1.3 %collective-permute-start.3 = (bf16[128,512]{1,0:T(8,128)(2,1)}, bf16[128,512]{1,0:T(8,128)(2,1)S(1)}, u32[]{:S(2)}, u32[]{:S(2)}) collective-permute-start(bf16[128,512]{1,0:T(8,128)(2,1)} %get-tuple-element.10), channel_id=1, source_target_pairs={{2,0},{4,2},{6,4},{3,1},{5,3},{7,5},{10,8},{12,10},{14,12},{11,9},... | collective-permute-start | bytes 393224 | tf_op jit(solution)/shard_map/ppermute | solution.py:18
  28.7 4.3 %collective-permute-done.5 = bf16[128,512]{1,0:T(8,128)(2,1)S(1)} collective-permute-done((bf16[128,512]{1,0:T(8,128)(2,1)}, bf16[128,512]{1,0:T(8,128)(2,1)S(1)}, u32[]{:S(2)}, u32[]{:S(2)}) %collective-permute-start.5) | collective-permute-done | bytes 131104 | tf_op jit(solution)/shard_map/ppermute | solution.py:18
  33.1 1.7 %collective-permute-done.4 = bf16[128,512]{1,0:T(8,128)(2,1)S(1)} collective-permute-done((bf16[128,512]{1,0:T(8,128)(2,1)}, bf16[128,512]{1,0:T(8,128)(2,1)S(1)}, u32[]{:S(2)}, u32[]{:S(2)}) %collective-permute-start.4) | collective-permute-done | bytes 131104 | tf_op jit(solution)/shard_map/ppermute | solution.py:18
  34.7 0.0 collective-permute-done.3
  34.7 1.0 %add_convert_fusion = bf16[128,512]{1,0:T(8,128)(2,1)S(1)} fusion(bf16[128,512]{1,0:T(8,128)(2,1)S(1)} %collective-permute-done.5, bf16[128,512]{1,0:T(8,128)(2,1)S(1)} %collective-permute-done.4, f32[128,512]{1,0:T(8,128)} %get-tuple-element.9, bf16[128,512]{1,0:T(8,128)(2,1)S(1)} %collective-permute-done.3), kind=kLoop, calls=%fused_computation.46 | loop fusion | flops 458752 | bytes 786432 | tf_op jit(solution)/shard_map/convert_element_type | solution.py:138
  35.8 0.1 collective-permute-start.6
  35.8 1.9 %fusion.10 = f32[128,2560]{1,0:T(8,128)S(1)} fusion(bf16[1,5120,256]{2,1,0:T(8,128)(2,1)} %param.10, s32[]{:T(128)S(6)} %select_n.29, bf16[128,512]{1,0:T(8,128)(2,1)S(1)} %add_convert_fusion), kind=kOutput, calls=%fused_computation.16 | convolution fusion | flops 167772160 | bytes 2686980 | tf_op jit(solution)/shard_map/dot_general | solution.py:152
  37.7 0.0 collective-permute-done.6
  37.7 0.0 collective-permute-done.7
  37.7 1.9 %fusion.7 = f32[128,2560]{1,0:T(8,128)S(1)} fusion(bf16[2560,512]{1,0:T(8,128)(2,1)} %collective-permute-done.7, bf16[128,512]{1,0:T(8,128)(2,1)S(1)} %collective-permute-done.6), kind=kOutput, calls=%fused_computation.13 | convolution fusion | flops 167772160 | bytes 2686976 | tf_op jit(solution)/shard_map/dot_general | solution.py:152
  39.6 0.0 copy-start.3
  39.6 2.0 %convolution_add_fusion = f32[128,2560]{1,0:T(8,128)S(1)} fusion(f32[128,2560]{1,0:T(8,128)S(1)} %fusion.7, bf16[2560,512]{1,0:T(8,128)(2,1)} %collective-permute-done.7, bf16[128,512]{1,0:T(8,128)(2,1)S(1)} %collective-permute-done.6), kind=kOutput, calls=%fused_computation.3 | convolution fusion | flops 168099840 | bytes 3997696 | tf_op jit(solution)/shard_map/dot_general | solution.py:151
  41.7 0.1 copy-done.3
  41.8 0.6 fusion
  42.3 0.2 broadcast_in_dim.12
  42.5 1.0 %fusion.2 = f32[5,64,2560]{2,1,0:T(8,128)S(1)} fusion(s32[]{:T(128)S(6)} %select_n.31, f32[3,64,2560]{2,1,0:T(8,128)S(1)} %broadcast_in_dim.12, f32[2,64,2560]{2,1,0:T(8,128)S(1)} %bitcast.99), kind=kLoop, calls=%fused_computation.7 | loop fusion | flops 1638400 | bytes 6553604 | tf_op jit(solution)/shard_map/concatenate | solution.py:27
  43.6 1.3 %collective-permute-start.8 = (bf16[64,2560]{1,0:T(8,128)(2,1)S(1)}, bf16[64,2560]{1,0:T(8,128)(2,1)S(1)}, u32[]{:S(2)}, u32[]{:S(2)}) collective-permute-start(bf16[64,2560]{1,0:T(8,128)(2,1)S(1)} %fusion.36), channel_id=1, source_target_pairs={{8,0},{16,8},{24,16},{9,1},{17,9},{25,17},{10,2},{18,10},{26,18},{... | collective-permute-start | bytes 983048 | tf_op jit(solution)/shard_map/ppermute | solution.py:37
  44.9 10.7 %collective-permute-done.8 = bf16[64,2560]{1,0:T(8,128)(2,1)S(1)} collective-permute-done((bf16[64,2560]{1,0:T(8,128)(2,1)S(1)}, bf16[64,2560]{1,0:T(8,128)(2,1)S(1)}, u32[]{:S(2)}, u32[]{:S(2)}) %collective-permute-start.8) | collective-permute-done | bytes 327712 | tf_op jit(solution)/shard_map/ppermute | solution.py:37
  55.6 0.1 fusion.33
  55.7 1.3 %collective-permute-start.9 = (bf16[64,2560]{1,0:T(8,128)(2,1)S(1)}, bf16[64,2560]{1,0:T(8,128)(2,1)S(1)}, u32[]{:S(2)}, u32[]{:S(2)}) collective-permute-start(bf16[64,2560]{1,0:T(8,128)(2,1)S(1)} %fusion.33), channel_id=1, source_target_pairs={{8,0},{16,8},{24,16},{9,1},{17,9},{25,17},{10,2},{18,10},{26,18},{... | collective-permute-start | bytes 983048 | tf_op jit(solution)/shard_map/ppermute | solution.py:37
  57.0 0.1 bitcast_dynamic-update-slice_fusion.2
  57.0 9.8 %collective-permute-done.9 = bf16[64,2560]{1,0:T(8,128)(2,1)S(1)} collective-permute-done((bf16[64,2560]{1,0:T(8,128)(2,1)S(1)}, bf16[64,2560]{1,0:T(8,128)(2,1)S(1)}, u32[]{:S(2)}, u32[]{:S(2)}) %collective-permute-start.9) | collective-permute-done | bytes 327712 | tf_op jit(solution)/shard_map/ppermute | solution.py:37
  66.8 0.1 fusion.34
  66.9 1.3 %collective-permute-start.10 = (bf16[64,2560]{1,0:T(8,128)(2,1)S(1)}, bf16[64,2560]{1,0:T(8,128)(2,1)S(1)}, u32[]{:S(2)}, u32[]{:S(2)}) collective-permute-start(bf16[64,2560]{1,0:T(8,128)(2,1)S(1)} %fusion.34), channel_id=1, source_target_pairs={{8,0},{16,8},{24,16},{9,1},{17,9},{25,17},{10,2},{18,10},{26,18},{... | collective-permute-start | bytes 983048 | tf_op jit(solution)/shard_map/ppermute | solution.py:37
  68.2 0.1 bitcast_dynamic-update-slice_fusion.1
  68.3 8.9 %collective-permute-done.10 = bf16[64,2560]{1,0:T(8,128)(2,1)S(1)} collective-permute-done((bf16[64,2560]{1,0:T(8,128)(2,1)S(1)}, bf16[64,2560]{1,0:T(8,128)(2,1)S(1)}, u32[]{:S(2)}, u32[]{:S(2)}) %collective-permute-start.10) | collective-permute-done | bytes 327712 | tf_op jit(solution)/shard_map/ppermute | solution.py:37
  77.2 0.1 fusion.35
  77.3 1.3 %collective-permute-start.11 = (bf16[64,2560]{1,0:T(8,128)(2,1)S(1)}, bf16[64,2560]{1,0:T(8,128)(2,1)S(1)}, u32[]{:S(2)}, u32[]{:S(2)}) collective-permute-start(bf16[64,2560]{1,0:T(8,128)(2,1)S(1)} %fusion.35), channel_id=1, source_target_pairs={{8,0},{16,8},{24,16},{9,1},{17,9},{25,17},{10,2},{18,10},{26,18},{... | collective-permute-start | bytes 983048 | tf_op jit(solution)/shard_map/ppermute | solution.py:37
  78.6 0.1 bitcast_dynamic-update-slice_fusion
  78.6 8.1 %collective-permute-done.11 = bf16[64,2560]{1,0:T(8,128)(2,1)S(1)} collective-permute-done((bf16[64,2560]{1,0:T(8,128)(2,1)S(1)}, bf16[64,2560]{1,0:T(8,128)(2,1)S(1)}, u32[]{:S(2)}, u32[]{:S(2)}) %collective-permute-start.11) | collective-permute-done | bytes 327712 | tf_op jit(solution)/shard_map/ppermute | solution.py:37
  86.7 0.1 fusion.29
  86.8 1.2 %constant_dynamic-slice_fusion = f32[2,64,2560]{2,1,0:T(8,128)} fusion(f32[5,64,2560]{2,1,0:T(8,128)S(1)} %fusion.29, s32[]{:T(128)S(6)} %select_n.32), kind=kLoop, calls=%fused_computation.55 | loop fusion | bytes 2621444 | tf_op jit(solution)/shard_map/dynamic_slice | solution.py:39
  (11 shorter events, 0.1 us)
Async XLA Ops:
  0.0 4.2 %copy-start = (bf16[1,128,5120]{2,1,0:T(8,128)(2,1)S(1)}, bf16[1,128,5120]{2,1,0:T(8,128)(2,1)}, u32[]{:S(2)}) copy-start(bf16[1,128,5120]{2,1,0:T(8,128)(2,1)} %param.6) | copy-start | bytes 3932164
  2.0 2.7 %copy-start.1 = (bf16[1,5120,256]{2,1,0:T(8,128)(2,1)S(1)}, bf16[1,5120,256]{2,1,0:T(8,128)(2,1)}, u32[]{:S(2)}) copy-start(bf16[1,5120,256]{2,1,0:T(8,128)(2,1)} %param.10) | copy-start | bytes 7864324
  3.7 1.9 %copy-start.2 = (bf16[1,5120,256]{2,1,0:T(8,128)(2,1)S(1)}, bf16[1,5120,256]{2,1,0:T(8,128)(2,1)}, u32[]{:S(2)}) copy-start(bf16[1,5120,256]{2,1,0:T(8,128)(2,1)} %param.9) | copy-start | bytes 7864324
  3.7 34.0 %collective-permute-start.7 = (bf16[2560,512]{1,0:T(8,128)(2,1)}, bf16[2560,512]{1,0:T(8,128)(2,1)}, u32[]{:S(2)}, u32[]{:S(2)}) collective-permute-start(bf16[2560,512]{1,0:T(8,128)(2,1)} %pad_maximum_fusion), channel_id=1, source_target_pairs={{0,1},{1,0},{2,3},{3,2},{4,5},{5,4},{6,7},{7,6},{8,9},{9,8},{10,11... | collective-permute-start | bytes 7864328 | tf_op jit(solution)/shard_map/ppermute | solution.py:160
  5.7 10.2 %copy-start.8 = (s32[512]{0:T(512)S(1)}, s32[512]{0:T(512)}, u32[]{:S(2)}) copy-start(s32[512]{0:T(512)} %param.11) | copy-start | bytes 6148
  6.2 12.1 %copy-start.4 = (bf16[128,512]{1,0:T(8,128)(2,1)}, bf16[128,512]{1,0:T(8,128)(2,1)S(1)}, u32[]{:S(2)}) copy-start(bf16[128,512]{1,0:T(8,128)(2,1)S(1)} %pad_maximum_fusion.1.refs_2_) | copy-start | bytes 393220
  6.2 11.3 %collective-permute-start = (bf16[128,512]{1,0:T(8,128)(2,1)S(1)}, bf16[128,512]{1,0:T(8,128)(2,1)S(1)}, u32[]{:S(2)}, u32[]{:S(2)}) collective-permute-start(bf16[128,512]{1,0:T(8,128)(2,1)S(1)} %pad_maximum_fusion.1.refs_2_), channel_id=1, source_target_pairs={{0,2},{2,4},{4,6},{1,3},{3,5},{5,7},{8,10},{10,12},{12,14},{9,11},... | collective-permute-start | bytes 393224 | tf_op jit(solution)/shard_map/ppermute | solution.py:18
  11.1 6.5 %collective-permute-start.1 = (bf16[128,512]{1,0:T(8,128)(2,1)S(1)}, bf16[128,512]{1,0:T(8,128)(2,1)S(1)}, u32[]{:S(2)}, u32[]{:S(2)}) collective-permute-start(bf16[128,512]{1,0:T(8,128)(2,1)S(1)} %pad_maximum_fusion.1.refs_2_), channel_id=1, source_target_pairs={{0,4},{2,6},{1,5},{3,7},{8,12},{10,14},{9,13},{11,15},{16,20},{18,... | collective-permute-start | bytes 393224 | tf_op jit(solution)/shard_map/ppermute | solution.py:18
  14.5 3.8 %collective-permute-start.2 = (bf16[128,512]{1,0:T(8,128)(2,1)S(1)}, bf16[128,512]{1,0:T(8,128)(2,1)S(1)}, u32[]{:S(2)}, u32[]{:S(2)}) collective-permute-start(bf16[128,512]{1,0:T(8,128)(2,1)S(1)} %pad_maximum_fusion.1.refs_2_), channel_id=1, source_target_pairs={{0,6},{1,7},{8,14},{9,15},{16,22},{17,23},{24,30},{25,31}} | collective-permute-start | bytes 393224 | tf_op jit(solution)/shard_map/ppermute | solution.py:18
  17.5 0.9 copy-start.5
  17.6 0.8 copy-start.6
  18.3 0.6 copy-start.7
  24.8 8.2 %collective-permute-start.5 = (bf16[128,512]{1,0:T(8,128)(2,1)}, bf16[128,512]{1,0:T(8,128)(2,1)S(1)}, u32[]{:S(2)}, u32[]{:S(2)}) collective-permute-start(bf16[128,512]{1,0:T(8,128)(2,1)} %get-tuple-element.12), channel_id=1, source_target_pairs={{6,0},{7,1},{14,8},{15,9},{22,16},{23,17},{30,24},{31,25}} | collective-permute-start | bytes 393224 | tf_op jit(solution)/shard_map/ppermute | solution.py:18
  26.1 8.6 %collective-permute-start.4 = (bf16[128,512]{1,0:T(8,128)(2,1)}, bf16[128,512]{1,0:T(8,128)(2,1)S(1)}, u32[]{:S(2)}, u32[]{:S(2)}) collective-permute-start(bf16[128,512]{1,0:T(8,128)(2,1)} %get-tuple-element.11), channel_id=1, source_target_pairs={{4,0},{6,2},{5,1},{7,3},{12,8},{14,10},{13,9},{15,11},{20,16},{22,... | collective-permute-start | bytes 393224 | tf_op jit(solution)/shard_map/ppermute | solution.py:18
  27.4 7.3 %collective-permute-start.3 = (bf16[128,512]{1,0:T(8,128)(2,1)}, bf16[128,512]{1,0:T(8,128)(2,1)S(1)}, u32[]{:S(2)}, u32[]{:S(2)}) collective-permute-start(bf16[128,512]{1,0:T(8,128)(2,1)} %get-tuple-element.10), channel_id=1, source_target_pairs={{2,0},{4,2},{6,4},{3,1},{5,3},{7,5},{10,8},{12,10},{14,12},{11,9},... | collective-permute-start | bytes 393224 | tf_op jit(solution)/shard_map/ppermute | solution.py:18
  35.8 2.0 %collective-permute-start.6 = (bf16[128,512]{1,0:T(8,128)(2,1)S(1)}, bf16[128,512]{1,0:T(8,128)(2,1)S(1)}, u32[]{:S(2)}, u32[]{:S(2)}) collective-permute-start(bf16[128,512]{1,0:T(8,128)(2,1)S(1)} %add_convert_fusion), channel_id=1, source_target_pairs={{0,1},{1,0},{2,3},{3,2},{4,5},{5,4},{6,7},{7,6},{8,9},{9,8},{10,11... | collective-permute-start | bytes 393224 | tf_op jit(solution)/shard_map/ppermute | solution.py:161
  39.6 2.1 %copy-start.3 = (bf16[1,5120,256]{2,1,0:T(8,128)(2,1)S(1)}, bf16[1,5120,256]{2,1,0:T(8,128)(2,1)}, u32[]{:S(2)}) copy-start(bf16[1,5120,256]{2,1,0:T(8,128)(2,1)} %param.9) | copy-start | bytes 7864324
  43.6 12.0 %collective-permute-start.8 = (bf16[64,2560]{1,0:T(8,128)(2,1)S(1)}, bf16[64,2560]{1,0:T(8,128)(2,1)S(1)}, u32[]{:S(2)}, u32[]{:S(2)}) collective-permute-start(bf16[64,2560]{1,0:T(8,128)(2,1)S(1)} %fusion.36), channel_id=1, source_target_pairs={{8,0},{16,8},{24,16},{9,1},{17,9},{25,17},{10,2},{18,10},{26,18},{... | collective-permute-start | bytes 983048 | tf_op jit(solution)/shard_map/ppermute | solution.py:37
  55.7 11.1 %collective-permute-start.9 = (bf16[64,2560]{1,0:T(8,128)(2,1)S(1)}, bf16[64,2560]{1,0:T(8,128)(2,1)S(1)}, u32[]{:S(2)}, u32[]{:S(2)}) collective-permute-start(bf16[64,2560]{1,0:T(8,128)(2,1)S(1)} %fusion.33), channel_id=1, source_target_pairs={{8,0},{16,8},{24,16},{9,1},{17,9},{25,17},{10,2},{18,10},{26,18},{... | collective-permute-start | bytes 983048 | tf_op jit(solution)/shard_map/ppermute | solution.py:37
  66.9 10.3 %collective-permute-start.10 = (bf16[64,2560]{1,0:T(8,128)(2,1)S(1)}, bf16[64,2560]{1,0:T(8,128)(2,1)S(1)}, u32[]{:S(2)}, u32[]{:S(2)}) collective-permute-start(bf16[64,2560]{1,0:T(8,128)(2,1)S(1)} %fusion.34), channel_id=1, source_target_pairs={{8,0},{16,8},{24,16},{9,1},{17,9},{25,17},{10,2},{18,10},{26,18},{... | collective-permute-start | bytes 983048 | tf_op jit(solution)/shard_map/ppermute | solution.py:37
  77.3 9.4 %collective-permute-start.11 = (bf16[64,2560]{1,0:T(8,128)(2,1)S(1)}, bf16[64,2560]{1,0:T(8,128)(2,1)S(1)}, u32[]{:S(2)}, u32[]{:S(2)}) collective-permute-start(bf16[64,2560]{1,0:T(8,128)(2,1)S(1)} %fusion.35), channel_id=1, source_target_pairs={{8,0},{16,8},{24,16},{9,1},{17,9},{25,17},{10,2},{18,10},{26,18},{... | collective-permute-start | bytes 983048 | tf_op jit(solution)/shard_map/ppermute | solution.py:37

commit v16 on v13

--- a/solution.py
+++ b/solution.py
@@ -4,6 +4,7 @@
 import jax.numpy as jnp
 from jax import lax
 from jax.experimental import pallas as pl
+from jax.experimental.pallas import tpu as pltpu
 from jax.sharding import PartitionSpec as P
 
 
@@ -94,6 +95,40 @@
     )(q3, g3, *kv_blocks, lower, upper)
 
 
+def projections(tokens, wk, wv, depth):
+    rows, width = tokens.shape
+    cols = wk.shape[1]
+    steps = width // depth
+
+    def kernel(t_ref, k_ref, v_ref, out_ref, acc_ref):
+        step = pl.program_id(0)
+
+        @pl.when(step == 0)
+        def _():
+            acc_ref[...] = jnp.zeros_like(acc_ref)
+
+        t = t_ref[...]
+        acc_ref[:, :cols] += jnp.dot(t, k_ref[...], preferred_element_type=jnp.float32)
+        acc_ref[:, cols:] += jnp.dot(t, v_ref[...], preferred_element_type=jnp.float32)
+
+        @pl.when(step == steps - 1)
+        def _():
+            out_ref[...] = acc_ref[...].astype(out_ref.dtype)
+
+    return pl.pallas_call(
+        kernel,
+        grid=(steps,),
+        in_specs=[
+            pl.BlockSpec((rows, depth), lambda i: (0, i)),
+            pl.BlockSpec((depth, cols), lambda i: (i, 0)),
+            pl.BlockSpec((depth, cols), lambda i: (i, 0)),
+        ],
+        out_specs=pl.BlockSpec((rows, 2 * cols), lambda i: (0, 0)),
+        out_shape=jax.ShapeDtypeStruct((rows, 2 * cols), jnp.bfloat16),
+        scratch_shapes=[pltpu.VMEM((rows, 2 * cols), jnp.float32)],
+    )(tokens, wk, wv)
+
+
 def per_device(inputs, query, grad_out, w_key, w_value, keep_mask):
     tok_rows = inputs.shape[1]
     local_heads = query.shape[2]
@@ -105,11 +140,7 @@
     ctx_len = lax.axis_size("ctx")
     ctx_index = lax.axis_index("ctx")
     tokens = inputs[0]
-    key_rows = jnp.dot(tokens, w_key[0], preferred_element_type=jnp.float32).astype(jnp.bfloat16)
-    value_rows = jnp.dot(tokens, w_value[0], preferred_element_type=jnp.float32).astype(
-        jnp.bfloat16
-    )
-    kv_own = jnp.concatenate((key_rows, value_rows), axis=1)
+    kv_own = projections(tokens, w_key[0], w_value[0], 1024)
     later = {d: shifted(kv_own, "ctx", d, ctx_len, True) for d in range(ctx_len - 1, 0, -1)}
     blocks = [kv_own] + [later[d] for d in range(1, ctx_len)]
     seq_rows = tok_rows * ctx_len

time: 83.3 us -> 86.3 us (1.036)
  Pallas kernels: 5.86 us -> 11.4 us
  local copies, waits for them, and re-layouts: 4.4 us -> 2.66 us
  waiting for transfers between devices: 44.5 us -> 43.6 us
    pallas_call x0 -> x1, Pallas kernels: none -> 5.52 us  [projections(): pl.pallas_call(kernel, grid=(steps,), in_specs=[pl.BlockSpec((rows, depth...]
    dot_general x2, matrix products: 1.12 us -> 3.75 us  [partial_for(): lax.dot_general(grad_value, wv, contract, preferred_element_type=jnp.floa...]
    dot_general x2 -> x0, matrix products: 2.53 us -> none  [the longest x1 2.02 us: per_device(): jnp.dot(tokens, w_value[0], preferred_element_type=jnp.float32)]
    unnamed x23 -> x13, local copies, waits for them, and re-layouts: 2.65 us -> 0.91 us
    ppermute x1, waiting for transfers between devices: 1.74 us -> 0.43 us  [per_device(): received.append(lax.ppermute(send, 'head', perm))]
  transfers between devices with their start and end apart: 11 -> 11, of which waited for: 9 -> 9; matrix products, arithmetic and copies ran while one was open for 3% -> 4% of each run, Pallas kernels for 0% -> 0%
where the time goes in v16:
time: 86.3 us; the launch traced here: 85.8 us
  waiting for transfers between devices  43.6 us (51%)
  starting transfers between devices  18.6 us (22%)
  Pallas kernels  11.4 us (13%)
  matrix products  5.74 us (7%)
  other arithmetic  3.57 us (4%)
  local copies, waits for them, and re-layouts  2.66 us (3%)
    ppermute x4, waiting for transfers between devices, suffix_pipeline(): recv = lax.ppermute(acc.astype(jnp.bfloat16), axis, perm)  36 us
    ppermute x6, starting transfers between devices, shifted(): return lax.ppermute(x, axis, perm)  13.4 us
    ppermute x6, waiting for transfers between devices, shifted(): return lax.ppermute(x, axis, perm)  7.17 us
    pallas_call x1, Pallas kernels, attention_terms(): pl.pallas_call(kernel, out_shape=(jax.ShapeDtypeStruct((tok_rows, 2 * kv_...  5.87 us
    pallas_call x1, Pallas kernels, projections(): pl.pallas_call(kernel, grid=(steps,), in_specs=[pl.BlockSpec((rows, depth...  5.52 us
    ppermute x4, starting transfers between devices, suffix_pipeline(): recv = lax.ppermute(acc.astype(jnp.bfloat16), axis, perm)  5.17 us
    dot_general x2, matrix products, partial_for(): lax.dot_general(grad_value, wv, contract, preferred_element_type=jnp.floa...  3.75 us
    dot_general x2, matrix products, partial_for(): lax.dot_general(grad_key, wk, contract, preferred_element_type=jnp.float32)  1.99 us
  transfers between devices with their start and end apart: 11, of which 9 were waited for; matrix products, arithmetic and copies ran while one was open for 4% of the time, Pallas kernels for 0%

profile of v16, /device:TPU:0, one launch (start us, length us, event | category | flops | bytes accessed | tf_op | source)
XLA Modules:
  0.0 85.8 jit_solution(16921736093698259280)
XLA Ops:
  0.0 0.0 copy-start.4
  0.0 5.5 %shard_map.64.refs_2_ = bf16[128,512]{1,0:T(8,128)(2,1)} custom-call(bf16[128,5120]{1,0:T(8,128)(2,1)} %bitcast.88, bf16[5120,256]{1,0:T(8,128)(2,1)} %bitcast.85, bf16[5120,256]{1,0:T(8,128)(2,1)} %bitcast.86), custom_call_target="tpu_custom_call" | custom-call | tf_op jit(solution)/shard_map/pallas_call | solution.py:118
  5.5 4.9 %collective-permute-start = (bf16[128,512]{1,0:T(8,128)(2,1)}, bf16[128,512]{1,0:T(8,128)(2,1)S(1)}, u32[]{:S(2)}, u32[]{:S(2)}) collective-permute-start(bf16[128,512]{1,0:T(8,128)(2,1)} %shard_map.64.refs_2_), channel_id=1, source_target_pairs={{0,2},{2,4},{4,6},{1,3},{3,5},{5,7},{8,10},{10,12},{12,14},{9,11},... | collective-permute-start | bytes 393224 | tf_op jit(solution)/shard_map/ppermute | solution.py:19
  10.4 3.4 %collective-permute-start.1 = (bf16[128,512]{1,0:T(8,128)(2,1)}, bf16[128,512]{1,0:T(8,128)(2,1)S(1)}, u32[]{:S(2)}, u32[]{:S(2)}) collective-permute-start(bf16[128,512]{1,0:T(8,128)(2,1)} %shard_map.64.refs_2_), channel_id=1, source_target_pairs={{0,4},{2,6},{1,5},{3,7},{8,12},{10,14},{9,13},{11,15},{16,20},{18,... | collective-permute-start | bytes 393224 | tf_op jit(solution)/shard_map/ppermute | solution.py:19
  13.8 1.3 %collective-permute-start.2 = (bf16[128,512]{1,0:T(8,128)(2,1)}, bf16[128,512]{1,0:T(8,128)(2,1)S(1)}, u32[]{:S(2)}, u32[]{:S(2)}) collective-permute-start(bf16[128,512]{1,0:T(8,128)(2,1)} %shard_map.64.refs_2_), channel_id=1, source_target_pairs={{0,6},{1,7},{8,14},{9,15},{16,22},{17,23},{24,30},{25,31}} | collective-permute-start | bytes 393224 | tf_op jit(solution)/shard_map/ppermute | solution.py:19
  15.2 0.0 copy-done.4
  15.2 0.2 copy.25
  15.4 0.1 fusion.34
  15.5 0.1 fusion.32
  15.5 0.2 copy.24
  15.7 0.2 copy.28
  15.9 0.9 broadcast_select_fusion
  16.8 0.0 copy-start
  16.8 0.0 collective-permute-done.refs_3_
  16.8 0.0 copy-start.1
  16.8 0.4 collective-permute-done.1.refs_4_
  17.2 0.0 copy-start.2
  17.2 0.8 collective-permute-done.2.refs_5_
  17.9 0.0 copy-start.3
  17.9 0.0 copy-done.1
  17.9 0.0 copy-done.2
  18.0 0.6 copy-done.3
  18.6 5.9 %shard_map.65 = (f32[128,512]{1,0:T(8,128)}, bf16[128,512]{1,0:T(8,128)(2,1)}, bf16[128,512]{1,0:T(8,128)(2,1)}, bf16[128,512]{1,0:T(8,128)(2,1)}) custom-call(bf16[10,128,128]{2,1,0:T(8,128)(2,1)} %bitcast.89, bf16[10,128,128]{2,1,0:T(8,128)(2,1)} %bitcast.90, bf16[128,512]{1,0:T(8,128)(2,1)} %shard_map.64.refs_2_, bf16[128,512]{1,0:T(8,128)(2,1)} %copy-done.1, ...), custom_call_target="tpu_custom_call" | custom-call | tf_op jit(solution)/shard_map/pallas_call | solution.py:89
  24.5 1.3 %collective-permute-start.5 = (bf16[128,512]{1,0:T(8,128)(2,1)}, bf16[128,512]{1,0:T(8,128)(2,1)S(1)}, u32[]{:S(2)}, u32[]{:S(2)}) collective-permute-start(bf16[128,512]{1,0:T(8,128)(2,1)} %get-tuple-element.12), channel_id=1, source_target_pairs={{6,0},{7,1},{14,8},{15,9},{22,16},{23,17},{30,24},{31,25}} | collective-permute-start | bytes 393224 | tf_op jit(solution)/shard_map/ppermute | solution.py:19
  25.8 1.3 %collective-permute-start.4 = (bf16[128,512]{1,0:T(8,128)(2,1)}, bf16[128,512]{1,0:T(8,128)(2,1)S(1)}, u32[]{:S(2)}, u32[]{:S(2)}) collective-permute-start(bf16[128,512]{1,0:T(8,128)(2,1)} %get-tuple-element.11), channel_id=1, source_target_pairs={{4,0},{6,2},{5,1},{7,3},{12,8},{14,10},{13,9},{15,11},{20,16},{22,... | collective-permute-start | bytes 393224 | tf_op jit(solution)/shard_map/ppermute | solution.py:19
  27.1 1.3 %collective-permute-start.3 = (bf16[128,512]{1,0:T(8,128)(2,1)}, bf16[128,512]{1,0:T(8,128)(2,1)S(1)}, u32[]{:S(2)}, u32[]{:S(2)}) collective-permute-start(bf16[128,512]{1,0:T(8,128)(2,1)} %get-tuple-element.10), channel_id=1, source_target_pairs={{2,0},{4,2},{6,4},{3,1},{5,3},{7,5},{10,8},{12,10},{14,12},{11,9},... | collective-permute-start | bytes 393224 | tf_op jit(solution)/shard_map/ppermute | solution.py:19
  28.4 4.3 %collective-permute-done.5 = bf16[128,512]{1,0:T(8,128)(2,1)S(1)} collective-permute-done((bf16[128,512]{1,0:T(8,128)(2,1)}, bf16[128,512]{1,0:T(8,128)(2,1)S(1)}, u32[]{:S(2)}, u32[]{:S(2)}) %collective-permute-start.5) | collective-permute-done | bytes 131104 | tf_op jit(solution)/shard_map/ppermute | solution.py:19
  32.7 1.7 %collective-permute-done.4 = bf16[128,512]{1,0:T(8,128)(2,1)S(1)} collective-permute-done((bf16[128,512]{1,0:T(8,128)(2,1)}, bf16[128,512]{1,0:T(8,128)(2,1)S(1)}, u32[]{:S(2)}, u32[]{:S(2)}) %collective-permute-start.4) | collective-permute-done | bytes 131104 | tf_op jit(solution)/shard_map/ppermute | solution.py:19
  34.4 0.0 collective-permute-done.3
  34.4 1.0 %add_convert_fusion = bf16[128,512]{1,0:T(8,128)(2,1)S(1)} fusion(bf16[128,512]{1,0:T(8,128)(2,1)S(1)} %collective-permute-done.5, bf16[128,512]{1,0:T(8,128)(2,1)S(1)} %collective-permute-done.4, f32[128,512]{1,0:T(8,128)} %get-tuple-element.9, bf16[128,512]{1,0:T(8,128)(2,1)S(1)} %collective-permute-done.3), kind=kLoop, calls=%fused_computation.38 | loop fusion | flops 458752 | bytes 786432 | tf_op jit(solution)/shard_map/convert.1
  35.4 1.9 %fusion.4 = f32[128,2560]{1,0:T(8,128)S(1)} fusion(bf16[1,5120,256]{2,1,0:T(8,128)(2,1)} %param.10, s32[]{:T(128)S(6)} %select_n.30, bf16[128,512]{1,0:T(8,128)(2,1)S(1)} %add_convert_fusion), kind=kOutput, calls=%fused_computation.9 | convolution fusion | flops 167772160 | bytes 2686980 | tf_op jit(solution)/shard_map/dot_general | solution.py:181
  37.3 0.0 copy-done
  37.3 1.4 %fusion.1 = bf16[128,2560]{1,0:T(8,128)(2,1)} fusion(f32[128,2560]{1,0:T(8,128)S(1)} %fusion.4, bf16[1,5120,256]{2,1,0:T(8,128)(2,1)S(1)} %copy-done, s32[]{:T(128)S(6)} %select_n.30, bf16[128,512]{1,0:T(8,128)(2,1)S(1)} %add_convert_fusion), kind=kOutput, calls=%fused_computation.6 | convolution fusion | flops 168427520 | bytes 3342340 | tf_op jit(solution)/shard_map/dot_general | solution.py:180
  38.7 0.0 collective-permute-start.6
  38.7 1.9 %fusion.7 = f32[128,2560]{1,0:T(8,128)S(1)} fusion(bf16[1,5120,256]{2,1,0:T(8,128)(2,1)} %param.10, s32[]{:T(128)S(6)} %select_n.29, bf16[128,512]{1,0:T(8,128)(2,1)S(1)} %add_convert_fusion), kind=kOutput, calls=%fused_computation.12 | convolution fusion | flops 167772160 | bytes 2686980 | tf_op jit(solution)/shard_map/dot_general | solution.py:181
  40.6 0.4 collective-permute-done.6
  41.0 0.6 fusion
  41.6 0.2 broadcast_in_dim.12
  41.8 1.0 %fusion.3 = f32[5,64,2560]{2,1,0:T(8,128)S(1)} fusion(s32[]{:T(128)S(6)} %select_n.31, f32[3,64,2560]{2,1,0:T(8,128)S(1)} %broadcast_in_dim.12, f32[2,64,2560]{2,1,0:T(8,128)S(1)} %bitcast.87), kind=kLoop, calls=%fused_computation.8 | loop fusion | flops 1638400 | bytes 6553604 | tf_op jit(solution)/shard_map/concatenate | solution.py:28
  42.8 1.3 %collective-permute-start.7 = (bf16[64,2560]{1,0:T(8,128)(2,1)S(1)}, bf16[64,2560]{1,0:T(8,128)(2,1)S(1)}, u32[]{:S(2)}, u32[]{:S(2)}) collective-permute-start(bf16[64,2560]{1,0:T(8,128)(2,1)S(1)} %fusion.23), channel_id=1, source_target_pairs={{8,0},{16,8},{24,16},{9,1},{17,9},{25,17},{10,2},{18,10},{26,18},{... | collective-permute-start | bytes 983048 | tf_op jit(solution)/shard_map/ppermute | solution.py:38
  44.2 10.3 %collective-permute-done.7 = bf16[64,2560]{1,0:T(8,128)(2,1)S(1)} collective-permute-done((bf16[64,2560]{1,0:T(8,128)(2,1)S(1)}, bf16[64,2560]{1,0:T(8,128)(2,1)S(1)}, u32[]{:S(2)}, u32[]{:S(2)}) %collective-permute-start.7) | collective-permute-done | bytes 327712 | tf_op jit(solution)/shard_map/ppermute | solution.py:38
  54.5 0.1 fusion.20
  54.6 1.3 %collective-permute-start.8 = (bf16[64,2560]{1,0:T(8,128)(2,1)S(1)}, bf16[64,2560]{1,0:T(8,128)(2,1)S(1)}, u32[]{:S(2)}, u32[]{:S(2)}) collective-permute-start(bf16[64,2560]{1,0:T(8,128)(2,1)S(1)} %fusion.20), channel_id=1, source_target_pairs={{8,0},{16,8},{24,16},{9,1},{17,9},{25,17},{10,2},{18,10},{26,18},{... | collective-permute-start | bytes 983048 | tf_op jit(solution)/shard_map/ppermute | solution.py:38
  55.9 0.1 bitcast_dynamic-update-slice_fusion.2
  56.0 9.4 %collective-permute-done.8 = bf16[64,2560]{1,0:T(8,128)(2,1)S(1)} collective-permute-done((bf16[64,2560]{1,0:T(8,128)(2,1)S(1)}, bf16[64,2560]{1,0:T(8,128)(2,1)S(1)}, u32[]{:S(2)}, u32[]{:S(2)}) %collective-permute-start.8) | collective-permute-done | bytes 327712 | tf_op jit(solution)/shard_map/ppermute | solution.py:38
  65.4 0.1 fusion.21
  65.4 1.3 %collective-permute-start.9 = (bf16[64,2560]{1,0:T(8,128)(2,1)S(1)}, bf16[64,2560]{1,0:T(8,128)(2,1)S(1)}, u32[]{:S(2)}, u32[]{:S(2)}) collective-permute-start(bf16[64,2560]{1,0:T(8,128)(2,1)S(1)} %fusion.21), channel_id=1, source_target_pairs={{8,0},{16,8},{24,16},{9,1},{17,9},{25,17},{10,2},{18,10},{26,18},{... | collective-permute-start | bytes 983048 | tf_op jit(solution)/shard_map/ppermute | solution.py:38
  66.7 0.1 bitcast_dynamic-update-slice_fusion.1
  66.8 8.6 %collective-permute-done.9 = bf16[64,2560]{1,0:T(8,128)(2,1)S(1)} collective-permute-done((bf16[64,2560]{1,0:T(8,128)(2,1)S(1)}, bf16[64,2560]{1,0:T(8,128)(2,1)S(1)}, u32[]{:S(2)}, u32[]{:S(2)}) %collective-permute-start.9) | collective-permute-done | bytes 327712 | tf_op jit(solution)/shard_map/ppermute | solution.py:38
  75.4 0.1 fusion.22
  75.5 1.3 %collective-permute-start.10 = (bf16[64,2560]{1,0:T(8,128)(2,1)S(1)}, bf16[64,2560]{1,0:T(8,128)(2,1)S(1)}, u32[]{:S(2)}, u32[]{:S(2)}) collective-permute-start(bf16[64,2560]{1,0:T(8,128)(2,1)S(1)} %fusion.22), channel_id=1, source_target_pairs={{8,0},{16,8},{24,16},{9,1},{17,9},{25,17},{10,2},{18,10},{26,18},{... | collective-permute-start | bytes 983048 | tf_op jit(solution)/shard_map/ppermute | solution.py:38
  76.8 0.1 bitcast_dynamic-update-slice_fusion
  76.8 7.7 %collective-permute-done.10 = bf16[64,2560]{1,0:T(8,128)(2,1)S(1)} collective-permute-done((bf16[64,2560]{1,0:T(8,128)(2,1)S(1)}, bf16[64,2560]{1,0:T(8,128)(2,1)S(1)}, u32[]{:S(2)}, u32[]{:S(2)}) %collective-permute-start.10) | collective-permute-done | bytes 327712 | tf_op jit(solution)/shard_map/ppermute | solution.py:38
  84.5 0.1 fusion.16
  84.6 1.2 %constant_dynamic-slice_fusion = f32[2,64,2560]{2,1,0:T(8,128)} fusion(f32[5,64,2560]{2,1,0:T(8,128)S(1)} %fusion.16, s32[]{:T(128)S(6)} %select_n.32), kind=kLoop, calls=%fused_computation.46 | loop fusion | bytes 2621444 | tf_op jit(solution)/shard_map/dynamic_slice | solution.py:40
  (6 shorter events, 0.1 us)
Async XLA Ops:
  0.0 15.2 %copy-start.4 = (s32[512]{0:T(512)S(1)}, s32[512]{0:T(512)}, u32[]{:S(2)}) copy-start(s32[512]{0:T(512)} %param.11) | copy-start | bytes 6148
  5.5 11.3 %collective-permute-start = (bf16[128,512]{1,0:T(8,128)(2,1)}, bf16[128,512]{1,0:T(8,128)(2,1)S(1)}, u32[]{:S(2)}, u32[]{:S(2)}) collective-permute-start(bf16[128,512]{1,0:T(8,128)(2,1)} %shard_map.64.refs_2_), channel_id=1, source_target_pairs={{0,2},{2,4},{4,6},{1,3},{3,5},{5,7},{8,10},{10,12},{12,14},{9,11},... | collective-permute-start | bytes 393224 | tf_op jit(solution)/shard_map/ppermute | solution.py:19
  10.4 6.8 %collective-permute-start.1 = (bf16[128,512]{1,0:T(8,128)(2,1)}, bf16[128,512]{1,0:T(8,128)(2,1)S(1)}, u32[]{:S(2)}, u32[]{:S(2)}) collective-permute-start(bf16[128,512]{1,0:T(8,128)(2,1)} %shard_map.64.refs_2_), channel_id=1, source_target_pairs={{0,4},{2,6},{1,5},{3,7},{8,12},{10,14},{9,13},{11,15},{16,20},{18,... | collective-permute-start | bytes 393224 | tf_op jit(solution)/shard_map/ppermute | solution.py:19
  13.8 4.1 %collective-permute-start.2 = (bf16[128,512]{1,0:T(8,128)(2,1)}, bf16[128,512]{1,0:T(8,128)(2,1)S(1)}, u32[]{:S(2)}, u32[]{:S(2)}) collective-permute-start(bf16[128,512]{1,0:T(8,128)(2,1)} %shard_map.64.refs_2_), channel_id=1, source_target_pairs={{0,6},{1,7},{8,14},{9,15},{16,22},{17,23},{24,30},{25,31}} | collective-permute-start | bytes 393224 | tf_op jit(solution)/shard_map/ppermute | solution.py:19
  16.8 20.5 %copy-start = (bf16[1,5120,256]{2,1,0:T(8,128)(2,1)S(1)}, bf16[1,5120,256]{2,1,0:T(8,128)(2,1)}, u32[]{:S(2)}) copy-start(bf16[1,5120,256]{2,1,0:T(8,128)(2,1)} %param.9) | copy-start | bytes 7864324
  16.8 1.2 %copy-start.1 = (bf16[128,512]{1,0:T(8,128)(2,1)}, bf16[128,512]{1,0:T(8,128)(2,1)S(1)}, u32[]{:S(2)}) copy-start(bf16[128,512]{1,0:T(8,128)(2,1)S(1)} %collective-permute-done.refs_3_) | copy-start | bytes 393220
  17.2 0.8 copy-start.2
  17.9 0.7 copy-start.3
  24.5 8.2 %collective-permute-start.5 = (bf16[128,512]{1,0:T(8,128)(2,1)}, bf16[128,512]{1,0:T(8,128)(2,1)S(1)}, u32[]{:S(2)}, u32[]{:S(2)}) collective-permute-start(bf16[128,512]{1,0:T(8,128)(2,1)} %get-tuple-element.12), channel_id=1, source_target_pairs={{6,0},{7,1},{14,8},{15,9},{22,16},{23,17},{30,24},{31,25}} | collective-permute-start | bytes 393224 | tf_op jit(solution)/shard_map/ppermute | solution.py:19
  25.8 8.6 %collective-permute-start.4 = (bf16[128,512]{1,0:T(8,128)(2,1)}, bf16[128,512]{1,0:T(8,128)(2,1)S(1)}, u32[]{:S(2)}, u32[]{:S(2)}) collective-permute-start(bf16[128,512]{1,0:T(8,128)(2,1)} %get-tuple-element.11), channel_id=1, source_target_pairs={{4,0},{6,2},{5,1},{7,3},{12,8},{14,10},{13,9},{15,11},{20,16},{22,... | collective-permute-start | bytes 393224 | tf_op jit(solution)/shard_map/ppermute | solution.py:19
  27.1 7.3 %collective-permute-start.3 = (bf16[128,512]{1,0:T(8,128)(2,1)}, bf16[128,512]{1,0:T(8,128)(2,1)S(1)}, u32[]{:S(2)}, u32[]{:S(2)}) collective-permute-start(bf16[128,512]{1,0:T(8,128)(2,1)} %get-tuple-element.10), channel_id=1, source_target_pairs={{2,0},{4,2},{6,4},{3,1},{5,3},{7,5},{10,8},{12,10},{14,12},{11,9},... | collective-permute-start | bytes 393224 | tf_op jit(solution)/shard_map/ppermute | solution.py:19
  38.7 2.3 %collective-permute-start.6 = (bf16[128,2560]{1,0:T(8,128)(2,1)}, bf16[128,2560]{1,0:T(8,128)(2,1)S(1)}, u32[]{:S(2)}, u32[]{:S(2)}) collective-permute-start(bf16[128,2560]{1,0:T(8,128)(2,1)} %fusion.1), channel_id=1, source_target_pairs={{0,1},{1,0},{2,3},{3,2},{4,5},{5,4},{6,7},{7,6},{8,9},{9,8},{10,11... | collective-permute-start | bytes 1966088 | tf_op jit(solution)/shard_map/ppermute | solution.py:188
  42.8 11.6 %collective-permute-start.7 = (bf16[64,2560]{1,0:T(8,128)(2,1)S(1)}, bf16[64,2560]{1,0:T(8,128)(2,1)S(1)}, u32[]{:S(2)}, u32[]{:S(2)}) collective-permute-start(bf16[64,2560]{1,0:T(8,128)(2,1)S(1)} %fusion.23), channel_id=1, source_target_pairs={{8,0},{16,8},{24,16},{9,1},{17,9},{25,17},{10,2},{18,10},{26,18},{... | collective-permute-start | bytes 983048 | tf_op jit(solution)/shard_map/ppermute | solution.py:38
  54.6 10.8 %collective-permute-start.8 = (bf16[64,2560]{1,0:T(8,128)(2,1)S(1)}, bf16[64,2560]{1,0:T(8,128)(2,1)S(1)}, u32[]{:S(2)}, u32[]{:S(2)}) collective-permute-start(bf16[64,2560]{1,0:T(8,128)(2,1)S(1)} %fusion.20), channel_id=1, source_target_pairs={{8,0},{16,8},{24,16},{9,1},{17,9},{25,17},{10,2},{18,10},{26,18},{... | collective-permute-start | bytes 983048 | tf_op jit(solution)/shard_map/ppermute | solution.py:38
  65.4 9.9 %collective-permute-start.9 = (bf16[64,2560]{1,0:T(8,128)(2,1)S(1)}, bf16[64,2560]{1,0:T(8,128)(2,1)S(1)}, u32[]{:S(2)}, u32[]{:S(2)}) collective-permute-start(bf16[64,2560]{1,0:T(8,128)(2,1)S(1)} %fusion.21), channel_id=1, source_target_pairs={{8,0},{16,8},{24,16},{9,1},{17,9},{25,17},{10,2},{18,10},{26,18},{... | collective-permute-start | bytes 983048 | tf_op jit(solution)/shard_map/ppermute | solution.py:38
  75.5 9.1 %collective-permute-start.10 = (bf16[64,2560]{1,0:T(8,128)(2,1)S(1)}, bf16[64,2560]{1,0:T(8,128)(2,1)S(1)}, u32[]{:S(2)}, u32[]{:S(2)}) collective-permute-start(bf16[64,2560]{1,0:T(8,128)(2,1)S(1)} %fusion.22), channel_id=1, source_target_pairs={{8,0},{16,8},{24,16},{9,1},{17,9},{25,17},{10,2},{18,10},{26,18},{... | collective-permute-start | bytes 983048 | tf_op jit(solution)/shard_map/ppermute | solution.py:38

commit v17 on v13

--- a/solution.py
+++ b/solution.py
@@ -18,12 +18,14 @@
     return lax.ppermute(x, axis, perm)
 
 
-def suffix_pipeline(own, axis, n_chunks):
+def suffix_pipeline(pieces, axis):
     length, index = (lax.axis_size(axis), lax.axis_index(axis))
-    rows, cols = own.shape
-    height = rows // n_chunks
-    chunks = own.reshape(n_chunks, height, cols)
-    pad = jnp.zeros((length - 1, height, cols), own.dtype)
+    n_chunks = len(pieces)
+    height, cols = pieces[0].shape
+    rows = n_chunks * height
+    own = pieces[0].dtype
+    chunks = jnp.stack(pieces, axis=0)
+    pad = jnp.zeros((length - 1, height, cols), own)
     padded = jnp.concatenate((pad, chunks, pad), axis=0)
     steps = n_chunks + length - 1
     ordered = lax.dynamic_slice_in_dim(padded, index, steps, axis=0)
@@ -31,7 +33,7 @@
     recv = jnp.zeros((height, cols), jnp.bfloat16)
     done = []
     for tau in range(steps):
-        acc = ordered[tau] + recv.astype(jnp.float32)
+        acc = (pieces[0] if tau == 0 else ordered[tau]) + recv.astype(jnp.float32)
         done.append(acc)
         if tau < steps - 1:
             recv = lax.ppermute(acc.astype(jnp.bfloat16), axis, perm)
@@ -142,23 +144,31 @@
     head_index = lax.axis_index("head")
     out_cols = w_key.shape[1] // head_len
 
-    def partial_for(b):
+    height = tok_rows // CHAIN_CHUNKS
+
+    def partial_for(b, rows):
         start = b * out_cols
         wk = lax.dynamic_slice_in_dim(w_key[0], start, out_cols, axis=0)
         wv = lax.dynamic_slice_in_dim(w_value[0], start, out_cols, axis=0)
-        part = lax.dot_general(grad_key, wk, contract, preferred_element_type=jnp.float32)
-        return part + lax.dot_general(grad_value, wv, contract, preferred_element_type=jnp.float32)
+        part = lax.dot_general(grad_key[rows], wk, contract, preferred_element_type=jnp.float32)
+        return part + lax.dot_general(
+            grad_value[rows], wv, contract, preferred_element_type=jnp.float32
+        )
 
-    received = []
-    for d in range(1, head_len):
-        target = lax.rem(head_index + d, head_len)
-        send = partial_for(target).astype(jnp.bfloat16)
-        perm = [(h, (h + d) % head_len) for h in range(head_len)]
-        received.append(lax.ppermute(send, "head", perm))
-    reduced = partial_for(head_index)
-    for got in received:
-        reduced = reduced + got.astype(jnp.float32)
-    result = suffix_pipeline(reduced, "segment", CHAIN_CHUNKS)
+    pieces = []
+    for c in range(CHAIN_CHUNKS):
+        rows = slice(c * height, (c + 1) * height)
+        received = []
+        for d in range(1, head_len):
+            target = lax.rem(head_index + d, head_len)
+            send = partial_for(target, rows).astype(jnp.bfloat16)
+            perm = [(h, (h + d) % head_len) for h in range(head_len)]
+            received.append(lax.ppermute(send, "head", perm))
+        reduced = partial_for(head_index, rows)
+        for got in received:
+            reduced = reduced + got.astype(jnp.float32)
+        pieces.append(reduced)
+    result = suffix_pipeline(pieces, "segment")
     return result[None]
 
 

time: 83.3 us -> 84.7 us (1.017)
  matrix products: 5.63 us -> 8.8 us
  local copies, waits for them, and re-layouts: 4.4 us -> 3.11 us
    ppermute x6, waiting for transfers between devices: 6.86 us -> 9.62 us  [shifted(): return lax.ppermute(x, axis, perm)]
    dot_general x4 -> x8, matrix products: 3.11 us -> 5.5 us  [the longest x4 3.38 us: partial_for(): lax.dot_general(grad_value[rows], wv, contract, preferred_element_type=jn...]
    ppermute x4, waiting for transfers between devices: 35.9 us -> 34 us  [suffix_pipeline(): recv = lax.ppermute(acc.astype(jnp.bfloat16), axis, perm)]
    ppermute x1 -> x2, waiting for transfers between devices: 1.74 us -> 0.01 us  [per_device(): received.append(lax.ppermute(send, 'head', perm))]
    unnamed x23 -> x18, local copies, waits for them, and re-layouts: 2.65 us -> 1.4 us
  transfers between devices with their start and end apart: 11 -> 12, of which waited for: 9 -> 7; matrix products, arithmetic and copies ran while one was open for 3% -> 6% of each run, Pallas kernels for 0% -> 0%
where the time goes in v17:
time: 84.7 us; the launch traced here: 84.3 us
  waiting for transfers between devices  43.7 us (52%)
  starting transfers between devices  19.2 us (23%)
  matrix products  8.8 us (10%)
  Pallas kernels  5.86 us (7%)
  other arithmetic  3.28 us (4%)
  local copies, waits for them, and re-layouts  3.11 us (4%)
    ppermute x4, waiting for transfers between devices, suffix_pipeline(): recv = lax.ppermute(acc.astype(jnp.bfloat16), axis, perm)  34 us
    ppermute x6, starting transfers between devices, shifted(): return lax.ppermute(x, axis, perm)  13.5 us
    ppermute x6, waiting for transfers between devices, shifted(): return lax.ppermute(x, axis, perm)  9.62 us
    pallas_call x1, Pallas kernels, attention_terms(): pl.pallas_call(kernel, out_shape=(jax.ShapeDtypeStruct((tok_rows, 2 * kv_...  5.86 us
    ppermute x4, starting transfers between devices, suffix_pipeline(): recv = lax.ppermute(acc.astype(jnp.bfloat16), axis, perm)  5.17 us
    dot_general x4, matrix products, partial_for(): lax.dot_general(grad_value[rows], wv, contract, preferred_element_type=jn...  3.38 us
    dot_general x1, matrix products, per_device(): jnp.dot(tokens, w_value[0], preferred_element_type=jnp.float32)  2.79 us
    dot_general x4, matrix products, partial_for(): lax.dot_general(grad_key[rows], wk, contract, preferred_element_type=jnp....  2.11 us
  transfers between devices with their start and end apart: 12, of which 7 were waited for; matrix products, arithmetic and copies ran while one was open for 6% of the time, Pallas kernels for 0%

profile of v17, /device:TPU:0, one launch (start us, length us, event | category | flops | bytes accessed | tf_op | source)
XLA Modules:
  0.0 84.3 jit_solution(6106342757706876697)
XLA Ops:
  0.0 0.0 copy-start
  0.0 0.0 copy-start.2
  0.0 2.8 %fusion.39 = bf16[128,256]{1,0:T(8,128)(2,1)S(1)} fusion(bf16[1,5120,256]{2,1,0:T(8,128)(2,1)} %param.10, bf16[1,128,5120]{2,1,0:T(8,128)(2,1)} %param.6), kind=kOutput, calls=%fused_computation.43 | convolution fusion | flops 335577088 | bytes 3997696 | tf_op jit(solution)/shard_map/dot_general | solution.py:111
  2.8 0.1 copy-done
  2.9 0.4 copy-done.2
  3.3 0.5 fusion.34
  3.8 0.0 copy-start.3
  3.8 5.8 %collective-permute-start.2 = (bf16[128,512]{1,0:T(8,128)(2,1)S(1)}, bf16[128,512]{1,0:T(8,128)(2,1)S(1)}, u32[]{:S(2)}, u32[]{:S(2)}) collective-permute-start(bf16[128,512]{1,0:T(8,128)(2,1)S(1)} %pad_maximum_fusion.refs_2_), channel_id=1, source_target_pairs={{0,6},{1,7},{8,14},{9,15},{16,22},{17,23},{24,30},{25,31}} | collective-permute-start | bytes 393224 | tf_op jit(solution)/shard_map/ppermute | solution.py:18
  9.7 1.3 %collective-permute-start.1 = (bf16[128,512]{1,0:T(8,128)(2,1)S(1)}, bf16[128,512]{1,0:T(8,128)(2,1)S(1)}, u32[]{:S(2)}, u32[]{:S(2)}) collective-permute-start(bf16[128,512]{1,0:T(8,128)(2,1)S(1)} %pad_maximum_fusion.refs_2_), channel_id=1, source_target_pairs={{0,4},{2,6},{1,5},{3,7},{8,12},{10,14},{9,13},{11,15},{16,20},{18,... | collective-permute-start | bytes 393224 | tf_op jit(solution)/shard_map/ppermute | solution.py:18
  11.0 2.5 %collective-permute-start = (bf16[128,512]{1,0:T(8,128)(2,1)S(1)}, bf16[128,512]{1,0:T(8,128)(2,1)S(1)}, u32[]{:S(2)}, u32[]{:S(2)}) collective-permute-start(bf16[128,512]{1,0:T(8,128)(2,1)S(1)} %pad_maximum_fusion.refs_2_), channel_id=1, source_target_pairs={{0,2},{2,4},{4,6},{1,3},{3,5},{5,7},{8,10},{10,12},{12,14},{9,11},... | collective-permute-start | bytes 393224 | tf_op jit(solution)/shard_map/ppermute | solution.py:18
  13.5 0.1 fusion.71
  13.6 0.1 fusion.69
  13.6 0.2 copy.28
  13.8 0.0 copy-done.7
  13.9 0.2 copy.25
  14.1 0.1 copy.24
  14.2 0.8 %broadcast_select_fusion = (s32[512,1]{1,0:T(8,128)}, s32[512,1]{1,0:T(8,128)}) fusion(pred[512,1]{1,0:T(8,128)(4,1)S(1)} %copy.25, s32[512,1]{1,0:T(8,128)S(1)} %copy.24, pred[1,512]{0,1:T(8,128)(4,1)S(1)} %copy.28), kind=kLoop, calls=%fused_computation.63 | loop fusion | flops 1024 | bytes 7168 | tf_op jit(solution)/shard_map/jit(_where)/select_n | solution.py:133
  15.1 0.0 collective-permute-done.2.refs_5_
  15.1 1.4 %collective-permute-done.1.refs_4_ = bf16[128,512]{1,0:T(8,128)(2,1)S(1)} collective-permute-done((bf16[128,512]{1,0:T(8,128)(2,1)S(1)}, bf16[128,512]{1,0:T(8,128)(2,1)S(1)}, u32[]{:S(2)}, u32[]{:S(2)}) %collective-permute-start.1) | collective-permute-done | bytes 131104 | tf_op jit(solution)/shard_map/ppermute | solution.py:18
  16.5 0.0 collective-permute-done.refs_3_
  16.5 0.0 copy-done.3
  16.5 0.0 copy-done.4
  16.5 0.6 copy-done.5
  17.2 0.1 copy-done.6
  17.2 5.9 %shard_map.64 = (f32[128,512]{1,0:T(8,128)}, bf16[128,512]{1,0:T(8,128)(2,1)}, bf16[128,512]{1,0:T(8,128)(2,1)}, bf16[128,512]{1,0:T(8,128)(2,1)}) custom-call(bf16[10,128,128]{2,1,0:T(8,128)(2,1)} %bitcast.113, bf16[10,128,128]{2,1,0:T(8,128)(2,1)} %bitcast.114, bf16[128,512]{1,0:T(8,128)(2,1)} %copy-done.3, bf16[128,512]{1,0:T(8,128)(2,1)} %copy-done.6, ...), custom_call_target="tpu_custom_call" | custom-call | tf_op jit(solution)/shard_map/pallas_call | solution.py:90
  23.1 1.3 %collective-permute-start.3 = (bf16[128,512]{1,0:T(8,128)(2,1)}, bf16[128,512]{1,0:T(8,128)(2,1)S(1)}, u32[]{:S(2)}, u32[]{:S(2)}) collective-permute-start(bf16[128,512]{1,0:T(8,128)(2,1)} %get-tuple-element.10), channel_id=1, source_target_pairs={{2,0},{4,2},{6,4},{3,1},{5,3},{7,5},{10,8},{12,10},{14,12},{11,9},... | collective-permute-start | bytes 393224 | tf_op jit(solution)/shard_map/ppermute | solution.py:18
  24.4 1.3 %collective-permute-start.4 = (bf16[128,512]{1,0:T(8,128)(2,1)}, bf16[128,512]{1,0:T(8,128)(2,1)S(1)}, u32[]{:S(2)}, u32[]{:S(2)}) collective-permute-start(bf16[128,512]{1,0:T(8,128)(2,1)} %get-tuple-element.11), channel_id=1, source_target_pairs={{4,0},{6,2},{5,1},{7,3},{12,8},{14,10},{13,9},{15,11},{20,16},{22,... | collective-permute-start | bytes 393224 | tf_op jit(solution)/shard_map/ppermute | solution.py:18
  25.7 1.3 %collective-permute-start.5 = (bf16[128,512]{1,0:T(8,128)(2,1)}, bf16[128,512]{1,0:T(8,128)(2,1)S(1)}, u32[]{:S(2)}, u32[]{:S(2)}) collective-permute-start(bf16[128,512]{1,0:T(8,128)(2,1)} %get-tuple-element.12), channel_id=1, source_target_pairs={{6,0},{7,1},{14,8},{15,9},{22,16},{23,17},{30,24},{31,25}} | collective-permute-start | bytes 393224 | tf_op jit(solution)/shard_map/ppermute | solution.py:18
  27.0 0.0 copy-start.1
  27.0 3.1 %collective-permute-done.3 = bf16[128,512]{1,0:T(8,128)(2,1)S(1)} collective-permute-done((bf16[128,512]{1,0:T(8,128)(2,1)}, bf16[128,512]{1,0:T(8,128)(2,1)S(1)}, u32[]{:S(2)}, u32[]{:S(2)}) %collective-permute-start.3) | collective-permute-done | bytes 131104 | tf_op jit(solution)/shard_map/ppermute | solution.py:18
  30.2 5.0 %collective-permute-done.4 = bf16[128,512]{1,0:T(8,128)(2,1)S(1)} collective-permute-done((bf16[128,512]{1,0:T(8,128)(2,1)}, bf16[128,512]{1,0:T(8,128)(2,1)S(1)}, u32[]{:S(2)}, u32[]{:S(2)}) %collective-permute-start.4) | collective-permute-done | bytes 131104 | tf_op jit(solution)/shard_map/ppermute | solution.py:18
  35.2 0.0 collective-permute-done.5
  35.2 1.0 %add_convert_fusion = bf16[128,512]{1,0:T(8,128)(2,1)S(1)} fusion(bf16[128,512]{1,0:T(8,128)(2,1)S(1)} %collective-permute-done.5, bf16[128,512]{1,0:T(8,128)(2,1)S(1)} %collective-permute-done.4, f32[128,512]{1,0:T(8,128)} %get-tuple-element.9, bf16[128,512]{1,0:T(8,128)(2,1)S(1)} %collective-permute-done.3), kind=kLoop, calls=%fused_computation.60 | loop fusion | flops 458752 | bytes 786432 | tf_op jit(solution)/shard_map/convert.1
  36.2 1.8 %fusion.14 = f32[64,2560]{1,0:T(8,128)S(1)} fusion(bf16[1,5120,256]{2,1,0:T(8,128)(2,1)} %param.10, s32[]{:T(128)S(6)} %select_n.34, bf16[128,512]{1,0:T(8,128)(2,1)S(1)} %add_convert_fusion), kind=kOutput, calls=%fused_computation.22 | convolution fusion | flops 83886080 | bytes 1998852 | tf_op jit(solution)/shard_map/dot_general | solution.py:154
  38.0 0.0 copy-done.1
  38.1 0.5 fusion.12
  38.6 0.5 fusion.3
  39.1 0.1 collective-permute-start.6
  39.2 0.5 fusion.4
  39.7 0.5 collective-permute-start.7
  40.3 0.5 fusion.18
  40.8 0.5 fusion.20
  41.3 0.0 collective-permute-done.6
  41.3 0.5 constant_dynamic-update-slice_fusion
  41.9 1.3 %collective-permute-start.8 = (bf16[64,2560]{1,0:T(8,128)(2,1)S(1)}, bf16[64,2560]{1,0:T(8,128)(2,1)S(1)}, u32[]{:S(2)}, u32[]{:S(2)}) collective-permute-start(bf16[64,2560]{1,0:T(8,128)(2,1)S(1)} %convert_element_type.64), channel_id=1, source_target_pairs={{8,0},{16,8},{24,16},{9,1},{17,9},{25,17},{10,2},{18,10},{26,18},{... | collective-permute-start | bytes 983048 | tf_op jit(solution)/shard_map/ppermute | solution.py:39
  43.2 0.0 collective-permute-done.7
  43.2 0.5 fusion.2
  43.7 0.2 broadcast_in_dim.13
  43.9 0.8 fusion.7
  44.8 8.7 %collective-permute-done.8 = bf16[64,2560]{1,0:T(8,128)(2,1)S(1)} collective-permute-done((bf16[64,2560]{1,0:T(8,128)(2,1)S(1)}, bf16[64,2560]{1,0:T(8,128)(2,1)S(1)}, u32[]{:S(2)}, u32[]{:S(2)}) %collective-permute-start.8) | collective-permute-done | bytes 327712 | tf_op jit(solution)/shard_map/ppermute | solution.py:39
  53.4 0.1 fusion.50
  53.5 1.3 %collective-permute-start.9 = (bf16[64,2560]{1,0:T(8,128)(2,1)S(1)}, bf16[64,2560]{1,0:T(8,128)(2,1)S(1)}, u32[]{:S(2)}, u32[]{:S(2)}) collective-permute-start(bf16[64,2560]{1,0:T(8,128)(2,1)S(1)} %fusion.50), channel_id=1, source_target_pairs={{8,0},{16,8},{24,16},{9,1},{17,9},{25,17},{10,2},{18,10},{26,18},{... | collective-permute-start | bytes 983048 | tf_op jit(solution)/shard_map/ppermute | solution.py:39
  54.8 0.1 bitcast_dynamic-update-slice_fusion.2
  54.8 9.3 %collective-permute-done.9 = bf16[64,2560]{1,0:T(8,128)(2,1)S(1)} collective-permute-done((bf16[64,2560]{1,0:T(8,128)(2,1)S(1)}, bf16[64,2560]{1,0:T(8,128)(2,1)S(1)}, u32[]{:S(2)}, u32[]{:S(2)}) %collective-permute-start.9) | collective-permute-done | bytes 327712 | tf_op jit(solution)/shard_map/ppermute | solution.py:39
  64.1 0.1 fusion.51
  64.2 1.3 %collective-permute-start.10 = (bf16[64,2560]{1,0:T(8,128)(2,1)S(1)}, bf16[64,2560]{1,0:T(8,128)(2,1)S(1)}, u32[]{:S(2)}, u32[]{:S(2)}) collective-permute-start(bf16[64,2560]{1,0:T(8,128)(2,1)S(1)} %fusion.51), channel_id=1, source_target_pairs={{8,0},{16,8},{24,16},{9,1},{17,9},{25,17},{10,2},{18,10},{26,18},{... | collective-permute-start | bytes 983048 | tf_op jit(solution)/shard_map/ppermute | solution.py:39
  65.5 0.1 bitcast_dynamic-update-slice_fusion.1
  65.6 8.5 %collective-permute-done.10 = bf16[64,2560]{1,0:T(8,128)(2,1)S(1)} collective-permute-done((bf16[64,2560]{1,0:T(8,128)(2,1)S(1)}, bf16[64,2560]{1,0:T(8,128)(2,1)S(1)}, u32[]{:S(2)}, u32[]{:S(2)}) %collective-permute-start.10) | collective-permute-done | bytes 327712 | tf_op jit(solution)/shard_map/ppermute | solution.py:39
  74.0 0.1 fusion.52
  74.1 1.3 %collective-permute-start.11 = (bf16[64,2560]{1,0:T(8,128)(2,1)S(1)}, bf16[64,2560]{1,0:T(8,128)(2,1)S(1)}, u32[]{:S(2)}, u32[]{:S(2)}) collective-permute-start(bf16[64,2560]{1,0:T(8,128)(2,1)S(1)} %fusion.52), channel_id=1, source_target_pairs={{8,0},{16,8},{24,16},{9,1},{17,9},{25,17},{10,2},{18,10},{26,18},{... | collective-permute-start | bytes 983048 | tf_op jit(solution)/shard_map/ppermute | solution.py:39
  75.4 0.1 bitcast_dynamic-update-slice_fusion
  75.5 7.6 %collective-permute-done.11 = bf16[64,2560]{1,0:T(8,128)(2,1)S(1)} collective-permute-done((bf16[64,2560]{1,0:T(8,128)(2,1)S(1)}, bf16[64,2560]{1,0:T(8,128)(2,1)S(1)}, u32[]{:S(2)}, u32[]{:S(2)}) %collective-permute-start.11) | collective-permute-done | bytes 327712 | tf_op jit(solution)/shard_map/ppermute | solution.py:39
  83.1 0.1 fusion.46
  83.1 1.2 %constant_dynamic-slice_fusion = f32[2,64,2560]{2,1,0:T(8,128)} fusion(f32[5,64,2560]{2,1,0:T(8,128)S(1)} %fusion.46, s32[]{:T(128)S(6)} %select_n.36), kind=kLoop, calls=%fused_computation.78 | loop fusion | bytes 2621444 | tf_op jit(solution)/shard_map/dynamic_slice | solution.py:41
  (10 shorter events, 0.1 us)
Async XLA Ops:
  0.0 2.9 %copy-start = (bf16[1,5120,256]{2,1,0:T(8,128)(2,1)S(1)}, bf16[1,5120,256]{2,1,0:T(8,128)(2,1)}, u32[]{:S(2)}) copy-start(bf16[1,5120,256]{2,1,0:T(8,128)(2,1)} %param.9) | copy-start | bytes 7864324
  0.0 3.3 %copy-start.2 = (bf16[1,128,5120]{2,1,0:T(8,128)(2,1)S(1)}, bf16[1,128,5120]{2,1,0:T(8,128)(2,1)}, u32[]{:S(2)}) copy-start(bf16[1,128,5120]{2,1,0:T(8,128)(2,1)} %param.6) | copy-start | bytes 3932164
  3.3 10.6 %copy-start.7 = (s32[512]{0:T(512)S(1)}, s32[512]{0:T(512)}, u32[]{:S(2)}) copy-start(s32[512]{0:T(512)} %param.11) | copy-start | bytes 6148
  3.8 12.7 %copy-start.3 = (bf16[128,512]{1,0:T(8,128)(2,1)}, bf16[128,512]{1,0:T(8,128)(2,1)S(1)}, u32[]{:S(2)}) copy-start(bf16[128,512]{1,0:T(8,128)(2,1)S(1)} %pad_maximum_fusion.refs_2_) | copy-start | bytes 393220
  3.8 11.3 %collective-permute-start.2 = (bf16[128,512]{1,0:T(8,128)(2,1)S(1)}, bf16[128,512]{1,0:T(8,128)(2,1)S(1)}, u32[]{:S(2)}, u32[]{:S(2)}) collective-permute-start(bf16[128,512]{1,0:T(8,128)(2,1)S(1)} %pad_maximum_fusion.refs_2_), channel_id=1, source_target_pairs={{0,6},{1,7},{8,14},{9,15},{16,22},{17,23},{24,30},{25,31}} | collective-permute-start | bytes 393224 | tf_op jit(solution)/shard_map/ppermute | solution.py:18
  9.7 6.8 %collective-permute-start.1 = (bf16[128,512]{1,0:T(8,128)(2,1)S(1)}, bf16[128,512]{1,0:T(8,128)(2,1)S(1)}, u32[]{:S(2)}, u32[]{:S(2)}) collective-permute-start(bf16[128,512]{1,0:T(8,128)(2,1)S(1)} %pad_maximum_fusion.refs_2_), channel_id=1, source_target_pairs={{0,4},{2,6},{1,5},{3,7},{8,12},{10,14},{9,13},{11,15},{16,20},{18,... | collective-permute-start | bytes 393224 | tf_op jit(solution)/shard_map/ppermute | solution.py:18
  11.0 5.5 %collective-permute-start = (bf16[128,512]{1,0:T(8,128)(2,1)S(1)}, bf16[128,512]{1,0:T(8,128)(2,1)S(1)}, u32[]{:S(2)}, u32[]{:S(2)}) collective-permute-start(bf16[128,512]{1,0:T(8,128)(2,1)S(1)} %pad_maximum_fusion.refs_2_), channel_id=1, source_target_pairs={{0,2},{2,4},{4,6},{1,3},{3,5},{5,7},{8,10},{10,12},{12,14},{9,11},... | collective-permute-start | bytes 393224 | tf_op jit(solution)/shard_map/ppermute | solution.py:18
  15.1 1.5 %copy-start.4 = (bf16[128,512]{1,0:T(8,128)(2,1)}, bf16[128,512]{1,0:T(8,128)(2,1)S(1)}, u32[]{:S(2)}) copy-start(bf16[128,512]{1,0:T(8,128)(2,1)S(1)} %collective-permute-done.2.refs_5_) | copy-start | bytes 393220
  16.5 0.7 copy-start.5
  16.5 0.7 copy-start.6
  23.1 7.1 %collective-permute-start.3 = (bf16[128,512]{1,0:T(8,128)(2,1)}, bf16[128,512]{1,0:T(8,128)(2,1)S(1)}, u32[]{:S(2)}, u32[]{:S(2)}) collective-permute-start(bf16[128,512]{1,0:T(8,128)(2,1)} %get-tuple-element.10), channel_id=1, source_target_pairs={{2,0},{4,2},{6,4},{3,1},{5,3},{7,5},{10,8},{12,10},{14,12},{11,9},... | collective-permute-start | bytes 393224 | tf_op jit(solution)/shard_map/ppermute | solution.py:18
  24.4 10.8 %collective-permute-start.4 = (bf16[128,512]{1,0:T(8,128)(2,1)}, bf16[128,512]{1,0:T(8,128)(2,1)S(1)}, u32[]{:S(2)}, u32[]{:S(2)}) collective-permute-start(bf16[128,512]{1,0:T(8,128)(2,1)} %get-tuple-element.11), channel_id=1, source_target_pairs={{4,0},{6,2},{5,1},{7,3},{12,8},{14,10},{13,9},{15,11},{20,16},{22,... | collective-permute-start | bytes 393224 | tf_op jit(solution)/shard_map/ppermute | solution.py:18
  25.7 9.5 %collective-permute-start.5 = (bf16[128,512]{1,0:T(8,128)(2,1)}, bf16[128,512]{1,0:T(8,128)(2,1)S(1)}, u32[]{:S(2)}, u32[]{:S(2)}) collective-permute-start(bf16[128,512]{1,0:T(8,128)(2,1)} %get-tuple-element.12), channel_id=1, source_target_pairs={{6,0},{7,1},{14,8},{15,9},{22,16},{23,17},{30,24},{31,25}} | collective-permute-start | bytes 393224 | tf_op jit(solution)/shard_map/ppermute | solution.py:18
  27.0 11.0 %copy-start.1 = (bf16[1,5120,256]{2,1,0:T(8,128)(2,1)S(1)}, bf16[1,5120,256]{2,1,0:T(8,128)(2,1)}, u32[]{:S(2)}) copy-start(bf16[1,5120,256]{2,1,0:T(8,128)(2,1)} %param.10) | copy-start | bytes 7864324
  39.1 2.2 %collective-permute-start.6 = (bf16[64,2560]{1,0:T(8,128)(2,1)S(1)}, bf16[64,2560]{1,0:T(8,128)(2,1)S(1)}, u32[]{:S(2)}, u32[]{:S(2)}) collective-permute-start(bf16[64,2560]{1,0:T(8,128)(2,1)S(1)} %fusion.3), channel_id=1, source_target_pairs={{0,1},{1,0},{2,3},{3,2},{4,5},{5,4},{6,7},{7,6},{8,9},{9,8},{10,11... | collective-permute-start | bytes 983048 | tf_op jit(solution)/shard_map/ppermute | solution.py:166
  39.7 3.5 %collective-permute-start.7 = (bf16[64,2560]{1,0:T(8,128)(2,1)S(1)}, bf16[64,2560]{1,0:T(8,128)(2,1)S(1)}, u32[]{:S(2)}, u32[]{:S(2)}) collective-permute-start(bf16[64,2560]{1,0:T(8,128)(2,1)S(1)} %fusion.4), channel_id=1, source_target_pairs={{0,1},{1,0},{2,3},{3,2},{4,5},{5,4},{6,7},{7,6},{8,9},{9,8},{10,11... | collective-permute-start | bytes 983048 | tf_op jit(solution)/shard_map/ppermute | solution.py:166
  41.9 11.5 %collective-permute-start.8 = (bf16[64,2560]{1,0:T(8,128)(2,1)S(1)}, bf16[64,2560]{1,0:T(8,128)(2,1)S(1)}, u32[]{:S(2)}, u32[]{:S(2)}) collective-permute-start(bf16[64,2560]{1,0:T(8,128)(2,1)S(1)} %convert_element_type.64), channel_id=1, source_target_pairs={{8,0},{16,8},{24,16},{9,1},{17,9},{25,17},{10,2},{18,10},{26,18},{... | collective-permute-start | bytes 983048 | tf_op jit(solution)/shard_map/ppermute | solution.py:39
  53.5 10.7 %collective-permute-start.9 = (bf16[64,2560]{1,0:T(8,128)(2,1)S(1)}, bf16[64,2560]{1,0:T(8,128)(2,1)S(1)}, u32[]{:S(2)}, u32[]{:S(2)}) collective-permute-start(bf16[64,2560]{1,0:T(8,128)(2,1)S(1)} %fusion.50), channel_id=1, source_target_pairs={{8,0},{16,8},{24,16},{9,1},{17,9},{25,17},{10,2},{18,10},{26,18},{... | collective-permute-start | bytes 983048 | tf_op jit(solution)/shard_map/ppermute | solution.py:39
  64.2 9.8 %collective-permute-start.10 = (bf16[64,2560]{1,0:T(8,128)(2,1)S(1)}, bf16[64,2560]{1,0:T(8,128)(2,1)S(1)}, u32[]{:S(2)}, u32[]{:S(2)}) collective-permute-start(bf16[64,2560]{1,0:T(8,128)(2,1)S(1)} %fusion.51), channel_id=1, source_target_pairs={{8,0},{16,8},{24,16},{9,1},{17,9},{25,17},{10,2},{18,10},{26,18},{... | collective-permute-start | bytes 983048 | tf_op jit(solution)/shard_map/ppermute | solution.py:39
  74.1 9.0 %collective-permute-start.11 = (bf16[64,2560]{1,0:T(8,128)(2,1)S(1)}, bf16[64,2560]{1,0:T(8,128)(2,1)S(1)}, u32[]{:S(2)}, u32[]{:S(2)}) collective-permute-start(bf16[64,2560]{1,0:T(8,128)(2,1)S(1)} %fusion.52), channel_id=1, source_target_pairs={{8,0},{16,8},{24,16},{9,1},{17,9},{25,17},{10,2},{18,10},{26,18},{... | collective-permute-start | bytes 983048 | tf_op jit(solution)/shard_map/ppermute | solution.py:39

commit v18 on v13

--- a/solution.py
+++ b/solution.py
@@ -31,7 +31,7 @@
     recv = jnp.zeros((height, cols), jnp.bfloat16)
     done = []
     for tau in range(steps):
-        acc = ordered[tau] + recv.astype(jnp.float32)
+        acc = (chunks[0] if tau == 0 else ordered[tau]) + recv.astype(jnp.float32)
         done.append(acc)
         if tau < steps - 1:
             recv = lax.ppermute(acc.astype(jnp.bfloat16), axis, perm)

time: 83.3 us -> 82.1 us (0.986)
  waiting for transfers between devices: 44.5 us -> 43.4 us
    ppermute x4, waiting for transfers between devices: 35.9 us -> 34.8 us  [suffix_pipeline(): recv = lax.ppermute(acc.astype(jnp.bfloat16), axis, perm)]
  transfers between devices with their start and end apart: 11 -> 11, of which waited for: 9 -> 9; matrix products, arithmetic and copies ran while one was open for 3% -> 4% of each run, Pallas kernels for 0% -> 0%
where the time goes in v18:
time: 82.1 us; the launch traced here: 81.7 us
  waiting for transfers between devices  43.4 us (53%)
  starting transfers between devices  18.6 us (23%)
  Pallas kernels  5.86 us (7%)
  matrix products  5.63 us (7%)
  local copies, waits for them, and re-layouts  4.4 us (5%)
  other arithmetic  3.46 us (4%)
    ppermute x4, waiting for transfers between devices, suffix_pipeline(): recv = lax.ppermute(acc.astype(jnp.bfloat16), axis, perm)  34.8 us
    ppermute x6, starting transfers between devices, shifted(): return lax.ppermute(x, axis, perm)  13.5 us
    ppermute x6, waiting for transfers between devices, shifted(): return lax.ppermute(x, axis, perm)  6.86 us
    pallas_call x1, Pallas kernels, attention_terms(): pl.pallas_call(kernel, out_shape=(jax.ShapeDtypeStruct((tok_rows, 2 * kv_...  5.86 us
    ppermute x4, starting transfers between devices, suffix_pipeline(): recv = lax.ppermute(acc.astype(jnp.bfloat16), axis, perm)  5.17 us
    unnamed x23, local copies, waits for them, and re-layouts  2.65 us
    dot_general x1, matrix products, per_device(): jnp.dot(tokens, w_value[0], preferred_element_type=jnp.float32)  2.02 us
    dot_general x2, matrix products, partial_for(): lax.dot_general(grad_key, wk, contract, preferred_element_type=jnp.float32)  1.99 us
  transfers between devices with their start and end apart: 11, of which 9 were waited for; matrix products, arithmetic and copies ran while one was open for 4% of the time, Pallas kernels for 0%

profile of v18, /device:TPU:0, one launch (start us, length us, event | category | flops | bytes accessed | tf_op | source)
XLA Modules:
  0.0 81.7 jit_solution(15171964901418191792)
XLA Ops:
  0.0 0.0 copy-start
  0.0 0.0 copy-start.4
  0.0 0.0 copy-start.1
  0.0 1.7 %copy-done = bf16[1,5120,256]{2,1,0:T(8,128)(2,1)S(1)} copy-done((bf16[1,5120,256]{2,1,0:T(8,128)(2,1)S(1)}, bf16[1,5120,256]{2,1,0:T(8,128)(2,1)}, u32[]{:S(2)}) %copy-start) | copy-done | bytes 2621464
  1.7 2.0 %fusion.25 = bf16[128,256]{1,0:T(8,128)(2,1)S(1)} fusion(bf16[1,5120,256]{2,1,0:T(8,128)(2,1)S(1)} %copy-done, bf16[1,128,5120]{2,1,0:T(8,128)(2,1)} %param.6), kind=kOutput, calls=%fused_computation.26 | convolution fusion | flops 335577088 | bytes 3997696 | tf_op jit(solution)/shard_map/dot_general | solution.py:109
  3.8 0.0 copy-done.4
  3.8 0.0 copy-done.1
  3.8 0.0 copy-start.9
  3.8 0.5 fusion.20
  4.3 0.0 copy-start.5
  4.3 4.9 %collective-permute-start = (bf16[128,512]{1,0:T(8,128)(2,1)S(1)}, bf16[128,512]{1,0:T(8,128)(2,1)S(1)}, u32[]{:S(2)}, u32[]{:S(2)}) collective-permute-start(bf16[128,512]{1,0:T(8,128)(2,1)S(1)} %pad_maximum_fusion.refs_2_), channel_id=1, source_target_pairs={{0,2},{2,4},{4,6},{1,3},{3,5},{5,7},{8,10},{10,12},{12,14},{9,11},... | collective-permute-start | bytes 393224 | tf_op jit(solution)/shard_map/ppermute | solution.py:18
  9.2 3.4 %collective-permute-start.1 = (bf16[128,512]{1,0:T(8,128)(2,1)S(1)}, bf16[128,512]{1,0:T(8,128)(2,1)S(1)}, u32[]{:S(2)}, u32[]{:S(2)}) collective-permute-start(bf16[128,512]{1,0:T(8,128)(2,1)S(1)} %pad_maximum_fusion.refs_2_), channel_id=1, source_target_pairs={{0,4},{2,6},{1,5},{3,7},{8,12},{10,14},{9,13},{11,15},{16,20},{18,... | collective-permute-start | bytes 393224 | tf_op jit(solution)/shard_map/ppermute | solution.py:18
  12.7 1.3 %collective-permute-start.2 = (bf16[128,512]{1,0:T(8,128)(2,1)S(1)}, bf16[128,512]{1,0:T(8,128)(2,1)S(1)}, u32[]{:S(2)}, u32[]{:S(2)}) collective-permute-start(bf16[128,512]{1,0:T(8,128)(2,1)S(1)} %pad_maximum_fusion.refs_2_), channel_id=1, source_target_pairs={{0,6},{1,7},{8,14},{9,15},{16,22},{17,23},{24,30},{25,31}} | collective-permute-start | bytes 393224 | tf_op jit(solution)/shard_map/ppermute | solution.py:18
  14.0 0.0 copy-done.9
  14.0 0.2 copy.25
  14.2 0.1 fusion.49
  14.3 0.1 fusion.47
  14.4 0.2 copy.24
  14.6 0.2 copy.28
  14.8 0.8 %broadcast_select_fusion = (s32[512,1]{1,0:T(8,128)}, s32[512,1]{1,0:T(8,128)}) fusion(pred[512,1]{1,0:T(8,128)(4,1)S(1)} %copy.25, s32[512,1]{1,0:T(8,128)S(1)} %copy.24, pred[1,512]{0,1:T(8,128)(4,1)S(1)} %copy.28), kind=kLoop, calls=%fused_computation.48 | loop fusion | flops 1024 | bytes 7168 | tf_op jit(solution)/shard_map/jit(_where)/select_n | solution.py:131
  15.6 0.0 collective-permute-done.refs_3_
  15.6 0.0 copy-start.6
  15.6 0.1 collective-permute-done.1.refs_4_
  15.7 0.0 copy-start.7
  15.7 0.8 collective-permute-done.2.refs_5_
  16.5 0.0 copy-done.5
  16.5 0.0 copy-done.6
  16.5 0.0 copy-done.7
  16.5 0.6 copy-done.8
  17.1 5.9 %shard_map.64 = (f32[128,512]{1,0:T(8,128)}, bf16[128,512]{1,0:T(8,128)(2,1)}, bf16[128,512]{1,0:T(8,128)(2,1)}, bf16[128,512]{1,0:T(8,128)(2,1)}) custom-call(bf16[10,128,128]{2,1,0:T(8,128)(2,1)} %bitcast.102, bf16[10,128,128]{2,1,0:T(8,128)(2,1)} %bitcast.103, bf16[128,512]{1,0:T(8,128)(2,1)} %copy-done.5, bf16[128,512]{1,0:T(8,128)(2,1)} %copy-done.6, ...), custom_call_target="tpu_custom_call" | custom-call | tf_op jit(solution)/shard_map/pallas_call | solution.py:88
  23.0 1.3 %collective-permute-start.5 = (bf16[128,512]{1,0:T(8,128)(2,1)}, bf16[128,512]{1,0:T(8,128)(2,1)S(1)}, u32[]{:S(2)}, u32[]{:S(2)}) collective-permute-start(bf16[128,512]{1,0:T(8,128)(2,1)} %get-tuple-element.12), channel_id=1, source_target_pairs={{6,0},{7,1},{14,8},{15,9},{22,16},{23,17},{30,24},{31,25}} | collective-permute-start | bytes 393224 | tf_op jit(solution)/shard_map/ppermute | solution.py:18
  24.3 1.3 %collective-permute-start.4 = (bf16[128,512]{1,0:T(8,128)(2,1)}, bf16[128,512]{1,0:T(8,128)(2,1)S(1)}, u32[]{:S(2)}, u32[]{:S(2)}) collective-permute-start(bf16[128,512]{1,0:T(8,128)(2,1)} %get-tuple-element.11), channel_id=1, source_target_pairs={{4,0},{6,2},{5,1},{7,3},{12,8},{14,10},{13,9},{15,11},{20,16},{22,... | collective-permute-start | bytes 393224 | tf_op jit(solution)/shard_map/ppermute | solution.py:18
  25.6 1.3 %collective-permute-start.3 = (bf16[128,512]{1,0:T(8,128)(2,1)}, bf16[128,512]{1,0:T(8,128)(2,1)S(1)}, u32[]{:S(2)}, u32[]{:S(2)}) collective-permute-start(bf16[128,512]{1,0:T(8,128)(2,1)} %get-tuple-element.10), channel_id=1, source_target_pairs={{2,0},{4,2},{6,4},{3,1},{5,3},{7,5},{10,8},{12,10},{14,12},{11,9},... | collective-permute-start | bytes 393224 | tf_op jit(solution)/shard_map/ppermute | solution.py:18
  26.9 0.0 copy-start.2
  26.9 4.3 %collective-permute-done.5 = bf16[128,512]{1,0:T(8,128)(2,1)S(1)} collective-permute-done((bf16[128,512]{1,0:T(8,128)(2,1)}, bf16[128,512]{1,0:T(8,128)(2,1)S(1)}, u32[]{:S(2)}, u32[]{:S(2)}) %collective-permute-start.5) | collective-permute-done | bytes 131104 | tf_op jit(solution)/shard_map/ppermute | solution.py:18
  31.2 1.7 %collective-permute-done.4 = bf16[128,512]{1,0:T(8,128)(2,1)S(1)} collective-permute-done((bf16[128,512]{1,0:T(8,128)(2,1)}, bf16[128,512]{1,0:T(8,128)(2,1)S(1)}, u32[]{:S(2)}, u32[]{:S(2)}) %collective-permute-start.4) | collective-permute-done | bytes 131104 | tf_op jit(solution)/shard_map/ppermute | solution.py:18
  32.9 0.0 collective-permute-done.3
  32.9 1.0 %add_convert_fusion = bf16[128,512]{1,0:T(8,128)(2,1)S(1)} fusion(bf16[128,512]{1,0:T(8,128)(2,1)S(1)} %collective-permute-done.5, bf16[128,512]{1,0:T(8,128)(2,1)S(1)} %collective-permute-done.4, f32[128,512]{1,0:T(8,128)} %get-tuple-element.9, bf16[128,512]{1,0:T(8,128)(2,1)S(1)} %collective-permute-done.3), kind=kLoop, calls=%fused_computation.45 | loop fusion | flops 458752 | bytes 786432 | tf_op jit(solution)/shard_map/convert.1
  33.9 0.6 fusion.8
  34.5 0.0 copy-done.2
  34.5 1.4 %fusion.1 = bf16[128,2560]{1,0:T(8,128)(2,1)} fusion(f32[128,2560]{1,0:T(8,128)S(1)} %fusion.8, bf16[1,5120,256]{2,1,0:T(8,128)(2,1)S(1)} %copy-done.2, s32[]{:T(128)S(6)} %select_n.30, bf16[128,512]{1,0:T(8,128)(2,1)S(1)} %add_convert_fusion), kind=kOutput, calls=%fused_computation.6 | convolution fusion | flops 168427520 | bytes 3342340 | tf_op jit(solution)/shard_map/dot_general | solution.py:149
  35.9 0.0 collective-permute-start.6
  35.9 0.6 fusion.11
  36.4 1.7 %collective-permute-done.6 = bf16[128,2560]{1,0:T(8,128)(2,1)S(1)} collective-permute-done((bf16[128,2560]{1,0:T(8,128)(2,1)}, bf16[128,2560]{1,0:T(8,128)(2,1)S(1)}, u32[]{:S(2)}, u32[]{:S(2)}) %collective-permute-start.6) | collective-permute-done | bytes 655392 | tf_op jit(solution)/shard_map/ppermute | solution.py:157
  38.2 0.0 copy-done.3
  38.2 0.6 fusion
  38.9 1.3 %collective-permute-start.7 = (bf16[64,2560]{1,0:T(8,128)(2,1)S(1)}, bf16[64,2560]{1,0:T(8,128)(2,1)S(1)}, u32[]{:S(2)}, u32[]{:S(2)}) collective-permute-start(bf16[64,2560]{1,0:T(8,128)(2,1)S(1)} %slice.76), channel_id=1, source_target_pairs={{8,0},{16,8},{24,16},{9,1},{17,9},{25,17},{10,2},{18,10},{26,18},{... | collective-permute-start | bytes 983048 | tf_op jit(solution)/shard_map/ppermute | solution.py:37
  40.2 0.2 broadcast_in_dim.13
  40.4 1.0 %fusion.3 = f32[5,64,2560]{2,1,0:T(8,128)S(1)} fusion(s32[]{:T(128)S(6)} %select_n.31, f32[3,64,2560]{2,1,0:T(8,128)S(1)} %broadcast_in_dim.13, f32[2,64,2560]{2,1,0:T(8,128)S(1)} %bitcast.101), kind=kLoop, calls=%fused_computation.8 | loop fusion | flops 1638400 | bytes 6553604 | tf_op jit(solution)/shard_map/concatenate | solution.py:27
  41.4 9.1 %collective-permute-done.7 = bf16[64,2560]{1,0:T(8,128)(2,1)S(1)} collective-permute-done((bf16[64,2560]{1,0:T(8,128)(2,1)S(1)}, bf16[64,2560]{1,0:T(8,128)(2,1)S(1)}, u32[]{:S(2)}, u32[]{:S(2)}) %collective-permute-start.7) | collective-permute-done | bytes 327712 | tf_op jit(solution)/shard_map/ppermute | solution.py:37
  50.5 0.1 fusion.36
  50.6 1.3 %collective-permute-start.8 = (bf16[64,2560]{1,0:T(8,128)(2,1)S(1)}, bf16[64,2560]{1,0:T(8,128)(2,1)S(1)}, u32[]{:S(2)}, u32[]{:S(2)}) collective-permute-start(bf16[64,2560]{1,0:T(8,128)(2,1)S(1)} %fusion.36), channel_id=1, source_target_pairs={{8,0},{16,8},{24,16},{9,1},{17,9},{25,17},{10,2},{18,10},{26,18},{... | collective-permute-start | bytes 983048 | tf_op jit(solution)/shard_map/ppermute | solution.py:37
  51.9 0.1 bitcast_dynamic-update-slice_fusion.2
  51.9 9.4 %collective-permute-done.8 = bf16[64,2560]{1,0:T(8,128)(2,1)S(1)} collective-permute-done((bf16[64,2560]{1,0:T(8,128)(2,1)S(1)}, bf16[64,2560]{1,0:T(8,128)(2,1)S(1)}, u32[]{:S(2)}, u32[]{:S(2)}) %collective-permute-start.8) | collective-permute-done | bytes 327712 | tf_op jit(solution)/shard_map/ppermute | solution.py:37
  61.4 0.1 fusion.37
  61.4 1.3 %collective-permute-start.9 = (bf16[64,2560]{1,0:T(8,128)(2,1)S(1)}, bf16[64,2560]{1,0:T(8,128)(2,1)S(1)}, u32[]{:S(2)}, u32[]{:S(2)}) collective-permute-start(bf16[64,2560]{1,0:T(8,128)(2,1)S(1)} %fusion.37), channel_id=1, source_target_pairs={{8,0},{16,8},{24,16},{9,1},{17,9},{25,17},{10,2},{18,10},{26,18},{... | collective-permute-start | bytes 983048 | tf_op jit(solution)/shard_map/ppermute | solution.py:37
  62.7 0.1 bitcast_dynamic-update-slice_fusion.1
  62.8 8.6 %collective-permute-done.9 = bf16[64,2560]{1,0:T(8,128)(2,1)S(1)} collective-permute-done((bf16[64,2560]{1,0:T(8,128)(2,1)S(1)}, bf16[64,2560]{1,0:T(8,128)(2,1)S(1)}, u32[]{:S(2)}, u32[]{:S(2)}) %collective-permute-start.9) | collective-permute-done | bytes 327712 | tf_op jit(solution)/shard_map/ppermute | solution.py:37
  71.4 0.1 fusion.38
  71.4 1.3 %collective-permute-start.10 = (bf16[64,2560]{1,0:T(8,128)(2,1)S(1)}, bf16[64,2560]{1,0:T(8,128)(2,1)S(1)}, u32[]{:S(2)}, u32[]{:S(2)}) collective-permute-start(bf16[64,2560]{1,0:T(8,128)(2,1)S(1)} %fusion.38), channel_id=1, source_target_pairs={{8,0},{16,8},{24,16},{9,1},{17,9},{25,17},{10,2},{18,10},{26,18},{... | collective-permute-start | bytes 983048 | tf_op jit(solution)/shard_map/ppermute | solution.py:37
  72.7 0.1 bitcast_dynamic-update-slice_fusion
  72.8 7.7 %collective-permute-done.10 = bf16[64,2560]{1,0:T(8,128)(2,1)S(1)} collective-permute-done((bf16[64,2560]{1,0:T(8,128)(2,1)S(1)}, bf16[64,2560]{1,0:T(8,128)(2,1)S(1)}, u32[]{:S(2)}, u32[]{:S(2)}) %collective-permute-start.10) | collective-permute-done | bytes 327712 | tf_op jit(solution)/shard_map/ppermute | solution.py:37
  80.5 0.1 fusion.32
  80.6 1.2 %constant_dynamic-slice_fusion = f32[2,64,2560]{2,1,0:T(8,128)} fusion(f32[5,64,2560]{2,1,0:T(8,128)S(1)} %fusion.32, s32[]{:T(128)S(6)} %select_n.32), kind=kLoop, calls=%fused_computation.54 | loop fusion | bytes 2621444 | tf_op jit(solution)/shard_map/dynamic_slice | solution.py:39
  (9 shorter events, 0.1 us)
Async XLA Ops:
  0.0 1.7 %copy-start = (bf16[1,5120,256]{2,1,0:T(8,128)(2,1)S(1)}, bf16[1,5120,256]{2,1,0:T(8,128)(2,1)}, u32[]{:S(2)}) copy-start(bf16[1,5120,256]{2,1,0:T(8,128)(2,1)} %param.10) | copy-start | bytes 7864324
  0.0 3.8 %copy-start.4 = (bf16[1,128,5120]{2,1,0:T(8,128)(2,1)S(1)}, bf16[1,128,5120]{2,1,0:T(8,128)(2,1)}, u32[]{:S(2)}) copy-start(bf16[1,128,5120]{2,1,0:T(8,128)(2,1)} %param.6) | copy-start | bytes 3932164
  0.0 3.8 %copy-start.1 = (bf16[1,5120,256]{2,1,0:T(8,128)(2,1)S(1)}, bf16[1,5120,256]{2,1,0:T(8,128)(2,1)}, u32[]{:S(2)}) copy-start(bf16[1,5120,256]{2,1,0:T(8,128)(2,1)} %param.9) | copy-start | bytes 7864324
  3.8 10.2 %copy-start.9 = (s32[512]{0:T(512)S(1)}, s32[512]{0:T(512)}, u32[]{:S(2)}) copy-start(s32[512]{0:T(512)} %param.11) | copy-start | bytes 6148
  4.3 12.1 %copy-start.5 = (bf16[128,512]{1,0:T(8,128)(2,1)}, bf16[128,512]{1,0:T(8,128)(2,1)S(1)}, u32[]{:S(2)}) copy-start(bf16[128,512]{1,0:T(8,128)(2,1)S(1)} %pad_maximum_fusion.refs_2_) | copy-start | bytes 393220
  4.3 11.3 %collective-permute-start = (bf16[128,512]{1,0:T(8,128)(2,1)S(1)}, bf16[128,512]{1,0:T(8,128)(2,1)S(1)}, u32[]{:S(2)}, u32[]{:S(2)}) collective-permute-start(bf16[128,512]{1,0:T(8,128)(2,1)S(1)} %pad_maximum_fusion.refs_2_), channel_id=1, source_target_pairs={{0,2},{2,4},{4,6},{1,3},{3,5},{5,7},{8,10},{10,12},{12,14},{9,11},... | collective-permute-start | bytes 393224 | tf_op jit(solution)/shard_map/ppermute | solution.py:18
  9.2 6.5 %collective-permute-start.1 = (bf16[128,512]{1,0:T(8,128)(2,1)S(1)}, bf16[128,512]{1,0:T(8,128)(2,1)S(1)}, u32[]{:S(2)}, u32[]{:S(2)}) collective-permute-start(bf16[128,512]{1,0:T(8,128)(2,1)S(1)} %pad_maximum_fusion.refs_2_), channel_id=1, source_target_pairs={{0,4},{2,6},{1,5},{3,7},{8,12},{10,14},{9,13},{11,15},{16,20},{18,... | collective-permute-start | bytes 393224 | tf_op jit(solution)/shard_map/ppermute | solution.py:18
  12.7 3.8 %collective-permute-start.2 = (bf16[128,512]{1,0:T(8,128)(2,1)S(1)}, bf16[128,512]{1,0:T(8,128)(2,1)S(1)}, u32[]{:S(2)}, u32[]{:S(2)}) collective-permute-start(bf16[128,512]{1,0:T(8,128)(2,1)S(1)} %pad_maximum_fusion.refs_2_), channel_id=1, source_target_pairs={{0,6},{1,7},{8,14},{9,15},{16,22},{17,23},{24,30},{25,31}} | collective-permute-start | bytes 393224 | tf_op jit(solution)/shard_map/ppermute | solution.py:18
  15.6 0.9 %copy-start.6 = (bf16[128,512]{1,0:T(8,128)(2,1)}, bf16[128,512]{1,0:T(8,128)(2,1)S(1)}, u32[]{:S(2)}) copy-start(bf16[128,512]{1,0:T(8,128)(2,1)S(1)} %collective-permute-done.refs_3_) | copy-start | bytes 393220
  15.7 0.8 copy-start.7
  16.5 0.6 copy-start.8
  23.0 8.2 %collective-permute-start.5 = (bf16[128,512]{1,0:T(8,128)(2,1)}, bf16[128,512]{1,0:T(8,128)(2,1)S(1)}, u32[]{:S(2)}, u32[]{:S(2)}) collective-permute-start(bf16[128,512]{1,0:T(8,128)(2,1)} %get-tuple-element.12), channel_id=1, source_target_pairs={{6,0},{7,1},{14,8},{15,9},{22,16},{23,17},{30,24},{31,25}} | collective-permute-start | bytes 393224 | tf_op jit(solution)/shard_map/ppermute | solution.py:18
  24.3 8.6 %collective-permute-start.4 = (bf16[128,512]{1,0:T(8,128)(2,1)}, bf16[128,512]{1,0:T(8,128)(2,1)S(1)}, u32[]{:S(2)}, u32[]{:S(2)}) collective-permute-start(bf16[128,512]{1,0:T(8,128)(2,1)} %get-tuple-element.11), channel_id=1, source_target_pairs={{4,0},{6,2},{5,1},{7,3},{12,8},{14,10},{13,9},{15,11},{20,16},{22,... | collective-permute-start | bytes 393224 | tf_op jit(solution)/shard_map/ppermute | solution.py:18
  25.6 7.3 %collective-permute-start.3 = (bf16[128,512]{1,0:T(8,128)(2,1)}, bf16[128,512]{1,0:T(8,128)(2,1)S(1)}, u32[]{:S(2)}, u32[]{:S(2)}) collective-permute-start(bf16[128,512]{1,0:T(8,128)(2,1)} %get-tuple-element.10), channel_id=1, source_target_pairs={{2,0},{4,2},{6,4},{3,1},{5,3},{7,5},{10,8},{12,10},{14,12},{11,9},... | collective-permute-start | bytes 393224 | tf_op jit(solution)/shard_map/ppermute | solution.py:18
  26.9 7.6 %copy-start.2 = (bf16[1,5120,256]{2,1,0:T(8,128)(2,1)S(1)}, bf16[1,5120,256]{2,1,0:T(8,128)(2,1)}, u32[]{:S(2)}) copy-start(bf16[1,5120,256]{2,1,0:T(8,128)(2,1)} %param.9) | copy-start | bytes 7864324
  35.9 2.3 %collective-permute-start.6 = (bf16[128,2560]{1,0:T(8,128)(2,1)}, bf16[128,2560]{1,0:T(8,128)(2,1)S(1)}, u32[]{:S(2)}, u32[]{:S(2)}) collective-permute-start(bf16[128,2560]{1,0:T(8,128)(2,1)} %fusion.1), channel_id=1, source_target_pairs={{0,1},{1,0},{2,3},{3,2},{4,5},{5,4},{6,7},{7,6},{8,9},{9,8},{10,11... | collective-permute-start | bytes 1966088 | tf_op jit(solution)/shard_map/ppermute | solution.py:157
  35.9 2.3 %copy-start.3 = (bf16[1,5120,256]{2,1,0:T(8,128)(2,1)S(1)}, bf16[1,5120,256]{2,1,0:T(8,128)(2,1)}, u32[]{:S(2)}) copy-start(bf16[1,5120,256]{2,1,0:T(8,128)(2,1)} %param.9) | copy-start | bytes 7864324
  38.9 11.6 %collective-permute-start.7 = (bf16[64,2560]{1,0:T(8,128)(2,1)S(1)}, bf16[64,2560]{1,0:T(8,128)(2,1)S(1)}, u32[]{:S(2)}, u32[]{:S(2)}) collective-permute-start(bf16[64,2560]{1,0:T(8,128)(2,1)S(1)} %slice.76), channel_id=1, source_target_pairs={{8,0},{16,8},{24,16},{9,1},{17,9},{25,17},{10,2},{18,10},{26,18},{... | collective-permute-start | bytes 983048 | tf_op jit(solution)/shard_map/ppermute | solution.py:37
  50.6 10.8 %collective-permute-start.8 = (bf16[64,2560]{1,0:T(8,128)(2,1)S(1)}, bf16[64,2560]{1,0:T(8,128)(2,1)S(1)}, u32[]{:S(2)}, u32[]{:S(2)}) collective-permute-start(bf16[64,2560]{1,0:T(8,128)(2,1)S(1)} %fusion.36), channel_id=1, source_target_pairs={{8,0},{16,8},{24,16},{9,1},{17,9},{25,17},{10,2},{18,10},{26,18},{... | collective-permute-start | bytes 983048 | tf_op jit(solution)/shard_map/ppermute | solution.py:37
  61.4 9.9 %collective-permute-start.9 = (bf16[64,2560]{1,0:T(8,128)(2,1)S(1)}, bf16[64,2560]{1,0:T(8,128)(2,1)S(1)}, u32[]{:S(2)}, u32[]{:S(2)}) collective-permute-start(bf16[64,2560]{1,0:T(8,128)(2,1)S(1)} %fusion.37), channel_id=1, source_target_pairs={{8,0},{16,8},{24,16},{9,1},{17,9},{25,17},{10,2},{18,10},{26,18},{... | collective-permute-start | bytes 983048 | tf_op jit(solution)/shard_map/ppermute | solution.py:37
  71.4 9.1 %collective-permute-start.10 = (bf16[64,2560]{1,0:T(8,128)(2,1)S(1)}, bf16[64,2560]{1,0:T(8,128)(2,1)S(1)}, u32[]{:S(2)}, u32[]{:S(2)}) collective-permute-start(bf16[64,2560]{1,0:T(8,128)(2,1)S(1)} %fusion.38), channel_id=1, source_target_pairs={{8,0},{16,8},{24,16},{9,1},{17,9},{25,17},{10,2},{18,10},{26,18},{... | collective-permute-start | bytes 983048 | tf_op jit(solution)/shard_map/ppermute | solution.py:37

commit v19 on v18

--- a/solution.py
+++ b/solution.py
@@ -142,19 +142,23 @@
     head_index = lax.axis_index("head")
     out_cols = w_key.shape[1] // head_len
 
-    def partial_for(b):
-        start = b * out_cols
-        wk = lax.dynamic_slice_in_dim(w_key[0], start, out_cols, axis=0)
-        wv = lax.dynamic_slice_in_dim(w_value[0], start, out_cols, axis=0)
+    def partial_for(b, width=out_cols, offset=0):
+        start = b * out_cols + offset
+        wk = lax.dynamic_slice_in_dim(w_key[0], start, width, axis=0)
+        wv = lax.dynamic_slice_in_dim(w_value[0], start, width, axis=0)
         part = lax.dot_general(grad_key, wk, contract, preferred_element_type=jnp.float32)
         return part + lax.dot_general(grad_value, wv, contract, preferred_element_type=jnp.float32)
 
+    half = out_cols // 2
     received = []
     for d in range(1, head_len):
         target = lax.rem(head_index + d, head_len)
-        send = partial_for(target).astype(jnp.bfloat16)
         perm = [(h, (h + d) % head_len) for h in range(head_len)]
-        received.append(lax.ppermute(send, "head", perm))
+        pieces = [
+            lax.ppermute(partial_for(target, half, i * half).astype(jnp.bfloat16), "head", perm)
+            for i in range(2)
+        ]
+        received.append(jnp.concatenate(pieces, axis=1))
     reduced = partial_for(head_index)
     for got in received:
         reduced = reduced + got.astype(jnp.float32)

time: 82.1 us -> 85.2 us (1.038)
  matrix products: 5.63 us -> 8.78 us
  waiting for transfers between devices: 43.4 us -> 42.5 us
    dot_general x2 -> x3, matrix products: 1.99 us -> 4.95 us  [partial_for(): lax.dot_general(grad_key, wk, contract, preferred_element_type=jnp.float32)]
    ppermute x1 -> x2, waiting for transfers between devices: 1.74 us -> 0.89 us  [per_device(): lax.ppermute(partial_for(target, half, i * half).astype(jnp.bfloat16), 'h...]
    unnamed x23 -> x21, local copies, waits for them, and re-layouts: 2.65 us -> 2.91 us
  transfers between devices with their start and end apart: 11 -> 12, of which waited for: 9 -> 9; matrix products, arithmetic and copies ran while one was open for 4% -> 7% of each run, Pallas kernels for 0% -> 0%
where the time goes in v19:
time: 85.2 us; the launch traced here: 84.7 us
  waiting for transfers between devices  42.5 us (50%)
  starting transfers between devices  19.1 us (22%)
  matrix products  8.78 us (10%)
  Pallas kernels  5.86 us (7%)
  local copies, waits for them, and re-layouts  4.66 us (5%)
  other arithmetic  3.46 us (4%)
    ppermute x4, waiting for transfers between devices, suffix_pipeline(): recv = lax.ppermute(acc.astype(jnp.bfloat16), axis, perm)  34.7 us
    ppermute x6, starting transfers between devices, shifted(): return lax.ppermute(x, axis, perm)  13.5 us
    ppermute x6, waiting for transfers between devices, shifted(): return lax.ppermute(x, axis, perm)  6.87 us
    pallas_call x1, Pallas kernels, attention_terms(): pl.pallas_call(kernel, out_shape=(jax.ShapeDtypeStruct((tok_rows, 2 * kv_...  5.86 us
    ppermute x4, starting transfers between devices, suffix_pipeline(): recv = lax.ppermute(acc.astype(jnp.bfloat16), axis, perm)  5.17 us
    dot_general x3, matrix products, partial_for(): lax.dot_general(grad_key, wk, contract, preferred_element_type=jnp.float32)  4.95 us
    unnamed x21, local copies, waits for them, and re-layouts  2.91 us
    dot_general x1, matrix products, per_device(): jnp.dot(tokens, w_value[0], preferred_element_type=jnp.float32)  2.02 us
  transfers between devices with their start and end apart: 12, of which 9 were waited for; matrix products, arithmetic and copies ran while one was open for 7% of the time, Pallas kernels for 0%

profile of v19, /device:TPU:0, one launch (start us, length us, event | category | flops | bytes accessed | tf_op | source)
XLA Modules:
  0.0 84.7 jit_solution(13826491821626248100)
XLA Ops:
  0.0 0.0 copy-start
  0.0 0.0 copy-start.3
  0.0 0.0 copy-start.1
  0.0 1.7 %copy-done = bf16[1,5120,256]{2,1,0:T(8,128)(2,1)S(1)} copy-done((bf16[1,5120,256]{2,1,0:T(8,128)(2,1)S(1)}, bf16[1,5120,256]{2,1,0:T(8,128)(2,1)}, u32[]{:S(2)}) %copy-start) | copy-done | bytes 2621464
  1.7 2.0 %fusion.21 = bf16[128,256]{1,0:T(8,128)(2,1)S(1)} fusion(bf16[1,5120,256]{2,1,0:T(8,128)(2,1)S(1)} %copy-done, bf16[1,128,5120]{2,1,0:T(8,128)(2,1)} %param.6), kind=kOutput, calls=%fused_computation.23 | convolution fusion | flops 335577088 | bytes 3997696 | tf_op jit(solution)/shard_map/dot_general | solution.py:109
  3.8 0.0 copy-done.3
  3.8 0.0 copy-done.1
  3.8 0.0 copy-start.8
  3.8 0.5 fusion.16
  4.3 0.0 copy-start.4
  4.3 4.9 %collective-permute-start = (bf16[128,512]{1,0:T(8,128)(2,1)S(1)}, bf16[128,512]{1,0:T(8,128)(2,1)S(1)}, u32[]{:S(2)}, u32[]{:S(2)}) collective-permute-start(bf16[128,512]{1,0:T(8,128)(2,1)S(1)} %pad_maximum_fusion.refs_2_), channel_id=1, source_target_pairs={{0,2},{2,4},{4,6},{1,3},{3,5},{5,7},{8,10},{10,12},{12,14},{9,11},... | collective-permute-start | bytes 393224 | tf_op jit(solution)/shard_map/ppermute | solution.py:18
  9.2 3.4 %collective-permute-start.1 = (bf16[128,512]{1,0:T(8,128)(2,1)S(1)}, bf16[128,512]{1,0:T(8,128)(2,1)S(1)}, u32[]{:S(2)}, u32[]{:S(2)}) collective-permute-start(bf16[128,512]{1,0:T(8,128)(2,1)S(1)} %pad_maximum_fusion.refs_2_), channel_id=1, source_target_pairs={{0,4},{2,6},{1,5},{3,7},{8,12},{10,14},{9,13},{11,15},{16,20},{18,... | collective-permute-start | bytes 393224 | tf_op jit(solution)/shard_map/ppermute | solution.py:18
  12.7 1.3 %collective-permute-start.2 = (bf16[128,512]{1,0:T(8,128)(2,1)S(1)}, bf16[128,512]{1,0:T(8,128)(2,1)S(1)}, u32[]{:S(2)}, u32[]{:S(2)}) collective-permute-start(bf16[128,512]{1,0:T(8,128)(2,1)S(1)} %pad_maximum_fusion.refs_2_), channel_id=1, source_target_pairs={{0,6},{1,7},{8,14},{9,15},{16,22},{17,23},{24,30},{25,31}} | collective-permute-start | bytes 393224 | tf_op jit(solution)/shard_map/ppermute | solution.py:18
  14.0 0.0 copy-done.8
  14.0 0.2 copy.25
  14.2 0.1 fusion.59
  14.3 0.1 fusion.57
  14.4 0.2 copy.24
  14.6 0.2 copy.28
  14.8 0.8 broadcast_select_fusion
  15.6 0.0 collective-permute-done.refs_3_
  15.6 0.1 collective-permute-done.1.refs_4_
  15.7 0.8 collective-permute-done.2.refs_5_
  16.5 0.0 copy-done.4
  16.5 0.0 copy-done.5
  16.5 0.0 copy-done.6
  16.5 0.6 copy-done.7
  17.1 5.9 %shard_map.64 = (f32[128,512]{1,0:T(8,128)}, bf16[128,512]{1,0:T(8,128)(2,1)}, bf16[128,512]{1,0:T(8,128)(2,1)}, bf16[128,512]{1,0:T(8,128)(2,1)}) custom-call(bf16[10,128,128]{2,1,0:T(8,128)(2,1)} %bitcast.108, bf16[10,128,128]{2,1,0:T(8,128)(2,1)} %bitcast.109, bf16[128,512]{1,0:T(8,128)(2,1)} %copy-done.4, bf16[128,512]{1,0:T(8,128)(2,1)} %copy-done.5, ...), custom_call_target="tpu_custom_call" | custom-call | tf_op jit(solution)/shard_map/pallas_call | solution.py:88
  23.0 1.3 %collective-permute-start.5 = (bf16[128,512]{1,0:T(8,128)(2,1)}, bf16[128,512]{1,0:T(8,128)(2,1)S(1)}, u32[]{:S(2)}, u32[]{:S(2)}) collective-permute-start(bf16[128,512]{1,0:T(8,128)(2,1)} %get-tuple-element.12), channel_id=1, source_target_pairs={{6,0},{7,1},{14,8},{15,9},{22,16},{23,17},{30,24},{31,25}} | collective-permute-start | bytes 393224 | tf_op jit(solution)/shard_map/ppermute | solution.py:18
  24.3 1.3 %collective-permute-start.4 = (bf16[128,512]{1,0:T(8,128)(2,1)}, bf16[128,512]{1,0:T(8,128)(2,1)S(1)}, u32[]{:S(2)}, u32[]{:S(2)}) collective-permute-start(bf16[128,512]{1,0:T(8,128)(2,1)} %get-tuple-element.11), channel_id=1, source_target_pairs={{4,0},{6,2},{5,1},{7,3},{12,8},{14,10},{13,9},{15,11},{20,16},{22,... | collective-permute-start | bytes 393224 | tf_op jit(solution)/shard_map/ppermute | solution.py:18
  25.6 1.3 %collective-permute-start.3 = (bf16[128,512]{1,0:T(8,128)(2,1)}, bf16[128,512]{1,0:T(8,128)(2,1)S(1)}, u32[]{:S(2)}, u32[]{:S(2)}) collective-permute-start(bf16[128,512]{1,0:T(8,128)(2,1)} %get-tuple-element.10), channel_id=1, source_target_pairs={{2,0},{4,2},{6,4},{3,1},{5,3},{7,5},{10,8},{12,10},{14,12},{11,9},... | collective-permute-start | bytes 393224 | tf_op jit(solution)/shard_map/ppermute | solution.py:18
  26.9 4.3 %collective-permute-done.5 = bf16[128,512]{1,0:T(8,128)(2,1)S(1)} collective-permute-done((bf16[128,512]{1,0:T(8,128)(2,1)}, bf16[128,512]{1,0:T(8,128)(2,1)S(1)}, u32[]{:S(2)}, u32[]{:S(2)}) %collective-permute-start.5) | collective-permute-done | bytes 131104 | tf_op jit(solution)/shard_map/ppermute | solution.py:18
  31.2 1.7 %collective-permute-done.4 = bf16[128,512]{1,0:T(8,128)(2,1)S(1)} collective-permute-done((bf16[128,512]{1,0:T(8,128)(2,1)}, bf16[128,512]{1,0:T(8,128)(2,1)S(1)}, u32[]{:S(2)}, u32[]{:S(2)}) %collective-permute-start.4) | collective-permute-done | bytes 131104 | tf_op jit(solution)/shard_map/ppermute | solution.py:18
  32.9 0.0 collective-permute-done.3
  32.9 1.0 %add_convert_fusion = bf16[128,512]{1,0:T(8,128)(2,1)S(1)} fusion(bf16[128,512]{1,0:T(8,128)(2,1)S(1)} %collective-permute-done.5, bf16[128,512]{1,0:T(8,128)(2,1)S(1)} %collective-permute-done.4, f32[128,512]{1,0:T(8,128)} %get-tuple-element.9, bf16[128,512]{1,0:T(8,128)(2,1)S(1)} %collective-permute-done.3), kind=kLoop, calls=%fused_computation.52 | loop fusion | flops 458752 | bytes 786432 | tf_op jit(solution)/shard_map/convert.1
  33.9 0.4 fusion.32
  34.3 2.2 %fusion.8 = bf16[128,1280]{1,0:T(8,128)(2,1)} fusion(f32[128,1280]{1,0:T(8,128)S(1)} %fusion.32, bf16[1,5120,256]{2,1,0:T(8,128)(2,1)} %param.9, s32[]{:T(128)S(6)} %select_n.35, bf16[128,512]{1,0:T(8,128)(2,1)S(1)} %add_convert_fusion), kind=kOutput, calls=%fused_computation.14 | convolution fusion | flops 84213760 | bytes 1703940 | tf_op jit(solution)/shard_map/dot_general | solution.py:149
  36.5 0.0 collective-permute-start.7
  36.5 0.4 fusion.35
  36.8 2.2 %fusion.7 = bf16[128,1280]{1,0:T(8,128)(2,1)} fusion(f32[128,1280]{1,0:T(8,128)S(1)} %fusion.35, bf16[1,5120,256]{2,1,0:T(8,128)(2,1)} %param.9, s32[]{:T(128)S(6)} %select_n.34, bf16[128,512]{1,0:T(8,128)(2,1)S(1)} %add_convert_fusion), kind=kOutput, calls=%fused_computation.13 | convolution fusion | flops 84213760 | bytes 1703940 | tf_op jit(solution)/shard_map/dot_general | solution.py:149
  39.0 0.5 collective-permute-start.6
  39.5 0.6 fusion.9
  40.1 0.0 collective-permute-done.7
  40.1 0.9 %collective-permute-done.6 = bf16[128,1280]{1,0:T(8,128)(2,1)S(1)} collective-permute-done((bf16[128,1280]{1,0:T(8,128)(2,1)}, bf16[128,1280]{1,0:T(8,128)(2,1)S(1)}, u32[]{:S(2)}, u32[]{:S(2)}) %collective-permute-start.6) | collective-permute-done | bytes 327712 | tf_op jit(solution)/shard_map/ppermute | solution.py:158
  41.0 0.3 copy-done.2
  41.3 0.6 fusion
  42.0 1.3 %collective-permute-start.8 = (bf16[64,2560]{1,0:T(8,128)(2,1)S(1)}, bf16[64,2560]{1,0:T(8,128)(2,1)S(1)}, u32[]{:S(2)}, u32[]{:S(2)}) collective-permute-start(bf16[64,2560]{1,0:T(8,128)(2,1)S(1)} %slice.80), channel_id=1, source_target_pairs={{8,0},{16,8},{24,16},{9,1},{17,9},{25,17},{10,2},{18,10},{26,18},{... | collective-permute-start | bytes 983048 | tf_op jit(solution)/shard_map/ppermute | solution.py:37
  43.3 0.2 broadcast_in_dim.13
  43.5 1.0 %fusion.2 = f32[5,64,2560]{2,1,0:T(8,128)S(1)} fusion(s32[]{:T(128)S(6)} %select_n.36, f32[3,64,2560]{2,1,0:T(8,128)S(1)} %broadcast_in_dim.13, f32[2,64,2560]{2,1,0:T(8,128)S(1)} %bitcast.107), kind=kLoop, calls=%fused_computation.6 | loop fusion | flops 1638400 | bytes 6553604 | tf_op jit(solution)/shard_map/concatenate | solution.py:27
  44.5 9.1 %collective-permute-done.8 = bf16[64,2560]{1,0:T(8,128)(2,1)S(1)} collective-permute-done((bf16[64,2560]{1,0:T(8,128)(2,1)S(1)}, bf16[64,2560]{1,0:T(8,128)(2,1)S(1)}, u32[]{:S(2)}, u32[]{:S(2)}) %collective-permute-start.8) | collective-permute-done | bytes 327712 | tf_op jit(solution)/shard_map/ppermute | solution.py:37
  53.6 0.1 fusion.42
  53.6 1.3 %collective-permute-start.9 = (bf16[64,2560]{1,0:T(8,128)(2,1)S(1)}, bf16[64,2560]{1,0:T(8,128)(2,1)S(1)}, u32[]{:S(2)}, u32[]{:S(2)}) collective-permute-start(bf16[64,2560]{1,0:T(8,128)(2,1)S(1)} %fusion.42), channel_id=1, source_target_pairs={{8,0},{16,8},{24,16},{9,1},{17,9},{25,17},{10,2},{18,10},{26,18},{... | collective-permute-start | bytes 983048 | tf_op jit(solution)/shard_map/ppermute | solution.py:37
  54.9 0.1 bitcast_dynamic-update-slice_fusion.2
  55.0 9.4 %collective-permute-done.9 = bf16[64,2560]{1,0:T(8,128)(2,1)S(1)} collective-permute-done((bf16[64,2560]{1,0:T(8,128)(2,1)S(1)}, bf16[64,2560]{1,0:T(8,128)(2,1)S(1)}, u32[]{:S(2)}, u32[]{:S(2)}) %collective-permute-start.9) | collective-permute-done | bytes 327712 | tf_op jit(solution)/shard_map/ppermute | solution.py:37
  64.4 0.1 fusion.43
  64.4 1.3 %collective-permute-start.10 = (bf16[64,2560]{1,0:T(8,128)(2,1)S(1)}, bf16[64,2560]{1,0:T(8,128)(2,1)S(1)}, u32[]{:S(2)}, u32[]{:S(2)}) collective-permute-start(bf16[64,2560]{1,0:T(8,128)(2,1)S(1)} %fusion.43), channel_id=1, source_target_pairs={{8,0},{16,8},{24,16},{9,1},{17,9},{25,17},{10,2},{18,10},{26,18},{... | collective-permute-start | bytes 983048 | tf_op jit(solution)/shard_map/ppermute | solution.py:37
  65.7 0.1 bitcast_dynamic-update-slice_fusion.1
  65.8 8.5 %collective-permute-done.10 = bf16[64,2560]{1,0:T(8,128)(2,1)S(1)} collective-permute-done((bf16[64,2560]{1,0:T(8,128)(2,1)S(1)}, bf16[64,2560]{1,0:T(8,128)(2,1)S(1)}, u32[]{:S(2)}, u32[]{:S(2)}) %collective-permute-start.10) | collective-permute-done | bytes 327712 | tf_op jit(solution)/shard_map/ppermute | solution.py:37
  74.3 0.1 fusion.44
  74.4 1.3 %collective-permute-start.11 = (bf16[64,2560]{1,0:T(8,128)(2,1)S(1)}, bf16[64,2560]{1,0:T(8,128)(2,1)S(1)}, u32[]{:S(2)}, u32[]{:S(2)}) collective-permute-start(bf16[64,2560]{1,0:T(8,128)(2,1)S(1)} %fusion.44), channel_id=1, source_target_pairs={{8,0},{16,8},{24,16},{9,1},{17,9},{25,17},{10,2},{18,10},{26,18},{... | collective-permute-start | bytes 983048 | tf_op jit(solution)/shard_map/ppermute | solution.py:37
  75.7 0.1 bitcast_dynamic-update-slice_fusion
  75.8 7.7 %collective-permute-done.11 = bf16[64,2560]{1,0:T(8,128)(2,1)S(1)} collective-permute-done((bf16[64,2560]{1,0:T(8,128)(2,1)S(1)}, bf16[64,2560]{1,0:T(8,128)(2,1)S(1)}, u32[]{:S(2)}, u32[]{:S(2)}) %collective-permute-start.11) | collective-permute-done | bytes 327712 | tf_op jit(solution)/shard_map/ppermute | solution.py:37
  83.5 0.1 fusion.28
  83.5 1.2 %constant_dynamic-slice_fusion = f32[2,64,2560]{2,1,0:T(8,128)} fusion(f32[5,64,2560]{2,1,0:T(8,128)S(1)} %fusion.28, s32[]{:T(128)S(6)} %select_n.37), kind=kLoop, calls=%fused_computation.63 | loop fusion | bytes 2621444 | tf_op jit(solution)/shard_map/dynamic_slice | solution.py:39
  (11 shorter events, 0.1 us)
Async XLA Ops:
  0.0 1.7 %copy-start = (bf16[1,5120,256]{2,1,0:T(8,128)(2,1)S(1)}, bf16[1,5120,256]{2,1,0:T(8,128)(2,1)}, u32[]{:S(2)}) copy-start(bf16[1,5120,256]{2,1,0:T(8,128)(2,1)} %param.10) | copy-start | bytes 7864324
  0.0 3.8 %copy-start.3 = (bf16[1,128,5120]{2,1,0:T(8,128)(2,1)S(1)}, bf16[1,128,5120]{2,1,0:T(8,128)(2,1)}, u32[]{:S(2)}) copy-start(bf16[1,128,5120]{2,1,0:T(8,128)(2,1)} %param.6) | copy-start | bytes 3932164
  0.0 3.8 %copy-start.1 = (bf16[1,5120,256]{2,1,0:T(8,128)(2,1)S(1)}, bf16[1,5120,256]{2,1,0:T(8,128)(2,1)}, u32[]{:S(2)}) copy-start(bf16[1,5120,256]{2,1,0:T(8,128)(2,1)} %param.9) | copy-start | bytes 7864324
  3.8 10.2 %copy-start.8 = (s32[512]{0:T(512)S(1)}, s32[512]{0:T(512)}, u32[]{:S(2)}) copy-start(s32[512]{0:T(512)} %param.11) | copy-start | bytes 6148
  4.3 12.1 %copy-start.4 = (bf16[128,512]{1,0:T(8,128)(2,1)}, bf16[128,512]{1,0:T(8,128)(2,1)S(1)}, u32[]{:S(2)}) copy-start(bf16[128,512]{1,0:T(8,128)(2,1)S(1)} %pad_maximum_fusion.refs_2_) | copy-start | bytes 393220
  4.3 11.3 %collective-permute-start = (bf16[128,512]{1,0:T(8,128)(2,1)S(1)}, bf16[128,512]{1,0:T(8,128)(2,1)S(1)}, u32[]{:S(2)}, u32[]{:S(2)}) collective-permute-start(bf16[128,512]{1,0:T(8,128)(2,1)S(1)} %pad_maximum_fusion.refs_2_), channel_id=1, source_target_pairs={{0,2},{2,4},{4,6},{1,3},{3,5},{5,7},{8,10},{10,12},{12,14},{9,11},... | collective-permute-start | bytes 393224 | tf_op jit(solution)/shard_map/ppermute | solution.py:18
  9.2 6.5 %collective-permute-start.1 = (bf16[128,512]{1,0:T(8,128)(2,1)S(1)}, bf16[128,512]{1,0:T(8,128)(2,1)S(1)}, u32[]{:S(2)}, u32[]{:S(2)}) collective-permute-start(bf16[128,512]{1,0:T(8,128)(2,1)S(1)} %pad_maximum_fusion.refs_2_), channel_id=1, source_target_pairs={{0,4},{2,6},{1,5},{3,7},{8,12},{10,14},{9,13},{11,15},{16,20},{18,... | collective-permute-start | bytes 393224 | tf_op jit(solution)/shard_map/ppermute | solution.py:18
  12.7 3.8 %collective-permute-start.2 = (bf16[128,512]{1,0:T(8,128)(2,1)S(1)}, bf16[128,512]{1,0:T(8,128)(2,1)S(1)}, u32[]{:S(2)}, u32[]{:S(2)}) collective-permute-start(bf16[128,512]{1,0:T(8,128)(2,1)S(1)} %pad_maximum_fusion.refs_2_), channel_id=1, source_target_pairs={{0,6},{1,7},{8,14},{9,15},{16,22},{17,23},{24,30},{25,31}} | collective-permute-start | bytes 393224 | tf_op jit(solution)/shard_map/ppermute | solution.py:18
  15.6 0.9 %copy-start.5 = (bf16[128,512]{1,0:T(8,128)(2,1)}, bf16[128,512]{1,0:T(8,128)(2,1)S(1)}, u32[]{:S(2)}) copy-start(bf16[128,512]{1,0:T(8,128)(2,1)S(1)} %collective-permute-done.refs_3_) | copy-start | bytes 393220
  15.7 0.8 copy-start.6
  16.5 0.6 copy-start.7
  23.0 8.2 %collective-permute-start.5 = (bf16[128,512]{1,0:T(8,128)(2,1)}, bf16[128,512]{1,0:T(8,128)(2,1)S(1)}, u32[]{:S(2)}, u32[]{:S(2)}) collective-permute-start(bf16[128,512]{1,0:T(8,128)(2,1)} %get-tuple-element.12), channel_id=1, source_target_pairs={{6,0},{7,1},{14,8},{15,9},{22,16},{23,17},{30,24},{31,25}} | collective-permute-start | bytes 393224 | tf_op jit(solution)/shard_map/ppermute | solution.py:18
  24.3 8.6 %collective-permute-start.4 = (bf16[128,512]{1,0:T(8,128)(2,1)}, bf16[128,512]{1,0:T(8,128)(2,1)S(1)}, u32[]{:S(2)}, u32[]{:S(2)}) collective-permute-start(bf16[128,512]{1,0:T(8,128)(2,1)} %get-tuple-element.11), channel_id=1, source_target_pairs={{4,0},{6,2},{5,1},{7,3},{12,8},{14,10},{13,9},{15,11},{20,16},{22,... | collective-permute-start | bytes 393224 | tf_op jit(solution)/shard_map/ppermute | solution.py:18
  25.6 7.3 %collective-permute-start.3 = (bf16[128,512]{1,0:T(8,128)(2,1)}, bf16[128,512]{1,0:T(8,128)(2,1)S(1)}, u32[]{:S(2)}, u32[]{:S(2)}) collective-permute-start(bf16[128,512]{1,0:T(8,128)(2,1)} %get-tuple-element.10), channel_id=1, source_target_pairs={{2,0},{4,2},{6,4},{3,1},{5,3},{7,5},{10,8},{12,10},{14,12},{11,9},... | collective-permute-start | bytes 393224 | tf_op jit(solution)/shard_map/ppermute | solution.py:18
  36.5 3.6 %collective-permute-start.7 = (bf16[128,1280]{1,0:T(8,128)(2,1)}, bf16[128,1280]{1,0:T(8,128)(2,1)S(1)}, u32[]{:S(2)}, u32[]{:S(2)}) collective-permute-start(bf16[128,1280]{1,0:T(8,128)(2,1)} %fusion.8), channel_id=1, source_target_pairs={{0,1},{1,0},{2,3},{3,2},{4,5},{5,4},{6,7},{7,6},{8,9},{9,8},{10,11... | collective-permute-start | bytes 983048 | tf_op jit(solution)/shard_map/ppermute | solution.py:158
  39.0 2.0 %collective-permute-start.6 = (bf16[128,1280]{1,0:T(8,128)(2,1)}, bf16[128,1280]{1,0:T(8,128)(2,1)S(1)}, u32[]{:S(2)}, u32[]{:S(2)}) collective-permute-start(bf16[128,1280]{1,0:T(8,128)(2,1)} %fusion.7), channel_id=1, source_target_pairs={{0,1},{1,0},{2,3},{3,2},{4,5},{5,4},{6,7},{7,6},{8,9},{9,8},{10,11... | collective-permute-start | bytes 983048 | tf_op jit(solution)/shard_map/ppermute | solution.py:158
  39.5 1.7 %copy-start.2 = (bf16[1,5120,256]{2,1,0:T(8,128)(2,1)S(1)}, bf16[1,5120,256]{2,1,0:T(8,128)(2,1)}, u32[]{:S(2)}) copy-start(bf16[1,5120,256]{2,1,0:T(8,128)(2,1)} %param.9) | copy-start | bytes 7864324
  42.0 11.6 %collective-permute-start.8 = (bf16[64,2560]{1,0:T(8,128)(2,1)S(1)}, bf16[64,2560]{1,0:T(8,128)(2,1)S(1)}, u32[]{:S(2)}, u32[]{:S(2)}) collective-permute-start(bf16[64,2560]{1,0:T(8,128)(2,1)S(1)} %slice.80), channel_id=1, source_target_pairs={{8,0},{16,8},{24,16},{9,1},{17,9},{25,17},{10,2},{18,10},{26,18},{... | collective-permute-start | bytes 983048 | tf_op jit(solution)/shard_map/ppermute | solution.py:37
  53.6 10.8 %collective-permute-start.9 = (bf16[64,2560]{1,0:T(8,128)(2,1)S(1)}, bf16[64,2560]{1,0:T(8,128)(2,1)S(1)}, u32[]{:S(2)}, u32[]{:S(2)}) collective-permute-start(bf16[64,2560]{1,0:T(8,128)(2,1)S(1)} %fusion.42), channel_id=1, source_target_pairs={{8,0},{16,8},{24,16},{9,1},{17,9},{25,17},{10,2},{18,10},{26,18},{... | collective-permute-start | bytes 983048 | tf_op jit(solution)/shard_map/ppermute | solution.py:37
  64.4 9.9 %collective-permute-start.10 = (bf16[64,2560]{1,0:T(8,128)(2,1)S(1)}, bf16[64,2560]{1,0:T(8,128)(2,1)S(1)}, u32[]{:S(2)}, u32[]{:S(2)}) collective-permute-start(bf16[64,2560]{1,0:T(8,128)(2,1)S(1)} %fusion.43), channel_id=1, source_target_pairs={{8,0},{16,8},{24,16},{9,1},{17,9},{25,17},{10,2},{18,10},{26,18},{... | collective-permute-start | bytes 983048 | tf_op jit(solution)/shard_map/ppermute | solution.py:37
  74.4 9.0 %collective-permute-start.11 = (bf16[64,2560]{1,0:T(8,128)(2,1)S(1)}, bf16[64,2560]{1,0:T(8,128)(2,1)S(1)}, u32[]{:S(2)}, u32[]{:S(2)}) collective-permute-start(bf16[64,2560]{1,0:T(8,128)(2,1)S(1)} %fusion.44), channel_id=1, source_target_pairs={{8,0},{16,8},{24,16},{9,1},{17,9},{25,17},{10,2},{18,10},{26,18},{... | collective-permute-start | bytes 983048 | tf_op jit(solution)/shard_map/ppermute | solution.py:37

commit v20 on v18

--- a/solution.py
+++ b/solution.py
@@ -69,7 +69,7 @@
                 s = lax.dot_general(key, q, nt, preferred_element_type=jnp.float32) * scaling
                 masked = jnp.where(allowed, s, -1e30)
                 top = jnp.max(masked, axis=0, keepdims=True)
-                e = jnp.where(allowed, jnp.exp(masked - top), 0.0)
+                e = jnp.exp(masked - top)
                 tot = jnp.sum(e, axis=0, keepdims=True)
                 p = e * (1.0 / tot)
                 pb = p.astype(jnp.bfloat16)

time: 82.1 us -> 82 us (level)
  no operation moved by 1% of the time
where the time goes in v20:
time: 82 us; the launch traced here: 81.6 us
  waiting for transfers between devices  43.4 us (53%)
  starting transfers between devices  18.6 us (23%)
  Pallas kernels  5.79 us (7%)
  matrix products  5.64 us (7%)
  local copies, waits for them, and re-layouts  4.4 us (5%)
  other arithmetic  3.46 us (4%)
    ppermute x4, waiting for transfers between devices, suffix_pipeline(): recv = lax.ppermute(acc.astype(jnp.bfloat16), axis, perm)  34.8 us
    ppermute x6, starting transfers between devices, shifted(): return lax.ppermute(x, axis, perm)  13.5 us
    ppermute x6, waiting for transfers between devices, shifted(): return lax.ppermute(x, axis, perm)  6.86 us
    pallas_call x1, Pallas kernels, attention_terms(): pl.pallas_call(kernel, out_shape=(jax.ShapeDtypeStruct((tok_rows, 2 * kv_...  5.79 us
    ppermute x4, starting transfers between devices, suffix_pipeline(): recv = lax.ppermute(acc.astype(jnp.bfloat16), axis, perm)  5.17 us
    unnamed x23, local copies, waits for them, and re-layouts  2.65 us
    dot_general x1, matrix products, per_device(): jnp.dot(tokens, w_value[0], preferred_element_type=jnp.float32)  2.02 us
    dot_general x2, matrix products, partial_for(): lax.dot_general(grad_key, wk, contract, preferred_element_type=jnp.float32)  1.99 us
  transfers between devices with their start and end apart: 11, of which 9 were waited for; matrix products, arithmetic and copies ran while one was open for 4% of the time, Pallas kernels for 0%

profile of v20, /device:TPU:0, one launch (start us, length us, event | category | flops | bytes accessed | tf_op | source)
XLA Modules:
  0.0 81.6 jit_solution(15318870679636043554)
XLA Ops:
  0.0 0.0 copy-start
  0.0 0.0 copy-start.4
  0.0 0.0 copy-start.1
  0.0 1.7 %copy-done = bf16[1,5120,256]{2,1,0:T(8,128)(2,1)S(1)} copy-done((bf16[1,5120,256]{2,1,0:T(8,128)(2,1)S(1)}, bf16[1,5120,256]{2,1,0:T(8,128)(2,1)}, u32[]{:S(2)}) %copy-start) | copy-done | bytes 2621464
  1.7 2.0 %fusion.25 = bf16[128,256]{1,0:T(8,128)(2,1)S(1)} fusion(bf16[1,5120,256]{2,1,0:T(8,128)(2,1)S(1)} %copy-done, bf16[1,128,5120]{2,1,0:T(8,128)(2,1)} %param.6), kind=kOutput, calls=%fused_computation.26 | convolution fusion | flops 335577088 | bytes 3997696 | tf_op jit(solution)/shard_map/dot_general | solution.py:109
  3.8 0.0 copy-done.4
  3.8 0.0 copy-done.1
  3.8 0.0 copy-start.9
  3.8 0.5 fusion.20
  4.3 0.0 copy-start.5
  4.3 4.9 %collective-permute-start = (bf16[128,512]{1,0:T(8,128)(2,1)S(1)}, bf16[128,512]{1,0:T(8,128)(2,1)S(1)}, u32[]{:S(2)}, u32[]{:S(2)}) collective-permute-start(bf16[128,512]{1,0:T(8,128)(2,1)S(1)} %pad_maximum_fusion.refs_2_), channel_id=1, source_target_pairs={{0,2},{2,4},{4,6},{1,3},{3,5},{5,7},{8,10},{10,12},{12,14},{9,11},... | collective-permute-start | bytes 393224 | tf_op jit(solution)/shard_map/ppermute | solution.py:18
  9.2 3.4 %collective-permute-start.1 = (bf16[128,512]{1,0:T(8,128)(2,1)S(1)}, bf16[128,512]{1,0:T(8,128)(2,1)S(1)}, u32[]{:S(2)}, u32[]{:S(2)}) collective-permute-start(bf16[128,512]{1,0:T(8,128)(2,1)S(1)} %pad_maximum_fusion.refs_2_), channel_id=1, source_target_pairs={{0,4},{2,6},{1,5},{3,7},{8,12},{10,14},{9,13},{11,15},{16,20},{18,... | collective-permute-start | bytes 393224 | tf_op jit(solution)/shard_map/ppermute | solution.py:18
  12.7 1.3 %collective-permute-start.2 = (bf16[128,512]{1,0:T(8,128)(2,1)S(1)}, bf16[128,512]{1,0:T(8,128)(2,1)S(1)}, u32[]{:S(2)}, u32[]{:S(2)}) collective-permute-start(bf16[128,512]{1,0:T(8,128)(2,1)S(1)} %pad_maximum_fusion.refs_2_), channel_id=1, source_target_pairs={{0,6},{1,7},{8,14},{9,15},{16,22},{17,23},{24,30},{25,31}} | collective-permute-start | bytes 393224 | tf_op jit(solution)/shard_map/ppermute | solution.py:18
  14.0 0.0 copy-done.9
  14.0 0.2 copy.25
  14.2 0.1 fusion.49
  14.3 0.1 fusion.47
  14.4 0.2 copy.24
  14.6 0.2 copy.28
  14.8 0.8 %broadcast_select_fusion = (s32[512,1]{1,0:T(8,128)}, s32[512,1]{1,0:T(8,128)}) fusion(pred[512,1]{1,0:T(8,128)(4,1)S(1)} %copy.25, s32[512,1]{1,0:T(8,128)S(1)} %copy.24, pred[1,512]{0,1:T(8,128)(4,1)S(1)} %copy.28), kind=kLoop, calls=%fused_computation.48 | loop fusion | flops 1024 | bytes 7168 | tf_op jit(solution)/shard_map/jit(_where)/select_n | solution.py:131
  15.6 0.0 collective-permute-done.refs_3_
  15.6 0.0 copy-start.6
  15.6 0.1 collective-permute-done.1.refs_4_
  15.7 0.0 copy-start.7
  15.7 0.8 collective-permute-done.2.refs_5_
  16.5 0.0 copy-done.5
  16.5 0.0 copy-done.6
  16.5 0.0 copy-done.7
  16.5 0.6 copy-done.8
  17.1 5.8 %shard_map.64 = (f32[128,512]{1,0:T(8,128)}, bf16[128,512]{1,0:T(8,128)(2,1)}, bf16[128,512]{1,0:T(8,128)(2,1)}, bf16[128,512]{1,0:T(8,128)(2,1)}) custom-call(bf16[10,128,128]{2,1,0:T(8,128)(2,1)} %bitcast.102, bf16[10,128,128]{2,1,0:T(8,128)(2,1)} %bitcast.103, bf16[128,512]{1,0:T(8,128)(2,1)} %copy-done.5, bf16[128,512]{1,0:T(8,128)(2,1)} %copy-done.6, ...), custom_call_target="tpu_custom_call" | custom-call | tf_op jit(solution)/shard_map/pallas_call | solution.py:88
  22.9 1.3 %collective-permute-start.5 = (bf16[128,512]{1,0:T(8,128)(2,1)}, bf16[128,512]{1,0:T(8,128)(2,1)S(1)}, u32[]{:S(2)}, u32[]{:S(2)}) collective-permute-start(bf16[128,512]{1,0:T(8,128)(2,1)} %get-tuple-element.12), channel_id=1, source_target_pairs={{6,0},{7,1},{14,8},{15,9},{22,16},{23,17},{30,24},{31,25}} | collective-permute-start | bytes 393224 | tf_op jit(solution)/shard_map/ppermute | solution.py:18
  24.2 1.3 %collective-permute-start.4 = (bf16[128,512]{1,0:T(8,128)(2,1)}, bf16[128,512]{1,0:T(8,128)(2,1)S(1)}, u32[]{:S(2)}, u32[]{:S(2)}) collective-permute-start(bf16[128,512]{1,0:T(8,128)(2,1)} %get-tuple-element.11), channel_id=1, source_target_pairs={{4,0},{6,2},{5,1},{7,3},{12,8},{14,10},{13,9},{15,11},{20,16},{22,... | collective-permute-start | bytes 393224 | tf_op jit(solution)/shard_map/ppermute | solution.py:18
  25.5 1.3 %collective-permute-start.3 = (bf16[128,512]{1,0:T(8,128)(2,1)}, bf16[128,512]{1,0:T(8,128)(2,1)S(1)}, u32[]{:S(2)}, u32[]{:S(2)}) collective-permute-start(bf16[128,512]{1,0:T(8,128)(2,1)} %get-tuple-element.10), channel_id=1, source_target_pairs={{2,0},{4,2},{6,4},{3,1},{5,3},{7,5},{10,8},{12,10},{14,12},{11,9},... | collective-permute-start | bytes 393224 | tf_op jit(solution)/shard_map/ppermute | solution.py:18
  26.8 0.0 copy-start.2
  26.8 4.3 %collective-permute-done.5 = bf16[128,512]{1,0:T(8,128)(2,1)S(1)} collective-permute-done((bf16[128,512]{1,0:T(8,128)(2,1)}, bf16[128,512]{1,0:T(8,128)(2,1)S(1)}, u32[]{:S(2)}, u32[]{:S(2)}) %collective-permute-start.5) | collective-permute-done | bytes 131104 | tf_op jit(solution)/shard_map/ppermute | solution.py:18
  31.1 1.7 %collective-permute-done.4 = bf16[128,512]{1,0:T(8,128)(2,1)S(1)} collective-permute-done((bf16[128,512]{1,0:T(8,128)(2,1)}, bf16[128,512]{1,0:T(8,128)(2,1)S(1)}, u32[]{:S(2)}, u32[]{:S(2)}) %collective-permute-start.4) | collective-permute-done | bytes 131104 | tf_op jit(solution)/shard_map/ppermute | solution.py:18
  32.8 0.0 collective-permute-done.3
  32.8 1.0 %add_convert_fusion = bf16[128,512]{1,0:T(8,128)(2,1)S(1)} fusion(bf16[128,512]{1,0:T(8,128)(2,1)S(1)} %collective-permute-done.5, bf16[128,512]{1,0:T(8,128)(2,1)S(1)} %collective-permute-done.4, f32[128,512]{1,0:T(8,128)} %get-tuple-element.9, bf16[128,512]{1,0:T(8,128)(2,1)S(1)} %collective-permute-done.3), kind=kLoop, calls=%fused_computation.45 | loop fusion | flops 458752 | bytes 786432 | tf_op jit(solution)/shard_map/convert.1
  33.8 0.6 fusion.8
  34.4 0.0 copy-done.2
  34.4 1.4 %fusion.1 = bf16[128,2560]{1,0:T(8,128)(2,1)} fusion(f32[128,2560]{1,0:T(8,128)S(1)} %fusion.8, bf16[1,5120,256]{2,1,0:T(8,128)(2,1)S(1)} %copy-done.2, s32[]{:T(128)S(6)} %select_n.30, bf16[128,512]{1,0:T(8,128)(2,1)S(1)} %add_convert_fusion), kind=kOutput, calls=%fused_computation.6 | convolution fusion | flops 168427520 | bytes 3342340 | tf_op jit(solution)/shard_map/dot_general | solution.py:149
  35.8 0.0 collective-permute-start.6
  35.8 0.6 fusion.11
  36.4 1.7 %collective-permute-done.6 = bf16[128,2560]{1,0:T(8,128)(2,1)S(1)} collective-permute-done((bf16[128,2560]{1,0:T(8,128)(2,1)}, bf16[128,2560]{1,0:T(8,128)(2,1)S(1)}, u32[]{:S(2)}, u32[]{:S(2)}) %collective-permute-start.6) | collective-permute-done | bytes 655392 | tf_op jit(solution)/shard_map/ppermute | solution.py:157
  38.1 0.0 copy-done.3
  38.1 0.6 fusion
  38.8 1.3 %collective-permute-start.7 = (bf16[64,2560]{1,0:T(8,128)(2,1)S(1)}, bf16[64,2560]{1,0:T(8,128)(2,1)S(1)}, u32[]{:S(2)}, u32[]{:S(2)}) collective-permute-start(bf16[64,2560]{1,0:T(8,128)(2,1)S(1)} %slice.76), channel_id=1, source_target_pairs={{8,0},{16,8},{24,16},{9,1},{17,9},{25,17},{10,2},{18,10},{26,18},{... | collective-permute-start | bytes 983048 | tf_op jit(solution)/shard_map/ppermute | solution.py:37
  40.1 0.2 broadcast_in_dim.13
  40.3 1.0 %fusion.3 = f32[5,64,2560]{2,1,0:T(8,128)S(1)} fusion(s32[]{:T(128)S(6)} %select_n.31, f32[3,64,2560]{2,1,0:T(8,128)S(1)} %broadcast_in_dim.13, f32[2,64,2560]{2,1,0:T(8,128)S(1)} %bitcast.101), kind=kLoop, calls=%fused_computation.8 | loop fusion | flops 1638400 | bytes 6553604 | tf_op jit(solution)/shard_map/concatenate | solution.py:27
  41.3 9.1 %collective-permute-done.7 = bf16[64,2560]{1,0:T(8,128)(2,1)S(1)} collective-permute-done((bf16[64,2560]{1,0:T(8,128)(2,1)S(1)}, bf16[64,2560]{1,0:T(8,128)(2,1)S(1)}, u32[]{:S(2)}, u32[]{:S(2)}) %collective-permute-start.7) | collective-permute-done | bytes 327712 | tf_op jit(solution)/shard_map/ppermute | solution.py:37
  50.4 0.1 fusion.36
  50.5 1.3 %collective-permute-start.8 = (bf16[64,2560]{1,0:T(8,128)(2,1)S(1)}, bf16[64,2560]{1,0:T(8,128)(2,1)S(1)}, u32[]{:S(2)}, u32[]{:S(2)}) collective-permute-start(bf16[64,2560]{1,0:T(8,128)(2,1)S(1)} %fusion.36), channel_id=1, source_target_pairs={{8,0},{16,8},{24,16},{9,1},{17,9},{25,17},{10,2},{18,10},{26,18},{... | collective-permute-start | bytes 983048 | tf_op jit(solution)/shard_map/ppermute | solution.py:37
  51.8 0.1 bitcast_dynamic-update-slice_fusion.2
  51.9 9.4 %collective-permute-done.8 = bf16[64,2560]{1,0:T(8,128)(2,1)S(1)} collective-permute-done((bf16[64,2560]{1,0:T(8,128)(2,1)S(1)}, bf16[64,2560]{1,0:T(8,128)(2,1)S(1)}, u32[]{:S(2)}, u32[]{:S(2)}) %collective-permute-start.8) | collective-permute-done | bytes 327712 | tf_op jit(solution)/shard_map/ppermute | solution.py:37
  61.3 0.1 fusion.37
  61.3 1.3 %collective-permute-start.9 = (bf16[64,2560]{1,0:T(8,128)(2,1)S(1)}, bf16[64,2560]{1,0:T(8,128)(2,1)S(1)}, u32[]{:S(2)}, u32[]{:S(2)}) collective-permute-start(bf16[64,2560]{1,0:T(8,128)(2,1)S(1)} %fusion.37), channel_id=1, source_target_pairs={{8,0},{16,8},{24,16},{9,1},{17,9},{25,17},{10,2},{18,10},{26,18},{... | collective-permute-start | bytes 983048 | tf_op jit(solution)/shard_map/ppermute | solution.py:37
  62.6 0.1 bitcast_dynamic-update-slice_fusion.1
  62.7 8.6 %collective-permute-done.9 = bf16[64,2560]{1,0:T(8,128)(2,1)S(1)} collective-permute-done((bf16[64,2560]{1,0:T(8,128)(2,1)S(1)}, bf16[64,2560]{1,0:T(8,128)(2,1)S(1)}, u32[]{:S(2)}, u32[]{:S(2)}) %collective-permute-start.9) | collective-permute-done | bytes 327712 | tf_op jit(solution)/shard_map/ppermute | solution.py:37
  71.3 0.1 fusion.38
  71.3 1.3 %collective-permute-start.10 = (bf16[64,2560]{1,0:T(8,128)(2,1)S(1)}, bf16[64,2560]{1,0:T(8,128)(2,1)S(1)}, u32[]{:S(2)}, u32[]{:S(2)}) collective-permute-start(bf16[64,2560]{1,0:T(8,128)(2,1)S(1)} %fusion.38), channel_id=1, source_target_pairs={{8,0},{16,8},{24,16},{9,1},{17,9},{25,17},{10,2},{18,10},{26,18},{... | collective-permute-start | bytes 983048 | tf_op jit(solution)/shard_map/ppermute | solution.py:37
  72.6 0.1 bitcast_dynamic-update-slice_fusion
  72.7 7.7 %collective-permute-done.10 = bf16[64,2560]{1,0:T(8,128)(2,1)S(1)} collective-permute-done((bf16[64,2560]{1,0:T(8,128)(2,1)S(1)}, bf16[64,2560]{1,0:T(8,128)(2,1)S(1)}, u32[]{:S(2)}, u32[]{:S(2)}) %collective-permute-start.10) | collective-permute-done | bytes 327712 | tf_op jit(solution)/shard_map/ppermute | solution.py:37
  80.4 0.1 fusion.32
  80.5 1.2 %constant_dynamic-slice_fusion = f32[2,64,2560]{2,1,0:T(8,128)} fusion(f32[5,64,2560]{2,1,0:T(8,128)S(1)} %fusion.32, s32[]{:T(128)S(6)} %select_n.32), kind=kLoop, calls=%fused_computation.54 | loop fusion | bytes 2621444 | tf_op jit(solution)/shard_map/dynamic_slice | solution.py:39
  (9 shorter events, 0.1 us)
Async XLA Ops:
  0.0 1.7 %copy-start = (bf16[1,5120,256]{2,1,0:T(8,128)(2,1)S(1)}, bf16[1,5120,256]{2,1,0:T(8,128)(2,1)}, u32[]{:S(2)}) copy-start(bf16[1,5120,256]{2,1,0:T(8,128)(2,1)} %param.10) | copy-start | bytes 7864324
  0.0 3.8 %copy-start.4 = (bf16[1,128,5120]{2,1,0:T(8,128)(2,1)S(1)}, bf16[1,128,5120]{2,1,0:T(8,128)(2,1)}, u32[]{:S(2)}) copy-start(bf16[1,128,5120]{2,1,0:T(8,128)(2,1)} %param.6) | copy-start | bytes 3932164
  0.0 3.8 %copy-start.1 = (bf16[1,5120,256]{2,1,0:T(8,128)(2,1)S(1)}, bf16[1,5120,256]{2,1,0:T(8,128)(2,1)}, u32[]{:S(2)}) copy-start(bf16[1,5120,256]{2,1,0:T(8,128)(2,1)} %param.9) | copy-start | bytes 7864324
  3.8 10.2 %copy-start.9 = (s32[512]{0:T(512)S(1)}, s32[512]{0:T(512)}, u32[]{:S(2)}) copy-start(s32[512]{0:T(512)} %param.11) | copy-start | bytes 6148
  4.3 12.1 %copy-start.5 = (bf16[128,512]{1,0:T(8,128)(2,1)}, bf16[128,512]{1,0:T(8,128)(2,1)S(1)}, u32[]{:S(2)}) copy-start(bf16[128,512]{1,0:T(8,128)(2,1)S(1)} %pad_maximum_fusion.refs_2_) | copy-start | bytes 393220
  4.3 11.3 %collective-permute-start = (bf16[128,512]{1,0:T(8,128)(2,1)S(1)}, bf16[128,512]{1,0:T(8,128)(2,1)S(1)}, u32[]{:S(2)}, u32[]{:S(2)}) collective-permute-start(bf16[128,512]{1,0:T(8,128)(2,1)S(1)} %pad_maximum_fusion.refs_2_), channel_id=1, source_target_pairs={{0,2},{2,4},{4,6},{1,3},{3,5},{5,7},{8,10},{10,12},{12,14},{9,11},... | collective-permute-start | bytes 393224 | tf_op jit(solution)/shard_map/ppermute | solution.py:18
  9.2 6.5 %collective-permute-start.1 = (bf16[128,512]{1,0:T(8,128)(2,1)S(1)}, bf16[128,512]{1,0:T(8,128)(2,1)S(1)}, u32[]{:S(2)}, u32[]{:S(2)}) collective-permute-start(bf16[128,512]{1,0:T(8,128)(2,1)S(1)} %pad_maximum_fusion.refs_2_), channel_id=1, source_target_pairs={{0,4},{2,6},{1,5},{3,7},{8,12},{10,14},{9,13},{11,15},{16,20},{18,... | collective-permute-start | bytes 393224 | tf_op jit(solution)/shard_map/ppermute | solution.py:18
  12.7 3.8 %collective-permute-start.2 = (bf16[128,512]{1,0:T(8,128)(2,1)S(1)}, bf16[128,512]{1,0:T(8,128)(2,1)S(1)}, u32[]{:S(2)}, u32[]{:S(2)}) collective-permute-start(bf16[128,512]{1,0:T(8,128)(2,1)S(1)} %pad_maximum_fusion.refs_2_), channel_id=1, source_target_pairs={{0,6},{1,7},{8,14},{9,15},{16,22},{17,23},{24,30},{25,31}} | collective-permute-start | bytes 393224 | tf_op jit(solution)/shard_map/ppermute | solution.py:18
  15.6 0.9 %copy-start.6 = (bf16[128,512]{1,0:T(8,128)(2,1)}, bf16[128,512]{1,0:T(8,128)(2,1)S(1)}, u32[]{:S(2)}) copy-start(bf16[128,512]{1,0:T(8,128)(2,1)S(1)} %collective-permute-done.refs_3_) | copy-start | bytes 393220
  15.7 0.8 copy-start.7
  16.5 0.6 copy-start.8
  22.9 8.2 %collective-permute-start.5 = (bf16[128,512]{1,0:T(8,128)(2,1)}, bf16[128,512]{1,0:T(8,128)(2,1)S(1)}, u32[]{:S(2)}, u32[]{:S(2)}) collective-permute-start(bf16[128,512]{1,0:T(8,128)(2,1)} %get-tuple-element.12), channel_id=1, source_target_pairs={{6,0},{7,1},{14,8},{15,9},{22,16},{23,17},{30,24},{31,25}} | collective-permute-start | bytes 393224 | tf_op jit(solution)/shard_map/ppermute | solution.py:18
  24.2 8.6 %collective-permute-start.4 = (bf16[128,512]{1,0:T(8,128)(2,1)}, bf16[128,512]{1,0:T(8,128)(2,1)S(1)}, u32[]{:S(2)}, u32[]{:S(2)}) collective-permute-start(bf16[128,512]{1,0:T(8,128)(2,1)} %get-tuple-element.11), channel_id=1, source_target_pairs={{4,0},{6,2},{5,1},{7,3},{12,8},{14,10},{13,9},{15,11},{20,16},{22,... | collective-permute-start | bytes 393224 | tf_op jit(solution)/shard_map/ppermute | solution.py:18
  25.5 7.3 %collective-permute-start.3 = (bf16[128,512]{1,0:T(8,128)(2,1)}, bf16[128,512]{1,0:T(8,128)(2,1)S(1)}, u32[]{:S(2)}, u32[]{:S(2)}) collective-permute-start(bf16[128,512]{1,0:T(8,128)(2,1)} %get-tuple-element.10), channel_id=1, source_target_pairs={{2,0},{4,2},{6,4},{3,1},{5,3},{7,5},{10,8},{12,10},{14,12},{11,9},... | collective-permute-start | bytes 393224 | tf_op jit(solution)/shard_map/ppermute | solution.py:18
  26.8 7.6 %copy-start.2 = (bf16[1,5120,256]{2,1,0:T(8,128)(2,1)S(1)}, bf16[1,5120,256]{2,1,0:T(8,128)(2,1)}, u32[]{:S(2)}) copy-start(bf16[1,5120,256]{2,1,0:T(8,128)(2,1)} %param.9) | copy-start | bytes 7864324
  35.8 2.3 %collective-permute-start.6 = (bf16[128,2560]{1,0:T(8,128)(2,1)}, bf16[128,2560]{1,0:T(8,128)(2,1)S(1)}, u32[]{:S(2)}, u32[]{:S(2)}) collective-permute-start(bf16[128,2560]{1,0:T(8,128)(2,1)} %fusion.1), channel_id=1, source_target_pairs={{0,1},{1,0},{2,3},{3,2},{4,5},{5,4},{6,7},{7,6},{8,9},{9,8},{10,11... | collective-permute-start | bytes 1966088 | tf_op jit(solution)/shard_map/ppermute | solution.py:157
  35.8 2.3 %copy-start.3 = (bf16[1,5120,256]{2,1,0:T(8,128)(2,1)S(1)}, bf16[1,5120,256]{2,1,0:T(8,128)(2,1)}, u32[]{:S(2)}) copy-start(bf16[1,5120,256]{2,1,0:T(8,128)(2,1)} %param.9) | copy-start | bytes 7864324
  38.8 11.6 %collective-permute-start.7 = (bf16[64,2560]{1,0:T(8,128)(2,1)S(1)}, bf16[64,2560]{1,0:T(8,128)(2,1)S(1)}, u32[]{:S(2)}, u32[]{:S(2)}) collective-permute-start(bf16[64,2560]{1,0:T(8,128)(2,1)S(1)} %slice.76), channel_id=1, source_target_pairs={{8,0},{16,8},{24,16},{9,1},{17,9},{25,17},{10,2},{18,10},{26,18},{... | collective-permute-start | bytes 983048 | tf_op jit(solution)/shard_map/ppermute | solution.py:37
  50.5 10.8 %collective-permute-start.8 = (bf16[64,2560]{1,0:T(8,128)(2,1)S(1)}, bf16[64,2560]{1,0:T(8,128)(2,1)S(1)}, u32[]{:S(2)}, u32[]{:S(2)}) collective-permute-start(bf16[64,2560]{1,0:T(8,128)(2,1)S(1)} %fusion.36), channel_id=1, source_target_pairs={{8,0},{16,8},{24,16},{9,1},{17,9},{25,17},{10,2},{18,10},{26,18},{... | collective-permute-start | bytes 983048 | tf_op jit(solution)/shard_map/ppermute | solution.py:37
  61.3 9.9 %collective-permute-start.9 = (bf16[64,2560]{1,0:T(8,128)(2,1)S(1)}, bf16[64,2560]{1,0:T(8,128)(2,1)S(1)}, u32[]{:S(2)}, u32[]{:S(2)}) collective-permute-start(bf16[64,2560]{1,0:T(8,128)(2,1)S(1)} %fusion.37), channel_id=1, source_target_pairs={{8,0},{16,8},{24,16},{9,1},{17,9},{25,17},{10,2},{18,10},{26,18},{... | collective-permute-start | bytes 983048 | tf_op jit(solution)/shard_map/ppermute | solution.py:37
  71.3 9.1 %collective-permute-start.10 = (bf16[64,2560]{1,0:T(8,128)(2,1)S(1)}, bf16[64,2560]{1,0:T(8,128)(2,1)S(1)}, u32[]{:S(2)}, u32[]{:S(2)}) collective-permute-start(bf16[64,2560]{1,0:T(8,128)(2,1)S(1)} %fusion.38), channel_id=1, source_target_pairs={{8,0},{16,8},{24,16},{9,1},{17,9},{25,17},{10,2},{18,10},{26,18},{... | collective-permute-start | bytes 983048 | tf_op jit(solution)/shard_map/ppermute | solution.py:37

commit v21 on v20

--- a/solution.py
+++ b/solution.py
@@ -35,9 +35,13 @@
         done.append(acc)
         if tau < steps - 1:
             recv = lax.ppermute(acc.astype(jnp.bfloat16), axis, perm)
-    stacked = jnp.stack(done, axis=0)
-    mine = lax.dynamic_slice_in_dim(stacked, length - 1 - index, n_chunks, axis=0)
-    return mine.reshape(rows, cols)
+    mine = [
+        lax.dynamic_index_in_dim(
+            jnp.stack(done[k : k + length], axis=0), length - 1 - index, 0, keepdims=False
+        )
+        for k in range(n_chunks)
+    ]
+    return jnp.concatenate(mine, axis=0)
 
 
 def attention_terms(q3, g3, kv_blocks, lower, upper, kv_local, head_dim, scaling):

time: 82 us -> 87.6 us (1.068)
  other arithmetic: 3.46 us -> 8.25 us
  local copies, waits for them, and re-layouts: 4.4 us -> 3.09 us
  waiting for transfers between devices: 43.4 us -> 44.6 us
    dot_general x1, matrix products: 0.51 us -> 2.79 us  [per_device(): jnp.dot(tokens, w_key[0], preferred_element_type=jnp.float32)]
    convert_element_type x3, other arithmetic: 0.19 us -> 2.39 us  [suffix_pipeline(): recv = lax.ppermute(acc.astype(jnp.bfloat16), axis, perm)]
    ppermute x6, waiting for transfers between devices: 6.86 us -> 8.69 us  [shifted(): return lax.ppermute(x, axis, perm)]
    dot_general x1, matrix products: 2.02 us -> 0.51 us  [per_device(): jnp.dot(tokens, w_value[0], preferred_element_type=jnp.float32)]
    unnamed x23 -> x26, local copies, waits for them, and re-layouts: 2.65 us -> 1.37 us
    dynamic_slice x1 -> x0, local copies, waits for them, and re-layouts: 1.16 us -> none  [suffix_pipeline(): lax.dynamic_slice_in_dim(stacked, length - 1 - index, n_chunks, axis=0)]
    broadcast_in_dim x0 -> x1, other arithmetic: none -> 1.15 us  [per_device(): return result[None]]
    squeeze x0 -> x1, local copies, waits for them, and re-layouts: none -> 1.13 us  [suffix_pipeline(): acc = (chunks[0] if tau == 0 else ordered[tau]) + recv.astype(jnp.float32)]
  transfers between devices with their start and end apart: 11 -> 11, of which waited for: 9 -> 10; matrix products, arithmetic and copies ran while one was open for 4% -> 5% of each run, Pallas kernels for 0% -> 0%
where the time goes in v21:
time: 87.6 us; the launch traced here: 87.1 us
  waiting for transfers between devices  44.6 us (51%)
  starting transfers between devices  18.6 us (21%)
  other arithmetic  8.25 us (9%)
  matrix products  6.41 us (7%)
  Pallas kernels  5.77 us (7%)
  local copies, waits for them, and re-layouts  3.09 us (4%)
    ppermute x4, waiting for transfers between devices, suffix_pipeline(): recv = lax.ppermute(acc.astype(jnp.bfloat16), axis, perm)  34.2 us
    ppermute x6, starting transfers between devices, shifted(): return lax.ppermute(x, axis, perm)  13.5 us
    ppermute x6, waiting for transfers between devices, shifted(): return lax.ppermute(x, axis, perm)  8.69 us
    pallas_call x1, Pallas kernels, attention_terms(): pl.pallas_call(kernel, out_shape=(jax.ShapeDtypeStruct((tok_rows, 2 * kv_...  5.77 us
    ppermute x4, starting transfers between devices, suffix_pipeline(): recv = lax.ppermute(acc.astype(jnp.bfloat16), axis, perm)  5.16 us
    dot_general x1, matrix products, per_device(): jnp.dot(tokens, w_key[0], preferred_element_type=jnp.float32)  2.79 us
    convert_element_type x3, other arithmetic, suffix_pipeline(): recv = lax.ppermute(acc.astype(jnp.bfloat16), axis, perm)  2.39 us
    dot_general x2, matrix products, partial_for(): lax.dot_general(grad_key, wk, contract, preferred_element_type=jnp.float32)  1.99 us
  transfers between devices with their start and end apart: 11, of which 10 were waited for; matrix products, arithmetic and copies ran while one was open for 5% of the time, Pallas kernels for 0%

profile of v21, /device:TPU:0, one launch (start us, length us, event | category | flops | bytes accessed | tf_op | source)
XLA Modules:
  0.0 87.1 jit_solution(5313367857314004860)
XLA Ops:
  0.0 0.0 copy-start
  0.0 0.0 copy-start.5
  0.0 2.8 %fusion.20 = bf16[128,256]{1,0:T(8,128)(2,1)S(1)} fusion(bf16[1,5120,256]{2,1,0:T(8,128)(2,1)} %param.9, bf16[1,128,5120]{2,1,0:T(8,128)(2,1)} %param.6), kind=kOutput, calls=%fused_computation.34 | convolution fusion | flops 335577088 | bytes 3997696 | tf_op jit(solution)/shard_map/dot_general | solution.py:112
  2.8 0.1 copy-done
  2.9 0.4 copy-done.5
  3.3 0.5 fusion.25
  3.8 0.0 copy-start.7
  3.8 4.9 %collective-permute-start = (bf16[128,512]{1,0:T(8,128)(2,1)S(1)}, bf16[128,512]{1,0:T(8,128)(2,1)S(1)}, u32[]{:S(2)}, u32[]{:S(2)}) collective-permute-start(bf16[128,512]{1,0:T(8,128)(2,1)S(1)} %pad_maximum_fusion.refs_2_), channel_id=1, source_target_pairs={{0,2},{2,4},{4,6},{1,3},{3,5},{5,7},{8,10},{10,12},{12,14},{9,11},... | collective-permute-start | bytes 393224 | tf_op jit(solution)/shard_map/ppermute | solution.py:18
  8.7 3.4 %collective-permute-start.1 = (bf16[128,512]{1,0:T(8,128)(2,1)S(1)}, bf16[128,512]{1,0:T(8,128)(2,1)S(1)}, u32[]{:S(2)}, u32[]{:S(2)}) collective-permute-start(bf16[128,512]{1,0:T(8,128)(2,1)S(1)} %pad_maximum_fusion.refs_2_), channel_id=1, source_target_pairs={{0,4},{2,6},{1,5},{3,7},{8,12},{10,14},{9,13},{11,15},{16,20},{18,... | collective-permute-start | bytes 393224 | tf_op jit(solution)/shard_map/ppermute | solution.py:18
  12.2 1.3 %collective-permute-start.2 = (bf16[128,512]{1,0:T(8,128)(2,1)S(1)}, bf16[128,512]{1,0:T(8,128)(2,1)S(1)}, u32[]{:S(2)}, u32[]{:S(2)}) collective-permute-start(bf16[128,512]{1,0:T(8,128)(2,1)S(1)} %pad_maximum_fusion.refs_2_), channel_id=1, source_target_pairs={{0,6},{1,7},{8,14},{9,15},{16,22},{17,23},{24,30},{25,31}} | collective-permute-start | bytes 393224 | tf_op jit(solution)/shard_map/ppermute | solution.py:18
  13.5 0.0 copy-done.11
  13.5 0.2 copy.25
  13.7 0.1 fusion.59
  13.8 0.1 fusion.57
  13.9 0.2 copy.24
  14.0 0.2 copy.28
  14.2 0.8 broadcast_select_fusion
  15.1 0.0 collective-permute-done.refs_3_
  15.1 0.1 collective-permute-done.1.refs_4_
  15.2 0.8 collective-permute-done.2.refs_5_
  16.0 0.0 copy-done.7
  16.0 0.0 copy-done.8
  16.0 0.0 copy-done.9
  16.0 0.6 copy-done.10
  16.6 5.8 %shard_map.64 = (f32[128,512]{1,0:T(8,128)}, bf16[128,512]{1,0:T(8,128)(2,1)}, bf16[128,512]{1,0:T(8,128)(2,1)}, bf16[128,512]{1,0:T(8,128)(2,1)}) custom-call(bf16[10,128,128]{2,1,0:T(8,128)(2,1)} %bitcast.103, bf16[10,128,128]{2,1,0:T(8,128)(2,1)} %bitcast.104, bf16[128,512]{1,0:T(8,128)(2,1)} %copy-done.7, bf16[128,512]{1,0:T(8,128)(2,1)} %copy-done.8, ...), custom_call_target="tpu_custom_call" | custom-call | tf_op jit(solution)/shard_map/pallas_call | solution.py:92
  22.4 1.3 %collective-permute-start.3 = (bf16[128,512]{1,0:T(8,128)(2,1)}, bf16[128,512]{1,0:T(8,128)(2,1)S(1)}, u32[]{:S(2)}, u32[]{:S(2)}) collective-permute-start(bf16[128,512]{1,0:T(8,128)(2,1)} %get-tuple-element.10), channel_id=1, source_target_pairs={{2,0},{4,2},{6,4},{3,1},{5,3},{7,5},{10,8},{12,10},{14,12},{11,9},... | collective-permute-start | bytes 393224 | tf_op jit(solution)/shard_map/ppermute | solution.py:18
  23.7 1.3 %collective-permute-start.4 = (bf16[128,512]{1,0:T(8,128)(2,1)}, bf16[128,512]{1,0:T(8,128)(2,1)S(1)}, u32[]{:S(2)}, u32[]{:S(2)}) collective-permute-start(bf16[128,512]{1,0:T(8,128)(2,1)} %get-tuple-element.11), channel_id=1, source_target_pairs={{4,0},{6,2},{5,1},{7,3},{12,8},{14,10},{13,9},{15,11},{20,16},{22,... | collective-permute-start | bytes 393224 | tf_op jit(solution)/shard_map/ppermute | solution.py:18
  25.0 1.3 %collective-permute-start.5 = (bf16[128,512]{1,0:T(8,128)(2,1)}, bf16[128,512]{1,0:T(8,128)(2,1)S(1)}, u32[]{:S(2)}, u32[]{:S(2)}) collective-permute-start(bf16[128,512]{1,0:T(8,128)(2,1)} %get-tuple-element.12), channel_id=1, source_target_pairs={{6,0},{7,1},{14,8},{15,9},{22,16},{23,17},{30,24},{31,25}} | collective-permute-start | bytes 393224 | tf_op jit(solution)/shard_map/ppermute | solution.py:18
  26.3 0.0 copy-start.2
  26.3 3.1 %collective-permute-done.3 = bf16[128,512]{1,0:T(8,128)(2,1)S(1)} collective-permute-done((bf16[128,512]{1,0:T(8,128)(2,1)}, bf16[128,512]{1,0:T(8,128)(2,1)S(1)}, u32[]{:S(2)}, u32[]{:S(2)}) %collective-permute-start.3) | collective-permute-done | bytes 131104 | tf_op jit(solution)/shard_map/ppermute | solution.py:18
  29.4 1.8 %collective-permute-done.4 = bf16[128,512]{1,0:T(8,128)(2,1)S(1)} collective-permute-done((bf16[128,512]{1,0:T(8,128)(2,1)}, bf16[128,512]{1,0:T(8,128)(2,1)S(1)}, u32[]{:S(2)}, u32[]{:S(2)}) %collective-permute-start.4) | collective-permute-done | bytes 131104 | tf_op jit(solution)/shard_map/ppermute | solution.py:18
  31.2 2.9 %collective-permute-done.5 = bf16[128,512]{1,0:T(8,128)(2,1)S(1)} collective-permute-done((bf16[128,512]{1,0:T(8,128)(2,1)}, bf16[128,512]{1,0:T(8,128)(2,1)S(1)}, u32[]{:S(2)}, u32[]{:S(2)}) %collective-permute-start.5) | collective-permute-done | bytes 131104 | tf_op jit(solution)/shard_map/ppermute | solution.py:18
  34.1 1.0 %add_convert_fusion = bf16[128,512]{1,0:T(8,128)(2,1)S(1)} fusion(bf16[128,512]{1,0:T(8,128)(2,1)S(1)} %collective-permute-done.5, bf16[128,512]{1,0:T(8,128)(2,1)S(1)} %collective-permute-done.4, f32[128,512]{1,0:T(8,128)} %get-tuple-element.9, bf16[128,512]{1,0:T(8,128)(2,1)S(1)} %collective-permute-done.3), kind=kLoop, calls=%fused_computation.61 | loop fusion | flops 458752 | bytes 786432 | tf_op jit(solution)/shard_map/convert.1
  35.1 0.6 fusion.8
  35.7 0.0 copy-done.2
  35.7 1.4 %fusion.1 = bf16[128,2560]{1,0:T(8,128)(2,1)} fusion(f32[128,2560]{1,0:T(8,128)S(1)} %fusion.8, bf16[1,5120,256]{2,1,0:T(8,128)(2,1)S(1)} %copy-done.2, s32[]{:T(128)S(6)} %select_n.32, bf16[128,512]{1,0:T(8,128)(2,1)S(1)} %add_convert_fusion), kind=kOutput, calls=%fused_computation.6 | convolution fusion | flops 168427520 | bytes 3342340 | tf_op jit(solution)/shard_map/dot_general | solution.py:153
  37.1 0.0 collective-permute-start.6
  37.1 0.6 fusion.11
  37.7 1.7 %collective-permute-done.6 = bf16[128,2560]{1,0:T(8,128)(2,1)S(1)} collective-permute-done((bf16[128,2560]{1,0:T(8,128)(2,1)}, bf16[128,2560]{1,0:T(8,128)(2,1)S(1)}, u32[]{:S(2)}, u32[]{:S(2)}) %collective-permute-start.6) | collective-permute-done | bytes 655392 | tf_op jit(solution)/shard_map/ppermute | solution.py:161
  39.4 0.0 copy-done.3
  39.4 0.6 fusion
  40.0 0.0 copy-start.4
  40.1 1.3 %collective-permute-start.7 = (bf16[64,2560]{1,0:T(8,128)(2,1)S(1)}, bf16[64,2560]{1,0:T(8,128)(2,1)S(1)}, u32[]{:S(2)}, u32[]{:S(2)}) collective-permute-start(bf16[64,2560]{1,0:T(8,128)(2,1)S(1)} %slice.74), channel_id=1, source_target_pairs={{8,0},{16,8},{24,16},{9,1},{17,9},{25,17},{10,2},{18,10},{26,18},{... | collective-permute-start | bytes 983048 | tf_op jit(solution)/shard_map/ppermute | solution.py:37
  41.4 0.2 broadcast_in_dim.16
  41.6 1.0 %fusion.3 = f32[5,64,2560]{2,1,0:T(8,128)S(1)} fusion(s32[]{:T(128)S(6)} %select_n.33, f32[3,64,2560]{2,1,0:T(8,128)S(1)} %broadcast_in_dim.16, f32[2,64,2560]{2,1,0:T(8,128)S(1)} %bitcast.102), kind=kLoop, calls=%fused_computation.8 | loop fusion | flops 1638400 | bytes 6553604 | tf_op jit(solution)/shard_map/concatenate | solution.py:27
  42.6 0.0 copy-done.4
  42.6 0.0 copy-start.1
  42.6 9.1 %collective-permute-done.7 = bf16[64,2560]{1,0:T(8,128)(2,1)S(1)} collective-permute-done((bf16[64,2560]{1,0:T(8,128)(2,1)S(1)}, bf16[64,2560]{1,0:T(8,128)(2,1)S(1)}, u32[]{:S(2)}, u32[]{:S(2)}) %collective-permute-start.7) | collective-permute-done | bytes 327712 | tf_op jit(solution)/shard_map/ppermute | solution.py:37
  51.7 0.1 fusion.43
  51.8 1.3 %collective-permute-start.8 = (bf16[64,2560]{1,0:T(8,128)(2,1)S(1)}, bf16[64,2560]{1,0:T(8,128)(2,1)S(1)}, u32[]{:S(2)}, u32[]{:S(2)}) collective-permute-start(bf16[64,2560]{1,0:T(8,128)(2,1)S(1)} %get-tuple-element.17), channel_id=1, source_target_pairs={{8,0},{16,8},{24,16},{9,1},{17,9},{25,17},{10,2},{18,10},{26,18},{... | collective-permute-start | bytes 983048 | tf_op jit(solution)/shard_map/ppermute | solution.py:37
  53.1 9.5 %collective-permute-done.8 = bf16[64,2560]{1,0:T(8,128)(2,1)S(1)} collective-permute-done((bf16[64,2560]{1,0:T(8,128)(2,1)S(1)}, bf16[64,2560]{1,0:T(8,128)(2,1)S(1)}, u32[]{:S(2)}, u32[]{:S(2)}) %collective-permute-start.8) | collective-permute-done | bytes 327712 | tf_op jit(solution)/shard_map/ppermute | solution.py:37
  62.6 0.0 copy-done.1
  62.6 1.0 %fusion.45 = (bf16[64,2560]{1,0:T(8,128)(2,1)}, f32[1,64,2560]{2,1,0:T(8,128)}) fusion(bf16[64,2560]{1,0:T(8,128)(2,1)S(1)} %collective-permute-done.8, f32[5,64,2560]{2,1,0:T(8,128)S(1)} %fusion.3), kind=kLoop, calls=%fused_computation.57 | loop fusion | flops 491520 | bytes 1966080 | tf_op jit(solution)/shard_map/convert_element_type | solution.py:37
  63.6 1.3 %collective-permute-start.9 = (bf16[64,2560]{1,0:T(8,128)(2,1)}, bf16[64,2560]{1,0:T(8,128)(2,1)}, u32[]{:S(2)}, u32[]{:S(2)}) collective-permute-start(bf16[64,2560]{1,0:T(8,128)(2,1)} %get-tuple-element.15), channel_id=1, source_target_pairs={{8,0},{16,8},{24,16},{9,1},{17,9},{25,17},{10,2},{18,10},{26,18},{... | collective-permute-start | bytes 983048 | tf_op jit(solution)/shard_map/ppermute | solution.py:37
  64.9 0.0 copy-start.6
  64.9 8.9 %collective-permute-done.9 = bf16[64,2560]{1,0:T(8,128)(2,1)} collective-permute-done((bf16[64,2560]{1,0:T(8,128)(2,1)}, bf16[64,2560]{1,0:T(8,128)(2,1)}, u32[]{:S(2)}, u32[]{:S(2)}) %collective-permute-start.9) | collective-permute-done | bytes 327712 | tf_op jit(solution)/shard_map/ppermute | solution.py:37
  73.9 1.3 %fusion.47 = (bf16[64,2560]{1,0:T(8,128)(2,1)S(1)}, f32[1,64,2560]{2,1,0:T(8,128)S(1)}) fusion(bf16[64,2560]{1,0:T(8,128)(2,1)} %collective-permute-done.9, f32[5,64,2560]{2,1,0:T(8,128)} %copy-done.1), kind=kLoop, calls=%fused_computation.59 | loop fusion | flops 491520 | bytes 1966080 | tf_op jit(solution)/shard_map/convert_element_type | solution.py:37
  75.1 1.3 %collective-permute-start.10 = (bf16[64,2560]{1,0:T(8,128)(2,1)S(1)}, bf16[64,2560]{1,0:T(8,128)(2,1)S(1)}, u32[]{:S(2)}, u32[]{:S(2)}) collective-permute-start(bf16[64,2560]{1,0:T(8,128)(2,1)S(1)} %get-tuple-element.13), channel_id=1, source_target_pairs={{8,0},{16,8},{24,16},{9,1},{17,9},{25,17},{10,2},{18,10},{26,18},{... | collective-permute-start | bytes 983048 | tf_op jit(solution)/shard_map/ppermute | solution.py:37
  76.4 1.1 %slice_bitcast_fusion.4 = f32[1,64,2560]{2,1,0:T(8,128)S(1)} fusion(f32[128,2560]{1,0:T(8,128)} %copy-done.4), kind=kLoop, calls=%fused_computation.54 | loop fusion | bytes 1310720 | tf_op jit(solution)/shard_map/squeeze | solution.py:34
  77.6 6.6 %collective-permute-done.10 = bf16[64,2560]{1,0:T(8,128)(2,1)S(1)} collective-permute-done((bf16[64,2560]{1,0:T(8,128)(2,1)S(1)}, bf16[64,2560]{1,0:T(8,128)(2,1)S(1)}, u32[]{:S(2)}, u32[]{:S(2)}) %collective-permute-start.10) | collective-permute-done | bytes 327712 | tf_op jit(solution)/shard_map/ppermute | solution.py:37
  84.2 1.2 %fusion.39 = f32[1,64,2560]{2,1,0:T(8,128)S(1)} fusion(f32[5,64,2560]{2,1,0:T(8,128)} %copy-done.1, bf16[64,2560]{1,0:T(8,128)(2,1)S(1)} %collective-permute-done.10), kind=kLoop, calls=%fused_computation.46 | loop fusion | flops 327680 | bytes 1638400 | tf_op jit(solution)/shard_map/stack | solution.py:40
  85.4 0.0 copy-done.6
  85.4 0.5 fusion.37
  85.9 1.1 %maximum_bitcast_fusion = f32[1,128,2560]{2,1,0:T(8,128)} fusion(f32[64,2560]{1,0:T(8,128)S(1)} %get-tuple-element.20, f32[64,2560]{1,0:T(8,128)S(1)} %get-tuple-element.19), kind=kLoop, calls=%fused_computation.21 | loop fusion | flops 327680 | bytes 2621440 | tf_op jit(solution)/shard_map/broadcast_in_dim | solution.py:166
  (11 shorter events, 0.1 us)
Async XLA Ops:
  0.0 2.9 %copy-start = (bf16[1,5120,256]{2,1,0:T(8,128)(2,1)S(1)}, bf16[1,5120,256]{2,1,0:T(8,128)(2,1)}, u32[]{:S(2)}) copy-start(bf16[1,5120,256]{2,1,0:T(8,128)(2,1)} %param.10) | copy-start | bytes 7864324
  0.0 3.3 %copy-start.5 = (bf16[1,128,5120]{2,1,0:T(8,128)(2,1)S(1)}, bf16[1,128,5120]{2,1,0:T(8,128)(2,1)}, u32[]{:S(2)}) copy-start(bf16[1,128,5120]{2,1,0:T(8,128)(2,1)} %param.6) | copy-start | bytes 3932164
  3.3 10.2 %copy-start.11 = (s32[512]{0:T(512)S(1)}, s32[512]{0:T(512)}, u32[]{:S(2)}) copy-start(s32[512]{0:T(512)} %param.11) | copy-start | bytes 6148
  3.8 12.1 %copy-start.7 = (bf16[128,512]{1,0:T(8,128)(2,1)}, bf16[128,512]{1,0:T(8,128)(2,1)S(1)}, u32[]{:S(2)}) copy-start(bf16[128,512]{1,0:T(8,128)(2,1)S(1)} %pad_maximum_fusion.refs_2_) | copy-start | bytes 393220
  3.8 11.3 %collective-permute-start = (bf16[128,512]{1,0:T(8,128)(2,1)S(1)}, bf16[128,512]{1,0:T(8,128)(2,1)S(1)}, u32[]{:S(2)}, u32[]{:S(2)}) collective-permute-start(bf16[128,512]{1,0:T(8,128)(2,1)S(1)} %pad_maximum_fusion.refs_2_), channel_id=1, source_target_pairs={{0,2},{2,4},{4,6},{1,3},{3,5},{5,7},{8,10},{10,12},{12,14},{9,11},... | collective-permute-start | bytes 393224 | tf_op jit(solution)/shard_map/ppermute | solution.py:18
  8.7 6.5 %collective-permute-start.1 = (bf16[128,512]{1,0:T(8,128)(2,1)S(1)}, bf16[128,512]{1,0:T(8,128)(2,1)S(1)}, u32[]{:S(2)}, u32[]{:S(2)}) collective-permute-start(bf16[128,512]{1,0:T(8,128)(2,1)S(1)} %pad_maximum_fusion.refs_2_), channel_id=1, source_target_pairs={{0,4},{2,6},{1,5},{3,7},{8,12},{10,14},{9,13},{11,15},{16,20},{18,... | collective-permute-start | bytes 393224 | tf_op jit(solution)/shard_map/ppermute | solution.py:18
  12.2 3.8 %collective-permute-start.2 = (bf16[128,512]{1,0:T(8,128)(2,1)S(1)}, bf16[128,512]{1,0:T(8,128)(2,1)S(1)}, u32[]{:S(2)}, u32[]{:S(2)}) collective-permute-start(bf16[128,512]{1,0:T(8,128)(2,1)S(1)} %pad_maximum_fusion.refs_2_), channel_id=1, source_target_pairs={{0,6},{1,7},{8,14},{9,15},{16,22},{17,23},{24,30},{25,31}} | collective-permute-start | bytes 393224 | tf_op jit(solution)/shard_map/ppermute | solution.py:18
  15.1 0.9 copy-start.8
  15.2 0.8 copy-start.9
  16.0 0.7 copy-start.10
  22.4 7.1 %collective-permute-start.3 = (bf16[128,512]{1,0:T(8,128)(2,1)}, bf16[128,512]{1,0:T(8,128)(2,1)S(1)}, u32[]{:S(2)}, u32[]{:S(2)}) collective-permute-start(bf16[128,512]{1,0:T(8,128)(2,1)} %get-tuple-element.10), channel_id=1, source_target_pairs={{2,0},{4,2},{6,4},{3,1},{5,3},{7,5},{10,8},{12,10},{14,12},{11,9},... | collective-permute-start | bytes 393224 | tf_op jit(solution)/shard_map/ppermute | solution.py:18
  23.7 7.6 %collective-permute-start.4 = (bf16[128,512]{1,0:T(8,128)(2,1)}, bf16[128,512]{1,0:T(8,128)(2,1)S(1)}, u32[]{:S(2)}, u32[]{:S(2)}) collective-permute-start(bf16[128,512]{1,0:T(8,128)(2,1)} %get-tuple-element.11), channel_id=1, source_target_pairs={{4,0},{6,2},{5,1},{7,3},{12,8},{14,10},{13,9},{15,11},{20,16},{22,... | collective-permute-start | bytes 393224 | tf_op jit(solution)/shard_map/ppermute | solution.py:18
  25.0 9.2 %collective-permute-start.5 = (bf16[128,512]{1,0:T(8,128)(2,1)}, bf16[128,512]{1,0:T(8,128)(2,1)S(1)}, u32[]{:S(2)}, u32[]{:S(2)}) collective-permute-start(bf16[128,512]{1,0:T(8,128)(2,1)} %get-tuple-element.12), channel_id=1, source_target_pairs={{6,0},{7,1},{14,8},{15,9},{22,16},{23,17},{30,24},{31,25}} | collective-permute-start | bytes 393224 | tf_op jit(solution)/shard_map/ppermute | solution.py:18
  26.3 9.4 %copy-start.2 = (bf16[1,5120,256]{2,1,0:T(8,128)(2,1)S(1)}, bf16[1,5120,256]{2,1,0:T(8,128)(2,1)}, u32[]{:S(2)}) copy-start(bf16[1,5120,256]{2,1,0:T(8,128)(2,1)} %param.9) | copy-start | bytes 7864324
  37.1 2.3 %collective-permute-start.6 = (bf16[128,2560]{1,0:T(8,128)(2,1)}, bf16[128,2560]{1,0:T(8,128)(2,1)S(1)}, u32[]{:S(2)}, u32[]{:S(2)}) collective-permute-start(bf16[128,2560]{1,0:T(8,128)(2,1)} %fusion.1), channel_id=1, source_target_pairs={{0,1},{1,0},{2,3},{3,2},{4,5},{5,4},{6,7},{7,6},{8,9},{9,8},{10,11... | collective-permute-start | bytes 1966088 | tf_op jit(solution)/shard_map/ppermute | solution.py:161
  37.1 2.3 %copy-start.3 = (bf16[1,5120,256]{2,1,0:T(8,128)(2,1)S(1)}, bf16[1,5120,256]{2,1,0:T(8,128)(2,1)}, u32[]{:S(2)}) copy-start(bf16[1,5120,256]{2,1,0:T(8,128)(2,1)} %param.9) | copy-start | bytes 7864324
  40.0 2.6 %copy-start.4 = (f32[128,2560]{1,0:T(8,128)}, f32[128,2560]{1,0:T(8,128)S(1)}, u32[]{:S(2)}) copy-start(f32[128,2560]{1,0:T(8,128)S(1)} %fusion) | copy-start | bytes 3932164
  40.1 11.6 %collective-permute-start.7 = (bf16[64,2560]{1,0:T(8,128)(2,1)S(1)}, bf16[64,2560]{1,0:T(8,128)(2,1)S(1)}, u32[]{:S(2)}, u32[]{:S(2)}) collective-permute-start(bf16[64,2560]{1,0:T(8,128)(2,1)S(1)} %slice.74), channel_id=1, source_target_pairs={{8,0},{16,8},{24,16},{9,1},{17,9},{25,17},{10,2},{18,10},{26,18},{... | collective-permute-start | bytes 983048 | tf_op jit(solution)/shard_map/ppermute | solution.py:37
  42.6 20.0 %copy-start.1 = (f32[5,64,2560]{2,1,0:T(8,128)}, f32[5,64,2560]{2,1,0:T(8,128)S(1)}, u32[]{:S(2)}) copy-start(f32[5,64,2560]{2,1,0:T(8,128)S(1)} %fusion.3) | copy-start | bytes 9830404
  51.8 10.8 %collective-permute-start.8 = (bf16[64,2560]{1,0:T(8,128)(2,1)S(1)}, bf16[64,2560]{1,0:T(8,128)(2,1)S(1)}, u32[]{:S(2)}, u32[]{:S(2)}) collective-permute-start(bf16[64,2560]{1,0:T(8,128)(2,1)S(1)} %get-tuple-element.17), channel_id=1, source_target_pairs={{8,0},{16,8},{24,16},{9,1},{17,9},{25,17},{10,2},{18,10},{26,18},{... | collective-permute-start | bytes 983048 | tf_op jit(solution)/shard_map/ppermute | solution.py:37
  63.6 10.2 %collective-permute-start.9 = (bf16[64,2560]{1,0:T(8,128)(2,1)}, bf16[64,2560]{1,0:T(8,128)(2,1)}, u32[]{:S(2)}, u32[]{:S(2)}) collective-permute-start(bf16[64,2560]{1,0:T(8,128)(2,1)} %get-tuple-element.15), channel_id=1, source_target_pairs={{8,0},{16,8},{24,16},{9,1},{17,9},{25,17},{10,2},{18,10},{26,18},{... | collective-permute-start | bytes 983048 | tf_op jit(solution)/shard_map/ppermute | solution.py:37
  64.9 20.5 %copy-start.6 = (f32[1,64,2560]{2,1,0:T(8,128)S(1)}, f32[1,64,2560]{2,1,0:T(8,128)}, u32[]{:S(2)}) copy-start(f32[1,64,2560]{2,1,0:T(8,128)} %get-tuple-element.16) | copy-start | bytes 1966084
  75.1 9.1 %collective-permute-start.10 = (bf16[64,2560]{1,0:T(8,128)(2,1)S(1)}, bf16[64,2560]{1,0:T(8,128)(2,1)S(1)}, u32[]{:S(2)}, u32[]{:S(2)}) collective-permute-start(bf16[64,2560]{1,0:T(8,128)(2,1)S(1)} %get-tuple-element.13), channel_id=1, source_target_pairs={{8,0},{16,8},{24,16},{9,1},{17,9},{25,17},{10,2},{18,10},{26,18},{... | collective-permute-start | bytes 983048 | tf_op jit(solution)/shard_map/ppermute | solution.py:37
